TPU v7x, 32 devices: a whole 2x2x4 slice. The times are simulated.
32 devices in a mesh: dp: 8 (over z, y), seq: 4 (over x, core).
Axes of the slice: x: 2, y: 2, z: 4, core: 2. Of those that a mesh axis runs over, the one named last changes fastest.
Arguments:
- frames: bfloat16 [8, 512, 1536], P('dp', 'seq'), may hold values from -6 to 6
- lengths: int32 [8, 4], P('dp'), may hold values from 1 to 256, 512 in all within a row
- ln1_gain: float32 [1536], replicated, may hold values from 0.5 to 12
- ln2_gain: float32 [1536], replicated, may hold values from 0.5 to 1.5
- w_qkv: bfloat16 [1536, 3, 1536], P('dp', None, 'seq'), may hold values from -0.15625 to 0.15625
- w_out: bfloat16 [1536, 1536], P('seq', 'dp'), may hold values from -0.15625 to 0.15625
- w_glu: bfloat16 [1536, 2, 1536], P('dp', None, 'seq'), may hold values from -0.15625 to 0.15625
- dw_kernel: bfloat16 [31, 1536], P(None, 'seq'), may hold values from -1 to 1
- w_proj: bfloat16 [1536, 1536], P('seq', 'dp'), may hold values from -0.15625 to 0.15625
Outputs:
- block_out: bfloat16 [8, 512, 1536], P('dp', 'seq')
Inputs may be any that keep to these rules, and one draw needn't show every extreme that they name: `lengths`: each row sums to 512, and its largest entry is 256.
All inputs are finite; a program needn't handle non-finite values.
Results may differ from a plain program's by a relative error of at most 0.013.
The roundings to bfloat16 on the way count: a program that leaves them out, or rounds other values in their place, can miss the bound.
Values may be sent and summed in bfloat16 or wider, within the bound.
No kernel may reach another device: no remote copies, remote signals or barrier semaphores. Data moves between devices by JAX's collectives and lax.ppermute only.
A program may use at most 64 MiB of HBM per device.

v0:
```python
import jax
import jax.numpy as jnp
from jax import lax
from jax.sharding import PartitionSpec as P

HD = 96


def layer_norm(values, gain_vec):
    mean_value = jnp.mean(values, axis=-1, keepdims=True)
    centered = values - mean_value
    variance = jnp.mean(centered * centered, axis=-1, keepdims=True)
    return (centered * lax.rsqrt(variance + 1e-05) * gain_vec).astype(jnp.bfloat16)


def segment_of(record_ends, positions):
    return jnp.sum((positions[:, None] >= record_ends[None, :]).astype(jnp.int32), axis=1)


def attend(projected, seg_all, head_size):
    group_rows = projected.shape[0]
    block_rows = 512
    heads_here = projected.shape[2] // head_size
    split = projected.reshape(group_rows, 3, heads_here, head_size)
    queries = split[:, 0]
    keys = split[:, 1]
    values = split[:, 2]
    blocks = group_rows // block_rows
    scale = 1.0 / head_size**0.5

    def one_block(block_data):
        query_block, seg_block = block_data
        scores = (
            jnp.einsum("qhe,khe->hqk", query_block, keys, preferred_element_type=jnp.float32)
            * scale
        )
        allowed = seg_block[:, None] == seg_all[None, :]
        scores = jnp.where(allowed[None], scores, -1e30)
        top_score = jnp.max(scores, axis=-1, keepdims=True)
        weights = jnp.exp(scores - top_score)
        probs = (weights / jnp.sum(weights, axis=-1, keepdims=True)).astype(jnp.bfloat16)
        mixed = jnp.einsum("hqk,khe->qhe", probs, values, preferred_element_type=jnp.float32)
        return mixed.astype(jnp.bfloat16).reshape(block_rows, heads_here * head_size)

    result = lax.map(
        one_block,
        (
            queries.reshape(blocks, block_rows, heads_here, head_size),
            seg_all.reshape(blocks, block_rows),
        ),
    )
    return result.reshape(group_rows, heads_here * head_size)


def depthwise(padded, kernel, seg_here, seg_near, count):
    total_acc = jnp.zeros((count, padded.shape[1]), jnp.float32)
    for tap_index in range(kernel.shape[0]):
        window = padded[tap_index : tap_index + count].astype(jnp.float32)
        same = (seg_near[tap_index : tap_index + count] == seg_here)[:, None]
        total_acc = total_acc + jnp.where(same, window * kernel[tap_index].astype(jnp.float32), 0.0)
    return jax.nn.silu(total_acc).astype(jnp.bfloat16)


def on_device(frames, lengths, ln1_gain, ln2_gain, w_qkv, w_out, w_glu, dw_kernel, w_proj):
    frame_rows = frames.shape[1]
    model_width = frames.shape[2]
    seq_count = lax.axis_size("seq")
    group_rows = frame_rows * seq_count
    group_width = model_width // seq_count
    kernel_reach = dw_kernel.shape[0] // 2
    qkv_local = lax.all_gather(w_qkv, "dp", axis=0, tiled=True)
    out_local = lax.all_gather(w_out, "dp", axis=1, tiled=True)
    glu_local = lax.all_gather(w_glu, "dp", axis=0, tiled=True)
    proj_local = lax.all_gather(w_proj, "dp", axis=1, tiled=True)
    qkv_matrix = qkv_local.reshape(model_width, 3 * group_width)
    glu_matrix = glu_local.reshape(model_width, 2 * group_width)
    inputs = frames[0].astype(jnp.float32)
    record_ends = jnp.cumsum(lengths[0])
    seg_all = segment_of(record_ends, jnp.arange(group_rows, dtype=jnp.int32))
    normed1 = layer_norm(inputs, ln1_gain)
    projected = (
        jnp.dot(
            lax.all_gather(normed1, "seq", axis=0, tiled=True),
            qkv_matrix,
            preferred_element_type=jnp.float32,
        )
        .astype(jnp.bfloat16)
        .reshape(group_rows, 3, group_width)
    )
    attended = attend(projected, seg_all, HD)
    rows_here = attended
    attn_sum = lax.psum_scatter(
        jnp.dot(rows_here, out_local, preferred_element_type=jnp.float32)
        .astype(jnp.bfloat16)
        .astype(jnp.float32)
        .astype(jnp.bfloat16),
        "seq",
        scatter_dimension=0,
        tiled=True,
    ).astype(jnp.float32)
    middle = (inputs + attn_sum).astype(jnp.bfloat16)
    normed2 = layer_norm(middle.astype(jnp.float32), ln2_gain)
    shard_piece = lax.all_gather(normed2, "seq", axis=0, tiled=True)
    paired = jnp.dot(shard_piece, glu_matrix, preferred_element_type=jnp.float32).reshape(
        shard_piece.shape[0], 2, group_width
    )
    gated = (paired[:, 0] * jax.nn.sigmoid(paired[:, 1])).astype(jnp.bfloat16)
    padded = jnp.pad(gated, ((kernel_reach, kernel_reach), (0, 0)))
    near_positions = jnp.arange(-kernel_reach, group_rows + kernel_reach, dtype=jnp.int32)
    activated = depthwise(
        padded, dw_kernel, seg_all, segment_of(record_ends, near_positions), group_rows
    )
    rows_here = activated
    conv_out = lax.psum_scatter(
        jnp.dot(rows_here, proj_local, preferred_element_type=jnp.float32)
        .astype(jnp.bfloat16)
        .astype(jnp.float32)
        .astype(jnp.bfloat16),
        "seq",
        scatter_dimension=0,
        tiled=True,
    ).astype(jnp.float32)
    results = [(middle.astype(jnp.float32) + conv_out).astype(jnp.bfloat16)]
    return jnp.stack(results, axis=0)


def solution(mesh):
    in_specs = (
        P("dp", "seq", None),
        P("dp", None),
        P(),
        P(),
        P("dp", None, "seq"),
        P("seq", "dp"),
        P("dp", None, "seq"),
        P(None, "seq"),
        P("seq", "dp"),
    )
    out_specs = P("dp", "seq", None)
    return jax.shard_map(
        on_device, mesh=mesh, in_specs=in_specs, out_specs=out_specs, check_vma=False
    )
```

profile of v0, /device:TPU:0, one launch (start us, length us, event | category | flops | bytes accessed | tf_op | source)
XLA Modules:
  0.0 334.3 jit_solution(194160202395441783)
XLA Ops:
  6.5 0.7 all-gather.9.cloned.1.call-update
  7.3 0.0 all-gather.7.cloned.1.call-start
  7.3 1.1 convert_reduce_fusion.1
  8.4 1.2 fusion.19
  9.7 2.0 fusion.21
  11.7 0.0 all-gather.7.cloned.1.call-update
  11.8 0.0 all-gather.11.cloned.1.call-start
  11.8 0.7 all-gather.11.cloned.1.call-update
  12.5 0.0 reduce-scatter.3.cloned.1.call-start
  12.6 0.2 reduce-window.8
  12.7 0.1 convert_reduce_fusion.3
  12.8 0.2 broadcast_compare_fusion
  13.0 64.4 %all-gather.9.cloned.1.call-done = bf16[1536,3,384]{2,0,1:T(8,128)(2,1)} async-done(((bf16[192,3,384]{2,0,1:T(8,128)(2,1)}), bf16[1536,3,384]{2,0,1:T(8,128)(2,1)}) %all-gather.9.cloned.1.call-update) | async-done | bytes 3538960 | tf_op jit(solution)/shard_map/all_gather | solution.py:71
  77.5 6.1 %copy.23 = bf16[1536,3,384]{0,2,1:T(8,128)(2,1)} copy(bf16[1536,3,384]{2,0,1:T(8,128)(2,1)} %all-gather.9.cloned.1.call-done) | data formatting | bytes 7077888 | tf_op jit(solution)/shard_map/all_gather | solution.py:71
  83.6 13.6 %all-gather.7.cloned.1.call-done = bf16[512,1536]{1,0:T(8,128)(2,1)} async-done(((bf16[128,1536]{1,0:T(8,128)(2,1)}), bf16[512,1536]{1,0:T(8,128)(2,1)}) %all-gather.7.cloned.1.call-update) | async-done | bytes 1572880 | tf_op jit(solution)/shard_map/all_gather | solution.py:83
  97.2 4.7 %convolution_convert_fusion = bf16[512,1152]{1,0:T(8,128)(2,1)S(1)} fusion(bf16[512,1536]{1,0:T(8,128)(2,1)} %all-gather.7.cloned.1.call-done, bf16[1536,1152]{0,1:T(8,128)(2,1)} %bitcast.70), kind=kOutput, calls=%fused_computation.5 | convolution fusion | flops 1812529152 | bytes 6291456 | tf_op jit(solution)/shard_map/dot_general | solution.py:82
  101.9 0.6 copy.24
  102.5 3.6 %fusion.40 = (f32[4,512]{1,0:T(4,128)S(1)}, f32[4,512,512]{1,2,0:T(8,128)}) fusion(pred[512,512]{0,1:T(8,128)(4,1)S(1)} %broadcast_compare_fusion, bf16[512,3,4,96]{0,3,2,1:T(8,128)(2,1)S(1)} %bitcast.71), kind=kOutput, calls=%fused_computation.130 | convolution fusion | flops 205521408 | bytes 5251072 | tf_op jit(solution)/shard_map/while/body/eval_jaxpr/sub | solution.py:40
  106.2 2.8 fusion.9
  108.9 31.5 %all-gather.11.cloned.1.call-done = bf16[384,1536]{0,1:T(8,128)(2,1)} async-done(((bf16[384,192]{0,1:T(8,128)(2,1)}), bf16[384,1536]{0,1:T(8,128)(2,1)}) %all-gather.11.cloned.1.call-update) | async-done | bytes 1179664 | tf_op jit(solution)/shard_map/all_gather | solution.py:72
  140.5 3.5 %convolution_convert_fusion.2 = bf16[512,1536]{1,0:T(8,128)(2,1)} fusion(bf16[512,384]{0,1:T(8,128)(2,1)S(1)} %bitcast.73, bf16[384,1536]{0,1:T(8,128)(2,1)} %all-gather.11.cloned.1.call-done), kind=kOutput, calls=%fused_computation.7 | convolution fusion | flops 604766208 | bytes 3145728 | tf_op jit(solution)/shard_map/dot_general | solution.py:93
  144.0 0.0 reduce-scatter.3.cloned.1.call-update
  144.0 0.0 all-gather.15.cloned.1.call-start
  144.0 0.5 all-gather.15.cloned.1.call-update
  144.6 0.0 all-gather.13.cloned.1.call-start
  144.6 26.5 %reduce-scatter.3.cloned.1.call-done = bf16[128,1536]{1,0:T(8,128)(2,1)} async-done(((bf16[512,1536]{1,0:T(8,128)(2,1)}), bf16[128,1536]{1,0:T(8,128)(2,1)}) %reduce-scatter.3.cloned.1.call-update) | async-done | bytes 393232 | tf_op jit(solution)/shard_map/reduce_scatter | solution.py:92
  171.1 1.2 convert_reduce_fusion
  172.3 0.3 fusion.16
  172.6 1.0 fusion.18
  173.6 0.0 all-gather.13.cloned.1.call-update
  173.6 0.0 all-gather.17.cloned.1.call-start
  173.7 0.7 all-gather.17.cloned.1.call-update
  174.4 0.0 reduce-scatter.5.cloned.1.call-start
  174.4 0.1 convert_reduce_fusion.2
  174.5 0.1 convert_reduce_fusion.33
  174.6 0.1 convert_reduce_fusion.34
  174.7 0.1 slice_compare_fusion.29
  174.8 0.1 slice_compare_fusion.30
  174.9 50.6 %all-gather.15.cloned.1.call-done = bf16[1536,2,384]{2,1,0:T(2,128)(2,1)} async-done(((bf16[192,2,384]{2,1,0:T(2,128)(2,1)}), bf16[1536,2,384]{2,1,0:T(2,128)(2,1)}) %all-gather.15.cloned.1.call-update) | async-done | bytes 2359312 | tf_op jit(solution)/shard_map/all_gather | solution.py:73
  225.5 5.6 %copy.28 = bf16[1536,2,384]{0,2,1:T(8,128)(2,1)S(1)} copy(bf16[1536,2,384]{2,1,0:T(2,128)(2,1)} %all-gather.15.cloned.1.call-done) | data formatting | bytes 4718592 | tf_op jit(solution)/shard_map/reshape | solution.py:76
  231.1 14.1 %all-gather.13.cloned.1.call-done = bf16[512,1536]{1,0:T(8,128)(2,1)} async-done(((bf16[128,1536]{1,0:T(8,128)(2,1)}), bf16[512,1536]{1,0:T(8,128)(2,1)}) %all-gather.13.cloned.1.call-update) | async-done | bytes 1572880 | tf_op jit(solution)/shard_map/all_gather | solution.py:103
  245.2 2.8 fusion.2
  248.0 0.2 fusion.32
  248.2 40.5 %all-gather.17.cloned.1.call-done = bf16[384,1536]{0,1:T(8,128)(2,1)} async-done(((bf16[384,192]{0,1:T(8,128)(2,1)}), bf16[384,1536]{0,1:T(8,128)(2,1)}) %all-gather.17.cloned.1.call-update) | async-done | bytes 1179664 | tf_op jit(solution)/shard_map/all_gather | solution.py:74
  288.7 9.8 %convolution_convert_fusion.1 = bf16[512,1536]{1,0:T(8,128)(2,1)} fusion(bf16[384,1536]{0,1:T(8,128)(2,1)} %all-gather.17.cloned.1.call-done, bf16[512,384]{1,0:T(8,128)(2,1)S(1)} %fusion.32, f32[384]{0:T(512)S(1)} %get-tuple-element.55, f32[384]{0:T(512)S(1)} %get-tuple-element.56, f32[384]{0:T(512)S(1)} %get-tuple-element.18, ...), kind=kOutput, calls=%fused_computation.6 | convolution fusion | flops 629932032 | bytes 3209216 | tf_op jit(solution)/shard_map/dot_general | solution.py:115
  298.5 0.0 reduce-scatter.5.cloned.1.call-update
  298.5 27.1 %reduce-scatter.5.cloned.1.call-done = bf16[128,1536]{1,0:T(8,128)(2,1)} async-done(((bf16[512,1536]{1,0:T(8,128)(2,1)}), bf16[128,1536]{1,0:T(8,128)(2,1)}) %reduce-scatter.5.cloned.1.call-update) | async-done | bytes 393232 | tf_op jit(solution)/shard_map/reduce_scatter | solution.py:114
  325.6 1.8 fusion.31
  (14 shorter events, 0.1 us)
Async XLA Ops:
  6.5 6.0 %copy-start.3 = (s32[1,4]{1,0:T(1,128)S(1)}, s32[1,4]{1,0:T(1,128)}, u32[]{:S(2)}) copy-start(s32[1,4]{1,0:T(1,128)} %param.10) | copy-start | bytes 52
  6.5 70.9 %all-gather.9.cloned.1.call-start = ((), (), s32[]{:S(2)}) async-start(), calls=%async_computation.3 | async-start | bytes 3981312 | tf_op jit(solution)/shard_map/all_gather | solution.py:71
  7.3 89.9 %all-gather.7.cloned.1.call-start = ((), (), s32[]{:S(2)}) async-start(), calls=%async_computation.2 | async-start | bytes 1966080 | tf_op jit(solution)/shard_map/all_gather | solution.py:83
  11.8 128.7 %all-gather.11.cloned.1.call-start = ((), (), s32[]{:S(2)}) async-start(), calls=%async_computation.4 | async-start | bytes 1327104 | tf_op jit(solution)/shard_map/all_gather | solution.py:72
  12.5 158.6 %reduce-scatter.3.cloned.1.call-start = ((), (), s32[]{:S(2)}) async-start(), calls=%async_computation.5 | async-start | bytes 1966080 | tf_op jit(solution)/shard_map/reduce_scatter | solution.py:92
  144.0 27.1 %copy-start = (bf16[1,128,1536]{2,1,0:T(8,128)(2,1)S(1)}, bf16[1,128,1536]{2,1,0:T(8,128)(2,1)}, u32[]{:S(2)}) copy-start(bf16[1,128,1536]{2,1,0:T(8,128)(2,1)} %param.9) | copy-start | bytes 1179652
  144.0 28.6 %copy-start.2 = (f32[1536]{0:T(1024)S(1)}, f32[1536]{0:T(1024)}, u32[]{:S(2)}) copy-start(f32[1536]{0:T(1024)} %param.12) | copy-start | bytes 18436
  144.0 30.5 %copy-start.1 = (bf16[31,384]{1,0:T(8,128)(2,1)S(1)}, bf16[31,384]{1,0:T(8,128)(2,1)}, u32[]{:S(2)}) copy-start(bf16[31,384]{1,0:T(8,128)(2,1)} %param.16) | copy-start | bytes 71428
  144.0 81.5 %all-gather.15.cloned.1.call-start = ((), (), s32[]{:S(2)}) async-start(), calls=%async_computation.7 | async-start | bytes 2654208 | tf_op jit(solution)/shard_map/all_gather | solution.py:73
  144.6 100.6 %all-gather.13.cloned.1.call-start = ((), (), s32[]{:S(2)}) async-start(), calls=%async_computation.6 | async-start | bytes 1966080 | tf_op jit(solution)/shard_map/all_gather | solution.py:103
  173.6 115.1 %all-gather.17.cloned.1.call-start = ((), (), s32[]{:S(2)}) async-start(), calls=%async_computation.8 | async-start | bytes 1327104 | tf_op jit(solution)/shard_map/all_gather | solution.py:74
  174.4 151.3 %reduce-scatter.5.cloned.1.call-start = ((), (), s32[]{:S(2)}) async-start(), calls=%async_computation.9 | async-start | bytes 1966080 | tf_op jit(solution)/shard_map/reduce_scatter | solution.py:114
Sparse Core Ops, SparseCore 0:
  9.5 67.8 all-gather.8
  79.0 18.1 all-gather.6
  99.4 41.0 all-gather.10
  144.1 26.9 reduce-scatter.2
  173.3 52.0 all-gather.14
  227.0 18.1 all-gather.12
  247.6 41.0 all-gather.16
  298.7 26.9 reduce-scatter.4
where the time goes:
time: 335 us; the launch traced here: 334 us
  waiting for transfers between devices  271 us (81%)
  matrix products  27.2 us (8%)
  between operations  13.6 us (4%)
  local copies, waits for them, and re-layouts  12.4 us (4%)
  other arithmetic  9.88 us (3%)
    all_gather x1, waiting for transfers between devices, on_device(): qkv_local = lax.all_gather(w_qkv, 'dp', axis=0, tiled=True)  64.4 us
    all_gather x1, waiting for transfers between devices, on_device(): glu_local = lax.all_gather(w_glu, 'dp', axis=0, tiled=True)  50.6 us
    all_gather x1, waiting for transfers between devices, on_device(): proj_local = lax.all_gather(w_proj, 'dp', axis=1, tiled=True)  40.5 us
    all_gather x1, waiting for transfers between devices, on_device(): out_local = lax.all_gather(w_out, 'dp', axis=1, tiled=True)  31.5 us
    reduce_scatter x1, waiting for transfers between devices, on_device(): lax.psum_scatter(jnp.dot(rows_here, proj_local, preferred_element_type=jn...  27.1 us
    reduce_scatter x1, waiting for transfers between devices, on_device(): lax.psum_scatter(jnp.dot(rows_here, out_local, preferred_element_type=jnp...  26.5 us
    all_gather x1, waiting for transfers between devices, on_device(): shard_piece = lax.all_gather(normed2, 'seq', axis=0, tiled=True)  14.1 us
    all_gather x1, waiting for transfers between devices, on_device(): lax.all_gather(normed1, 'seq', axis=0, tiled=True)  13.6 us
  transfers between devices with their start and end apart: 8, of which 8 were waited for; matrix products, arithmetic and copies ran while one was open for 10% of the time, Pallas kernels for 0%

commit v1 on v0

--- a/solution.py
+++ b/solution.py
@@ -15,6 +15,31 @@
 
 def segment_of(record_ends, positions):
     return jnp.sum((positions[:, None] >= record_ends[None, :]).astype(jnp.int32), axis=1)
+
+
+def seq_gather(block):
+    count = lax.axis_size("seq")
+    me = lax.axis_index("seq")
+    parts = [block]
+    for shift in range(1, count):
+        parts.append(
+            lax.ppermute(block, "seq", [(i, (i - shift) % count) for i in range(count)])
+        )
+    ring = jnp.concatenate(parts + parts, axis=0)
+    rows = block.shape[0]
+    return lax.dynamic_slice_in_dim(ring, ((count - me) % count) * rows, count * rows, axis=0)
+
+
+def seq_scatter_sum(full):
+    count = lax.axis_size("seq")
+    me = lax.axis_index("seq")
+    rows = full.shape[0] // count
+    total = lax.dynamic_slice_in_dim(full, me * rows, rows, axis=0).astype(jnp.float32)
+    for shift in range(1, count):
+        piece = lax.dynamic_slice_in_dim(full, ((me + shift) % count) * rows, rows, axis=0)
+        got = lax.ppermute(piece, "seq", [(i, (i + shift) % count) for i in range(count)])
+        total = total + got.astype(jnp.float32)
+    return total
 
 
 def attend(projected, seg_all, head_size):
@@ -68,39 +93,30 @@
     group_rows = frame_rows * seq_count
     group_width = model_width // seq_count
     kernel_reach = dw_kernel.shape[0] // 2
-    qkv_local = lax.all_gather(w_qkv, "dp", axis=0, tiled=True)
+    qkv_matrix = lax.all_gather(
+        w_qkv.reshape(w_qkv.shape[0], 3 * group_width), "dp", axis=0, tiled=True
+    )
     out_local = lax.all_gather(w_out, "dp", axis=1, tiled=True)
-    glu_local = lax.all_gather(w_glu, "dp", axis=0, tiled=True)
+    glu_matrix = lax.all_gather(
+        w_glu.reshape(w_glu.shape[0], 2 * group_width), "dp", axis=0, tiled=True
+    )
     proj_local = lax.all_gather(w_proj, "dp", axis=1, tiled=True)
-    qkv_matrix = qkv_local.reshape(model_width, 3 * group_width)
-    glu_matrix = glu_local.reshape(model_width, 2 * group_width)
     inputs = frames[0].astype(jnp.float32)
     record_ends = jnp.cumsum(lengths[0])
     seg_all = segment_of(record_ends, jnp.arange(group_rows, dtype=jnp.int32))
     normed1 = layer_norm(inputs, ln1_gain)
     projected = (
-        jnp.dot(
-            lax.all_gather(normed1, "seq", axis=0, tiled=True),
-            qkv_matrix,
-            preferred_element_type=jnp.float32,
-        )
+        jnp.dot(seq_gather(normed1), qkv_matrix, preferred_element_type=jnp.float32)
         .astype(jnp.bfloat16)
         .reshape(group_rows, 3, group_width)
     )
     attended = attend(projected, seg_all, HD)
-    rows_here = attended
-    attn_sum = lax.psum_scatter(
-        jnp.dot(rows_here, out_local, preferred_element_type=jnp.float32)
-        .astype(jnp.bfloat16)
-        .astype(jnp.float32)
-        .astype(jnp.bfloat16),
-        "seq",
-        scatter_dimension=0,
-        tiled=True,
-    ).astype(jnp.float32)
+    attn_sum = seq_scatter_sum(
+        jnp.dot(attended, out_local, preferred_element_type=jnp.float32).astype(jnp.bfloat16)
+    )
     middle = (inputs + attn_sum).astype(jnp.bfloat16)
     normed2 = layer_norm(middle.astype(jnp.float32), ln2_gain)
-    shard_piece = lax.all_gather(normed2, "seq", axis=0, tiled=True)
+    shard_piece = seq_gather(normed2)
     paired = jnp.dot(shard_piece, glu_matrix, preferred_element_type=jnp.float32).reshape(
         shard_piece.shape[0], 2, group_width
     )
@@ -110,16 +126,9 @@
     activated = depthwise(
         padded, dw_kernel, seg_all, segment_of(record_ends, near_positions), group_rows
     )
-    rows_here = activated
-    conv_out = lax.psum_scatter(
-        jnp.dot(rows_here, proj_local, preferred_element_type=jnp.float32)
-        .astype(jnp.bfloat16)
-        .astype(jnp.float32)
-        .astype(jnp.bfloat16),
-        "seq",
-        scatter_dimension=0,
-        tiled=True,
-    ).astype(jnp.float32)
+    conv_out = seq_scatter_sum(
+        jnp.dot(activated, proj_local, preferred_element_type=jnp.float32).astype(jnp.bfloat16)
+    )
     results = [(middle.astype(jnp.float32) + conv_out).astype(jnp.bfloat16)]
     return jnp.stack(results, axis=0)
 

time: 335 us -> 247 us (0.74)
  waiting for transfers between devices: 271 us -> 168 us
  starting transfers between devices: 0.28 us -> 11.5 us
  local copies, waits for them, and re-layouts: 12.4 us -> 18.8 us
    all_gather x4 -> x2, waiting for transfers between devices: 143 us -> 40.7 us  [the longest x1 37.2 us: on_device(): lax.all_gather(w_qkv.reshape(w_qkv.shape[0], 3 * group_width), 'dp', axis...]
    ppermute x0 -> x12, waiting for transfers between devices: none -> 62.8 us  [the longest x6 33.3 us: seq_gather(): lax.ppermute(block, 'seq', [(i, (i - shift) % count) for i in range(count)])]
    reduce_scatter x2 -> x0, waiting for transfers between devices: 53.5 us -> none  [the longest x1 27.1 us: on_device(): lax.psum_scatter(jnp.dot(rows_here, proj_local, preferred_element_type=jn...]
    ppermute x0 -> x12, starting transfers between devices: none -> 11.4 us  [the longest x6 6.33 us: seq_gather(): lax.ppermute(block, 'seq', [(i, (i - shift) % count) for i in range(count)])]
    unnamed x8 -> x61, local copies, waits for them, and re-layouts: 0.02 us -> 11.2 us
    all_gather x1, waiting for transfers between devices: 40.5 us -> 33.2 us  [on_device(): proj_local = lax.all_gather(w_proj, 'dp', axis=1, tiled=True)]
    all_gather x1 -> x0, local copies, waits for them, and re-layouts: 6.11 us -> none  [on_device(): qkv_local = lax.all_gather(w_qkv, 'dp', axis=0, tiled=True)]
  transfers between devices with their start and end apart: 8 -> 16, of which waited for: 8 -> 13; matrix products, arithmetic and copies ran while one was open for 10% -> 17% of each run, Pallas kernels for 0% -> 0%
where the time goes in v1:
time: 247 us
  waiting for transfers between devices  168 us (68%)
  matrix products  25.7 us (10%)
  local copies, waits for them, and re-layouts  18.8 us (8%)
  between operations  13.6 us (6%)
  starting transfers between devices  11.5 us (5%)
  other arithmetic  9.38 us (4%)
    all_gather x1, waiting for transfers between devices, on_device(): lax.all_gather(w_qkv.reshape(w_qkv.shape[0], 3 * group_width), 'dp', axis...  37.2 us
    ppermute x6, waiting for transfers between devices, seq_gather(): lax.ppermute(block, 'seq', [(i, (i - shift) % count) for i in range(count)])  33.3 us
    all_gather x1, waiting for transfers between devices, on_device(): proj_local = lax.all_gather(w_proj, 'dp', axis=1, tiled=True)  33.2 us
    all_gather x1, waiting for transfers between devices, on_device(): out_local = lax.all_gather(w_out, 'dp', axis=1, tiled=True)  30.1 us
    ppermute x6, waiting for transfers between devices, seq_scatter_sum(): lax.ppermute(piece, 'seq', [(i, (i + shift) % count) for i in range(count)])  29.5 us
    unnamed x61, local copies, waits for them, and re-layouts  11.2 us
    dot_general x1, matrix products, on_device(): jnp.dot(activated, proj_local, preferred_element_type=jnp.float32)  7.81 us
    ppermute x6, starting transfers between devices, seq_gather(): lax.ppermute(block, 'seq', [(i, (i - shift) % count) for i in range(count)])  6.33 us
  transfers between devices with their start and end apart: 16, of which 13 were waited for; matrix products, arithmetic and copies ran while one was open for 17% of the time, Pallas kernels for 0%

profile of v1, /device:TPU:0, one launch (start us, length us, event | category | flops | bytes accessed | tf_op | source)
XLA Modules:
  0.0 246.6 jit_solution(16871168828461402253)
XLA Ops:
  6.5 1.9 copy.27
  9.2 1.7 copy.28
  11.0 1.1 convert_reduce_fusion.1
  12.2 1.2 fusion.19
  13.4 0.9 constant_dynamic-update-slice_fusion.7
  14.4 2.4 collective-permute-start
  18.1 8.0 %collective-permute-done = bf16[128,1536]{1,0:T(8,128)(2,1)S(1)} collective-permute-done((bf16[128,1536]{1,0:T(8,128)(2,1)S(1)}, bf16[128,1536]{1,0:T(8,128)(2,1)S(1)}, u32[]{:S(2)}, u32[]{:S(2)}) %collective-permute-start) | collective-permute-done | bytes 393248 | tf_op jit(solution)/shard_map/ppermute | solution.py:26
  26.2 0.8 constant_dynamic-update-slice_fusion.6
  26.9 8.6 %collective-permute-done.1 = bf16[128,1536]{1,0:T(8,128)(2,1)S(1)} collective-permute-done((bf16[128,1536]{1,0:T(8,128)(2,1)S(1)}, bf16[128,1536]{1,0:T(8,128)(2,1)S(1)}, u32[]{:S(2)}, u32[]{:S(2)}) %collective-permute-start.1) | collective-permute-done | bytes 393248 | tf_op jit(solution)/shard_map/ppermute | solution.py:26
  35.5 0.8 constant_dynamic-update-slice_fusion.5
  36.3 0.8 constant_dynamic-update-slice_fusion.4
  37.1 0.8 constant_dynamic-update-slice_fusion.3
  37.9 0.8 constant_dynamic-update-slice_fusion.2
  38.7 0.8 constant_dynamic-update-slice_fusion.1
  39.5 0.8 constant_dynamic-update-slice_fusion
  40.3 37.2 %all-gather.5.cloned.1.call-done = bf16[1536,1152]{1,0:T(8,128)(2,1)} async-done(((bf16[192,1152]{1,0:T(8,128)(2,1)}), bf16[1536,1152]{1,0:T(8,128)(2,1)}) %all-gather.5.cloned.1.call-update) | async-done | bytes 3538960 | tf_op jit(solution)/shard_map/all_gather | solution.py:96
  77.5 4.7 %convolution_convert_fusion = bf16[512,1152]{1,0:T(8,128)(2,1)S(1)} fusion(bf16[1536,1152]{1,0:T(8,128)(2,1)} %all-gather.5.cloned.1.call-done, bf16[1024,1536]{1,0:T(8,128)(2,1)} %constant_dynamic-update-slice_fusion, s32[]{:T(128)S(6)} %select_n.147), kind=kOutput, calls=%fused_computation.5 | convolution fusion | flops 1812529152 | bytes 6291460 | tf_op jit(solution)/shard_map/dot_general | solution.py:109
  82.8 3.6 %fusion.45 = (f32[4,512]{1,0:T(4,128)S(1)}, f32[4,512,512]{1,2,0:T(8,128)}) fusion(pred[512,512]{0,1:T(8,128)(4,1)S(1)} %broadcast_compare_fusion, bf16[512,3,4,96]{0,3,2,1:T(8,128)(2,1)S(1)} %bitcast.65), kind=kOutput, calls=%fused_computation.155 | convolution fusion | flops 205521408 | bytes 5251072 | tf_op jit(solution)/shard_map/while/body/eval_jaxpr/sub | solution.py:65
  86.4 2.7 %fusion.9 = bf16[4,96,512]{2,1,0:T(8,128)(2,1)S(1)} fusion(f32[4,512,512]{1,2,0:T(8,128)} %get-tuple-element.103, f32[4,512]{1,0:T(4,128)S(1)} %get-tuple-element.102, bf16[512,3,4,96]{0,3,2,1:T(8,128)(2,1)S(1)} %bitcast.66), kind=kOutput, calls=%fused_computation.15 | convolution fusion | flops 203620352 | bytes 4988928 | tf_op jit(solution)/shard_map/while/body/eval_jaxpr/hqk,khe->qhe/dot_general | solution.py:67
  89.1 30.1 %all-gather.7.cloned.1.call-done = bf16[384,1536]{0,1:T(8,128)(2,1)} async-done(((bf16[384,192]{0,1:T(8,128)(2,1)}), bf16[384,1536]{0,1:T(8,128)(2,1)}) %all-gather.7.cloned.1.call-update) | async-done | bytes 1179664 | tf_op jit(solution)/shard_map/all_gather | solution.py:99
  119.2 2.3 convolution_convert_fusion.2
  121.7 1.5 collective-permute-start.4
  123.2 1.4 collective-permute-start.5
  126.1 6.4 %collective-permute-done.3 = bf16[128,1536]{1,0:T(8,128)(2,1)S(1)} collective-permute-done((bf16[128,1536]{1,0:T(8,128)(2,1)S(1)}, bf16[128,1536]{1,0:T(8,128)(2,1)S(1)}, u32[]{:S(2)}, u32[]{:S(2)}) %collective-permute-start.3) | collective-permute-done | bytes 393248 | tf_op jit(solution)/shard_map/ppermute | solution.py:40
  132.5 1.3 collective-permute-done.4
  133.8 6.7 %collective-permute-done.5 = bf16[128,1536]{1,0:T(8,128)(2,1)} collective-permute-done((bf16[128,1536]{1,0:T(8,128)(2,1)S(1)}, bf16[128,1536]{1,0:T(8,128)(2,1)}, u32[]{:S(2)}, u32[]{:S(2)}) %collective-permute-start.5) | collective-permute-done | bytes 393248 | tf_op jit(solution)/shard_map/ppermute | solution.py:40
  140.5 1.5 convert_reduce_fusion
  142.3 0.9 constant_dynamic-update-slice_fusion.15
  143.2 2.3 collective-permute-start.6
  146.7 8.3 %collective-permute-done.6 = bf16[128,1536]{1,0:T(8,128)(2,1)S(1)} collective-permute-done((bf16[128,1536]{1,0:T(8,128)(2,1)S(1)}, bf16[128,1536]{1,0:T(8,128)(2,1)S(1)}, u32[]{:S(2)}, u32[]{:S(2)}) %collective-permute-start.6) | collective-permute-done | bytes 393248 | tf_op jit(solution)/shard_map/ppermute | solution.py:26
  155.0 0.8 constant_dynamic-update-slice_fusion.14
  155.7 8.3 %collective-permute-done.7 = bf16[128,1536]{1,0:T(8,128)(2,1)S(1)} collective-permute-done((bf16[128,1536]{1,0:T(8,128)(2,1)S(1)}, bf16[128,1536]{1,0:T(8,128)(2,1)S(1)}, u32[]{:S(2)}, u32[]{:S(2)}) %collective-permute-start.7) | collective-permute-done | bytes 393248 | tf_op jit(solution)/shard_map/ppermute | solution.py:26
  164.1 0.8 constant_dynamic-update-slice_fusion.13
  164.8 0.8 constant_dynamic-update-slice_fusion.12
  165.6 0.8 constant_dynamic-update-slice_fusion.11
  166.4 0.8 constant_dynamic-update-slice_fusion.10
  167.2 0.8 constant_dynamic-update-slice_fusion.9
  168.0 0.8 constant_dynamic-update-slice_fusion.8
  168.8 3.5 %all-gather.9.cloned.1.call-done = bf16[1536,768]{1,0:T(8,128)(2,1)} async-done(((bf16[192,768]{1,0:T(8,128)(2,1)}), bf16[1536,768]{1,0:T(8,128)(2,1)}) %all-gather.9.cloned.1.call-update) | async-done | bytes 2359312 | tf_op jit(solution)/shard_map/all_gather | solution.py:100
  172.3 4.7 %fusion.6 = f32[512,768]{1,0:T(8,128)} fusion(bf16[1536,768]{1,0:T(8,128)(2,1)} %all-gather.9.cloned.1.call-done, bf16[1024,1536]{1,0:T(8,128)(2,1)} %constant_dynamic-update-slice_fusion.8, s32[]{:T(128)S(6)} %select_n.147), kind=kOutput, calls=%fused_computation.12 | convolution fusion | flops 1207959552 | bytes 5505028 | tf_op jit(solution)/shard_map/dot_general | solution.py:120
  177.0 2.1 reshape.147
  179.3 1.2 fusion.44
  180.7 33.2 %all-gather.11.cloned.1.call-done = bf16[384,1536]{0,1:T(8,128)(2,1)} async-done(((bf16[384,192]{0,1:T(8,128)(2,1)}), bf16[384,1536]{0,1:T(8,128)(2,1)}) %all-gather.11.cloned.1.call-update) | async-done | bytes 1179664 | tf_op jit(solution)/shard_map/all_gather | solution.py:103
  214.1 7.8 %convolution_convert_fusion.1 = bf16[512,1536]{1,0:T(8,128)(2,1)S(1)} fusion(bf16[384,1536]{0,1:T(8,128)(2,1)} %all-gather.11.cloned.1.call-done, bf16[512,384]{1,0:T(8,128)(2,1)S(1)} %fusion.32, f32[384]{0:T(512)S(1)} %get-tuple-element.55, f32[384]{0:T(512)S(1)} %get-tuple-element.56, f32[384]{0:T(512)S(1)} %get-tuple-element.18, ...), kind=kOutput, calls=%fused_computation.6 | convolution fusion | flops 629932032 | bytes 3209216 | tf_op jit(solution)/shard_map/dot_general | solution.py:130
  222.0 1.5 collective-permute-start.10
  224.1 10.1 %collective-permute-done.10 = bf16[128,1536]{1,0:T(8,128)(2,1)S(1)} collective-permute-done((bf16[128,1536]{1,0:T(8,128)(2,1)S(1)}, bf16[128,1536]{1,0:T(8,128)(2,1)S(1)}, u32[]{:S(2)}, u32[]{:S(2)}) %collective-permute-start.10) | collective-permute-done | bytes 393248 | tf_op jit(solution)/shard_map/ppermute | solution.py:40
  234.1 5.0 %collective-permute-done.11 = bf16[128,1536]{1,0:T(8,128)(2,1)S(1)} collective-permute-done((bf16[128,1536]{1,0:T(8,128)(2,1)S(1)}, bf16[128,1536]{1,0:T(8,128)(2,1)S(1)}, u32[]{:S(2)}, u32[]{:S(2)}) %collective-permute-start.11) | collective-permute-done | bytes 393248 | tf_op jit(solution)/shard_map/ppermute | solution.py:40
  239.1 1.0 fusion.31
  (84 shorter events, 6.7 us)
Async XLA Ops:
  6.5 6.9 %copy-start = (bf16[1,128,1536]{2,1,0:T(8,128)(2,1)S(1)}, bf16[1,128,1536]{2,1,0:T(8,128)(2,1)}, u32[]{:S(2)}) copy-start(bf16[1,128,1536]{2,1,0:T(8,128)(2,1)} %param.9) | copy-start | bytes 1179652
  6.5 6.9 %copy-start.2 = (f32[1536]{0:T(1024)S(1)}, f32[1536]{0:T(1024)}, u32[]{:S(2)}) copy-start(f32[1536]{0:T(1024)} %param.11) | copy-start | bytes 18436
  6.5 11.1 %copy-start.23 = (s32[1,4]{1,0:T(1,128)S(1)}, s32[1,4]{1,0:T(1,128)}, u32[]{:S(2)}) copy-start(s32[1,4]{1,0:T(1,128)} %param.10) | copy-start | bytes 52
  6.5 70.9 %all-gather.5.cloned.1.call-start = ((), (), s32[]{:S(2)}) async-start(), calls=%async_computation | async-start | bytes 3981312 | tf_op jit(solution)/shard_map/all_gather | solution.py:96
  8.4 110.8 %all-gather.7.cloned.1.call-start = ((), (), s32[]{:S(2)}) async-start(), calls=%async_computation.1 | async-start | bytes 1327104 | tf_op jit(solution)/shard_map/all_gather | solution.py:99
  9.2 163.1 %all-gather.9.cloned.1.call-start = ((), (), s32[]{:S(2)}) async-start(), calls=%async_computation.2 | async-start | bytes 2654208 | tf_op jit(solution)/shard_map/all_gather | solution.py:100
  11.0 203.0 %all-gather.11.cloned.1.call-start = ((), (), s32[]{:S(2)}) async-start(), calls=%async_computation.3 | async-start | bytes 1327104 | tf_op jit(solution)/shard_map/all_gather | solution.py:103
  14.4 11.8 %collective-permute-start = (bf16[128,1536]{1,0:T(8,128)(2,1)S(1)}, bf16[128,1536]{1,0:T(8,128)(2,1)S(1)}, u32[]{:S(2)}, u32[]{:S(2)}) collective-permute-start(bf16[128,1536]{1,0:T(8,128)(2,1)S(1)} %get-tuple-element.62), channel_id=1, source_target_pairs={{0,3},{1,0},{2,1},{3,2},{4,7},{5,4},{6,5},{7,6},{8,11},{9,8},{10,9... | collective-permute-start | bytes 1179656 | tf_op jit(solution)/shard_map/ppermute | solution.py:26
  16.8 18.8 %collective-permute-start.1 = (bf16[128,1536]{1,0:T(8,128)(2,1)S(1)}, bf16[128,1536]{1,0:T(8,128)(2,1)S(1)}, u32[]{:S(2)}, u32[]{:S(2)}) collective-permute-start(bf16[128,1536]{1,0:T(8,128)(2,1)S(1)} %get-tuple-element.62), channel_id=1, source_target_pairs={{0,2},{1,3},{2,0},{3,1},{4,6},{5,7},{6,4},{7,5},{8,10},{9,11},{10,... | collective-permute-start | bytes 1179656 | tf_op jit(solution)/shard_map/ppermute | solution.py:26
  17.3 19.0 %collective-permute-start.2 = (bf16[128,1536]{1,0:T(8,128)(2,1)S(1)}, bf16[128,1536]{1,0:T(8,128)(2,1)S(1)}, u32[]{:S(2)}, u32[]{:S(2)}) collective-permute-start(bf16[128,1536]{1,0:T(8,128)(2,1)S(1)} %get-tuple-element.62), channel_id=1, source_target_pairs={{0,1},{1,2},{2,3},{3,0},{4,5},{5,6},{6,7},{7,4},{8,9},{9,10},{10,1... | collective-permute-start | bytes 1179656 | tf_op jit(solution)/shard_map/ppermute | solution.py:26
  17.8 22.4 %copy-start.4 = (s32[4,1]{0,1:T(1,128)}, s32[4,1]{0,1:T(1,128)S(1)}, u32[]{:S(2)}) copy-start(s32[4,1]{0,1:T(1,128)S(1)} %reduce-window.8) | copy-start | bytes 52
  121.5 20.7 %copy-start.3 = (f32[1536]{0:T(1024)S(1)}, f32[1536]{0:T(1024)}, u32[]{:S(2)}) copy-start(f32[1536]{0:T(1024)} %param.12) | copy-start | bytes 18436
  121.7 10.9 %collective-permute-start.3 = (bf16[128,1536]{1,0:T(8,128)(2,1)S(1)}, bf16[128,1536]{1,0:T(8,128)(2,1)S(1)}, u32[]{:S(2)}, u32[]{:S(2)}) collective-permute-start(bf16[128,1536]{1,0:T(8,128)(2,1)S(1)} %get-tuple-element.68), channel_id=1, source_target_pairs={{0,1},{1,2},{2,3},{3,0},{4,5},{5,6},{6,7},{7,4},{8,9},{9,10},{10,1... | collective-permute-start | bytes 1179656 | tf_op jit(solution)/shard_map/ppermute | solution.py:40
  121.7 12.1 %collective-permute-start.4 = (bf16[128,1536]{1,0:T(8,128)(2,1)S(1)}, bf16[128,1536]{1,0:T(8,128)(2,1)}, u32[]{:S(2)}, u32[]{:S(2)}) collective-permute-start(bf16[128,1536]{1,0:T(8,128)(2,1)S(1)} %get-tuple-element.70), channel_id=1, source_target_pairs={{0,2},{1,3},{2,0},{3,1},{4,6},{5,7},{6,4},{7,5},{8,10},{9,11},{10,... | collective-permute-start | bytes 1179656 | tf_op jit(solution)/shard_map/ppermute | solution.py:40
  123.2 17.3 %collective-permute-start.5 = (bf16[128,1536]{1,0:T(8,128)(2,1)S(1)}, bf16[128,1536]{1,0:T(8,128)(2,1)}, u32[]{:S(2)}, u32[]{:S(2)}) collective-permute-start(bf16[128,1536]{1,0:T(8,128)(2,1)S(1)} %get-tuple-element.69), channel_id=1, source_target_pairs={{0,3},{1,0},{2,1},{3,2},{4,7},{5,4},{6,5},{7,6},{8,11},{9,8},{10,9... | collective-permute-start | bytes 1179656 | tf_op jit(solution)/shard_map/ppermute | solution.py:40
  124.7 21.6 %copy-start.1 = (bf16[31,384]{1,0:T(8,128)(2,1)S(1)}, bf16[31,384]{1,0:T(8,128)(2,1)}, u32[]{:S(2)}) copy-start(bf16[31,384]{1,0:T(8,128)(2,1)} %param.16) | copy-start | bytes 71428
  143.2 11.7 %collective-permute-start.6 = (bf16[128,1536]{1,0:T(8,128)(2,1)S(1)}, bf16[128,1536]{1,0:T(8,128)(2,1)S(1)}, u32[]{:S(2)}, u32[]{:S(2)}) collective-permute-start(bf16[128,1536]{1,0:T(8,128)(2,1)S(1)} %get-tuple-element.58), channel_id=1, source_target_pairs={{0,3},{1,0},{2,1},{3,2},{4,7},{5,4},{6,5},{7,6},{8,11},{9,8},{10,9... | collective-permute-start | bytes 1179656 | tf_op jit(solution)/shard_map/ppermute | solution.py:26
  145.6 18.4 %collective-permute-start.7 = (bf16[128,1536]{1,0:T(8,128)(2,1)S(1)}, bf16[128,1536]{1,0:T(8,128)(2,1)S(1)}, u32[]{:S(2)}, u32[]{:S(2)}) collective-permute-start(bf16[128,1536]{1,0:T(8,128)(2,1)S(1)} %get-tuple-element.58), channel_id=1, source_target_pairs={{0,2},{1,3},{2,0},{3,1},{4,6},{5,7},{6,4},{7,5},{8,10},{9,11},{10,... | collective-permute-start | bytes 1179656 | tf_op jit(solution)/shard_map/ppermute | solution.py:26
  146.4 18.4 %collective-permute-start.8 = (bf16[128,1536]{1,0:T(8,128)(2,1)S(1)}, bf16[128,1536]{1,0:T(8,128)(2,1)S(1)}, u32[]{:S(2)}, u32[]{:S(2)}) collective-permute-start(bf16[128,1536]{1,0:T(8,128)(2,1)S(1)} %get-tuple-element.58), channel_id=1, source_target_pairs={{0,1},{1,2},{2,3},{3,0},{4,5},{5,6},{6,7},{7,4},{8,9},{9,10},{10,1... | collective-permute-start | bytes 1179656 | tf_op jit(solution)/shard_map/ppermute | solution.py:26
  179.1 34.9 %copy-start.5 = (pred[512]{0:T(512)(128)(4,1)S(1)}, pred[512]{0:T(512)(128)(4,1)}, u32[]{:S(2)}) copy-start(pred[512]{0:T(512)(128)(4,1)} %get-tuple-element.71) | copy-start | bytes 1540
  179.1 34.9 %copy-start.6 = (pred[512]{0:T(512)(128)(4,1)S(1)}, pred[512]{0:T(512)(128)(4,1)}, u32[]{:S(2)}) copy-start(pred[512]{0:T(512)(128)(4,1)} %get-tuple-element.72) | copy-start | bytes 1540
  179.1 34.9 %copy-start.7 = (pred[512]{0:T(512)(128)(4,1)S(1)}, pred[512]{0:T(512)(128)(4,1)}, u32[]{:S(2)}) copy-start(pred[512]{0:T(512)(128)(4,1)} %get-tuple-element.73) | copy-start | bytes 1540
  179.1 34.9 %copy-start.8 = (pred[512]{0:T(512)(128)(4,1)S(1)}, pred[512]{0:T(512)(128)(4,1)}, u32[]{:S(2)}) copy-start(pred[512]{0:T(512)(128)(4,1)} %get-tuple-element.74) | copy-start | bytes 1540
  179.1 34.8 %copy-start.9 = (pred[512]{0:T(512)(128)(4,1)S(1)}, pred[512]{0:T(512)(128)(4,1)}, u32[]{:S(2)}) copy-start(pred[512]{0:T(512)(128)(4,1)} %get-tuple-element.75) | copy-start | bytes 1540
  179.1 34.8 %copy-start.10 = (pred[512]{0:T(512)(128)(4,1)S(1)}, pred[512]{0:T(512)(128)(4,1)}, u32[]{:S(2)}) copy-start(pred[512]{0:T(512)(128)(4,1)} %get-tuple-element.76) | copy-start | bytes 1540
  179.1 34.8 %copy-start.11 = (pred[512]{0:T(512)(128)(4,1)S(1)}, pred[512]{0:T(512)(128)(4,1)}, u32[]{:S(2)}) copy-start(pred[512]{0:T(512)(128)(4,1)} %get-tuple-element.77) | copy-start | bytes 1540
  179.2 34.8 %copy-start.12 = (pred[512]{0:T(512)(128)(4,1)S(1)}, pred[512]{0:T(512)(128)(4,1)}, u32[]{:S(2)}) copy-start(pred[512]{0:T(512)(128)(4,1)} %get-tuple-element.78) | copy-start | bytes 1540
  179.2 34.8 %copy-start.13 = (pred[512]{0:T(512)(128)(4,1)S(1)}, pred[512]{0:T(512)(128)(4,1)}, u32[]{:S(2)}) copy-start(pred[512]{0:T(512)(128)(4,1)} %get-tuple-element.79) | copy-start | bytes 1540
  179.2 34.8 %copy-start.14 = (pred[512]{0:T(512)(128)(4,1)S(1)}, pred[512]{0:T(512)(128)(4,1)}, u32[]{:S(2)}) copy-start(pred[512]{0:T(512)(128)(4,1)} %get-tuple-element.80) | copy-start | bytes 1540
  179.2 34.8 %copy-start.15 = (pred[512]{0:T(512)(128)(4,1)S(1)}, pred[512]{0:T(512)(128)(4,1)}, u32[]{:S(2)}) copy-start(pred[512]{0:T(512)(128)(4,1)} %get-tuple-element.81) | copy-start | bytes 1540
  179.2 34.8 %copy-start.16 = (pred[512]{0:T(512)(128)(4,1)S(1)}, pred[512]{0:T(512)(128)(4,1)}, u32[]{:S(2)}) copy-start(pred[512]{0:T(512)(128)(4,1)} %get-tuple-element.82) | copy-start | bytes 1540
  179.2 34.8 %copy-start.17 = (pred[512]{0:T(512)(128)(4,1)S(1)}, pred[512]{0:T(512)(128)(4,1)}, u32[]{:S(2)}) copy-start(pred[512]{0:T(512)(128)(4,1)} %get-tuple-element.83) | copy-start | bytes 1540
  179.2 34.8 %copy-start.18 = (pred[512]{0:T(512)(128)(4,1)S(1)}, pred[512]{0:T(512)(128)(4,1)}, u32[]{:S(2)}) copy-start(pred[512]{0:T(512)(128)(4,1)} %get-tuple-element.84) | copy-start | bytes 1540
  179.2 34.8 %copy-start.19 = (pred[512]{0:T(512)(128)(4,1)S(1)}, pred[512]{0:T(512)(128)(4,1)}, u32[]{:S(2)}) copy-start(pred[512]{0:T(512)(128)(4,1)} %get-tuple-element.85) | copy-start | bytes 1540
  179.2 34.8 %copy-start.20 = (pred[512]{0:T(512)(128)(4,1)S(1)}, pred[512]{0:T(512)(128)(4,1)}, u32[]{:S(2)}) copy-start(pred[512]{0:T(512)(128)(4,1)} %get-tuple-element.86) | copy-start | bytes 1540
  179.2 34.8 %copy-start.21 = (pred[512]{0:T(512)(128)(4,1)S(1)}, pred[512]{0:T(512)(128)(4,1)}, u32[]{:S(2)}) copy-start(pred[512]{0:T(512)(128)(4,1)} %get-tuple-element.87) | copy-start | bytes 1540
  179.3 34.8 %copy-start.22 = (pred[512]{0:T(512)(128)(4,1)S(1)}, pred[512]{0:T(512)(128)(4,1)}, u32[]{:S(2)}) copy-start(pred[512]{0:T(512)(128)(4,1)} %get-tuple-element.88) | copy-start | bytes 1540
  222.0 12.1 %collective-permute-start.10 = (bf16[128,1536]{1,0:T(8,128)(2,1)S(1)}, bf16[128,1536]{1,0:T(8,128)(2,1)S(1)}, u32[]{:S(2)}, u32[]{:S(2)}) collective-permute-start(bf16[128,1536]{1,0:T(8,128)(2,1)S(1)} %get-tuple-element.65), channel_id=1, source_target_pairs={{0,2},{1,3},{2,0},{3,1},{4,6},{5,7},{6,4},{7,5},{8,10},{9,11},{10,... | collective-permute-start | bytes 1179656 | tf_op jit(solution)/shard_map/ppermute | solution.py:40
  223.6 15.5 %collective-permute-start.11 = (bf16[128,1536]{1,0:T(8,128)(2,1)S(1)}, bf16[128,1536]{1,0:T(8,128)(2,1)S(1)}, u32[]{:S(2)}, u32[]{:S(2)}) collective-permute-start(bf16[128,1536]{1,0:T(8,128)(2,1)S(1)} %get-tuple-element.64), channel_id=1, source_target_pairs={{0,3},{1,0},{2,1},{3,2},{4,7},{5,4},{6,5},{7,6},{8,11},{9,8},{10,9... | collective-permute-start | bytes 1179656 | tf_op jit(solution)/shard_map/ppermute | solution.py:40
  223.6 15.5 %collective-permute-start.9 = (bf16[128,1536]{1,0:T(8,128)(2,1)S(1)}, bf16[128,1536]{1,0:T(8,128)(2,1)S(1)}, u32[]{:S(2)}, u32[]{:S(2)}) collective-permute-start(bf16[128,1536]{1,0:T(8,128)(2,1)S(1)} %get-tuple-element.63), channel_id=1, source_target_pairs={{0,1},{1,2},{2,3},{3,0},{4,5},{5,6},{6,7},{7,4},{8,9},{9,10},{10,1... | collective-permute-start | bytes 1179656 | tf_op jit(solution)/shard_map/ppermute | solution.py:40
Sparse Core Ops, SparseCore 0:
  9.5 67.8 all-gather.4
  79.6 39.5 all-gather.6
  121.4 50.8 all-gather.8
  174.3 39.5 all-gather.10

commit v2 on v1

--- a/solution.py
+++ b/solution.py
@@ -1,3 +1,5 @@
+import functools
+
 import jax
 import jax.numpy as jnp
 from jax import lax
@@ -40,6 +42,63 @@
         got = lax.ppermute(piece, "seq", [(i, (i + shift) % count) for i in range(count)])
         total = total + got.astype(jnp.float32)
     return total
+
+
+def dp_ring(mesh):
+    count = mesh.shape["dp"]
+    plain = list(range(count))
+    try:
+        coords = [tuple(int(c) for c in d.coords) for d in mesh.devices[:, 0]]
+    except (AttributeError, TypeError, IndexError):
+        return plain
+    axes = [k for k in range(len(coords[0])) if len({c[k] for c in coords}) > 1]
+    if len(axes) != 2:
+        return plain
+    low = [min(c[k] for c in coords) for k in axes]
+    spots = {(c[axes[0]] - low[0], c[axes[1]] - low[1]): i for i, c in enumerate(coords)}
+    sizes = [len({c[k] for c in coords}) for k in axes]
+    if sizes[0] * sizes[1] != count or len(spots) != count:
+        return plain
+    if sizes[0] % 2 == 0:
+        first, second, swap = sizes[0], sizes[1], False
+    elif sizes[1] % 2 == 0:
+        first, second, swap = sizes[1], sizes[0], True
+    else:
+        return plain
+    path = [(0, 0)]
+    for a in range(first):
+        cols = range(1, second) if a % 2 == 0 else range(second - 1, 0, -1)
+        path += [(a, b) for b in cols]
+    path += [(a, 0) for a in range(first - 1, 0, -1)]
+    if swap:
+        path = [(b, a) for a, b in path]
+    cycle = [spots.get(p) for p in path]
+    if None in cycle or sorted(cycle) != plain:
+        return plain
+    return cycle
+
+
+def ring_gather(block, ring):
+    count = len(ring)
+    me = lax.axis_index("dp")
+    my_pos = jnp.asarray([ring.index(i) for i in range(count)], jnp.int32)[me]
+    order = jnp.asarray(ring, jnp.int32)
+    forward = [(ring[p], ring[(p + 1) % count]) for p in range(count)]
+    backward = [(ring[p], ring[(p - 1) % count]) for p in range(count)]
+    out = jnp.zeros((count,) + block.shape, block.dtype)
+    out = lax.dynamic_update_index_in_dim(out, block, me, 0)
+    ahead = behind = block
+    for step in range(1, count // 2 + 1):
+        ahead = lax.ppermute(ahead, "dp", forward)
+        out = lax.dynamic_update_index_in_dim(out, ahead, order[(my_pos - step) % count], 0)
+        if step <= count - 1 - count // 2:
+            behind = lax.ppermute(behind, "dp", backward)
+            out = lax.dynamic_update_index_in_dim(out, behind, order[(my_pos + step) % count], 0)
+    return out
+
+
+def after(token, value):
+    return lax.optimization_barrier((token, value))[1]
 
 
 def attend(projected, seg_all, head_size):
@@ -86,21 +145,21 @@
     return jax.nn.silu(total_acc).astype(jnp.bfloat16)
 
 
-def on_device(frames, lengths, ln1_gain, ln2_gain, w_qkv, w_out, w_glu, dw_kernel, w_proj):
+def on_device(ring, frames, lengths, ln1_gain, ln2_gain, w_qkv, w_out, w_glu, dw_kernel, w_proj):
     frame_rows = frames.shape[1]
     model_width = frames.shape[2]
     seq_count = lax.axis_size("seq")
     group_rows = frame_rows * seq_count
     group_width = model_width // seq_count
     kernel_reach = dw_kernel.shape[0] // 2
-    qkv_matrix = lax.all_gather(
-        w_qkv.reshape(w_qkv.shape[0], 3 * group_width), "dp", axis=0, tiled=True
-    )
-    out_local = lax.all_gather(w_out, "dp", axis=1, tiled=True)
-    glu_matrix = lax.all_gather(
-        w_glu.reshape(w_glu.shape[0], 2 * group_width), "dp", axis=0, tiled=True
-    )
-    proj_local = lax.all_gather(w_proj, "dp", axis=1, tiled=True)
+    qkv_parts = ring_gather(w_qkv.reshape(w_qkv.shape[0], 3 * group_width), ring)
+    qkv_matrix = qkv_parts.reshape(model_width, 3 * group_width)
+    out_parts = ring_gather(after(qkv_parts, w_out), ring)
+    out_local = jnp.einsum("nrc->rnc", out_parts).reshape(w_out.shape[0], model_width)
+    glu_parts = ring_gather(after(out_parts, w_glu.reshape(w_glu.shape[0], 2 * group_width)), ring)
+    glu_matrix = glu_parts.reshape(model_width, 2 * group_width)
+    proj_parts = ring_gather(after(glu_parts, w_proj), ring)
+    proj_local = jnp.einsum("nrc->rnc", proj_parts).reshape(w_proj.shape[0], model_width)
     inputs = frames[0].astype(jnp.float32)
     record_ends = jnp.cumsum(lengths[0])
     seg_all = segment_of(record_ends, jnp.arange(group_rows, dtype=jnp.int32))
@@ -147,5 +206,5 @@
     )
     out_specs = P("dp", "seq", None)
     return jax.shard_map(
-        on_device, mesh=mesh, in_specs=in_specs, out_specs=out_specs, check_vma=False
-    )
+        functools.partial(on_device, dp_ring(mesh)), mesh=mesh, in_specs=in_specs, out_specs=out_specs, check_vma=False
+    )

time: 247 us -> 233 us (0.943)
  waiting for transfers between devices: 168 us -> 101 us
  starting transfers between devices: 11.5 us -> 43.2 us
  local copies, waits for them, and re-layouts: 18.8 us -> 31.6 us
  between operations: 13.6 us -> 19.2 us
  other arithmetic: 9.38 us -> 12.6 us
  matrix products: 25.7 us -> 23.2 us
    all_gather x4 -> x0, waiting for transfers between devices: 104 us -> none  [the longest x1 37.2 us: on_device(): lax.all_gather(w_qkv.reshape(w_qkv.shape[0], 3 * group_width), 'dp', axis...]
    ppermute x0 -> x28, waiting for transfers between devices: none -> 57.1 us  [the longest x16 56.1 us: ring_gather(): ahead = lax.ppermute(ahead, 'dp', forward)]
    ppermute x0 -> x28, starting transfers between devices: none -> 32.2 us  [the longest x16 26.9 us: ring_gather(): ahead = lax.ppermute(ahead, 'dp', forward)]
    ppermute x6, waiting for transfers between devices: 33.3 us -> 15.8 us  [seq_gather(): lax.ppermute(block, 'seq', [(i, (i - shift) % count) for i in range(count)])]
    dynamic_update_slice x0 -> x32, local copies, waits for them, and re-layouts: none -> 6.71 us  [the longest x16 2.42 us: ring_gather(): lax.dynamic_update_index_in_dim(out, ahead, order[(my_pos - step) % count...]
    mul x2, other arithmetic: 0.17 us -> 3.37 us  [depthwise(): window * kernel[tap_index].astype(jnp.float32)]
    unnamed x61 -> x116, local copies, waits for them, and re-layouts: 11.2 us -> 13.7 us
  transfers between devices with their start and end apart: 16 -> 40, of which waited for: 13 -> 20; matrix products, arithmetic and copies ran while one was open for 17% -> 24% of each run, Pallas kernels for 0% -> 0%
where the time goes in v2:
time: 233 us; the launch traced here: 231 us
  waiting for transfers between devices  101 us (43%)
  starting transfers between devices  43.2 us (19%)
  local copies, waits for them, and re-layouts  31.6 us (14%)
  matrix products  23.2 us (10%)
  between operations  19.2 us (8%)
  other arithmetic  12.6 us (5%)
    ppermute x16, waiting for transfers between devices, ring_gather(): ahead = lax.ppermute(ahead, 'dp', forward)  56.1 us
    ppermute x6, waiting for transfers between devices, seq_scatter_sum(): lax.ppermute(piece, 'seq', [(i, (i + shift) % count) for i in range(count)])  28.5 us
    ppermute x16, starting transfers between devices, ring_gather(): ahead = lax.ppermute(ahead, 'dp', forward)  26.9 us
    ppermute x6, waiting for transfers between devices, seq_gather(): lax.ppermute(block, 'seq', [(i, (i - shift) % count) for i in range(count)])  15.8 us
    unnamed x116, local copies, waits for them, and re-layouts  13.7 us
    dot_general x1, matrix products, on_device(): jnp.dot(activated, proj_local, preferred_element_type=jnp.float32)  9.09 us
    ppermute x6, starting transfers between devices, seq_scatter_sum(): lax.ppermute(piece, 'seq', [(i, (i + shift) % count) for i in range(count)])  5.51 us
    ppermute x6, starting transfers between devices, seq_gather(): lax.ppermute(block, 'seq', [(i, (i - shift) % count) for i in range(count)])  5.46 us
  transfers between devices with their start and end apart: 40, of which 20 were waited for; matrix products, arithmetic and copies ran while one was open for 24% of the time, Pallas kernels for 0%

profile of v2, /device:TPU:0, one launch (start us, length us, event | category | flops | bytes accessed | tf_op | source)
XLA Modules:
  0.0 231.2 jit_solution(4438373523649338973)
XLA Ops:
  0.0 1.9 copy.37
  1.9 3.0 %collective-permute-start.3 = (bf16[192,1152]{1,0:T(8,128)(2,1)}, bf16[192,1152]{1,0:T(8,128)(2,1)}, u32[]{:S(2)}, u32[]{:S(2)}) collective-permute-start(bf16[192,1152]{1,0:T(8,128)(2,1)} %bitcast.70), channel_id=1, source_target_pairs={{0,8},{8,16},{16,24},{24,28},{28,20},{20,12},{12,4},{4,0},{1,9},{9... | collective-permute-start | bytes 1327112 | tf_op jit(solution)/shard_map/ppermute | solution.py:92
  7.3 2.1 constant_dynamic-update-slice_fusion.7
  16.9 1.6 convert_reduce_fusion.33
  33.4 1.7 copy.38
  39.6 1.7 convert_reduce_fusion.34
  41.3 1.8 constant_dynamic-update-slice_fusion.6
  43.1 1.8 constant_dynamic-update-slice_fusion.5
  44.9 1.8 constant_dynamic-update-slice_fusion.4
  46.7 1.8 constant_dynamic-update-slice_fusion.3
  48.4 1.8 constant_dynamic-update-slice_fusion.2
  50.2 1.8 constant_dynamic-update-slice_fusion.1
  52.0 1.8 constant_dynamic-update-slice_fusion
  53.8 1.6 collective-permute-start.5
  57.9 8.9 %collective-permute-done.5 = bf16[192,1152]{1,0:T(8,128)(2,1)S(1)} collective-permute-done((bf16[192,1152]{1,0:T(8,128)(2,1)}, bf16[192,1152]{1,0:T(8,128)(2,1)S(1)}, u32[]{:S(2)}, u32[]{:S(2)}) %collective-permute-start.5) | collective-permute-done | bytes 442400 | tf_op jit(solution)/shard_map/ppermute | solution.py:92
  66.8 1.6 collective-permute-start.7
  69.0 9.9 %collective-permute-done.7 = bf16[192,1152]{1,0:T(8,128)(2,1)S(1)} collective-permute-done((bf16[192,1152]{1,0:T(8,128)(2,1)S(1)}, bf16[192,1152]{1,0:T(8,128)(2,1)S(1)}, u32[]{:S(2)}, u32[]{:S(2)}) %collective-permute-start.7) | collective-permute-done | bytes 442400 | tf_op jit(solution)/shard_map/ppermute | solution.py:92
  78.8 1.6 collective-permute-start.9
  80.5 9.5 %collective-permute-done.9 = bf16[192,1152]{1,0:T(8,128)(2,1)S(1)} collective-permute-done((bf16[192,1152]{1,0:T(8,128)(2,1)S(1)}, bf16[192,1152]{1,0:T(8,128)(2,1)S(1)}, u32[]{:S(2)}, u32[]{:S(2)}) %collective-permute-start.9) | collective-permute-done | bytes 442400 | tf_op jit(solution)/shard_map/ppermute | solution.py:92
  90.0 1.6 collective-permute-start.10
  92.1 3.2 %convolution_convert_fusion = bf16[512,1152]{1,0:T(8,128)(2,1)} fusion(bf16[1536,1152]{1,0:T(8,128)(2,1)S(1)} %bitcast.156, bf16[1024,1536]{1,0:T(8,128)(2,1)S(1)} %copy-done.5, s32[]{:T(128)S(6)} %select_n.440), kind=kOutput, calls=%fused_computation.5 | convolution fusion | flops 1812529152 | bytes 6291460 | tf_op jit(solution)/shard_map/dot_general | solution.py:168
  95.3 1.6 copy.32
  96.9 3.6 %fusion.46 = (f32[4,512]{1,0:T(4,128)S(1)}, f32[4,512,512]{1,2,0:T(8,128)}) fusion(pred[512,512]{0,1:T(8,128)(4,1)S(1)} %copy-done.4, bf16[512,3,4,96]{0,3,2,1:T(8,128)(2,1)S(1)} %bitcast.159), kind=kOutput, calls=%fused_computation.188 | convolution fusion | flops 205521408 | bytes 5251072 | tf_op jit(solution)/shard_map/while/body/eval_jaxpr/sub | solution.py:124
  100.6 2.7 %fusion.10 = bf16[4,96,512]{2,1,0:T(8,128)(2,1)S(1)} fusion(f32[4,512,512]{1,2,0:T(8,128)} %get-tuple-element.114, f32[4,512]{1,0:T(4,128)S(1)} %get-tuple-element.113, bf16[512,3,4,96]{0,3,2,1:T(8,128)(2,1)S(1)} %bitcast.160), kind=kOutput, calls=%fused_computation.16 | convolution fusion | flops 203620352 | bytes 4988928 | tf_op jit(solution)/shard_map/while/body/eval_jaxpr/hqk,khe->qhe/dot_general | solution.py:126
  104.3 1.6 collective-permute-start.12
  108.4 2.3 %collective-permute-done.12 = bf16[384,192]{0,1:T(8,128)(2,1)S(1)} collective-permute-done((bf16[384,192]{0,1:T(8,128)(2,1)}, bf16[384,192]{0,1:T(8,128)(2,1)S(1)}, u32[]{:S(2)}, u32[]{:S(2)}) %collective-permute-start.12) | collective-permute-done | bytes 147488 | tf_op jit(solution)/shard_map/ppermute | solution.py:92
  114.0 3.2 %collective-permute-done.14 = bf16[384,192]{0,1:T(8,128)(2,1)S(1)} collective-permute-done((bf16[384,192]{0,1:T(8,128)(2,1)S(1)}, bf16[384,192]{0,1:T(8,128)(2,1)S(1)}, u32[]{:S(2)}, u32[]{:S(2)}) %collective-permute-start.14) | collective-permute-done | bytes 147488 | tf_op jit(solution)/shard_map/ppermute | solution.py:92
  118.8 5.1 %collective-permute-done.16 = bf16[384,192]{0,1:T(8,128)(2,1)S(1)} collective-permute-done((bf16[384,192]{0,1:T(8,128)(2,1)S(1)}, bf16[384,192]{0,1:T(8,128)(2,1)S(1)}, u32[]{:S(2)}, u32[]{:S(2)}) %collective-permute-start.16) | collective-permute-done | bytes 147488 | tf_op jit(solution)/shard_map/ppermute | solution.py:92
  124.0 1.6 collective-permute-start.23
  132.8 5.2 %collective-permute-done.17 = bf16[128,1536]{1,0:T(8,128)(2,1)S(1)} collective-permute-done((bf16[128,1536]{1,0:T(8,128)(2,1)S(1)}, bf16[128,1536]{1,0:T(8,128)(2,1)S(1)}, u32[]{:S(2)}, u32[]{:S(2)}) %collective-permute-start.17) | collective-permute-done | bytes 393248 | tf_op jit(solution)/shard_map/ppermute | solution.py:42
  139.3 6.2 %collective-permute-done.19 = bf16[128,1536]{1,0:T(8,128)(2,1)S(1)} collective-permute-done((bf16[128,1536]{1,0:T(8,128)(2,1)S(1)}, bf16[128,1536]{1,0:T(8,128)(2,1)S(1)}, u32[]{:S(2)}, u32[]{:S(2)}) %collective-permute-start.19) | collective-permute-done | bytes 393248 | tf_op jit(solution)/shard_map/ppermute | solution.py:42
  146.3 2.1 collective-permute-start.20
  149.6 1.6 collective-permute-start.27
  151.7 6.2 %collective-permute-done.20 = bf16[128,1536]{1,0:T(8,128)(2,1)S(1)} collective-permute-done((bf16[128,1536]{1,0:T(8,128)(2,1)S(1)}, bf16[128,1536]{1,0:T(8,128)(2,1)S(1)}, u32[]{:S(2)}, u32[]{:S(2)}) %collective-permute-start.20) | collective-permute-done | bytes 393248 | tf_op jit(solution)/shard_map/ppermute | solution.py:28
  158.0 9.6 %collective-permute-done.21 = bf16[128,1536]{1,0:T(8,128)(2,1)S(1)} collective-permute-done((bf16[128,1536]{1,0:T(8,128)(2,1)S(1)}, bf16[128,1536]{1,0:T(8,128)(2,1)S(1)}, u32[]{:S(2)}, u32[]{:S(2)}) %collective-permute-start.21) | collective-permute-done | bytes 393248 | tf_op jit(solution)/shard_map/ppermute | solution.py:28
  167.8 1.6 collective-permute-start.29
  169.5 5.3 %collective-permute-done.29 = bf16[192,768]{1,0:T(8,128)(2,1)S(1)} collective-permute-done((bf16[192,768]{1,0:T(8,128)(2,1)S(1)}, bf16[192,768]{1,0:T(8,128)(2,1)S(1)}, u32[]{:S(2)}, u32[]{:S(2)}) %collective-permute-start.29) | collective-permute-done | bytes 294944 | tf_op jit(solution)/shard_map/ppermute | solution.py:92
  174.8 1.6 collective-permute-start.30
  176.9 2.4 %copy.36 = bf16[768,1536]{1,0:T(8,128)(2,1)} copy(bf16[768,1536]{0,1:T(8,128)(2,1)S(1)} %bitcast.154) | data formatting | bytes 4718592 | tf_op jit(solution)/shard_map/dot_general | solution.py:179
  179.3 3.6 %fusion.6 = f32[512,2,384]{2,0,1:T(8,128)S(1)} fusion(bf16[2,384,1536]{2,1,0:T(8,128)(2,1)} %bitcast.157, bf16[1024,1536]{1,0:T(8,128)(2,1)} %copy-done.6, s32[]{:T(128)S(6)} %select_n.440), kind=kOutput, calls=%fused_computation.12 | convolution fusion | flops 1207959552 | bytes 5505028 | tf_op jit(solution)/shard_map/dot_general | solution.py:179
  184.6 1.6 collective-permute-start.32
  186.8 4.2 %collective-permute-done.32 = bf16[384,192]{0,1:T(8,128)(2,1)S(1)} collective-permute-done((bf16[384,192]{0,1:T(8,128)(2,1)S(1)}, bf16[384,192]{0,1:T(8,128)(2,1)S(1)}, u32[]{:S(2)}, u32[]{:S(2)}) %collective-permute-start.32) | collective-permute-done | bytes 147488 | tf_op jit(solution)/shard_map/ppermute | solution.py:92
  193.1 3.4 %collective-permute-done.34 = bf16[384,192]{0,1:T(8,128)(2,1)S(1)} collective-permute-done((bf16[384,192]{0,1:T(8,128)(2,1)S(1)}, bf16[384,192]{0,1:T(8,128)(2,1)S(1)}, u32[]{:S(2)}, u32[]{:S(2)}) %collective-permute-start.34) | collective-permute-done | bytes 147488 | tf_op jit(solution)/shard_map/ppermute | solution.py:92
  198.1 3.5 %collective-permute-done.36 = bf16[384,192]{0,1:T(8,128)(2,1)S(1)} collective-permute-done((bf16[384,192]{0,1:T(8,128)(2,1)S(1)}, bf16[384,192]{0,1:T(8,128)(2,1)S(1)}, u32[]{:S(2)}, u32[]{:S(2)}) %collective-permute-start.36) | collective-permute-done | bytes 147488 | tf_op jit(solution)/shard_map/ppermute | solution.py:92
  202.0 9.1 %convolution_convert_fusion.1 = bf16[512,1536]{1,0:T(8,128)(2,1)S(1)} fusion(bf16[384,1536]{0,1:T(8,128)(2,1)S(1)} %bitcast.161, bf16[512,384]{1,0:T(8,128)(2,1)S(1)} %fusion.33, f32[384]{0:T(512)S(1)} %copy-done.34, f32[384]{0:T(512)S(1)} %copy-done.35, f32[384]{0:T(512)S(1)} %get-tuple-element.33, f32[384]{0:T(512)S(1)} %get-tuple-element.34, ...), kind=kOutput, calls=%fused_computation.6 | convolution fusion | flops 629932032 | bytes 3209216 | tf_op jit(solution)/shard_map/dot_general | solution.py:189
  211.3 1.7 collective-permute-start.38
  214.4 7.7 %collective-permute-done.37 = bf16[128,1536]{1,0:T(8,128)(2,1)S(1)} collective-permute-done((bf16[128,1536]{1,0:T(8,128)(2,1)S(1)}, bf16[128,1536]{1,0:T(8,128)(2,1)S(1)}, u32[]{:S(2)}, u32[]{:S(2)}) %collective-permute-start.37) | collective-permute-done | bytes 393248 | tf_op jit(solution)/shard_map/ppermute | solution.py:42
  223.3 7.0 %collective-permute-done.39 = bf16[128,1536]{1,0:T(8,128)(2,1)S(1)} collective-permute-done((bf16[128,1536]{1,0:T(8,128)(2,1)S(1)}, bf16[128,1536]{1,0:T(8,128)(2,1)S(1)}, u32[]{:S(2)}, u32[]{:S(2)}) %collective-permute-start.39) | collective-permute-done | bytes 393248 | tf_op jit(solution)/shard_map/ppermute | solution.py:42
  (221 shorter events, 44.4 us)
Async XLA Ops:
  1.9 51.9 %collective-permute-start.3 = (bf16[192,1152]{1,0:T(8,128)(2,1)}, bf16[192,1152]{1,0:T(8,128)(2,1)}, u32[]{:S(2)}, u32[]{:S(2)}) collective-permute-start(bf16[192,1152]{1,0:T(8,128)(2,1)} %bitcast.70), channel_id=1, source_target_pairs={{0,8},{8,16},{16,24},{24,28},{28,20},{20,12},{12,4},{4,0},{1,9},{9... | collective-permute-start | bytes 1327112 | tf_op jit(solution)/shard_map/ppermute | solution.py:92
  4.9 50.4 %collective-permute-start.4 = (bf16[192,1152]{1,0:T(8,128)(2,1)}, bf16[192,1152]{1,0:T(8,128)(2,1)}, u32[]{:S(2)}, u32[]{:S(2)}) collective-permute-start(bf16[192,1152]{1,0:T(8,128)(2,1)} %bitcast.70), channel_id=1, source_target_pairs={{0,4},{8,0},{16,8},{24,16},{28,24},{20,28},{12,20},{4,12},{1,5},{9... | collective-permute-start | bytes 1327112 | tf_op jit(solution)/shard_map/ppermute | solution.py:95
  9.4 31.9 %collective-permute-start = (bf16[128,1536]{1,0:T(8,128)(2,1)}, bf16[128,1536]{1,0:T(8,128)(2,1)}, u32[]{:S(2)}, u32[]{:S(2)}) collective-permute-start(bf16[128,1536]{1,0:T(8,128)(2,1)} %get-tuple-element.68), channel_id=1, source_target_pairs={{0,3},{1,0},{2,1},{3,2},{4,7},{5,4},{6,5},{7,6},{8,11},{9,8},{10,9... | collective-permute-start | bytes 1179656 | tf_op jit(solution)/shard_map/ppermute | solution.py:28
  10.2 32.9 %collective-permute-start.1 = (bf16[128,1536]{1,0:T(8,128)(2,1)}, bf16[128,1536]{1,0:T(8,128)(2,1)}, u32[]{:S(2)}, u32[]{:S(2)}) collective-permute-start(bf16[128,1536]{1,0:T(8,128)(2,1)} %get-tuple-element.68), channel_id=1, source_target_pairs={{0,2},{1,3},{2,0},{3,1},{4,6},{5,7},{6,4},{7,5},{8,10},{9,11},{10,... | collective-permute-start | bytes 1179656 | tf_op jit(solution)/shard_map/ppermute | solution.py:28
  11.3 33.5 %collective-permute-start.2 = (bf16[128,1536]{1,0:T(8,128)(2,1)}, bf16[128,1536]{1,0:T(8,128)(2,1)}, u32[]{:S(2)}, u32[]{:S(2)}) collective-permute-start(bf16[128,1536]{1,0:T(8,128)(2,1)} %get-tuple-element.68), channel_id=1, source_target_pairs={{0,1},{1,2},{2,3},{3,0},{4,5},{5,6},{6,7},{7,4},{8,9},{9,10},{10,1... | collective-permute-start | bytes 1179656 | tf_op jit(solution)/shard_map/ppermute | solution.py:28
  53.8 13.1 %collective-permute-start.5 = (bf16[192,1152]{1,0:T(8,128)(2,1)}, bf16[192,1152]{1,0:T(8,128)(2,1)S(1)}, u32[]{:S(2)}, u32[]{:S(2)}) collective-permute-start(bf16[192,1152]{1,0:T(8,128)(2,1)} %collective-permute-done.3), channel_id=1, source_target_pairs={{0,8},{8,16},{16,24},{24,28},{28,20},{20,12},{12,4},{4,0},{1,9},{9... | collective-permute-start | bytes 1327112 | tf_op jit(solution)/shard_map/ppermute | solution.py:92
  55.3 13.1 %collective-permute-start.6 = (bf16[192,1152]{1,0:T(8,128)(2,1)}, bf16[192,1152]{1,0:T(8,128)(2,1)S(1)}, u32[]{:S(2)}, u32[]{:S(2)}) collective-permute-start(bf16[192,1152]{1,0:T(8,128)(2,1)} %collective-permute-done.4), channel_id=1, source_target_pairs={{0,4},{8,0},{16,8},{24,16},{28,24},{20,28},{12,20},{4,12},{1,5},{9... | collective-permute-start | bytes 1327112 | tf_op jit(solution)/shard_map/ppermute | solution.py:95
  57.9 34.2 %copy-start.5 = (bf16[1024,1536]{1,0:T(8,128)(2,1)S(1)}, bf16[1024,1536]{1,0:T(8,128)(2,1)}, u32[]{:S(2)}) copy-start(bf16[1024,1536]{1,0:T(8,128)(2,1)} %constant_dynamic-update-slice_fusion) | copy-start | bytes 9437188
  66.8 12.0 %collective-permute-start.7 = (bf16[192,1152]{1,0:T(8,128)(2,1)S(1)}, bf16[192,1152]{1,0:T(8,128)(2,1)S(1)}, u32[]{:S(2)}, u32[]{:S(2)}) collective-permute-start(bf16[192,1152]{1,0:T(8,128)(2,1)S(1)} %collective-permute-done.5), channel_id=1, source_target_pairs={{0,8},{8,16},{16,24},{24,28},{28,20},{20,12},{12,4},{4,0},{1,9},{9... | collective-permute-start | bytes 1327112 | tf_op jit(solution)/shard_map/ppermute | solution.py:92
  68.4 12.1 %collective-permute-start.8 = (bf16[192,1152]{1,0:T(8,128)(2,1)S(1)}, bf16[192,1152]{1,0:T(8,128)(2,1)S(1)}, u32[]{:S(2)}, u32[]{:S(2)}) collective-permute-start(bf16[192,1152]{1,0:T(8,128)(2,1)S(1)} %collective-permute-done.6), channel_id=1, source_target_pairs={{0,4},{8,0},{16,8},{24,16},{28,24},{20,28},{12,20},{4,12},{1,5},{9... | collective-permute-start | bytes 1327112 | tf_op jit(solution)/shard_map/ppermute | solution.py:95
  78.8 11.2 %collective-permute-start.9 = (bf16[192,1152]{1,0:T(8,128)(2,1)S(1)}, bf16[192,1152]{1,0:T(8,128)(2,1)S(1)}, u32[]{:S(2)}, u32[]{:S(2)}) collective-permute-start(bf16[192,1152]{1,0:T(8,128)(2,1)S(1)} %collective-permute-done.7), channel_id=1, source_target_pairs={{0,8},{8,16},{16,24},{24,28},{28,20},{20,12},{12,4},{4,0},{1,9},{9... | collective-permute-start | bytes 1327112 | tf_op jit(solution)/shard_map/ppermute | solution.py:92
  90.0 14.3 %collective-permute-start.10 = (bf16[384,192]{0,1:T(8,128)(2,1)}, bf16[384,192]{0,1:T(8,128)(2,1)}, u32[]{:S(2)}, u32[]{:S(2)}) collective-permute-start(bf16[384,192]{0,1:T(8,128)(2,1)} %param.22), channel_id=1, source_target_pairs={{0,8},{8,16},{16,24},{24,28},{28,20},{20,12},{12,4},{4,0},{1,9},{9... | collective-permute-start | bytes 442376 | tf_op jit(solution)/shard_map/ppermute | solution.py:92
  91.7 15.3 %collective-permute-start.11 = (bf16[384,192]{0,1:T(8,128)(2,1)}, bf16[384,192]{0,1:T(8,128)(2,1)}, u32[]{:S(2)}, u32[]{:S(2)}) collective-permute-start(bf16[384,192]{0,1:T(8,128)(2,1)} %param.22), channel_id=1, source_target_pairs={{0,4},{8,0},{16,8},{24,16},{28,24},{20,28},{12,20},{4,12},{1,5},{9... | collective-permute-start | bytes 442376 | tf_op jit(solution)/shard_map/ppermute | solution.py:95
  103.3 20.7 %copy-start.3 = (bf16[24,8,2,384]{3,1,2,0:T(8,128)(2,1)S(1)}, bf16[24,8,2,384]{3,1,2,0:T(8,128)(2,1)}, u32[]{:S(2)}) copy-start(bf16[24,8,2,384]{3,1,2,0:T(8,128)(2,1)} %copy.38) | copy-start | bytes 884740
  104.3 6.4 %collective-permute-start.12 = (bf16[384,192]{0,1:T(8,128)(2,1)}, bf16[384,192]{0,1:T(8,128)(2,1)S(1)}, u32[]{:S(2)}, u32[]{:S(2)}) collective-permute-start(bf16[384,192]{0,1:T(8,128)(2,1)} %collective-permute-done.10), channel_id=1, source_target_pairs={{0,8},{8,16},{16,24},{24,28},{28,20},{20,12},{12,4},{4,0},{1,9},{9... | collective-permute-start | bytes 442376 | tf_op jit(solution)/shard_map/ppermute | solution.py:92
  106.9 6.4 %collective-permute-start.13 = (bf16[384,192]{0,1:T(8,128)(2,1)}, bf16[384,192]{0,1:T(8,128)(2,1)S(1)}, u32[]{:S(2)}, u32[]{:S(2)}) collective-permute-start(bf16[384,192]{0,1:T(8,128)(2,1)} %collective-permute-done.11), channel_id=1, source_target_pairs={{0,4},{8,0},{16,8},{24,16},{28,24},{20,28},{12,20},{4,12},{1,5},{9... | collective-permute-start | bytes 442376 | tf_op jit(solution)/shard_map/ppermute | solution.py:95
  110.8 6.4 %collective-permute-start.14 = (bf16[384,192]{0,1:T(8,128)(2,1)S(1)}, bf16[384,192]{0,1:T(8,128)(2,1)S(1)}, u32[]{:S(2)}, u32[]{:S(2)}) collective-permute-start(bf16[384,192]{0,1:T(8,128)(2,1)S(1)} %collective-permute-done.12), channel_id=1, source_target_pairs={{0,8},{8,16},{16,24},{24,28},{28,20},{20,12},{12,4},{4,0},{1,9},{9... | collective-permute-start | bytes 442376 | tf_op jit(solution)/shard_map/ppermute | solution.py:92
  113.3 5.5 %collective-permute-start.15 = (bf16[384,192]{0,1:T(8,128)(2,1)S(1)}, bf16[384,192]{0,1:T(8,128)(2,1)S(1)}, u32[]{:S(2)}, u32[]{:S(2)}) collective-permute-start(bf16[384,192]{0,1:T(8,128)(2,1)S(1)} %collective-permute-done.13), channel_id=1, source_target_pairs={{0,4},{8,0},{16,8},{24,16},{28,24},{20,28},{12,20},{4,12},{1,5},{9... | collective-permute-start | bytes 442376 | tf_op jit(solution)/shard_map/ppermute | solution.py:95
  117.2 6.7 %collective-permute-start.16 = (bf16[384,192]{0,1:T(8,128)(2,1)S(1)}, bf16[384,192]{0,1:T(8,128)(2,1)S(1)}, u32[]{:S(2)}, u32[]{:S(2)}) collective-permute-start(bf16[384,192]{0,1:T(8,128)(2,1)S(1)} %collective-permute-done.14), channel_id=1, source_target_pairs={{0,8},{8,16},{16,24},{24,28},{28,20},{20,12},{12,4},{4,0},{1,9},{9... | collective-permute-start | bytes 442376 | tf_op jit(solution)/shard_map/ppermute | solution.py:92
  124.0 6.8 %collective-permute-start.23 = (bf16[192,768]{1,0:T(8,128)(2,1)S(1)}, bf16[192,768]{1,0:T(8,128)(2,1)S(1)}, u32[]{:S(2)}, u32[]{:S(2)}) collective-permute-start(bf16[192,768]{1,0:T(8,128)(2,1)S(1)} %bitcast.162), channel_id=1, source_target_pairs={{0,8},{8,16},{16,24},{24,28},{28,20},{20,12},{12,4},{4,0},{1,9},{9... | collective-permute-start | bytes 884744 | tf_op jit(solution)/shard_map/ppermute | solution.py:92
  125.6 6.7 %collective-permute-start.24 = (bf16[192,768]{1,0:T(8,128)(2,1)S(1)}, bf16[192,768]{1,0:T(8,128)(2,1)S(1)}, u32[]{:S(2)}, u32[]{:S(2)}) collective-permute-start(bf16[192,768]{1,0:T(8,128)(2,1)S(1)} %bitcast.163), channel_id=1, source_target_pairs={{0,4},{8,0},{16,8},{24,16},{28,24},{20,28},{12,20},{4,12},{1,5},{9... | collective-permute-start | bytes 884744 | tf_op jit(solution)/shard_map/ppermute | solution.py:95
  127.2 10.9 %collective-permute-start.17 = (bf16[128,1536]{1,0:T(8,128)(2,1)S(1)}, bf16[128,1536]{1,0:T(8,128)(2,1)S(1)}, u32[]{:S(2)}, u32[]{:S(2)}) collective-permute-start(bf16[128,1536]{1,0:T(8,128)(2,1)S(1)} %get-tuple-element.72), channel_id=1, source_target_pairs={{0,1},{1,2},{2,3},{3,0},{4,5},{5,6},{6,7},{7,4},{8,9},{9,10},{10,1... | collective-permute-start | bytes 1179656 | tf_op jit(solution)/shard_map/ppermute | solution.py:42
  127.3 12.0 %collective-permute-start.18 = (bf16[128,1536]{1,0:T(8,128)(2,1)S(1)}, bf16[128,1536]{1,0:T(8,128)(2,1)S(1)}, u32[]{:S(2)}, u32[]{:S(2)}) collective-permute-start(bf16[128,1536]{1,0:T(8,128)(2,1)S(1)} %get-tuple-element.74), channel_id=1, source_target_pairs={{0,2},{1,3},{2,0},{3,1},{4,6},{5,7},{6,4},{7,5},{8,10},{9,11},{10,... | collective-permute-start | bytes 1179656 | tf_op jit(solution)/shard_map/ppermute | solution.py:42
  128.2 17.3 %collective-permute-start.19 = (bf16[128,1536]{1,0:T(8,128)(2,1)S(1)}, bf16[128,1536]{1,0:T(8,128)(2,1)S(1)}, u32[]{:S(2)}, u32[]{:S(2)}) collective-permute-start(bf16[128,1536]{1,0:T(8,128)(2,1)S(1)} %get-tuple-element.73), channel_id=1, source_target_pairs={{0,3},{1,0},{2,1},{3,2},{4,7},{5,4},{6,5},{7,6},{8,11},{9,8},{10,9... | collective-permute-start | bytes 1179656 | tf_op jit(solution)/shard_map/ppermute | solution.py:42
  130.7 18.9 %collective-permute-start.25 = (bf16[192,768]{1,0:T(8,128)(2,1)S(1)}, bf16[192,768]{1,0:T(8,128)(2,1)S(1)}, u32[]{:S(2)}, u32[]{:S(2)}) collective-permute-start(bf16[192,768]{1,0:T(8,128)(2,1)S(1)} %collective-permute-done.23), channel_id=1, source_target_pairs={{0,8},{8,16},{16,24},{24,28},{28,20},{20,12},{12,4},{4,0},{1,9},{9... | collective-permute-start | bytes 884744 | tf_op jit(solution)/shard_map/ppermute | solution.py:92
  132.3 18.9 %collective-permute-start.26 = (bf16[192,768]{1,0:T(8,128)(2,1)S(1)}, bf16[192,768]{1,0:T(8,128)(2,1)S(1)}, u32[]{:S(2)}, u32[]{:S(2)}) collective-permute-start(bf16[192,768]{1,0:T(8,128)(2,1)S(1)} %collective-permute-done.24), channel_id=1, source_target_pairs={{0,4},{8,0},{16,8},{24,16},{28,24},{20,28},{12,20},{4,12},{1,5},{9... | collective-permute-start | bytes 884744 | tf_op jit(solution)/shard_map/ppermute | solution.py:95
  146.3 11.6 %collective-permute-start.20 = (bf16[128,1536]{1,0:T(8,128)(2,1)S(1)}, bf16[128,1536]{1,0:T(8,128)(2,1)S(1)}, u32[]{:S(2)}, u32[]{:S(2)}) collective-permute-start(bf16[128,1536]{1,0:T(8,128)(2,1)S(1)} %get-tuple-element.64), channel_id=1, source_target_pairs={{0,3},{1,0},{2,1},{3,2},{4,7},{5,4},{6,5},{7,6},{8,11},{9,8},{10,9... | collective-permute-start | bytes 1179656 | tf_op jit(solution)/shard_map/ppermute | solution.py:28
  148.5 19.0 %collective-permute-start.21 = (bf16[128,1536]{1,0:T(8,128)(2,1)S(1)}, bf16[128,1536]{1,0:T(8,128)(2,1)S(1)}, u32[]{:S(2)}, u32[]{:S(2)}) collective-permute-start(bf16[128,1536]{1,0:T(8,128)(2,1)S(1)} %get-tuple-element.64), channel_id=1, source_target_pairs={{0,2},{1,3},{2,0},{3,1},{4,6},{5,7},{6,4},{7,5},{8,10},{9,11},{10,... | collective-permute-start | bytes 1179656 | tf_op jit(solution)/shard_map/ppermute | solution.py:28
  149.6 17.9 %collective-permute-start.22 = (bf16[128,1536]{1,0:T(8,128)(2,1)S(1)}, bf16[128,1536]{1,0:T(8,128)(2,1)S(1)}, u32[]{:S(2)}, u32[]{:S(2)}) collective-permute-start(bf16[128,1536]{1,0:T(8,128)(2,1)S(1)} %get-tuple-element.64), channel_id=1, source_target_pairs={{0,1},{1,2},{2,3},{3,0},{4,5},{5,6},{6,7},{7,4},{8,9},{9,10},{10,1... | collective-permute-start | bytes 1179656 | tf_op jit(solution)/shard_map/ppermute | solution.py:28
  149.6 18.1 %collective-permute-start.27 = (bf16[192,768]{1,0:T(8,128)(2,1)S(1)}, bf16[192,768]{1,0:T(8,128)(2,1)S(1)}, u32[]{:S(2)}, u32[]{:S(2)}) collective-permute-start(bf16[192,768]{1,0:T(8,128)(2,1)S(1)} %collective-permute-done.25), channel_id=1, source_target_pairs={{0,8},{8,16},{16,24},{24,28},{28,20},{20,12},{12,4},{4,0},{1,9},{9... | collective-permute-start | bytes 884744 | tf_op jit(solution)/shard_map/ppermute | solution.py:92
  151.2 18.2 %collective-permute-start.28 = (bf16[192,768]{1,0:T(8,128)(2,1)S(1)}, bf16[192,768]{1,0:T(8,128)(2,1)S(1)}, u32[]{:S(2)}, u32[]{:S(2)}) collective-permute-start(bf16[192,768]{1,0:T(8,128)(2,1)S(1)} %collective-permute-done.26), channel_id=1, source_target_pairs={{0,4},{8,0},{16,8},{24,16},{28,24},{20,28},{12,20},{4,12},{1,5},{9... | collective-permute-start | bytes 884744 | tf_op jit(solution)/shard_map/ppermute | solution.py:95
  167.8 7.0 %collective-permute-start.29 = (bf16[192,768]{1,0:T(8,128)(2,1)S(1)}, bf16[192,768]{1,0:T(8,128)(2,1)S(1)}, u32[]{:S(2)}, u32[]{:S(2)}) collective-permute-start(bf16[192,768]{1,0:T(8,128)(2,1)S(1)} %collective-permute-done.27), channel_id=1, source_target_pairs={{0,8},{8,16},{16,24},{24,28},{28,20},{20,12},{12,4},{4,0},{1,9},{9... | collective-permute-start | bytes 884744 | tf_op jit(solution)/shard_map/ppermute | solution.py:92
  174.8 9.8 %collective-permute-start.30 = (bf16[384,192]{0,1:T(8,128)(2,1)}, bf16[384,192]{0,1:T(8,128)(2,1)S(1)}, u32[]{:S(2)}, u32[]{:S(2)}) collective-permute-start(bf16[384,192]{0,1:T(8,128)(2,1)} %param.25), channel_id=1, source_target_pairs={{0,8},{8,16},{16,24},{24,28},{28,20},{20,12},{12,4},{4,0},{1,9},{9... | collective-permute-start | bytes 442376 | tf_op jit(solution)/shard_map/ppermute | solution.py:92
  176.4 9.8 %collective-permute-start.31 = (bf16[384,192]{0,1:T(8,128)(2,1)}, bf16[384,192]{0,1:T(8,128)(2,1)S(1)}, u32[]{:S(2)}, u32[]{:S(2)}) collective-permute-start(bf16[384,192]{0,1:T(8,128)(2,1)} %param.25), channel_id=1, source_target_pairs={{0,4},{8,0},{16,8},{24,16},{28,24},{20,28},{12,20},{4,12},{1,5},{9... | collective-permute-start | bytes 442376 | tf_op jit(solution)/shard_map/ppermute | solution.py:95
  182.9 18.7 %copy-start.9 = (f32[384]{0:T(512)S(1)}, f32[384]{0:T(512)}, u32[]{:S(2)}) copy-start(f32[384]{0:T(512)} %get-tuple-element.36) | copy-start | bytes 4612
  182.9 18.7 %copy-start.10 = (f32[384]{0:T(512)S(1)}, f32[384]{0:T(512)}, u32[]{:S(2)}) copy-start(f32[384]{0:T(512)} %get-tuple-element.37) | copy-start | bytes 4612
  182.9 18.7 %copy-start.11 = (f32[384]{0:T(512)S(1)}, f32[384]{0:T(512)}, u32[]{:S(2)}) copy-start(f32[384]{0:T(512)} %get-tuple-element.38) | copy-start | bytes 4612
  182.9 18.7 %copy-start.12 = (f32[384]{0:T(512)S(1)}, f32[384]{0:T(512)}, u32[]{:S(2)}) copy-start(f32[384]{0:T(512)} %get-tuple-element.39) | copy-start | bytes 4612
  182.9 18.7 %copy-start.13 = (f32[384]{0:T(512)S(1)}, f32[384]{0:T(512)}, u32[]{:S(2)}) copy-start(f32[384]{0:T(512)} %get-tuple-element.40) | copy-start | bytes 4612
  182.9 18.7 %copy-start.14 = (f32[384]{0:T(512)S(1)}, f32[384]{0:T(512)}, u32[]{:S(2)}) copy-start(f32[384]{0:T(512)} %get-tuple-element.41) | copy-start | bytes 4612
  184.6 6.3 %collective-permute-start.32 = (bf16[384,192]{0,1:T(8,128)(2,1)S(1)}, bf16[384,192]{0,1:T(8,128)(2,1)S(1)}, u32[]{:S(2)}, u32[]{:S(2)}) collective-permute-start(bf16[384,192]{0,1:T(8,128)(2,1)S(1)} %collective-permute-done.30), channel_id=1, source_target_pairs={{0,8},{8,16},{16,24},{24,28},{28,20},{20,12},{12,4},{4,0},{1,9},{9... | collective-permute-start | bytes 442376 | tf_op jit(solution)/shard_map/ppermute | solution.py:92
  186.2 6.3 %collective-permute-start.33 = (bf16[384,192]{0,1:T(8,128)(2,1)S(1)}, bf16[384,192]{0,1:T(8,128)(2,1)S(1)}, u32[]{:S(2)}, u32[]{:S(2)}) collective-permute-start(bf16[384,192]{0,1:T(8,128)(2,1)S(1)} %collective-permute-done.31), channel_id=1, source_target_pairs={{0,4},{8,0},{16,8},{24,16},{28,24},{20,28},{12,20},{4,12},{1,5},{9... | collective-permute-start | bytes 442376 | tf_op jit(solution)/shard_map/ppermute | solution.py:95
  190.9 5.5 %collective-permute-start.34 = (bf16[384,192]{0,1:T(8,128)(2,1)S(1)}, bf16[384,192]{0,1:T(8,128)(2,1)S(1)}, u32[]{:S(2)}, u32[]{:S(2)}) collective-permute-start(bf16[384,192]{0,1:T(8,128)(2,1)S(1)} %collective-permute-done.32), channel_id=1, source_target_pairs={{0,8},{8,16},{16,24},{24,28},{28,20},{20,12},{12,4},{4,0},{1,9},{9... | collective-permute-start | bytes 442376 | tf_op jit(solution)/shard_map/ppermute | solution.py:92
  192.5 5.5 %collective-permute-start.35 = (bf16[384,192]{0,1:T(8,128)(2,1)S(1)}, bf16[384,192]{0,1:T(8,128)(2,1)S(1)}, u32[]{:S(2)}, u32[]{:S(2)}) collective-permute-start(bf16[384,192]{0,1:T(8,128)(2,1)S(1)} %collective-permute-done.33), channel_id=1, source_target_pairs={{0,4},{8,0},{16,8},{24,16},{28,24},{20,28},{12,20},{4,12},{1,5},{9... | collective-permute-start | bytes 442376 | tf_op jit(solution)/shard_map/ppermute | solution.py:95
  196.4 5.1 %collective-permute-start.36 = (bf16[384,192]{0,1:T(8,128)(2,1)S(1)}, bf16[384,192]{0,1:T(8,128)(2,1)S(1)}, u32[]{:S(2)}, u32[]{:S(2)}) collective-permute-start(bf16[384,192]{0,1:T(8,128)(2,1)S(1)} %collective-permute-done.34), channel_id=1, source_target_pairs={{0,8},{8,16},{16,24},{24,28},{28,20},{20,12},{12,4},{4,0},{1,9},{9... | collective-permute-start | bytes 442376 | tf_op jit(solution)/shard_map/ppermute | solution.py:92
  211.2 10.9 %collective-permute-start.37 = (bf16[128,1536]{1,0:T(8,128)(2,1)S(1)}, bf16[128,1536]{1,0:T(8,128)(2,1)S(1)}, u32[]{:S(2)}, u32[]{:S(2)}) collective-permute-start(bf16[128,1536]{1,0:T(8,128)(2,1)S(1)} %get-tuple-element.69), channel_id=1, source_target_pairs={{0,1},{1,2},{2,3},{3,0},{4,5},{5,6},{6,7},{7,4},{8,9},{9,10},{10,1... | collective-permute-start | bytes 1179656 | tf_op jit(solution)/shard_map/ppermute | solution.py:42
  211.3 12.0 %collective-permute-start.38 = (bf16[128,1536]{1,0:T(8,128)(2,1)S(1)}, bf16[128,1536]{1,0:T(8,128)(2,1)S(1)}, u32[]{:S(2)}, u32[]{:S(2)}) collective-permute-start(bf16[128,1536]{1,0:T(8,128)(2,1)S(1)} %get-tuple-element.71), channel_id=1, source_target_pairs={{0,2},{1,3},{2,0},{3,1},{4,6},{5,7},{6,4},{7,5},{8,10},{9,11},{10,... | collective-permute-start | bytes 1179656 | tf_op jit(solution)/shard_map/ppermute | solution.py:42
  213.0 17.3 %collective-permute-start.39 = (bf16[128,1536]{1,0:T(8,128)(2,1)S(1)}, bf16[128,1536]{1,0:T(8,128)(2,1)S(1)}, u32[]{:S(2)}, u32[]{:S(2)}) collective-permute-start(bf16[128,1536]{1,0:T(8,128)(2,1)S(1)} %get-tuple-element.70), channel_id=1, source_target_pairs={{0,3},{1,0},{2,1},{3,2},{4,7},{5,4},{6,5},{7,6},{8,11},{9,8},{10,9... | collective-permute-start | bytes 1179656 | tf_op jit(solution)/shard_map/ppermute | solution.py:42
  (43 other events, 719.8 us)

commit v3 on v2

--- a/solution.py
+++ b/solution.py
@@ -19,17 +19,44 @@
     return jnp.sum((positions[:, None] >= record_ends[None, :]).astype(jnp.int32), axis=1)
 
 
-def seq_gather(block):
+def seq_gather(block, paired):
     count = lax.axis_size("seq")
     me = lax.axis_index("seq")
-    parts = [block]
-    for shift in range(1, count):
-        parts.append(
-            lax.ppermute(block, "seq", [(i, (i - shift) % count) for i in range(count)])
+    out = jnp.zeros((count,) + block.shape, block.dtype)
+    out = lax.dynamic_update_index_in_dim(out, block, me, 0)
+    if not paired:
+        for shift in range(1, count):
+            got = lax.ppermute(block, "seq", [(i, (i + shift) % count) for i in range(count)])
+            out = lax.dynamic_update_index_in_dim(out, got, (me - shift) % count, 0)
+        return out
+    half = count // 2
+    mine = jnp.zeros((half,) + block.shape, block.dtype)
+    mine = lax.dynamic_update_index_in_dim(mine, block, me // 2, 0)
+    for shift in range(1, half):
+        got = lax.ppermute(
+            block, "seq", [(i, (i + 2 * shift) % count) for i in range(count)]
         )
-    ring = jnp.concatenate(parts + parts, axis=0)
-    rows = block.shape[0]
-    return lax.dynamic_slice_in_dim(ring, ((count - me) % count) * rows, count * rows, axis=0)
+        src_dev = (me - 2 * shift) % count
+        mine = lax.dynamic_update_index_in_dim(mine, got, src_dev // 2, 0)
+        out = lax.dynamic_update_index_in_dim(out, got, src_dev, 0)
+    other = lax.ppermute(mine, "seq", [(i, i ^ 1) for i in range(count)])
+    partner = me ^ 1
+    for k in range(half):
+        out = lax.dynamic_update_index_in_dim(out, other[k], 2 * k + partner % 2, 0)
+    return out
+
+
+def cores_paired(mesh):
+    count = mesh.shape["seq"]
+    if count % 2:
+        return False
+    try:
+        row = mesh.devices[0]
+        return all(
+            tuple(row[2 * k].coords) == tuple(row[2 * k + 1].coords) for k in range(count // 2)
+        )
+    except (AttributeError, TypeError, IndexError):
+        return False
 
 
 def seq_scatter_sum(full):
@@ -145,7 +172,7 @@
     return jax.nn.silu(total_acc).astype(jnp.bfloat16)
 
 
-def on_device(ring, frames, lengths, ln1_gain, ln2_gain, w_qkv, w_out, w_glu, dw_kernel, w_proj):
+def on_device(ring, paired, frames, lengths, ln1_gain, ln2_gain, w_qkv, w_out, w_glu, dw_kernel, w_proj):
     frame_rows = frames.shape[1]
     model_width = frames.shape[2]
     seq_count = lax.axis_size("seq")
@@ -165,7 +192,7 @@
     seg_all = segment_of(record_ends, jnp.arange(group_rows, dtype=jnp.int32))
     normed1 = layer_norm(inputs, ln1_gain)
     projected = (
-        jnp.dot(seq_gather(normed1), qkv_matrix, preferred_element_type=jnp.float32)
+        jnp.dot(seq_gather(normed1, paired).reshape(group_rows, model_width), qkv_matrix, preferred_element_type=jnp.float32)
         .astype(jnp.bfloat16)
         .reshape(group_rows, 3, group_width)
     )
@@ -175,11 +202,11 @@
     )
     middle = (inputs + attn_sum).astype(jnp.bfloat16)
     normed2 = layer_norm(middle.astype(jnp.float32), ln2_gain)
-    shard_piece = seq_gather(normed2)
-    paired = jnp.dot(shard_piece, glu_matrix, preferred_element_type=jnp.float32).reshape(
+    shard_piece = seq_gather(normed2, paired).reshape(group_rows, model_width)
+    glu_pair = jnp.dot(shard_piece, glu_matrix, preferred_element_type=jnp.float32).reshape(
         shard_piece.shape[0], 2, group_width
     )
-    gated = (paired[:, 0] * jax.nn.sigmoid(paired[:, 1])).astype(jnp.bfloat16)
+    gated = (glu_pair[:, 0] * jax.nn.sigmoid(glu_pair[:, 1])).astype(jnp.bfloat16)
     padded = jnp.pad(gated, ((kernel_reach, kernel_reach), (0, 0)))
     near_positions = jnp.arange(-kernel_reach, group_rows + kernel_reach, dtype=jnp.int32)
     activated = depthwise(
@@ -206,5 +233,5 @@
     )
     out_specs = P("dp", "seq", None)
     return jax.shard_map(
-        functools.partial(on_device, dp_ring(mesh)), mesh=mesh, in_specs=in_specs, out_specs=out_specs, check_vma=False
-    )
+        functools.partial(on_device, dp_ring(mesh), cores_paired(mesh)), mesh=mesh, in_specs=in_specs, out_specs=out_specs, check_vma=False
+    )

time: 233 us -> 206 us (0.88)
  waiting for transfers between devices: 101 us -> 88.1 us
  local copies, waits for them, and re-layouts: 31.6 us -> 24.6 us
  other arithmetic: 12.6 us -> 9.89 us
    unnamed x116 -> x110, local copies, waits for them, and re-layouts: 13.7 us -> 0.97 us
    ppermute x6 -> x4, waiting for transfers between devices: 15.8 us -> 7.5 us  [the longest x2 7.49 us: seq_gather(): lax.ppermute(block, 'seq', [(i, (i + 2 * shift) % count) for i in range(c...]
    ppermute x16, waiting for transfers between devices: 56.1 us -> 51.3 us  [ring_gather(): ahead = lax.ppermute(ahead, 'dp', forward)]
    dynamic_update_slice x0 -> x7, local copies, waits for them, and re-layouts: none -> 4.02 us  [the longest x4 2.12 us: seq_gather(): out = lax.dynamic_update_index_in_dim(out, other[k], 2 * k + partner % 2, 0)]
    ppermute x6 -> x4, starting transfers between devices: 5.46 us -> 4.36 us  [the longest x2 3.45 us: seq_gather(): lax.ppermute(block, 'seq', [(i, (i + 2 * shift) % count) for i in range(c...]
  transfers between devices with their start and end apart: 40 -> 38, of which waited for: 20 -> 19; matrix products, arithmetic and copies ran while one was open for 24% -> 21% of each run, Pallas kernels for 0% -> 0%
where the time goes in v3:
time: 206 us; the launch traced here: 205 us
  waiting for transfers between devices  88.1 us (43%)
  starting transfers between devices  41.7 us (20%)
  local copies, waits for them, and re-layouts  24.6 us (12%)
  matrix products  21.7 us (11%)
  between operations  19.3 us (9%)
  other arithmetic  9.89 us (5%)
    ppermute x16, waiting for transfers between devices, ring_gather(): ahead = lax.ppermute(ahead, 'dp', forward)  51.3 us
    ppermute x6, waiting for transfers between devices, seq_scatter_sum(): lax.ppermute(piece, 'seq', [(i, (i + shift) % count) for i in range(count)])  28.2 us
    ppermute x16, starting transfers between devices, ring_gather(): ahead = lax.ppermute(ahead, 'dp', forward)  26.7 us
    dot_general x1, matrix products, on_device(): jnp.dot(activated, proj_local, preferred_element_type=jnp.float32)  8.73 us
    ppermute x2, waiting for transfers between devices, seq_gather(): lax.ppermute(block, 'seq', [(i, (i + 2 * shift) % count) for i in range(c...  7.49 us
    ppermute x12, starting transfers between devices, ring_gather(): behind = lax.ppermute(behind, 'dp', backward)  5.45 us
    ppermute x6, starting transfers between devices, seq_scatter_sum(): lax.ppermute(piece, 'seq', [(i, (i + shift) % count) for i in range(count)])  5.15 us
    dynamic_update_slice x16, local copies, waits for them, and re-layouts, ring_gather(): lax.dynamic_update_index_in_dim(out, ahead, order[(my_pos - step) % count...  4.45 us
  transfers between devices with their start and end apart: 38, of which 19 were waited for; matrix products, arithmetic and copies ran while one was open for 21% of the time, Pallas kernels for 0%

profile of v3, /device:TPU:0, one launch (start us, length us, event | category | flops | bytes accessed | tf_op | source)
XLA Modules:
  0.0 205.1 jit_solution(15979965411789606697)
XLA Ops:
  0.0 1.9 copy.37
  1.9 3.0 %collective-permute-start.2 = (bf16[192,1152]{1,0:T(8,128)(2,1)}, bf16[192,1152]{1,0:T(8,128)(2,1)S(1)}, u32[]{:S(2)}, u32[]{:S(2)}) collective-permute-start(bf16[192,1152]{1,0:T(8,128)(2,1)} %bitcast.76), channel_id=1, source_target_pairs={{0,8},{8,16},{16,24},{24,28},{28,20},{20,12},{12,4},{4,0},{1,9},{9... | collective-permute-start | bytes 1327112 | tf_op jit(solution)/shard_map/ppermute | solution.py:119
  5.0 1.1 convert_reduce_fusion.1
  6.1 1.2 fusion.16
  7.7 2.0 collective-permute-start
  30.2 2.2 %broadcast_in_dim.420 = bf16[8,192,1152]{2,1,0:T(8,128)(2,1)} broadcast(bf16[]{:T(256)} %constant.379.clone.1), dimensions={} | broadcast | bytes 3538946 | tf_op jit(solution)/shard_map/broadcast_in_dim | solution.py:115
  38.6 1.6 collective-permute-start.4
  42.3 8.9 %collective-permute-done.4 = bf16[192,1152]{1,0:T(8,128)(2,1)S(1)} collective-permute-done((bf16[192,1152]{1,0:T(8,128)(2,1)S(1)}, bf16[192,1152]{1,0:T(8,128)(2,1)S(1)}, u32[]{:S(2)}, u32[]{:S(2)}) %collective-permute-start.4) | collective-permute-done | bytes 442400 | tf_op jit(solution)/shard_map/ppermute | solution.py:119
  51.1 1.6 collective-permute-start.6
  54.9 8.0 %collective-permute-done.6 = bf16[192,1152]{1,0:T(8,128)(2,1)S(1)} collective-permute-done((bf16[192,1152]{1,0:T(8,128)(2,1)S(1)}, bf16[192,1152]{1,0:T(8,128)(2,1)S(1)}, u32[]{:S(2)}, u32[]{:S(2)}) %collective-permute-start.6) | collective-permute-done | bytes 442400 | tf_op jit(solution)/shard_map/ppermute | solution.py:119
  62.9 1.6 collective-permute-start.8
  66.1 7.6 %collective-permute-done.8 = bf16[192,1152]{1,0:T(8,128)(2,1)S(1)} collective-permute-done((bf16[192,1152]{1,0:T(8,128)(2,1)S(1)}, bf16[192,1152]{1,0:T(8,128)(2,1)S(1)}, u32[]{:S(2)}, u32[]{:S(2)}) %collective-permute-start.8) | collective-permute-done | bytes 442400 | tf_op jit(solution)/shard_map/ppermute | solution.py:119
  74.5 1.6 collective-permute-start.9
  76.5 4.2 %convolution_convert_fusion = bf16[512,1152]{1,0:T(8,128)(2,1)S(1)} fusion(bf16[512,1536]{1,0:T(8,128)(2,1)S(1)} %bitcast.169, bf16[1536,1152]{1,0:T(8,128)(2,1)} %bitcast.24), kind=kOutput, calls=%fused_computation.5 | convolution fusion | flops 1812529152 | bytes 6291456 | tf_op jit(solution)/shard_map/dot_general | solution.py:195
  81.7 3.6 %fusion.42 = (f32[4,512]{1,0:T(4,128)S(1)}, f32[4,512,512]{1,2,0:T(8,128)}) fusion(pred[512,512]{0,1:T(8,128)(4,1)S(1)} %copy-done.6, bf16[512,3,4,96]{0,3,2,1:T(8,128)(2,1)S(1)} %bitcast.171), kind=kOutput, calls=%fused_computation.182 | convolution fusion | flops 205521408 | bytes 5251072 | tf_op jit(solution)/shard_map/while/body/eval_jaxpr/sub | solution.py:151
  85.3 2.7 %fusion.6 = bf16[4,96,512]{2,1,0:T(8,128)(2,1)S(1)} fusion(f32[4,512,512]{1,2,0:T(8,128)} %get-tuple-element.118, f32[4,512]{1,0:T(4,128)S(1)} %get-tuple-element.117, bf16[512,3,4,96]{0,3,2,1:T(8,128)(2,1)S(1)} %bitcast.172), kind=kOutput, calls=%fused_computation.12 | convolution fusion | flops 203620352 | bytes 4988928 | tf_op jit(solution)/shard_map/while/body/eval_jaxpr/hqk,khe->qhe/dot_general | solution.py:153
  88.1 1.6 collective-permute-start.11
  92.2 2.6 %collective-permute-done.11 = bf16[384,192]{0,1:T(8,128)(2,1)S(1)} collective-permute-done((bf16[384,192]{0,1:T(8,128)(2,1)}, bf16[384,192]{0,1:T(8,128)(2,1)S(1)}, u32[]{:S(2)}, u32[]{:S(2)}) %collective-permute-start.11) | collective-permute-done | bytes 147488 | tf_op jit(solution)/shard_map/ppermute | solution.py:119
  94.8 1.6 collective-permute-start.13
  98.0 3.0 %collective-permute-done.13 = bf16[384,192]{0,1:T(8,128)(2,1)S(1)} collective-permute-done((bf16[384,192]{0,1:T(8,128)(2,1)S(1)}, bf16[384,192]{0,1:T(8,128)(2,1)S(1)}, u32[]{:S(2)}, u32[]{:S(2)}) %collective-permute-start.13) | collective-permute-done | bytes 147488 | tf_op jit(solution)/shard_map/ppermute | solution.py:119
  101.0 1.6 collective-permute-start.15
  102.7 5.1 %collective-permute-done.15 = bf16[384,192]{0,1:T(8,128)(2,1)S(1)} collective-permute-done((bf16[384,192]{0,1:T(8,128)(2,1)S(1)}, bf16[384,192]{0,1:T(8,128)(2,1)S(1)}, u32[]{:S(2)}, u32[]{:S(2)}) %collective-permute-start.15) | collective-permute-done | bytes 147488 | tf_op jit(solution)/shard_map/ppermute | solution.py:119
  107.8 1.6 collective-permute-start.21
  111.7 1.4 collective-permute-start.18
  113.3 1.2 collective-permute-done.21
  114.6 1.6 collective-permute-start.23
  116.7 5.2 %collective-permute-done.16 = bf16[128,1536]{1,0:T(8,128)(2,1)S(1)} collective-permute-done((bf16[128,1536]{1,0:T(8,128)(2,1)S(1)}, bf16[128,1536]{1,0:T(8,128)(2,1)S(1)}, u32[]{:S(2)}, u32[]{:S(2)}) %collective-permute-start.16) | collective-permute-done | bytes 393248 | tf_op jit(solution)/shard_map/ppermute | solution.py:69
  121.9 1.2 collective-permute-done.17
  123.1 5.9 %collective-permute-done.18 = bf16[128,1536]{1,0:T(8,128)(2,1)S(1)} collective-permute-done((bf16[128,1536]{1,0:T(8,128)(2,1)S(1)}, bf16[128,1536]{1,0:T(8,128)(2,1)S(1)}, u32[]{:S(2)}, u32[]{:S(2)}) %collective-permute-start.18) | collective-permute-done | bytes 393248 | tf_op jit(solution)/shard_map/ppermute | solution.py:69
  131.7 1.4 collective-permute-start.19
  133.3 1.6 collective-permute-start.25
  135.4 7.5 %collective-permute-done.19 = bf16[128,1536]{1,0:T(8,128)(2,1)S(1)} collective-permute-done((bf16[128,1536]{1,0:T(8,128)(2,1)S(1)}, bf16[128,1536]{1,0:T(8,128)(2,1)S(1)}, u32[]{:S(2)}, u32[]{:S(2)}) %collective-permute-start.19) | collective-permute-done | bytes 393248 | tf_op jit(solution)/shard_map/ppermute | solution.py:36
  144.6 1.5 collective-permute-start.27
  146.2 7.4 %collective-permute-done.27 = bf16[192,768]{1,0:T(8,128)(2,1)S(1)} collective-permute-done((bf16[192,768]{1,0:T(8,128)(2,1)S(1)}, bf16[192,768]{1,0:T(8,128)(2,1)S(1)}, u32[]{:S(2)}, u32[]{:S(2)}) %collective-permute-start.27) | collective-permute-done | bytes 294944 | tf_op jit(solution)/shard_map/ppermute | solution.py:119
  153.6 1.6 collective-permute-start.28
  155.7 2.4 %copy.36 = bf16[768,1536]{1,0:T(8,128)(2,1)} copy(bf16[768,1536]{0,1:T(8,128)(2,1)S(1)} %bitcast.165) | data formatting | bytes 4718592 | tf_op jit(solution)/shard_map/dot_general | solution.py:206
  158.8 1.5 collective-permute-start.30
  160.9 3.3 %collective-permute-done.30 = bf16[384,192]{0,1:T(8,128)(2,1)S(1)} collective-permute-done((bf16[384,192]{0,1:T(8,128)(2,1)S(1)}, bf16[384,192]{0,1:T(8,128)(2,1)S(1)}, u32[]{:S(2)}, u32[]{:S(2)}) %collective-permute-start.30) | collective-permute-done | bytes 147488 | tf_op jit(solution)/shard_map/ppermute | solution.py:119
  164.3 1.5 collective-permute-start.32
  168.7 1.4 fusion.43
  170.7 1.4 collective-permute-start.34
  172.2 3.7 %collective-permute-done.34 = bf16[384,192]{0,1:T(8,128)(2,1)S(1)} collective-permute-done((bf16[384,192]{0,1:T(8,128)(2,1)S(1)}, bf16[384,192]{0,1:T(8,128)(2,1)S(1)}, u32[]{:S(2)}, u32[]{:S(2)}) %collective-permute-start.34) | collective-permute-done | bytes 147488 | tf_op jit(solution)/shard_map/ppermute | solution.py:119
  176.3 8.7 %convolution_convert_fusion.1 = bf16[512,1536]{1,0:T(8,128)(2,1)S(1)} fusion(bf16[384,1536]{0,1:T(8,128)(2,1)S(1)} %bitcast.173, bf16[512,384]{1,0:T(8,128)(2,1)S(1)} %fusion.32, f32[384]{0:T(512)S(1)} %copy-done.26, f32[384]{0:T(512)S(1)} %copy-done.27, f32[384]{0:T(512)S(1)} %get-tuple-element.33, f32[384]{0:T(512)S(1)} %get-tuple-element.34, ...), kind=kOutput, calls=%fused_computation.6 | convolution fusion | flops 629932032 | bytes 3209216 | tf_op jit(solution)/shard_map/dot_general | solution.py:216
  185.2 1.6 collective-permute-start.36
  186.9 1.4 collective-permute-start.37
  188.2 7.8 %collective-permute-done.35 = bf16[128,1536]{1,0:T(8,128)(2,1)S(1)} collective-permute-done((bf16[128,1536]{1,0:T(8,128)(2,1)S(1)}, bf16[128,1536]{1,0:T(8,128)(2,1)S(1)}, u32[]{:S(2)}, u32[]{:S(2)}) %collective-permute-start.35) | collective-permute-done | bytes 393248 | tf_op jit(solution)/shard_map/ppermute | solution.py:69
  196.0 1.2 collective-permute-done.36
  197.2 6.9 %collective-permute-done.37 = bf16[128,1536]{1,0:T(8,128)(2,1)S(1)} collective-permute-done((bf16[128,1536]{1,0:T(8,128)(2,1)S(1)}, bf16[128,1536]{1,0:T(8,128)(2,1)S(1)}, u32[]{:S(2)}, u32[]{:S(2)}) %collective-permute-start.37) | collective-permute-done | bytes 393248 | tf_op jit(solution)/shard_map/ppermute | solution.py:69
  (221 shorter events, 35.2 us)
Async XLA Ops:
  0.0 14.9 %copy-start.11 = (s32[8]{0:T(128)S(1)}, s32[8]{0:T(128)}, u32[]{:S(2)}) copy-start(s32[8]{0:T(128)} %constant.411.clone) | copy-start | bytes 100
  0.0 17.0 %copy-start.2 = (bf16[192,3,384]{2,0,1:T(8,128)(2,1)S(1)}, bf16[192,3,384]{2,0,1:T(8,128)(2,1)}, u32[]{:S(2)}) copy-start(bf16[192,3,384]{2,0,1:T(8,128)(2,1)} %param.21) | copy-start | bytes 1327108
  1.9 23.0 %copy-start.52 = (s32[1,4]{1,0:T(1,128)S(1)}, s32[1,4]{1,0:T(1,128)}, u32[]{:S(2)}) copy-start(s32[1,4]{1,0:T(1,128)} %param.18) | copy-start | bytes 52
  1.9 36.6 %collective-permute-start.2 = (bf16[192,1152]{1,0:T(8,128)(2,1)}, bf16[192,1152]{1,0:T(8,128)(2,1)S(1)}, u32[]{:S(2)}, u32[]{:S(2)}) collective-permute-start(bf16[192,1152]{1,0:T(8,128)(2,1)} %bitcast.76), channel_id=1, source_target_pairs={{0,8},{8,16},{16,24},{24,28},{28,20},{20,12},{12,4},{4,0},{1,9},{9... | collective-permute-start | bytes 1327112 | tf_op jit(solution)/shard_map/ppermute | solution.py:119
  5.0 35.2 %collective-permute-start.3 = (bf16[192,1152]{1,0:T(8,128)(2,1)}, bf16[192,1152]{1,0:T(8,128)(2,1)S(1)}, u32[]{:S(2)}, u32[]{:S(2)}) collective-permute-start(bf16[192,1152]{1,0:T(8,128)(2,1)} %bitcast.76), channel_id=1, source_target_pairs={{0,4},{8,0},{16,8},{24,16},{28,24},{20,28},{12,20},{4,12},{1,5},{9... | collective-permute-start | bytes 1327112 | tf_op jit(solution)/shard_map/ppermute | solution.py:122
  6.1 21.6 %copy-start.9 = (bf16[31,384]{1,0:T(8,128)(2,1)S(1)}, bf16[31,384]{1,0:T(8,128)(2,1)}, u32[]{:S(2)}) copy-start(bf16[31,384]{1,0:T(8,128)(2,1)} %param.24) | copy-start | bytes 71428
  7.7 21.7 %copy-start.5 = (bf16[192,2,384]{2,1,0:T(2,128)(2,1)S(1)}, bf16[192,2,384]{2,1,0:T(2,128)(2,1)}, u32[]{:S(2)}) copy-start(bf16[192,2,384]{2,1,0:T(2,128)(2,1)} %param.23) | copy-start | bytes 884740
  7.7 29.7 %collective-permute-start = (bf16[128,1536]{1,0:T(8,128)(2,1)S(1)}, bf16[128,1536]{1,0:T(8,128)(2,1)}, u32[]{:S(2)}, u32[]{:S(2)}) collective-permute-start(bf16[128,1536]{1,0:T(8,128)(2,1)S(1)} %fusion.18), channel_id=1, source_target_pairs={{0,2},{1,3},{2,0},{3,1},{4,6},{5,7},{6,4},{7,5},{8,10},{9,11},{10,... | collective-permute-start | bytes 1179656 | tf_op jit(solution)/shard_map/ppermute | solution.py:36
  38.5 16.3 %collective-permute-start.1 = (bf16[2,128,1536]{2,1,0:T(8,128)(2,1)S(1)}, bf16[2,128,1536]{2,1,0:T(8,128)(2,1)S(1)}, u32[]{:S(2)}, u32[]{:S(2)}) collective-permute-start(bf16[2,128,1536]{2,1,0:T(8,128)(2,1)S(1)} %get-tuple-element.77), channel_id=1, source_target_pairs={{0,1},{1,0},{2,3},{3,2},{4,5},{5,4},{6,7},{7,6},{8,9},{9,8},{10,11... | collective-permute-start | bytes 2359304 | tf_op jit(solution)/shard_map/ppermute | solution.py:42
  38.6 12.6 %collective-permute-start.4 = (bf16[192,1152]{1,0:T(8,128)(2,1)S(1)}, bf16[192,1152]{1,0:T(8,128)(2,1)S(1)}, u32[]{:S(2)}, u32[]{:S(2)}) collective-permute-start(bf16[192,1152]{1,0:T(8,128)(2,1)S(1)} %collective-permute-done.2), channel_id=1, source_target_pairs={{0,8},{8,16},{16,24},{24,28},{28,20},{20,12},{12,4},{4,0},{1,9},{9... | collective-permute-start | bytes 1327112 | tf_op jit(solution)/shard_map/ppermute | solution.py:119
  40.2 12.5 %collective-permute-start.5 = (bf16[192,1152]{1,0:T(8,128)(2,1)S(1)}, bf16[192,1152]{1,0:T(8,128)(2,1)S(1)}, u32[]{:S(2)}, u32[]{:S(2)}) collective-permute-start(bf16[192,1152]{1,0:T(8,128)(2,1)S(1)} %collective-permute-done.3), channel_id=1, source_target_pairs={{0,4},{8,0},{16,8},{24,16},{28,24},{20,28},{12,20},{4,12},{1,5},{9... | collective-permute-start | bytes 1327112 | tf_op jit(solution)/shard_map/ppermute | solution.py:122
  51.1 11.7 %collective-permute-start.6 = (bf16[192,1152]{1,0:T(8,128)(2,1)S(1)}, bf16[192,1152]{1,0:T(8,128)(2,1)S(1)}, u32[]{:S(2)}, u32[]{:S(2)}) collective-permute-start(bf16[192,1152]{1,0:T(8,128)(2,1)S(1)} %collective-permute-done.4), channel_id=1, source_target_pairs={{0,8},{8,16},{16,24},{24,28},{28,20},{20,12},{12,4},{4,0},{1,9},{9... | collective-permute-start | bytes 1327112 | tf_op jit(solution)/shard_map/ppermute | solution.py:119
  52.7 12.5 %collective-permute-start.7 = (bf16[192,1152]{1,0:T(8,128)(2,1)S(1)}, bf16[192,1152]{1,0:T(8,128)(2,1)S(1)}, u32[]{:S(2)}, u32[]{:S(2)}) collective-permute-start(bf16[192,1152]{1,0:T(8,128)(2,1)S(1)} %collective-permute-done.5), channel_id=1, source_target_pairs={{0,4},{8,0},{16,8},{24,16},{28,24},{20,28},{12,20},{4,12},{1,5},{9... | collective-permute-start | bytes 1327112 | tf_op jit(solution)/shard_map/ppermute | solution.py:122
  54.8 19.7 %copy-start.7 = (bf16[384,192]{0,1:T(8,128)(2,1)S(1)}, bf16[384,192]{0,1:T(8,128)(2,1)}, u32[]{:S(2)}) copy-start(bf16[384,192]{0,1:T(8,128)(2,1)} %param.22) | copy-start | bytes 442372
  62.9 10.8 %collective-permute-start.8 = (bf16[192,1152]{1,0:T(8,128)(2,1)S(1)}, bf16[192,1152]{1,0:T(8,128)(2,1)S(1)}, u32[]{:S(2)}, u32[]{:S(2)}) collective-permute-start(bf16[192,1152]{1,0:T(8,128)(2,1)S(1)} %collective-permute-done.6), channel_id=1, source_target_pairs={{0,8},{8,16},{16,24},{24,28},{28,20},{20,12},{12,4},{4,0},{1,9},{9... | collective-permute-start | bytes 1327112 | tf_op jit(solution)/shard_map/ppermute | solution.py:119
  74.5 13.6 %collective-permute-start.9 = (bf16[384,192]{0,1:T(8,128)(2,1)S(1)}, bf16[384,192]{0,1:T(8,128)(2,1)}, u32[]{:S(2)}, u32[]{:S(2)}) collective-permute-start(bf16[384,192]{0,1:T(8,128)(2,1)S(1)} %copy-done.7), channel_id=1, source_target_pairs={{0,8},{8,16},{16,24},{24,28},{28,20},{20,12},{12,4},{4,0},{1,9},{9... | collective-permute-start | bytes 442376 | tf_op jit(solution)/shard_map/ppermute | solution.py:119
  76.1 14.7 %collective-permute-start.10 = (bf16[384,192]{0,1:T(8,128)(2,1)S(1)}, bf16[384,192]{0,1:T(8,128)(2,1)}, u32[]{:S(2)}, u32[]{:S(2)}) collective-permute-start(bf16[384,192]{0,1:T(8,128)(2,1)S(1)} %copy-done.7), channel_id=1, source_target_pairs={{0,4},{8,0},{16,8},{24,16},{28,24},{20,28},{12,20},{4,12},{1,5},{9... | collective-permute-start | bytes 442376 | tf_op jit(solution)/shard_map/ppermute | solution.py:122
  88.1 6.7 %collective-permute-start.11 = (bf16[384,192]{0,1:T(8,128)(2,1)}, bf16[384,192]{0,1:T(8,128)(2,1)S(1)}, u32[]{:S(2)}, u32[]{:S(2)}) collective-permute-start(bf16[384,192]{0,1:T(8,128)(2,1)} %collective-permute-done.9), channel_id=1, source_target_pairs={{0,8},{8,16},{16,24},{24,28},{28,20},{20,12},{12,4},{4,0},{1,9},{9... | collective-permute-start | bytes 442376 | tf_op jit(solution)/shard_map/ppermute | solution.py:119
  90.7 6.7 %collective-permute-start.12 = (bf16[384,192]{0,1:T(8,128)(2,1)}, bf16[384,192]{0,1:T(8,128)(2,1)S(1)}, u32[]{:S(2)}, u32[]{:S(2)}) collective-permute-start(bf16[384,192]{0,1:T(8,128)(2,1)} %collective-permute-done.10), channel_id=1, source_target_pairs={{0,4},{8,0},{16,8},{24,16},{28,24},{20,28},{12,20},{4,12},{1,5},{9... | collective-permute-start | bytes 442376 | tf_op jit(solution)/shard_map/ppermute | solution.py:122
  94.8 6.2 %collective-permute-start.13 = (bf16[384,192]{0,1:T(8,128)(2,1)S(1)}, bf16[384,192]{0,1:T(8,128)(2,1)S(1)}, u32[]{:S(2)}, u32[]{:S(2)}) collective-permute-start(bf16[384,192]{0,1:T(8,128)(2,1)S(1)} %collective-permute-done.11), channel_id=1, source_target_pairs={{0,8},{8,16},{16,24},{24,28},{28,20},{20,12},{12,4},{4,0},{1,9},{9... | collective-permute-start | bytes 442376 | tf_op jit(solution)/shard_map/ppermute | solution.py:119
  97.4 5.2 %collective-permute-start.14 = (bf16[384,192]{0,1:T(8,128)(2,1)S(1)}, bf16[384,192]{0,1:T(8,128)(2,1)S(1)}, u32[]{:S(2)}, u32[]{:S(2)}) collective-permute-start(bf16[384,192]{0,1:T(8,128)(2,1)S(1)} %collective-permute-done.12), channel_id=1, source_target_pairs={{0,4},{8,0},{16,8},{24,16},{28,24},{20,28},{12,20},{4,12},{1,5},{9... | collective-permute-start | bytes 442376 | tf_op jit(solution)/shard_map/ppermute | solution.py:122
  101.0 6.8 %collective-permute-start.15 = (bf16[384,192]{0,1:T(8,128)(2,1)S(1)}, bf16[384,192]{0,1:T(8,128)(2,1)S(1)}, u32[]{:S(2)}, u32[]{:S(2)}) collective-permute-start(bf16[384,192]{0,1:T(8,128)(2,1)S(1)} %collective-permute-done.13), channel_id=1, source_target_pairs={{0,8},{8,16},{16,24},{24,28},{28,20},{20,12},{12,4},{4,0},{1,9},{9... | collective-permute-start | bytes 442376 | tf_op jit(solution)/shard_map/ppermute | solution.py:119
  107.8 6.8 %collective-permute-start.21 = (bf16[192,768]{1,0:T(8,128)(2,1)S(1)}, bf16[192,768]{1,0:T(8,128)(2,1)S(1)}, u32[]{:S(2)}, u32[]{:S(2)}) collective-permute-start(bf16[192,768]{1,0:T(8,128)(2,1)S(1)} %bitcast.174), channel_id=1, source_target_pairs={{0,8},{8,16},{16,24},{24,28},{28,20},{20,12},{12,4},{4,0},{1,9},{9... | collective-permute-start | bytes 884744 | tf_op jit(solution)/shard_map/ppermute | solution.py:119
  109.4 6.7 %collective-permute-start.22 = (bf16[192,768]{1,0:T(8,128)(2,1)S(1)}, bf16[192,768]{1,0:T(8,128)(2,1)S(1)}, u32[]{:S(2)}, u32[]{:S(2)}) collective-permute-start(bf16[192,768]{1,0:T(8,128)(2,1)S(1)} %bitcast.175), channel_id=1, source_target_pairs={{0,4},{8,0},{16,8},{24,16},{28,24},{20,28},{12,20},{4,12},{1,5},{9... | collective-permute-start | bytes 884744 | tf_op jit(solution)/shard_map/ppermute | solution.py:122
  111.0 10.9 %collective-permute-start.16 = (bf16[128,1536]{1,0:T(8,128)(2,1)S(1)}, bf16[128,1536]{1,0:T(8,128)(2,1)S(1)}, u32[]{:S(2)}, u32[]{:S(2)}) collective-permute-start(bf16[128,1536]{1,0:T(8,128)(2,1)S(1)} %get-tuple-element.70), channel_id=1, source_target_pairs={{0,1},{1,2},{2,3},{3,0},{4,5},{5,6},{6,7},{7,4},{8,9},{9,10},{10,1... | collective-permute-start | bytes 1179656 | tf_op jit(solution)/shard_map/ppermute | solution.py:69
  111.1 12.0 %collective-permute-start.17 = (bf16[128,1536]{1,0:T(8,128)(2,1)S(1)}, bf16[128,1536]{1,0:T(8,128)(2,1)S(1)}, u32[]{:S(2)}, u32[]{:S(2)}) collective-permute-start(bf16[128,1536]{1,0:T(8,128)(2,1)S(1)} %get-tuple-element.72), channel_id=1, source_target_pairs={{0,2},{1,3},{2,0},{3,1},{4,6},{5,7},{6,4},{7,5},{8,10},{9,11},{10,... | collective-permute-start | bytes 1179656 | tf_op jit(solution)/shard_map/ppermute | solution.py:69
  111.7 17.3 %collective-permute-start.18 = (bf16[128,1536]{1,0:T(8,128)(2,1)S(1)}, bf16[128,1536]{1,0:T(8,128)(2,1)S(1)}, u32[]{:S(2)}, u32[]{:S(2)}) collective-permute-start(bf16[128,1536]{1,0:T(8,128)(2,1)S(1)} %get-tuple-element.71), channel_id=1, source_target_pairs={{0,3},{1,0},{2,1},{3,2},{4,7},{5,4},{6,5},{7,6},{8,11},{9,8},{10,9... | collective-permute-start | bytes 1179656 | tf_op jit(solution)/shard_map/ppermute | solution.py:69
  114.6 18.7 %collective-permute-start.23 = (bf16[192,768]{1,0:T(8,128)(2,1)S(1)}, bf16[192,768]{1,0:T(8,128)(2,1)S(1)}, u32[]{:S(2)}, u32[]{:S(2)}) collective-permute-start(bf16[192,768]{1,0:T(8,128)(2,1)S(1)} %collective-permute-done.21), channel_id=1, source_target_pairs={{0,8},{8,16},{16,24},{24,28},{28,20},{20,12},{12,4},{4,0},{1,9},{9... | collective-permute-start | bytes 884744 | tf_op jit(solution)/shard_map/ppermute | solution.py:119
  116.1 18.8 %collective-permute-start.24 = (bf16[192,768]{1,0:T(8,128)(2,1)S(1)}, bf16[192,768]{1,0:T(8,128)(2,1)S(1)}, u32[]{:S(2)}, u32[]{:S(2)}) collective-permute-start(bf16[192,768]{1,0:T(8,128)(2,1)S(1)} %collective-permute-done.22), channel_id=1, source_target_pairs={{0,4},{8,0},{16,8},{24,16},{28,24},{20,28},{12,20},{4,12},{1,5},{9... | collective-permute-start | bytes 884744 | tf_op jit(solution)/shard_map/ppermute | solution.py:122
  116.7 14.0 %copy-start.12 = (f32[1536]{0:T(1024)S(1)}, f32[1536]{0:T(1024)}, u32[]{:S(2)}) copy-start(f32[1536]{0:T(1024)} %param.20) | copy-start | bytes 18436
  131.7 11.3 %collective-permute-start.19 = (bf16[128,1536]{1,0:T(8,128)(2,1)S(1)}, bf16[128,1536]{1,0:T(8,128)(2,1)S(1)}, u32[]{:S(2)}, u32[]{:S(2)}) collective-permute-start(bf16[128,1536]{1,0:T(8,128)(2,1)S(1)} %get-tuple-element.64), channel_id=1, source_target_pairs={{0,2},{1,3},{2,0},{3,1},{4,6},{5,7},{6,4},{7,5},{8,10},{9,11},{10,... | collective-permute-start | bytes 1179656 | tf_op jit(solution)/shard_map/ppermute | solution.py:36
  133.3 11.3 %collective-permute-start.25 = (bf16[192,768]{1,0:T(8,128)(2,1)S(1)}, bf16[192,768]{1,0:T(8,128)(2,1)S(1)}, u32[]{:S(2)}, u32[]{:S(2)}) collective-permute-start(bf16[192,768]{1,0:T(8,128)(2,1)S(1)} %collective-permute-done.23), channel_id=1, source_target_pairs={{0,8},{8,16},{16,24},{24,28},{28,20},{20,12},{12,4},{4,0},{1,9},{9... | collective-permute-start | bytes 884744 | tf_op jit(solution)/shard_map/ppermute | solution.py:119
  134.9 11.2 %collective-permute-start.26 = (bf16[192,768]{1,0:T(8,128)(2,1)S(1)}, bf16[192,768]{1,0:T(8,128)(2,1)S(1)}, u32[]{:S(2)}, u32[]{:S(2)}) collective-permute-start(bf16[192,768]{1,0:T(8,128)(2,1)S(1)} %collective-permute-done.24), channel_id=1, source_target_pairs={{0,4},{8,0},{16,8},{24,16},{28,24},{20,28},{12,20},{4,12},{1,5},{9... | collective-permute-start | bytes 884744 | tf_op jit(solution)/shard_map/ppermute | solution.py:122
  135.4 18.2 %copy-start.8 = (bf16[384,192]{0,1:T(8,128)(2,1)S(1)}, bf16[384,192]{0,1:T(8,128)(2,1)}, u32[]{:S(2)}) copy-start(bf16[384,192]{0,1:T(8,128)(2,1)} %param.25) | copy-start | bytes 442372
  143.7 9.8 %copy-start.3 = (bf16[4,128,1536]{2,1,0:T(8,128)(2,1)}, bf16[4,128,1536]{2,1,0:T(8,128)(2,1)S(1)}, u32[]{:S(2)}) copy-start(bf16[4,128,1536]{2,1,0:T(8,128)(2,1)S(1)} %get-tuple-element.76) | copy-start | bytes 4718596
  143.7 22.8 %collective-permute-start.20 = (bf16[2,128,1536]{2,1,0:T(8,128)(2,1)}, bf16[2,128,1536]{2,1,0:T(8,128)(2,1)}, u32[]{:S(2)}, u32[]{:S(2)}) collective-permute-start(bf16[2,128,1536]{2,1,0:T(8,128)(2,1)} %get-tuple-element.75), channel_id=1, source_target_pairs={{0,1},{1,0},{2,3},{3,2},{4,5},{5,4},{6,7},{7,6},{8,9},{9,8},{10,11... | collective-permute-start | bytes 2359304 | tf_op jit(solution)/shard_map/ppermute | solution.py:42
  144.6 9.0 %collective-permute-start.27 = (bf16[192,768]{1,0:T(8,128)(2,1)S(1)}, bf16[192,768]{1,0:T(8,128)(2,1)S(1)}, u32[]{:S(2)}, u32[]{:S(2)}) collective-permute-start(bf16[192,768]{1,0:T(8,128)(2,1)S(1)} %collective-permute-done.25), channel_id=1, source_target_pairs={{0,8},{8,16},{16,24},{24,28},{28,20},{20,12},{12,4},{4,0},{1,9},{9... | collective-permute-start | bytes 884744 | tf_op jit(solution)/shard_map/ppermute | solution.py:119
  153.6 5.2 %collective-permute-start.28 = (bf16[384,192]{0,1:T(8,128)(2,1)S(1)}, bf16[384,192]{0,1:T(8,128)(2,1)S(1)}, u32[]{:S(2)}, u32[]{:S(2)}) collective-permute-start(bf16[384,192]{0,1:T(8,128)(2,1)S(1)} %copy-done.8), channel_id=1, source_target_pairs={{0,8},{8,16},{16,24},{24,28},{28,20},{20,12},{12,4},{4,0},{1,9},{9... | collective-permute-start | bytes 442376 | tf_op jit(solution)/shard_map/ppermute | solution.py:119
  155.2 5.2 %collective-permute-start.29 = (bf16[384,192]{0,1:T(8,128)(2,1)S(1)}, bf16[384,192]{0,1:T(8,128)(2,1)S(1)}, u32[]{:S(2)}, u32[]{:S(2)}) collective-permute-start(bf16[384,192]{0,1:T(8,128)(2,1)S(1)} %copy-done.8), channel_id=1, source_target_pairs={{0,4},{8,0},{16,8},{24,16},{28,24},{20,28},{12,20},{4,12},{1,5},{9... | collective-permute-start | bytes 442376 | tf_op jit(solution)/shard_map/ppermute | solution.py:122
  158.2 10.4 %copy-start.1 = (bf16[768,1536]{1,0:T(8,128)(2,1)S(1)}, bf16[768,1536]{1,0:T(8,128)(2,1)}, u32[]{:S(2)}) copy-start(bf16[768,1536]{1,0:T(8,128)(2,1)} %copy.36) | copy-start | bytes 7077892
  158.8 5.5 %collective-permute-start.30 = (bf16[384,192]{0,1:T(8,128)(2,1)S(1)}, bf16[384,192]{0,1:T(8,128)(2,1)S(1)}, u32[]{:S(2)}, u32[]{:S(2)}) collective-permute-start(bf16[384,192]{0,1:T(8,128)(2,1)S(1)} %collective-permute-done.28), channel_id=1, source_target_pairs={{0,8},{8,16},{16,24},{24,28},{28,20},{20,12},{12,4},{4,0},{1,9},{9... | collective-permute-start | bytes 442376 | tf_op jit(solution)/shard_map/ppermute | solution.py:119
  160.4 5.4 %collective-permute-start.31 = (bf16[384,192]{0,1:T(8,128)(2,1)S(1)}, bf16[384,192]{0,1:T(8,128)(2,1)S(1)}, u32[]{:S(2)}, u32[]{:S(2)}) collective-permute-start(bf16[384,192]{0,1:T(8,128)(2,1)S(1)} %collective-permute-done.29), channel_id=1, source_target_pairs={{0,4},{8,0},{16,8},{24,16},{28,24},{20,28},{12,20},{4,12},{1,5},{9... | collective-permute-start | bytes 442376 | tf_op jit(solution)/shard_map/ppermute | solution.py:122
  164.3 6.4 %collective-permute-start.32 = (bf16[384,192]{0,1:T(8,128)(2,1)S(1)}, bf16[384,192]{0,1:T(8,128)(2,1)S(1)}, u32[]{:S(2)}, u32[]{:S(2)}) collective-permute-start(bf16[384,192]{0,1:T(8,128)(2,1)S(1)} %collective-permute-done.30), channel_id=1, source_target_pairs={{0,8},{8,16},{16,24},{24,28},{28,20},{20,12},{12,4},{4,0},{1,9},{9... | collective-permute-start | bytes 442376 | tf_op jit(solution)/shard_map/ppermute | solution.py:119
  165.8 6.3 %collective-permute-start.33 = (bf16[384,192]{0,1:T(8,128)(2,1)S(1)}, bf16[384,192]{0,1:T(8,128)(2,1)S(1)}, u32[]{:S(2)}, u32[]{:S(2)}) collective-permute-start(bf16[384,192]{0,1:T(8,128)(2,1)S(1)} %collective-permute-done.31), channel_id=1, source_target_pairs={{0,4},{8,0},{16,8},{24,16},{28,24},{20,28},{12,20},{4,12},{1,5},{9... | collective-permute-start | bytes 442376 | tf_op jit(solution)/shard_map/ppermute | solution.py:122
  170.7 5.2 %collective-permute-start.34 = (bf16[384,192]{0,1:T(8,128)(2,1)S(1)}, bf16[384,192]{0,1:T(8,128)(2,1)S(1)}, u32[]{:S(2)}, u32[]{:S(2)}) collective-permute-start(bf16[384,192]{0,1:T(8,128)(2,1)S(1)} %collective-permute-done.32), channel_id=1, source_target_pairs={{0,8},{8,16},{16,24},{24,28},{28,20},{20,12},{12,4},{4,0},{1,9},{9... | collective-permute-start | bytes 442376 | tf_op jit(solution)/shard_map/ppermute | solution.py:119
  185.2 10.9 %collective-permute-start.35 = (bf16[128,1536]{1,0:T(8,128)(2,1)S(1)}, bf16[128,1536]{1,0:T(8,128)(2,1)S(1)}, u32[]{:S(2)}, u32[]{:S(2)}) collective-permute-start(bf16[128,1536]{1,0:T(8,128)(2,1)S(1)} %get-tuple-element.67), channel_id=1, source_target_pairs={{0,1},{1,2},{2,3},{3,0},{4,5},{5,6},{6,7},{7,4},{8,9},{9,10},{10,1... | collective-permute-start | bytes 1179656 | tf_op jit(solution)/shard_map/ppermute | solution.py:69
  185.2 12.0 %collective-permute-start.36 = (bf16[128,1536]{1,0:T(8,128)(2,1)S(1)}, bf16[128,1536]{1,0:T(8,128)(2,1)S(1)}, u32[]{:S(2)}, u32[]{:S(2)}) collective-permute-start(bf16[128,1536]{1,0:T(8,128)(2,1)S(1)} %get-tuple-element.69), channel_id=1, source_target_pairs={{0,2},{1,3},{2,0},{3,1},{4,6},{5,7},{6,4},{7,5},{8,10},{9,11},{10,... | collective-permute-start | bytes 1179656 | tf_op jit(solution)/shard_map/ppermute | solution.py:69
  186.9 17.3 %collective-permute-start.37 = (bf16[128,1536]{1,0:T(8,128)(2,1)S(1)}, bf16[128,1536]{1,0:T(8,128)(2,1)S(1)}, u32[]{:S(2)}, u32[]{:S(2)}) collective-permute-start(bf16[128,1536]{1,0:T(8,128)(2,1)S(1)} %get-tuple-element.68), channel_id=1, source_target_pairs={{0,3},{1,0},{2,1},{3,2},{4,7},{5,4},{6,5},{7,6},{8,11},{9,8},{10,9... | collective-permute-start | bytes 1179656 | tf_op jit(solution)/shard_map/ppermute | solution.py:69
  (44 other events, 261.9 us)

commit v4 on v3

--- a/solution.py
+++ b/solution.py
@@ -128,14 +128,14 @@
     return lax.optimization_barrier((token, value))[1]
 
 
-def attend(projected, seg_all, head_size):
-    group_rows = projected.shape[0]
+def attend(query_rows, kv_rows, seg_all, head_size):
+    group_rows = query_rows.shape[0]
     block_rows = 512
-    heads_here = projected.shape[2] // head_size
-    split = projected.reshape(group_rows, 3, heads_here, head_size)
-    queries = split[:, 0]
-    keys = split[:, 1]
-    values = split[:, 2]
+    heads_here = query_rows.shape[1] // head_size
+    queries = query_rows.reshape(group_rows, heads_here, head_size)
+    split = kv_rows.reshape(group_rows, 2, heads_here, head_size)
+    keys = split[:, 0]
+    values = split[:, 1]
     blocks = group_rows // block_rows
     scale = 1.0 / head_size**0.5
 
@@ -179,9 +179,10 @@
     group_rows = frame_rows * seq_count
     group_width = model_width // seq_count
     kernel_reach = dw_kernel.shape[0] // 2
-    qkv_parts = ring_gather(w_qkv.reshape(w_qkv.shape[0], 3 * group_width), ring)
-    qkv_matrix = qkv_parts.reshape(model_width, 3 * group_width)
-    out_parts = ring_gather(after(qkv_parts, w_out), ring)
+    query_matrix = lax.all_gather(w_qkv[:, 0], "dp", axis=0, tiled=True)
+    kv_parts = ring_gather(w_qkv[:, 1:].reshape(w_qkv.shape[0], 2 * group_width), ring)
+    kv_matrix = kv_parts.reshape(model_width, 2 * group_width)
+    out_parts = ring_gather(after(kv_parts, w_out), ring)
     out_local = jnp.einsum("nrc->rnc", out_parts).reshape(w_out.shape[0], model_width)
     glu_parts = ring_gather(after(out_parts, w_glu.reshape(w_glu.shape[0], 2 * group_width)), ring)
     glu_matrix = glu_parts.reshape(model_width, 2 * group_width)
@@ -191,12 +192,14 @@
     record_ends = jnp.cumsum(lengths[0])
     seg_all = segment_of(record_ends, jnp.arange(group_rows, dtype=jnp.int32))
     normed1 = layer_norm(inputs, ln1_gain)
-    projected = (
-        jnp.dot(seq_gather(normed1, paired).reshape(group_rows, model_width), qkv_matrix, preferred_element_type=jnp.float32)
-        .astype(jnp.bfloat16)
-        .reshape(group_rows, 3, group_width)
-    )
-    attended = attend(projected, seg_all, HD)
+    group_normed = seq_gather(normed1, paired).reshape(group_rows, model_width)
+    query_rows = jnp.dot(
+        group_normed, query_matrix, preferred_element_type=jnp.float32
+    ).astype(jnp.bfloat16)
+    kv_rows = jnp.dot(group_normed, kv_matrix, preferred_element_type=jnp.float32).astype(
+        jnp.bfloat16
+    )
+    attended = attend(query_rows, kv_rows, seg_all, HD)
     attn_sum = seq_scatter_sum(
         jnp.dot(attended, out_local, preferred_element_type=jnp.float32).astype(jnp.bfloat16)
     )
@@ -212,6 +215,7 @@
     activated = depthwise(
         padded, dw_kernel, seg_all, segment_of(record_ends, near_positions), group_rows
     )
+    activated = lax.optimization_barrier(activated)
     conv_out = seq_scatter_sum(
         jnp.dot(activated, proj_local, preferred_element_type=jnp.float32).astype(jnp.bfloat16)
     )

time: 206 us -> 211 us (1.024)
  between operations: 19.3 us -> 31.9 us
  other arithmetic: 9.89 us -> 15.2 us
  matrix products: 21.7 us -> 16.7 us
  waiting for transfers between devices: 88.1 us -> 83.1 us
    dot_general x1, matrix products: 8.73 us -> 1.01 us  [on_device(): jnp.dot(activated, proj_local, preferred_element_type=jnp.float32)]
    convert_element_type x0 -> x1, other arithmetic: none -> 6.5 us  [depthwise(): return jax.nn.silu(total_acc).astype(jnp.bfloat16)]
    ppermute x16, starting transfers between devices: 26.7 us -> 32 us  [ring_gather(): ahead = lax.ppermute(ahead, 'dp', forward)]
    ppermute x6, waiting for transfers between devices: 28.2 us -> 24.4 us  [seq_scatter_sum(): lax.ppermute(piece, 'seq', [(i, (i + shift) % count) for i in range(count)])]
    ppermute x6, starting transfers between devices: 5.15 us -> 1.67 us  [seq_scatter_sum(): lax.ppermute(piece, 'seq', [(i, (i + shift) % count) for i in range(count)])]
    unnamed x110, local copies, waits for them, and re-layouts: 0.97 us -> 3.92 us
    ppermute x12, starting transfers between devices: 5.45 us -> 2.73 us  [ring_gather(): behind = lax.ppermute(behind, 'dp', backward)]
    broadcast_in_dim x2 -> x0, local copies, waits for them, and re-layouts: 2.36 us -> none  [ring_gather(): out = jnp.zeros((count,) + block.shape, block.dtype)]
  transfers between devices with their start and end apart: 38 -> 39, of which waited for: 19 -> 19; matrix products, arithmetic and copies ran while one was open for 21% -> 18% of each run, Pallas kernels for 0% -> 0%
where the time goes in v4:
time: 211 us; the launch traced here: 210 us
  waiting for transfers between devices  83.1 us (39%)
  starting transfers between devices  40 us (19%)
  between operations  31.9 us (15%)
  local copies, waits for them, and re-layouts  23.4 us (11%)
  matrix products  16.7 us (8%)
  other arithmetic  15.2 us (7%)
    ppermute x16, waiting for transfers between devices, ring_gather(): ahead = lax.ppermute(ahead, 'dp', forward)  50.3 us
    ppermute x16, starting transfers between devices, ring_gather(): ahead = lax.ppermute(ahead, 'dp', forward)  32 us
    ppermute x6, waiting for transfers between devices, seq_scatter_sum(): lax.ppermute(piece, 'seq', [(i, (i + shift) % count) for i in range(count)])  24.4 us
    ppermute x2, waiting for transfers between devices, seq_gather(): lax.ppermute(block, 'seq', [(i, (i + 2 * shift) % count) for i in range(c...  6.58 us
    convert_element_type x1, other arithmetic, depthwise(): return jax.nn.silu(total_acc).astype(jnp.bfloat16)  6.5 us
    sub x1, matrix products, one_block(): weights = jnp.exp(scores - top_score)  4.82 us
  transfers between devices with their start and end apart: 39, of which 19 were waited for; matrix products, arithmetic and copies ran while one was open for 18% of the time, Pallas kernels for 0%

profile of v4, /device:TPU:0, one launch (start us, length us, event | category | flops | bytes accessed | tf_op | source)
XLA Modules:
  0.0 210.4 jit_solution(4624747187865461719)
XLA Ops:
  6.5 1.1 slice_bitcast_fusion.9
  8.4 3.0 %collective-permute-start.2 = (bf16[192,768]{1,0:T(8,128)(2,1)}, bf16[192,768]{1,0:T(8,128)(2,1)}, u32[]{:S(2)}, u32[]{:S(2)}) collective-permute-start(bf16[192,768]{1,0:T(8,128)(2,1)} %bitcast.77), channel_id=1, source_target_pairs={{0,8},{8,16},{16,24},{24,28},{28,20},{20,12},{12,4},{4,0},{1,9},{9... | collective-permute-start | bytes 884744 | tf_op jit(solution)/shard_map/ppermute | solution.py:119
  12.9 1.9 collective-permute-start
  14.8 1.6 slice.311
  40.6 1.6 collective-permute-start.4
  44.6 1.1 bitcast_dynamic-update-slice_fusion.4
  45.7 9.3 %collective-permute-done.4 = bf16[192,768]{1,0:T(8,128)(2,1)S(1)} collective-permute-done((bf16[192,768]{1,0:T(8,128)(2,1)}, bf16[192,768]{1,0:T(8,128)(2,1)S(1)}, u32[]{:S(2)}, u32[]{:S(2)}) %collective-permute-start.4) | collective-permute-done | bytes 294944 | tf_op jit(solution)/shard_map/ppermute | solution.py:119
  55.0 1.4 collective-permute-start.6
  56.5 1.6 collective-permute-done.5
  58.2 6.8 %collective-permute-done.6 = bf16[192,768]{1,0:T(8,128)(2,1)S(1)} collective-permute-done((bf16[192,768]{1,0:T(8,128)(2,1)S(1)}, bf16[192,768]{1,0:T(8,128)(2,1)S(1)}, u32[]{:S(2)}, u32[]{:S(2)}) %collective-permute-start.6) | collective-permute-done | bytes 294944 | tf_op jit(solution)/shard_map/ppermute | solution.py:119
  65.0 2.5 %collective-permute-start.8 = (bf16[192,768]{1,0:T(8,128)(2,1)S(1)}, bf16[192,768]{1,0:T(8,128)(2,1)S(1)}, u32[]{:S(2)}, u32[]{:S(2)}) collective-permute-start(bf16[192,768]{1,0:T(8,128)(2,1)S(1)} %collective-permute-done.6), channel_id=1, source_target_pairs={{0,8},{8,16},{16,24},{24,28},{28,20},{20,12},{12,4},{4,0},{1,9},{9... | collective-permute-start | bytes 884744 | tf_op jit(solution)/shard_map/ppermute | solution.py:119
  67.6 5.6 %collective-permute-done.8 = bf16[192,768]{1,0:T(8,128)(2,1)S(1)} collective-permute-done((bf16[192,768]{1,0:T(8,128)(2,1)S(1)}, bf16[192,768]{1,0:T(8,128)(2,1)S(1)}, u32[]{:S(2)}, u32[]{:S(2)}) %collective-permute-start.8) | collective-permute-done | bytes 294944 | tf_op jit(solution)/shard_map/ppermute | solution.py:119
  73.2 2.5 %collective-permute-start.9 = (bf16[384,192]{0,1:T(8,128)(2,1)S(1)}, bf16[384,192]{0,1:T(8,128)(2,1)S(1)}, u32[]{:S(2)}, u32[]{:S(2)}) collective-permute-start(bf16[384,192]{0,1:T(8,128)(2,1)S(1)} %copy-done.8), channel_id=1, source_target_pairs={{0,8},{8,16},{16,24},{24,28},{28,20},{20,12},{12,4},{4,0},{1,9},{9... | collective-permute-start | bytes 442376 | tf_op jit(solution)/shard_map/ppermute | solution.py:119
  75.9 1.1 copy-done.4
  77.0 2.3 %convolution_convert_fusion.2 = bf16[512,768]{1,0:T(8,128)(2,1)} fusion(bf16[512,1536]{1,0:T(8,128)(2,1)S(1)} %bitcast.169, bf16[1536,768]{1,0:T(8,128)(2,1)S(1)} %bitcast.167), kind=kOutput, calls=%fused_computation.11 | convolution fusion | flops 1208352768 | bytes 4718592 | tf_op jit(solution)/shard_map/dot_general | solution.py:199
  79.3 2.3 %copy.31 = bf16[512,768]{0,1:T(8,128)(2,1)} copy(bf16[512,768]{1,0:T(8,128)(2,1)} %convolution_convert_fusion.2) | data formatting | bytes 1572864 | tf_op jit(solution)/shard_map/convert_element_type | solution.py:199
  81.8 2.1 collective-permute-start.11
  83.9 3.5 %collective-permute-done.11 = bf16[384,192]{0,1:T(8,128)(2,1)S(1)} collective-permute-done((bf16[384,192]{0,1:T(8,128)(2,1)S(1)}, bf16[384,192]{0,1:T(8,128)(2,1)S(1)}, u32[]{:S(2)}, u32[]{:S(2)}) %collective-permute-start.11) | collective-permute-done | bytes 147488 | tf_op jit(solution)/shard_map/ppermute | solution.py:119
  87.4 2.3 %collective-permute-start.13 = (bf16[384,192]{0,1:T(8,128)(2,1)S(1)}, bf16[384,192]{0,1:T(8,128)(2,1)S(1)}, u32[]{:S(2)}, u32[]{:S(2)}) collective-permute-start(bf16[384,192]{0,1:T(8,128)(2,1)S(1)} %collective-permute-done.11), channel_id=1, source_target_pairs={{0,8},{8,16},{16,24},{24,28},{28,20},{20,12},{12,4},{4,0},{1,9},{9... | collective-permute-start | bytes 442376 | tf_op jit(solution)/shard_map/ppermute | solution.py:119
  89.8 4.1 %collective-permute-done.13 = bf16[384,192]{0,1:T(8,128)(2,1)S(1)} collective-permute-done((bf16[384,192]{0,1:T(8,128)(2,1)S(1)}, bf16[384,192]{0,1:T(8,128)(2,1)S(1)}, u32[]{:S(2)}, u32[]{:S(2)}) %collective-permute-start.13) | collective-permute-done | bytes 147488 | tf_op jit(solution)/shard_map/ppermute | solution.py:119
  93.9 2.5 %collective-permute-start.15 = (bf16[384,192]{0,1:T(8,128)(2,1)S(1)}, bf16[384,192]{0,1:T(8,128)(2,1)S(1)}, u32[]{:S(2)}, u32[]{:S(2)}) collective-permute-start(bf16[384,192]{0,1:T(8,128)(2,1)S(1)} %collective-permute-done.13), channel_id=1, source_target_pairs={{0,8},{8,16},{16,24},{24,28},{28,20},{20,12},{12,4},{4,0},{1,9},{9... | collective-permute-start | bytes 442376 | tf_op jit(solution)/shard_map/ppermute | solution.py:119
  96.5 4.1 %collective-permute-done.15 = bf16[384,192]{0,1:T(8,128)(2,1)S(1)} collective-permute-done((bf16[384,192]{0,1:T(8,128)(2,1)S(1)}, bf16[384,192]{0,1:T(8,128)(2,1)S(1)}, u32[]{:S(2)}, u32[]{:S(2)}) %collective-permute-start.15) | collective-permute-done | bytes 147488 | tf_op jit(solution)/shard_map/ppermute | solution.py:119
  100.7 2.5 %collective-permute-start.21 = (bf16[192,768]{1,0:T(8,128)(2,1)S(1)}, bf16[192,768]{1,0:T(8,128)(2,1)}, u32[]{:S(2)}, u32[]{:S(2)}) collective-permute-start(bf16[192,768]{1,0:T(8,128)(2,1)S(1)} %bitcast.172), channel_id=1, source_target_pairs={{0,8},{8,16},{16,24},{24,28},{28,20},{20,12},{12,4},{4,0},{1,9},{9... | collective-permute-start | bytes 884744 | tf_op jit(solution)/shard_map/ppermute | solution.py:119
  103.4 3.3 %convolution_convert_fusion.3 = bf16[512,384]{0,1:T(8,128)(2,1)} fusion(bf16[512,1536]{1,0:T(8,128)(2,1)} %bitcast.170, bf16[1536,1,384]{2,0,1:T(8,128)(2,1)} %all-gather.3.cloned.1.call-done), kind=kOutput, calls=%fused_computation.13 | convolution fusion | flops 604176384 | bytes 3145728 | tf_op jit(solution)/shard_map/dot_general | solution.py:196
  106.8 4.8 %fusion.40 = (f32[4,512]{1,0:T(4,128)S(1)}, f32[4,512,512]{1,2,0:T(8,128)}) fusion(pred[512,512]{0,1:T(8,128)(4,1)} %broadcast_compare_fusion, bf16[512,4,96]{0,2,1:T(8,128)(2,1)} %bitcast.182, bf16[512,2,4,96]{0,3,2,1:T(8,128)(2,1)} %bitcast.175), kind=kOutput, calls=%fused_computation.181 | convolution fusion | flops 205521408 | bytes 5251072 | tf_op jit(solution)/shard_map/while/body/eval_jaxpr/sub | solution.py:151
  111.6 2.9 %fusion.6 = bf16[4,96,512]{2,1,0:T(8,128)(2,1)S(1)} fusion(f32[4,512,512]{1,2,0:T(8,128)} %get-tuple-element.120, f32[4,512]{1,0:T(4,128)S(1)} %get-tuple-element.119, bf16[512,2,4,96]{0,3,2,1:T(8,128)(2,1)} %bitcast.176), kind=kOutput, calls=%fused_computation.12 | convolution fusion | flops 203620352 | bytes 4988928 | tf_op jit(solution)/shard_map/while/body/eval_jaxpr/hqk,khe->qhe/dot_general | solution.py:153
  116.4 1.8 collective-permute-start.23
  119.6 6.6 %collective-permute-done.23 = bf16[192,768]{1,0:T(8,128)(2,1)S(1)} collective-permute-done((bf16[192,768]{1,0:T(8,128)(2,1)}, bf16[192,768]{1,0:T(8,128)(2,1)S(1)}, u32[]{:S(2)}, u32[]{:S(2)}) %collective-permute-start.23) | collective-permute-done | bytes 294944 | tf_op jit(solution)/shard_map/ppermute | solution.py:119
  126.2 1.4 collective-permute-start.25
  128.3 5.3 %collective-permute-done.17 = bf16[128,1536]{1,0:T(8,128)(2,1)S(1)} collective-permute-done((bf16[128,1536]{1,0:T(8,128)(2,1)S(1)}, bf16[128,1536]{1,0:T(8,128)(2,1)S(1)}, u32[]{:S(2)}, u32[]{:S(2)}) %collective-permute-start.17) | collective-permute-done | bytes 393248 | tf_op jit(solution)/shard_map/ppermute | solution.py:69
  136.2 1.1 bitcast_dynamic-update-slice_fusion.2
  137.2 1.5 collective-permute-start.19
  138.9 1.9 collective-permute-start.27
  140.9 6.6 %collective-permute-done.19 = bf16[128,1536]{1,0:T(8,128)(2,1)S(1)} collective-permute-done((bf16[128,1536]{1,0:T(8,128)(2,1)S(1)}, bf16[128,1536]{1,0:T(8,128)(2,1)S(1)}, u32[]{:S(2)}, u32[]{:S(2)}) %collective-permute-start.19) | collective-permute-done | bytes 393248 | tf_op jit(solution)/shard_map/ppermute | solution.py:36
  148.3 1.1 copy-done.5
  149.4 1.6 collective-permute-start.28
  151.4 2.4 %copy.35 = bf16[768,1536]{1,0:T(8,128)(2,1)} copy(bf16[768,1536]{0,1:T(8,128)(2,1)S(1)} %bitcast.164) | data formatting | bytes 4718592 | tf_op jit(solution)/shard_map/dot_general | solution.py:209
  154.0 1.0 bitcast_dynamic-update-slice_fusion.28
  155.0 1.6 collective-permute-start.30
  157.2 3.0 %collective-permute-done.30 = bf16[384,192]{0,1:T(8,128)(2,1)S(1)} collective-permute-done((bf16[384,192]{0,1:T(8,128)(2,1)S(1)}, bf16[384,192]{0,1:T(8,128)(2,1)S(1)}, u32[]{:S(2)}, u32[]{:S(2)}) %collective-permute-start.30) | collective-permute-done | bytes 147488 | tf_op jit(solution)/shard_map/ppermute | solution.py:119
  160.2 1.6 collective-permute-start.32
  162.4 3.8 %collective-permute-done.32 = bf16[384,192]{0,1:T(8,128)(2,1)S(1)} collective-permute-done((bf16[384,192]{0,1:T(8,128)(2,1)S(1)}, bf16[384,192]{0,1:T(8,128)(2,1)S(1)}, u32[]{:S(2)}, u32[]{:S(2)}) %collective-permute-start.32) | collective-permute-done | bytes 147488 | tf_op jit(solution)/shard_map/ppermute | solution.py:119
  166.1 1.7 collective-permute-start.34
  167.9 3.4 %collective-permute-done.34 = bf16[384,192]{0,1:T(8,128)(2,1)S(1)} collective-permute-done((bf16[384,192]{0,1:T(8,128)(2,1)S(1)}, bf16[384,192]{0,1:T(8,128)(2,1)S(1)}, u32[]{:S(2)}, u32[]{:S(2)}) %collective-permute-start.34) | collective-permute-done | bytes 147488 | tf_op jit(solution)/shard_map/ppermute | solution.py:119
  173.4 1.4 fusion.41
  175.9 6.5 %multiply_convert_fusion = bf16[512,384]{1,0:T(8,128)(2,1)S(1)} fusion(bf16[512,384]{1,0:T(8,128)(2,1)S(1)} %fusion.33, f32[384]{0:T(512)S(1)} %copy-done.26, f32[384]{0:T(512)S(1)} %copy-done.27, f32[384]{0:T(512)S(1)} %get-tuple-element.33, f32[384]{0:T(512)S(1)} %get-tuple-element.34, f32[384]{0:T(512)S(1)} %get-tuple-element.35, ...), kind=kLoop, calls=%fused_computation.43 | loop fusion | flops 25165824 | bytes 849920 | tf_op jit(solution)/shard_map/convert_element_type | solution.py:172
  184.4 8.5 %collective-permute-done.37 = bf16[128,1536]{1,0:T(8,128)(2,1)S(1)} collective-permute-done((bf16[128,1536]{1,0:T(8,128)(2,1)S(1)}, bf16[128,1536]{1,0:T(8,128)(2,1)S(1)}, u32[]{:S(2)}, u32[]{:S(2)}) %collective-permute-start.37) | collective-permute-done | bytes 393248 | tf_op jit(solution)/shard_map/ppermute | solution.py:69
  192.9 8.6 %collective-permute-done.36 = bf16[128,1536]{1,0:T(8,128)(2,1)S(1)} collective-permute-done((bf16[128,1536]{1,0:T(8,128)(2,1)S(1)}, bf16[128,1536]{1,0:T(8,128)(2,1)S(1)}, u32[]{:S(2)}, u32[]{:S(2)}) %collective-permute-start.36) | collective-permute-done | bytes 393248 | tf_op jit(solution)/shard_map/ppermute | solution.py:69
  (228 shorter events, 28.1 us)
Async XLA Ops:
  6.5 96.9 %all-gather.3.cloned.1.call-start = ((), (), s32[]{:S(2)}) async-start(), calls=%async_computation | async-start | bytes 1327104 | tf_op jit(solution)/shard_map/all_gather | solution.py:182
  7.6 8.9 %copy-start.53 = (s32[8]{0:T(128)S(1)}, s32[8]{0:T(128)}, u32[]{:S(2)}) copy-start(s32[8]{0:T(128)} %constant.407.clone) | copy-start | bytes 100
  7.6 13.6 %copy-start.11 = (s32[8]{0:T(128)S(1)}, s32[8]{0:T(128)}, u32[]{:S(2)}) copy-start(s32[8]{0:T(128)} %constant.408.clone) | copy-start | bytes 100
  7.6 23.2 %copy-start.52 = (s32[1,4]{1,0:T(1,128)S(1)}, s32[1,4]{1,0:T(1,128)}, u32[]{:S(2)}) copy-start(s32[1,4]{1,0:T(1,128)} %param.18) | copy-start | bytes 52
  8.4 32.2 %collective-permute-start.2 = (bf16[192,768]{1,0:T(8,128)(2,1)}, bf16[192,768]{1,0:T(8,128)(2,1)}, u32[]{:S(2)}, u32[]{:S(2)}) collective-permute-start(bf16[192,768]{1,0:T(8,128)(2,1)} %bitcast.77), channel_id=1, source_target_pairs={{0,8},{8,16},{16,24},{24,28},{28,20},{20,12},{12,4},{4,0},{1,9},{9... | collective-permute-start | bytes 884744 | tf_op jit(solution)/shard_map/ppermute | solution.py:119
  11.4 30.7 %collective-permute-start.3 = (bf16[192,768]{1,0:T(8,128)(2,1)}, bf16[192,768]{1,0:T(8,128)(2,1)}, u32[]{:S(2)}, u32[]{:S(2)}) collective-permute-start(bf16[192,768]{1,0:T(8,128)(2,1)} %bitcast.77), channel_id=1, source_target_pairs={{0,4},{8,0},{16,8},{24,16},{28,24},{20,28},{12,20},{4,12},{1,5},{9... | collective-permute-start | bytes 884744 | tf_op jit(solution)/shard_map/ppermute | solution.py:122
  11.8 21.3 %copy-start.7 = (bf16[192,2,384]{2,1,0:T(2,128)(2,1)S(1)}, bf16[192,2,384]{2,1,0:T(2,128)(2,1)}, u32[]{:S(2)}) copy-start(bf16[192,2,384]{2,1,0:T(2,128)(2,1)} %param.23) | copy-start | bytes 884740
  12.9 20.3 %copy-start.9 = (bf16[31,384]{1,0:T(8,128)(2,1)S(1)}, bf16[31,384]{1,0:T(8,128)(2,1)}, u32[]{:S(2)}) copy-start(bf16[31,384]{1,0:T(8,128)(2,1)} %param.24) | copy-start | bytes 71428
  12.9 31.7 %collective-permute-start = (bf16[128,1536]{1,0:T(8,128)(2,1)}, bf16[128,1536]{1,0:T(8,128)(2,1)}, u32[]{:S(2)}, u32[]{:S(2)}) collective-permute-start(bf16[128,1536]{1,0:T(8,128)(2,1)} %fusion.19), channel_id=1, source_target_pairs={{0,2},{1,3},{2,0},{3,1},{4,6},{5,7},{6,4},{7,5},{8,10},{9,11},{10,... | collective-permute-start | bytes 1179656 | tf_op jit(solution)/shard_map/ppermute | solution.py:36
  40.6 14.5 %collective-permute-start.4 = (bf16[192,768]{1,0:T(8,128)(2,1)}, bf16[192,768]{1,0:T(8,128)(2,1)S(1)}, u32[]{:S(2)}, u32[]{:S(2)}) collective-permute-start(bf16[192,768]{1,0:T(8,128)(2,1)} %collective-permute-done.2), channel_id=1, source_target_pairs={{0,8},{8,16},{16,24},{24,28},{28,20},{20,12},{12,4},{4,0},{1,9},{9... | collective-permute-start | bytes 884744 | tf_op jit(solution)/shard_map/ppermute | solution.py:119
  42.1 15.9 %collective-permute-start.5 = (bf16[192,768]{1,0:T(8,128)(2,1)}, bf16[192,768]{1,0:T(8,128)(2,1)S(1)}, u32[]{:S(2)}, u32[]{:S(2)}) collective-permute-start(bf16[192,768]{1,0:T(8,128)(2,1)} %collective-permute-done.3), channel_id=1, source_target_pairs={{0,4},{8,0},{16,8},{24,16},{28,24},{20,28},{12,20},{4,12},{1,5},{9... | collective-permute-start | bytes 884744 | tf_op jit(solution)/shard_map/ppermute | solution.py:122
  45.6 27.6 %copy-start.8 = (bf16[384,192]{0,1:T(8,128)(2,1)S(1)}, bf16[384,192]{0,1:T(8,128)(2,1)}, u32[]{:S(2)}) copy-start(bf16[384,192]{0,1:T(8,128)(2,1)} %param.22) | copy-start | bytes 442372
  45.6 30.1 %collective-permute-start.1 = (bf16[2,128,1536]{2,1,0:T(8,128)(2,1)S(1)}, bf16[2,128,1536]{2,1,0:T(8,128)(2,1)S(1)}, u32[]{:S(2)}, u32[]{:S(2)}) collective-permute-start(bf16[2,128,1536]{2,1,0:T(8,128)(2,1)S(1)} %get-tuple-element.79), channel_id=1, source_target_pairs={{0,1},{1,0},{2,3},{3,2},{4,5},{5,4},{6,7},{7,6},{8,9},{9,8},{10,11... | collective-permute-start | bytes 2359304 | tf_op jit(solution)/shard_map/ppermute | solution.py:42
  55.0 10.0 %collective-permute-start.6 = (bf16[192,768]{1,0:T(8,128)(2,1)S(1)}, bf16[192,768]{1,0:T(8,128)(2,1)S(1)}, u32[]{:S(2)}, u32[]{:S(2)}) collective-permute-start(bf16[192,768]{1,0:T(8,128)(2,1)S(1)} %collective-permute-done.4), channel_id=1, source_target_pairs={{0,8},{8,16},{16,24},{24,28},{28,20},{20,12},{12,4},{4,0},{1,9},{9... | collective-permute-start | bytes 884744 | tf_op jit(solution)/shard_map/ppermute | solution.py:119
  58.1 9.4 %collective-permute-start.7 = (bf16[192,768]{1,0:T(8,128)(2,1)S(1)}, bf16[192,768]{1,0:T(8,128)(2,1)S(1)}, u32[]{:S(2)}, u32[]{:S(2)}) collective-permute-start(bf16[192,768]{1,0:T(8,128)(2,1)S(1)} %collective-permute-done.5), channel_id=1, source_target_pairs={{0,4},{8,0},{16,8},{24,16},{28,24},{20,28},{12,20},{4,12},{1,5},{9... | collective-permute-start | bytes 884744 | tf_op jit(solution)/shard_map/ppermute | solution.py:122
  65.0 8.2 %collective-permute-start.8 = (bf16[192,768]{1,0:T(8,128)(2,1)S(1)}, bf16[192,768]{1,0:T(8,128)(2,1)S(1)}, u32[]{:S(2)}, u32[]{:S(2)}) collective-permute-start(bf16[192,768]{1,0:T(8,128)(2,1)S(1)} %collective-permute-done.6), channel_id=1, source_target_pairs={{0,8},{8,16},{16,24},{24,28},{28,20},{20,12},{12,4},{4,0},{1,9},{9... | collective-permute-start | bytes 884744 | tf_op jit(solution)/shard_map/ppermute | solution.py:119
  73.2 8.5 %collective-permute-start.9 = (bf16[384,192]{0,1:T(8,128)(2,1)S(1)}, bf16[384,192]{0,1:T(8,128)(2,1)S(1)}, u32[]{:S(2)}, u32[]{:S(2)}) collective-permute-start(bf16[384,192]{0,1:T(8,128)(2,1)S(1)} %copy-done.8), channel_id=1, source_target_pairs={{0,8},{8,16},{16,24},{24,28},{28,20},{20,12},{12,4},{4,0},{1,9},{9... | collective-permute-start | bytes 442376 | tf_op jit(solution)/shard_map/ppermute | solution.py:119
  75.8 8.1 %collective-permute-start.10 = (bf16[384,192]{0,1:T(8,128)(2,1)S(1)}, bf16[384,192]{0,1:T(8,128)(2,1)S(1)}, u32[]{:S(2)}, u32[]{:S(2)}) collective-permute-start(bf16[384,192]{0,1:T(8,128)(2,1)S(1)} %copy-done.8), channel_id=1, source_target_pairs={{0,4},{8,0},{16,8},{24,16},{28,24},{20,28},{12,20},{4,12},{1,5},{9... | collective-permute-start | bytes 442376 | tf_op jit(solution)/shard_map/ppermute | solution.py:122
  81.8 5.7 %collective-permute-start.11 = (bf16[384,192]{0,1:T(8,128)(2,1)S(1)}, bf16[384,192]{0,1:T(8,128)(2,1)S(1)}, u32[]{:S(2)}, u32[]{:S(2)}) collective-permute-start(bf16[384,192]{0,1:T(8,128)(2,1)S(1)} %collective-permute-done.9), channel_id=1, source_target_pairs={{0,8},{8,16},{16,24},{24,28},{28,20},{20,12},{12,4},{4,0},{1,9},{9... | collective-permute-start | bytes 442376 | tf_op jit(solution)/shard_map/ppermute | solution.py:119
  83.8 5.9 %collective-permute-start.12 = (bf16[384,192]{0,1:T(8,128)(2,1)S(1)}, bf16[384,192]{0,1:T(8,128)(2,1)S(1)}, u32[]{:S(2)}, u32[]{:S(2)}) collective-permute-start(bf16[384,192]{0,1:T(8,128)(2,1)S(1)} %collective-permute-done.10), channel_id=1, source_target_pairs={{0,4},{8,0},{16,8},{24,16},{28,24},{20,28},{12,20},{4,12},{1,5},{9... | collective-permute-start | bytes 442376 | tf_op jit(solution)/shard_map/ppermute | solution.py:122
  87.4 6.5 %collective-permute-start.13 = (bf16[384,192]{0,1:T(8,128)(2,1)S(1)}, bf16[384,192]{0,1:T(8,128)(2,1)S(1)}, u32[]{:S(2)}, u32[]{:S(2)}) collective-permute-start(bf16[384,192]{0,1:T(8,128)(2,1)S(1)} %collective-permute-done.11), channel_id=1, source_target_pairs={{0,8},{8,16},{16,24},{24,28},{28,20},{20,12},{12,4},{4,0},{1,9},{9... | collective-permute-start | bytes 442376 | tf_op jit(solution)/shard_map/ppermute | solution.py:119
  89.8 6.7 %collective-permute-start.14 = (bf16[384,192]{0,1:T(8,128)(2,1)S(1)}, bf16[384,192]{0,1:T(8,128)(2,1)S(1)}, u32[]{:S(2)}, u32[]{:S(2)}) collective-permute-start(bf16[384,192]{0,1:T(8,128)(2,1)S(1)} %collective-permute-done.12), channel_id=1, source_target_pairs={{0,4},{8,0},{16,8},{24,16},{28,24},{20,28},{12,20},{4,12},{1,5},{9... | collective-permute-start | bytes 442376 | tf_op jit(solution)/shard_map/ppermute | solution.py:122
  93.9 6.7 %collective-permute-start.15 = (bf16[384,192]{0,1:T(8,128)(2,1)S(1)}, bf16[384,192]{0,1:T(8,128)(2,1)S(1)}, u32[]{:S(2)}, u32[]{:S(2)}) collective-permute-start(bf16[384,192]{0,1:T(8,128)(2,1)S(1)} %collective-permute-done.13), channel_id=1, source_target_pairs={{0,8},{8,16},{16,24},{24,28},{28,20},{20,12},{12,4},{4,0},{1,9},{9... | collective-permute-start | bytes 442376 | tf_op jit(solution)/shard_map/ppermute | solution.py:119
  100.7 15.7 %collective-permute-start.21 = (bf16[192,768]{1,0:T(8,128)(2,1)S(1)}, bf16[192,768]{1,0:T(8,128)(2,1)}, u32[]{:S(2)}, u32[]{:S(2)}) collective-permute-start(bf16[192,768]{1,0:T(8,128)(2,1)S(1)} %bitcast.172), channel_id=1, source_target_pairs={{0,8},{8,16},{16,24},{24,28},{28,20},{20,12},{12,4},{4,0},{1,9},{9... | collective-permute-start | bytes 884744 | tf_op jit(solution)/shard_map/ppermute | solution.py:119
  103.2 15.0 %collective-permute-start.22 = (bf16[192,768]{1,0:T(8,128)(2,1)S(1)}, bf16[192,768]{1,0:T(8,128)(2,1)S(1)}, u32[]{:S(2)}, u32[]{:S(2)}) collective-permute-start(bf16[192,768]{1,0:T(8,128)(2,1)S(1)} %bitcast.173), channel_id=1, source_target_pairs={{0,4},{8,0},{16,8},{24,16},{28,24},{20,28},{12,20},{4,12},{1,5},{9... | collective-permute-start | bytes 884744 | tf_op jit(solution)/shard_map/ppermute | solution.py:122
  115.6 12.7 %collective-permute-start.18 = (bf16[128,1536]{1,0:T(8,128)(2,1)S(1)}, bf16[128,1536]{1,0:T(8,128)(2,1)S(1)}, u32[]{:S(2)}, u32[]{:S(2)}) collective-permute-start(bf16[128,1536]{1,0:T(8,128)(2,1)S(1)} %get-tuple-element.71), channel_id=1, source_target_pairs={{0,3},{1,0},{2,1},{3,2},{4,7},{5,4},{6,5},{7,6},{8,11},{9,8},{10,9... | collective-permute-start | bytes 1179656 | tf_op jit(solution)/shard_map/ppermute | solution.py:69
  115.7 17.9 %collective-permute-start.17 = (bf16[128,1536]{1,0:T(8,128)(2,1)S(1)}, bf16[128,1536]{1,0:T(8,128)(2,1)S(1)}, u32[]{:S(2)}, u32[]{:S(2)}) collective-permute-start(bf16[128,1536]{1,0:T(8,128)(2,1)S(1)} %get-tuple-element.72), channel_id=1, source_target_pairs={{0,2},{1,3},{2,0},{3,1},{4,6},{5,7},{6,4},{7,5},{8,10},{9,11},{10,... | collective-permute-start | bytes 1179656 | tf_op jit(solution)/shard_map/ppermute | solution.py:69
  116.2 18.3 %collective-permute-start.16 = (bf16[128,1536]{1,0:T(8,128)(2,1)S(1)}, bf16[128,1536]{1,0:T(8,128)(2,1)S(1)}, u32[]{:S(2)}, u32[]{:S(2)}) collective-permute-start(bf16[128,1536]{1,0:T(8,128)(2,1)S(1)} %get-tuple-element.70), channel_id=1, source_target_pairs={{0,1},{1,2},{2,3},{3,0},{4,5},{5,6},{6,7},{7,4},{8,9},{9,10},{10,1... | collective-permute-start | bytes 1179656 | tf_op jit(solution)/shard_map/ppermute | solution.py:69
  116.4 9.8 %collective-permute-start.23 = (bf16[192,768]{1,0:T(8,128)(2,1)}, bf16[192,768]{1,0:T(8,128)(2,1)S(1)}, u32[]{:S(2)}, u32[]{:S(2)}) collective-permute-start(bf16[192,768]{1,0:T(8,128)(2,1)} %collective-permute-done.21), channel_id=1, source_target_pairs={{0,8},{8,16},{16,24},{24,28},{28,20},{20,12},{12,4},{4,0},{1,9},{9... | collective-permute-start | bytes 884744 | tf_op jit(solution)/shard_map/ppermute | solution.py:119
  118.2 9.5 %collective-permute-start.24 = (bf16[192,768]{1,0:T(8,128)(2,1)S(1)}, bf16[192,768]{1,0:T(8,128)(2,1)S(1)}, u32[]{:S(2)}, u32[]{:S(2)}) collective-permute-start(bf16[192,768]{1,0:T(8,128)(2,1)S(1)} %collective-permute-done.22), channel_id=1, source_target_pairs={{0,4},{8,0},{16,8},{24,16},{28,24},{20,28},{12,20},{4,12},{1,5},{9... | collective-permute-start | bytes 884744 | tf_op jit(solution)/shard_map/ppermute | solution.py:122
  126.2 12.7 %collective-permute-start.25 = (bf16[192,768]{1,0:T(8,128)(2,1)S(1)}, bf16[192,768]{1,0:T(8,128)(2,1)S(1)}, u32[]{:S(2)}, u32[]{:S(2)}) collective-permute-start(bf16[192,768]{1,0:T(8,128)(2,1)S(1)} %collective-permute-done.23), channel_id=1, source_target_pairs={{0,8},{8,16},{16,24},{24,28},{28,20},{20,12},{12,4},{4,0},{1,9},{9... | collective-permute-start | bytes 884744 | tf_op jit(solution)/shard_map/ppermute | solution.py:119
  127.7 13.1 %collective-permute-start.26 = (bf16[192,768]{1,0:T(8,128)(2,1)S(1)}, bf16[192,768]{1,0:T(8,128)(2,1)S(1)}, u32[]{:S(2)}, u32[]{:S(2)}) collective-permute-start(bf16[192,768]{1,0:T(8,128)(2,1)S(1)} %collective-permute-done.24), channel_id=1, source_target_pairs={{0,4},{8,0},{16,8},{24,16},{28,24},{20,28},{12,20},{4,12},{1,5},{9... | collective-permute-start | bytes 884744 | tf_op jit(solution)/shard_map/ppermute | solution.py:122
  128.3 7.9 %copy-start.12 = (f32[1536]{0:T(1024)S(1)}, f32[1536]{0:T(1024)}, u32[]{:S(2)}) copy-start(f32[1536]{0:T(1024)} %param.20) | copy-start | bytes 18436
  137.2 10.2 %collective-permute-start.19 = (bf16[128,1536]{1,0:T(8,128)(2,1)S(1)}, bf16[128,1536]{1,0:T(8,128)(2,1)S(1)}, u32[]{:S(2)}, u32[]{:S(2)}) collective-permute-start(bf16[128,1536]{1,0:T(8,128)(2,1)S(1)} %get-tuple-element.64), channel_id=1, source_target_pairs={{0,2},{1,3},{2,0},{3,1},{4,6},{5,7},{6,4},{7,5},{8,10},{9,11},{10,... | collective-permute-start | bytes 1179656 | tf_op jit(solution)/shard_map/ppermute | solution.py:36
  138.9 9.4 %collective-permute-start.27 = (bf16[192,768]{1,0:T(8,128)(2,1)S(1)}, bf16[192,768]{1,0:T(8,128)(2,1)S(1)}, u32[]{:S(2)}, u32[]{:S(2)}) collective-permute-start(bf16[192,768]{1,0:T(8,128)(2,1)S(1)} %collective-permute-done.25), channel_id=1, source_target_pairs={{0,8},{8,16},{16,24},{24,28},{28,20},{20,12},{12,4},{4,0},{1,9},{9... | collective-permute-start | bytes 884744 | tf_op jit(solution)/shard_map/ppermute | solution.py:119
  148.3 23.1 %collective-permute-start.20 = (bf16[2,128,1536]{2,1,0:T(8,128)(2,1)}, bf16[2,128,1536]{2,1,0:T(8,128)(2,1)}, u32[]{:S(2)}, u32[]{:S(2)}) collective-permute-start(bf16[2,128,1536]{2,1,0:T(8,128)(2,1)} %get-tuple-element.77), channel_id=1, source_target_pairs={{0,1},{1,0},{2,3},{3,2},{4,5},{5,4},{6,7},{7,6},{8,9},{9,8},{10,11... | collective-permute-start | bytes 2359304 | tf_op jit(solution)/shard_map/ppermute | solution.py:42
  149.4 5.6 %collective-permute-start.28 = (bf16[384,192]{0,1:T(8,128)(2,1)}, bf16[384,192]{0,1:T(8,128)(2,1)S(1)}, u32[]{:S(2)}, u32[]{:S(2)}) collective-permute-start(bf16[384,192]{0,1:T(8,128)(2,1)} %param.25), channel_id=1, source_target_pairs={{0,8},{8,16},{16,24},{24,28},{28,20},{20,12},{12,4},{4,0},{1,9},{9... | collective-permute-start | bytes 442376 | tf_op jit(solution)/shard_map/ppermute | solution.py:119
  151.0 5.7 %collective-permute-start.29 = (bf16[384,192]{0,1:T(8,128)(2,1)}, bf16[384,192]{0,1:T(8,128)(2,1)S(1)}, u32[]{:S(2)}, u32[]{:S(2)}) collective-permute-start(bf16[384,192]{0,1:T(8,128)(2,1)} %param.25), channel_id=1, source_target_pairs={{0,4},{8,0},{16,8},{24,16},{28,24},{20,28},{12,20},{4,12},{1,5},{9... | collective-permute-start | bytes 442376 | tf_op jit(solution)/shard_map/ppermute | solution.py:122
  153.9 17.5 %copy-start.6 = (bf16[4,128,1536]{2,1,0:T(8,128)(2,1)S(1)}, bf16[4,128,1536]{2,1,0:T(8,128)(2,1)}, u32[]{:S(2)}) copy-start(bf16[4,128,1536]{2,1,0:T(8,128)(2,1)} %copy-done.5) | copy-start | bytes 4718596
  155.0 5.2 %collective-permute-start.30 = (bf16[384,192]{0,1:T(8,128)(2,1)S(1)}, bf16[384,192]{0,1:T(8,128)(2,1)S(1)}, u32[]{:S(2)}, u32[]{:S(2)}) collective-permute-start(bf16[384,192]{0,1:T(8,128)(2,1)S(1)} %collective-permute-done.28), channel_id=1, source_target_pairs={{0,8},{8,16},{16,24},{24,28},{28,20},{20,12},{12,4},{4,0},{1,9},{9... | collective-permute-start | bytes 442376 | tf_op jit(solution)/shard_map/ppermute | solution.py:119
  156.7 5.2 %collective-permute-start.31 = (bf16[384,192]{0,1:T(8,128)(2,1)S(1)}, bf16[384,192]{0,1:T(8,128)(2,1)S(1)}, u32[]{:S(2)}, u32[]{:S(2)}) collective-permute-start(bf16[384,192]{0,1:T(8,128)(2,1)S(1)} %collective-permute-done.29), channel_id=1, source_target_pairs={{0,4},{8,0},{16,8},{24,16},{28,24},{20,28},{12,20},{4,12},{1,5},{9... | collective-permute-start | bytes 442376 | tf_op jit(solution)/shard_map/ppermute | solution.py:122
  157.2 16.2 %copy-start.3 = (bf16[768,1536]{1,0:T(8,128)(2,1)S(1)}, bf16[768,1536]{1,0:T(8,128)(2,1)}, u32[]{:S(2)}) copy-start(bf16[768,1536]{1,0:T(8,128)(2,1)} %copy.35) | copy-start | bytes 7077892
  160.2 5.9 %collective-permute-start.32 = (bf16[384,192]{0,1:T(8,128)(2,1)S(1)}, bf16[384,192]{0,1:T(8,128)(2,1)S(1)}, u32[]{:S(2)}, u32[]{:S(2)}) collective-permute-start(bf16[384,192]{0,1:T(8,128)(2,1)S(1)} %collective-permute-done.30), channel_id=1, source_target_pairs={{0,8},{8,16},{16,24},{24,28},{28,20},{20,12},{12,4},{4,0},{1,9},{9... | collective-permute-start | bytes 442376 | tf_op jit(solution)/shard_map/ppermute | solution.py:119
  161.9 5.9 %collective-permute-start.33 = (bf16[384,192]{0,1:T(8,128)(2,1)S(1)}, bf16[384,192]{0,1:T(8,128)(2,1)S(1)}, u32[]{:S(2)}, u32[]{:S(2)}) collective-permute-start(bf16[384,192]{0,1:T(8,128)(2,1)S(1)} %collective-permute-done.31), channel_id=1, source_target_pairs={{0,4},{8,0},{16,8},{24,16},{28,24},{20,28},{12,20},{4,12},{1,5},{9... | collective-permute-start | bytes 442376 | tf_op jit(solution)/shard_map/ppermute | solution.py:122
  166.1 5.1 %collective-permute-start.34 = (bf16[384,192]{0,1:T(8,128)(2,1)S(1)}, bf16[384,192]{0,1:T(8,128)(2,1)S(1)}, u32[]{:S(2)}, u32[]{:S(2)}) collective-permute-start(bf16[384,192]{0,1:T(8,128)(2,1)S(1)} %collective-permute-done.32), channel_id=1, source_target_pairs={{0,8},{8,16},{16,24},{24,28},{28,20},{20,12},{12,4},{4,0},{1,9},{9... | collective-permute-start | bytes 442376 | tf_op jit(solution)/shard_map/ppermute | solution.py:119
  183.5 9.4 %collective-permute-start.37 = (bf16[128,1536]{1,0:T(8,128)(2,1)S(1)}, bf16[128,1536]{1,0:T(8,128)(2,1)S(1)}, u32[]{:S(2)}, u32[]{:S(2)}) collective-permute-start(bf16[128,1536]{1,0:T(8,128)(2,1)S(1)} %get-tuple-element.68), channel_id=1, source_target_pairs={{0,3},{1,0},{2,1},{3,2},{4,7},{5,4},{6,5},{7,6},{8,11},{9,8},{10,9... | collective-permute-start | bytes 1179656 | tf_op jit(solution)/shard_map/ppermute | solution.py:69
  183.6 18.0 %collective-permute-start.36 = (bf16[128,1536]{1,0:T(8,128)(2,1)S(1)}, bf16[128,1536]{1,0:T(8,128)(2,1)S(1)}, u32[]{:S(2)}, u32[]{:S(2)}) collective-permute-start(bf16[128,1536]{1,0:T(8,128)(2,1)S(1)} %get-tuple-element.69), channel_id=1, source_target_pairs={{0,2},{1,3},{2,0},{3,1},{4,6},{5,7},{6,4},{7,5},{8,10},{9,11},{10,... | collective-permute-start | bytes 1179656 | tf_op jit(solution)/shard_map/ppermute | solution.py:69
  184.2 18.3 %collective-permute-start.35 = (bf16[128,1536]{1,0:T(8,128)(2,1)S(1)}, bf16[128,1536]{1,0:T(8,128)(2,1)S(1)}, u32[]{:S(2)}, u32[]{:S(2)}) collective-permute-start(bf16[128,1536]{1,0:T(8,128)(2,1)S(1)} %get-tuple-element.67), channel_id=1, source_target_pairs={{0,1},{1,2},{2,3},{3,0},{4,5},{5,6},{6,7},{7,4},{8,9},{9,10},{10,1... | collective-permute-start | bytes 1179656 | tf_op jit(solution)/shard_map/ppermute | solution.py:69
  (45 other events, 44.1 us)
Sparse Core Ops, SparseCore 0:
  16.5 45.6 all-gather.2

commit v5 on v3

--- a/solution.py
+++ b/solution.py
@@ -183,9 +183,13 @@
     qkv_matrix = qkv_parts.reshape(model_width, 3 * group_width)
     out_parts = ring_gather(after(qkv_parts, w_out), ring)
     out_local = jnp.einsum("nrc->rnc", out_parts).reshape(w_out.shape[0], model_width)
-    glu_parts = ring_gather(after(out_parts, w_glu.reshape(w_glu.shape[0], 2 * group_width)), ring)
-    glu_matrix = glu_parts.reshape(model_width, 2 * group_width)
-    proj_parts = ring_gather(after(glu_parts, w_proj), ring)
+    glu_rows = w_glu.shape[0]
+    glu_local = w_glu.reshape(glu_rows, 2 * group_width)
+    both_parts = ring_gather(
+        after(out_parts, jnp.concatenate([glu_local, w_proj.reshape(-1, 2 * group_width)])), ring
+    )
+    glu_matrix = both_parts[:, :glu_rows].reshape(model_width, 2 * group_width)
+    proj_parts = both_parts[:, glu_rows:].reshape(-1, *w_proj.shape)
     proj_local = jnp.einsum("nrc->rnc", proj_parts).reshape(w_proj.shape[0], model_width)
     inputs = frames[0].astype(jnp.float32)
     record_ends = jnp.cumsum(lengths[0])
@@ -212,6 +216,7 @@
     activated = depthwise(
         padded, dw_kernel, seg_all, segment_of(record_ends, near_positions), group_rows
     )
+    activated = lax.optimization_barrier(activated)
     conv_out = seq_scatter_sum(
         jnp.dot(activated, proj_local, preferred_element_type=jnp.float32).astype(jnp.bfloat16)
     )

time: 206 us -> 200 us (0.971)
  starting transfers between devices: 41.7 us -> 29.2 us
  other arithmetic: 9.89 us -> 17.5 us
  waiting for transfers between devices: 88.1 us -> 94 us
  matrix products: 21.7 us -> 16.1 us
    dot_general x1, matrix products: 8.73 us -> 1.01 us  [on_device(): jnp.dot(activated, proj_local, preferred_element_type=jnp.float32)]
    convert_element_type x0 -> x1, other arithmetic: none -> 6.56 us  [depthwise(): return jax.nn.silu(total_acc).astype(jnp.bfloat16)]
    ppermute x16 -> x12, starting transfers between devices: 26.7 us -> 20.5 us  [ring_gather(): ahead = lax.ppermute(ahead, 'dp', forward)]
    ppermute x6, waiting for transfers between devices: 28.2 us -> 32.8 us  [seq_scatter_sum(): lax.ppermute(piece, 'seq', [(i, (i + shift) % count) for i in range(count)])]
    ppermute x6, starting transfers between devices: 5.15 us -> 1.38 us  [seq_scatter_sum(): lax.ppermute(piece, 'seq', [(i, (i + shift) % count) for i in range(count)])]
    ppermute x16 -> x12, waiting for transfers between devices: 51.3 us -> 54.8 us  [ring_gather(): ahead = lax.ppermute(ahead, 'dp', forward)]
    dot_general x1, matrix products: 1.42 us -> 3.55 us  [on_device(): jnp.dot(shard_piece, glu_matrix, preferred_element_type=jnp.float32)]
    ppermute x12 -> x9, starting transfers between devices: 5.45 us -> 3.78 us  [ring_gather(): behind = lax.ppermute(behind, 'dp', backward)]
  transfers between devices with their start and end apart: 38 -> 31, of which waited for: 19 -> 17; matrix products, arithmetic and copies ran while one was open for 21% -> 17% of each run, Pallas kernels for 0% -> 0%
where the time goes in v5:
time: 200 us; the launch traced here: 199 us
  waiting for transfers between devices  94 us (47%)
  starting transfers between devices  29.2 us (15%)
  local copies, waits for them, and re-layouts  24.3 us (12%)
  between operations  18.4 us (9%)
  other arithmetic  17.5 us (9%)
  matrix products  16.1 us (8%)
    ppermute x12, waiting for transfers between devices, ring_gather(): ahead = lax.ppermute(ahead, 'dp', forward)  54.8 us
    ppermute x6, waiting for transfers between devices, seq_scatter_sum(): lax.ppermute(piece, 'seq', [(i, (i + shift) % count) for i in range(count)])  32.8 us
    ppermute x12, starting transfers between devices, ring_gather(): ahead = lax.ppermute(ahead, 'dp', forward)  20.5 us
    convert_element_type x1, other arithmetic, depthwise(): return jax.nn.silu(total_acc).astype(jnp.bfloat16)  6.56 us
    ppermute x2, waiting for transfers between devices, seq_gather(): lax.ppermute(block, 'seq', [(i, (i + 2 * shift) % count) for i in range(c...  6.12 us
    dot_general x1, matrix products, on_device(): jnp.dot(seq_gather(normed1, paired).reshape(group_rows, model_width), qkv...  4.19 us
  transfers between devices with their start and end apart: 31, of which 17 were waited for; matrix products, arithmetic and copies ran while one was open for 17% of the time, Pallas kernels for 0%

profile of v5, /device:TPU:0, one launch (start us, length us, event | category | flops | bytes accessed | tf_op | source)
XLA Modules:
  0.0 199.5 jit_solution(5856354646492211099)
XLA Ops:
  0.0 1.1 copy.43
  1.2 3.1 %collective-permute-start.2 = (bf16[192,1152]{1,0:T(8,128)(2,1)S(1)}, bf16[192,1152]{1,0:T(8,128)(2,1)S(1)}, u32[]{:S(2)}, u32[]{:S(2)}) collective-permute-start(bf16[192,1152]{1,0:T(8,128)(2,1)S(1)} %bitcast.160), channel_id=1, source_target_pairs={{0,8},{8,16},{16,24},{24,28},{28,20},{20,12},{12,4},{4,0},{1,9},{9... | collective-permute-start | bytes 1327112 | tf_op jit(solution)/shard_map/ppermute | solution.py:119
  4.3 1.1 convert_reduce_fusion.1
  5.4 1.2 fusion.16
  7.5 2.0 %collective-permute-start = (bf16[128,1536]{1,0:T(8,128)(2,1)S(1)}, bf16[128,1536]{1,0:T(8,128)(2,1)S(1)}, u32[]{:S(2)}, u32[]{:S(2)}) collective-permute-start(bf16[128,1536]{1,0:T(8,128)(2,1)S(1)} %fusion.18), channel_id=1, source_target_pairs={{0,2},{1,3},{2,0},{3,1},{4,6},{5,7},{6,4},{7,5},{8,10},{9,11},{10,... | collective-permute-start | bytes 1179656 | tf_op jit(solution)/shard_map/ppermute | solution.py:36
  9.8 1.2 dynamic_slice.102
  25.3 0.9 broadcast_compare_fusion
  28.1 1.8 convert_reduce_fusion.34
  29.9 2.2 %broadcast_in_dim.399 = bf16[8,192,1152]{2,1,0:T(8,128)(2,1)} broadcast(bf16[]{:T(256)} %constant.324.clone.1), dimensions={} | broadcast | bytes 3538946 | tf_op jit(solution)/shard_map/broadcast_in_dim | solution.py:115
  37.8 1.6 collective-permute-start.4
  41.5 8.9 %collective-permute-done.4 = bf16[192,1152]{1,0:T(8,128)(2,1)S(1)} collective-permute-done((bf16[192,1152]{1,0:T(8,128)(2,1)S(1)}, bf16[192,1152]{1,0:T(8,128)(2,1)S(1)}, u32[]{:S(2)}, u32[]{:S(2)}) %collective-permute-start.4) | collective-permute-done | bytes 442400 | tf_op jit(solution)/shard_map/ppermute | solution.py:119
  50.4 1.6 collective-permute-start.6
  54.2 8.0 %collective-permute-done.6 = bf16[192,1152]{1,0:T(8,128)(2,1)S(1)} collective-permute-done((bf16[192,1152]{1,0:T(8,128)(2,1)S(1)}, bf16[192,1152]{1,0:T(8,128)(2,1)S(1)}, u32[]{:S(2)}, u32[]{:S(2)}) %collective-permute-start.6) | collective-permute-done | bytes 442400 | tf_op jit(solution)/shard_map/ppermute | solution.py:119
  62.1 1.6 collective-permute-start.8
  65.3 7.6 %collective-permute-done.8 = bf16[192,1152]{1,0:T(8,128)(2,1)S(1)} collective-permute-done((bf16[192,1152]{1,0:T(8,128)(2,1)S(1)}, bf16[192,1152]{1,0:T(8,128)(2,1)S(1)}, u32[]{:S(2)}, u32[]{:S(2)}) %collective-permute-start.8) | collective-permute-done | bytes 442400 | tf_op jit(solution)/shard_map/ppermute | solution.py:119
  73.8 1.6 collective-permute-start.9
  75.8 4.2 %convolution_convert_fusion = bf16[512,1152]{1,0:T(8,128)(2,1)S(1)} fusion(bf16[512,1536]{1,0:T(8,128)(2,1)S(1)} %bitcast.155, bf16[1536,1152]{1,0:T(8,128)(2,1)} %bitcast.24), kind=kOutput, calls=%fused_computation.5 | convolution fusion | flops 1812529152 | bytes 6291456 | tf_op jit(solution)/shard_map/dot_general | solution.py:199
  80.9 3.6 %fusion.39 = (f32[4,512]{1,0:T(4,128)S(1)}, f32[4,512,512]{1,2,0:T(8,128)}) fusion(pred[512,512]{0,1:T(8,128)(4,1)S(1)} %copy-done.4, bf16[512,3,4,96]{0,3,2,1:T(8,128)(2,1)S(1)} %bitcast.158), kind=kOutput, calls=%fused_computation.172 | convolution fusion | flops 205521408 | bytes 5251072 | tf_op jit(solution)/shard_map/while/body/eval_jaxpr/sub | solution.py:151
  84.6 2.7 %fusion.6 = bf16[4,96,512]{2,1,0:T(8,128)(2,1)S(1)} fusion(f32[4,512,512]{1,2,0:T(8,128)} %get-tuple-element.116, f32[4,512]{1,0:T(4,128)S(1)} %get-tuple-element.115, bf16[512,3,4,96]{0,3,2,1:T(8,128)(2,1)S(1)} %bitcast.159), kind=kOutput, calls=%fused_computation.12 | convolution fusion | flops 203620352 | bytes 4988928 | tf_op jit(solution)/shard_map/while/body/eval_jaxpr/hqk,khe->qhe/dot_general | solution.py:153
  87.4 1.6 collective-permute-start.11
  89.6 4.3 %collective-permute-done.11 = bf16[384,192]{0,1:T(8,128)(2,1)S(1)} collective-permute-done((bf16[384,192]{0,1:T(8,128)(2,1)S(1)}, bf16[384,192]{0,1:T(8,128)(2,1)S(1)}, u32[]{:S(2)}, u32[]{:S(2)}) %collective-permute-start.11) | collective-permute-done | bytes 147488 | tf_op jit(solution)/shard_map/ppermute | solution.py:119
  93.9 1.6 collective-permute-start.13
  96.3 3.8 %collective-permute-done.13 = bf16[384,192]{0,1:T(8,128)(2,1)S(1)} collective-permute-done((bf16[384,192]{0,1:T(8,128)(2,1)S(1)}, bf16[384,192]{0,1:T(8,128)(2,1)S(1)}, u32[]{:S(2)}, u32[]{:S(2)}) %collective-permute-start.13) | collective-permute-done | bytes 147488 | tf_op jit(solution)/shard_map/ppermute | solution.py:119
  100.1 1.6 collective-permute-start.15
  101.7 3.5 %collective-permute-done.15 = bf16[384,192]{0,1:T(8,128)(2,1)S(1)} collective-permute-done((bf16[384,192]{0,1:T(8,128)(2,1)S(1)}, bf16[384,192]{0,1:T(8,128)(2,1)S(1)}, u32[]{:S(2)}, u32[]{:S(2)}) %collective-permute-start.15) | collective-permute-done | bytes 147488 | tf_op jit(solution)/shard_map/ppermute | solution.py:119
  105.2 1.0 convolution_convert_fusion.2
  108.4 1.0 copy.44
  109.5 1.6 collective-permute-start.21
  111.8 5.1 %collective-permute-done.18 = bf16[128,1536]{1,0:T(8,128)(2,1)} collective-permute-done((bf16[128,1536]{1,0:T(8,128)(2,1)}, bf16[128,1536]{1,0:T(8,128)(2,1)}, u32[]{:S(2)}, u32[]{:S(2)}) %collective-permute-start.18) | collective-permute-done | bytes 393248 | tf_op jit(solution)/shard_map/ppermute | solution.py:69
  117.0 8.7 %collective-permute-done.17 = bf16[128,1536]{1,0:T(8,128)(2,1)} collective-permute-done((bf16[128,1536]{1,0:T(8,128)(2,1)S(1)}, bf16[128,1536]{1,0:T(8,128)(2,1)}, u32[]{:S(2)}, u32[]{:S(2)}) %collective-permute-start.17) | collective-permute-done | bytes 393248 | tf_op jit(solution)/shard_map/ppermute | solution.py:69
  126.5 1.6 convert_reduce_fusion
  128.7 1.4 collective-permute-start.19
  130.3 1.6 collective-permute-start.23
  132.5 6.1 %collective-permute-done.19 = bf16[128,1536]{1,0:T(8,128)(2,1)S(1)} collective-permute-done((bf16[128,1536]{1,0:T(8,128)(2,1)S(1)}, bf16[128,1536]{1,0:T(8,128)(2,1)S(1)}, u32[]{:S(2)}, u32[]{:S(2)}) %collective-permute-start.19) | collective-permute-done | bytes 393248 | tf_op jit(solution)/shard_map/ppermute | solution.py:36
  138.7 1.6 collective-permute-done.23
  140.3 1.5 collective-permute-start.25
  142.5 8.8 %collective-permute-done.25 = bf16[288,768]{1,0:T(8,128)(2,1)S(1)} collective-permute-done((bf16[288,768]{1,0:T(8,128)(2,1)S(1)}, bf16[288,768]{1,0:T(8,128)(2,1)S(1)}, u32[]{:S(2)}, u32[]{:S(2)}) %collective-permute-start.25) | collective-permute-done | bytes 442400 | tf_op jit(solution)/shard_map/ppermute | solution.py:119
  151.3 1.5 collective-permute-start.27
  153.0 8.4 %collective-permute-done.27 = bf16[288,768]{1,0:T(8,128)(2,1)S(1)} collective-permute-done((bf16[288,768]{1,0:T(8,128)(2,1)S(1)}, bf16[288,768]{1,0:T(8,128)(2,1)S(1)}, u32[]{:S(2)}, u32[]{:S(2)}) %collective-permute-start.27) | collective-permute-done | bytes 442400 | tf_op jit(solution)/shard_map/ppermute | solution.py:119
  161.5 1.1 slice.423
  162.6 2.4 %copy.40 = bf16[768,1536]{1,0:T(8,128)(2,1)} copy(bf16[768,1536]{0,1:T(8,128)(2,1)S(1)} %bitcast.149) | data formatting | bytes 4718592 | tf_op jit(solution)/shard_map/dot_general | solution.py:210
  165.1 3.5 %fusion.40 = f32[512,2,384]{2,0,1:T(8,128)S(1)} fusion(bf16[512,1536,1]{1,0,2:T(8,128)(2,1)} %bitcast.156, bf16[2,384,1536]{2,1,0:T(8,128)(2,1)} %bitcast.153), kind=kOutput, calls=%fused_computation.173 | convolution fusion | flops 1207959552 | bytes 5505024 | tf_op jit(solution)/shard_map/dot_general | solution.py:210
  169.7 6.6 %multiply_convert_fusion = bf16[512,384]{1,0:T(8,128)(2,1)S(1)} fusion(bf16[512,384]{1,0:T(8,128)(2,1)S(1)} %fusion.32, f32[384]{0:T(512)S(1)} %get-tuple-element.59, f32[384]{0:T(512)S(1)} %get-tuple-element.60, f32[384]{0:T(512)S(1)} %get-tuple-element.30, f32[384]{0:T(512)S(1)} %copy-done.11, f32[384]{0:T(512)S(1)} %copy-done.12, f32[384]{0:T(512)S(1)} %copy-done.13, ...), kind=kLoop, calls=%fused_computation.41 | loop fusion | flops 25165824 | bytes 849920 | tf_op jit(solution)/shard_map/convert_element_type | solution.py:172
  176.2 1.5 reshape.239
  178.6 1.0 convolution_convert_fusion.1
  180.3 9.0 %collective-permute-done.30 = bf16[128,1536]{1,0:T(8,128)(2,1)S(1)} collective-permute-done((bf16[128,1536]{1,0:T(8,128)(2,1)S(1)}, bf16[128,1536]{1,0:T(8,128)(2,1)S(1)}, u32[]{:S(2)}, u32[]{:S(2)}) %collective-permute-start.30) | collective-permute-done | bytes 393248 | tf_op jit(solution)/shard_map/ppermute | solution.py:69
  189.3 8.2 %collective-permute-done.29 = bf16[128,1536]{1,0:T(8,128)(2,1)S(1)} collective-permute-done((bf16[128,1536]{1,0:T(8,128)(2,1)S(1)}, bf16[128,1536]{1,0:T(8,128)(2,1)S(1)}, u32[]{:S(2)}, u32[]{:S(2)}) %collective-permute-start.29) | collective-permute-done | bytes 393248 | tf_op jit(solution)/shard_map/ppermute | solution.py:69
  198.5 1.0 fusion.31
  (208 shorter events, 24.1 us)
Async XLA Ops:
  0.0 9.5 %copy-start.2 = (bf16[192,3,384]{2,0,1:T(8,128)(2,1)S(1)}, bf16[192,3,384]{2,0,1:T(8,128)(2,1)}, u32[]{:S(2)}) copy-start(bf16[192,3,384]{2,0,1:T(8,128)(2,1)} %param.19) | copy-start | bytes 1327108
  0.0 7.2 %copy-start = (bf16[1,128,1536]{2,1,0:T(8,128)(2,1)S(1)}, bf16[1,128,1536]{2,1,0:T(8,128)(2,1)}, u32[]{:S(2)}) copy-start(bf16[1,128,1536]{2,1,0:T(8,128)(2,1)} %param.15) | copy-start | bytes 1179652
  0.0 7.2 %copy-start.8 = (f32[1536]{0:T(1024)S(1)}, f32[1536]{0:T(1024)}, u32[]{:S(2)}) copy-start(f32[1536]{0:T(1024)} %param.17) | copy-start | bytes 18436
  1.1 14.6 %copy-start.9 = (s32[8]{0:T(128)S(1)}, s32[8]{0:T(128)}, u32[]{:S(2)}) copy-start(s32[8]{0:T(128)} %constant.356.clone) | copy-start | bytes 100
  1.2 23.8 %copy-start.54 = (s32[1,4]{1,0:T(1,128)S(1)}, s32[1,4]{1,0:T(1,128)}, u32[]{:S(2)}) copy-start(s32[1,4]{1,0:T(1,128)} %param.16) | copy-start | bytes 52
  1.2 36.7 %collective-permute-start.2 = (bf16[192,1152]{1,0:T(8,128)(2,1)S(1)}, bf16[192,1152]{1,0:T(8,128)(2,1)S(1)}, u32[]{:S(2)}, u32[]{:S(2)}) collective-permute-start(bf16[192,1152]{1,0:T(8,128)(2,1)S(1)} %bitcast.160), channel_id=1, source_target_pairs={{0,8},{8,16},{16,24},{24,28},{28,20},{20,12},{12,4},{4,0},{1,9},{9... | collective-permute-start | bytes 1327112 | tf_op jit(solution)/shard_map/ppermute | solution.py:119
  4.2 35.2 %collective-permute-start.3 = (bf16[192,1152]{1,0:T(8,128)(2,1)S(1)}, bf16[192,1152]{1,0:T(8,128)(2,1)S(1)}, u32[]{:S(2)}, u32[]{:S(2)}) collective-permute-start(bf16[192,1152]{1,0:T(8,128)(2,1)S(1)} %bitcast.161), channel_id=1, source_target_pairs={{0,4},{8,0},{16,8},{24,16},{28,24},{20,28},{12,20},{4,12},{1,5},{9... | collective-permute-start | bytes 1327112 | tf_op jit(solution)/shard_map/ppermute | solution.py:122
  5.4 1.3 copy-start.28
  7.5 30.2 %collective-permute-start = (bf16[128,1536]{1,0:T(8,128)(2,1)S(1)}, bf16[128,1536]{1,0:T(8,128)(2,1)S(1)}, u32[]{:S(2)}, u32[]{:S(2)}) collective-permute-start(bf16[128,1536]{1,0:T(8,128)(2,1)S(1)} %fusion.18), channel_id=1, source_target_pairs={{0,2},{1,3},{2,0},{3,1},{4,6},{5,7},{6,4},{7,5},{8,10},{9,11},{10,... | collective-permute-start | bytes 1179656 | tf_op jit(solution)/shard_map/ppermute | solution.py:36
  32.1 5.3 %copy-start.29 = (f32[128]{0:T(128)S(1)}, f32[128]{0:T(128)}, u32[]{:S(2)}) copy-start(f32[128]{0:T(128)} %copy-done.28) | copy-start | bytes 1540
  32.1 5.3 %copy-start.31 = (f32[128]{0:T(128)S(1)}, f32[128]{0:T(128)}, u32[]{:S(2)}) copy-start(f32[128]{0:T(128)} %copy-done.30) | copy-start | bytes 1540
  37.8 16.3 %collective-permute-start.1 = (bf16[2,128,1536]{2,1,0:T(8,128)(2,1)S(1)}, bf16[2,128,1536]{2,1,0:T(8,128)(2,1)S(1)}, u32[]{:S(2)}, u32[]{:S(2)}) collective-permute-start(bf16[2,128,1536]{2,1,0:T(8,128)(2,1)S(1)} %get-tuple-element.75), channel_id=1, source_target_pairs={{0,1},{1,0},{2,3},{3,2},{4,5},{5,4},{6,7},{7,6},{8,9},{9,8},{10,11... | collective-permute-start | bytes 2359304 | tf_op jit(solution)/shard_map/ppermute | solution.py:42
  37.8 12.6 %collective-permute-start.4 = (bf16[192,1152]{1,0:T(8,128)(2,1)S(1)}, bf16[192,1152]{1,0:T(8,128)(2,1)S(1)}, u32[]{:S(2)}, u32[]{:S(2)}) collective-permute-start(bf16[192,1152]{1,0:T(8,128)(2,1)S(1)} %collective-permute-done.2), channel_id=1, source_target_pairs={{0,8},{8,16},{16,24},{24,28},{28,20},{20,12},{12,4},{4,0},{1,9},{9... | collective-permute-start | bytes 1327112 | tf_op jit(solution)/shard_map/ppermute | solution.py:119
  39.5 12.5 %collective-permute-start.5 = (bf16[192,1152]{1,0:T(8,128)(2,1)S(1)}, bf16[192,1152]{1,0:T(8,128)(2,1)S(1)}, u32[]{:S(2)}, u32[]{:S(2)}) collective-permute-start(bf16[192,1152]{1,0:T(8,128)(2,1)S(1)} %collective-permute-done.3), channel_id=1, source_target_pairs={{0,4},{8,0},{16,8},{24,16},{28,24},{20,28},{12,20},{4,12},{1,5},{9... | collective-permute-start | bytes 1327112 | tf_op jit(solution)/shard_map/ppermute | solution.py:122
  50.4 11.7 %collective-permute-start.6 = (bf16[192,1152]{1,0:T(8,128)(2,1)S(1)}, bf16[192,1152]{1,0:T(8,128)(2,1)S(1)}, u32[]{:S(2)}, u32[]{:S(2)}) collective-permute-start(bf16[192,1152]{1,0:T(8,128)(2,1)S(1)} %collective-permute-done.4), channel_id=1, source_target_pairs={{0,8},{8,16},{16,24},{24,28},{28,20},{20,12},{12,4},{4,0},{1,9},{9... | collective-permute-start | bytes 1327112 | tf_op jit(solution)/shard_map/ppermute | solution.py:119
  52.0 12.5 %collective-permute-start.7 = (bf16[192,1152]{1,0:T(8,128)(2,1)S(1)}, bf16[192,1152]{1,0:T(8,128)(2,1)S(1)}, u32[]{:S(2)}, u32[]{:S(2)}) collective-permute-start(bf16[192,1152]{1,0:T(8,128)(2,1)S(1)} %collective-permute-done.5), channel_id=1, source_target_pairs={{0,4},{8,0},{16,8},{24,16},{28,24},{20,28},{12,20},{4,12},{1,5},{9... | collective-permute-start | bytes 1327112 | tf_op jit(solution)/shard_map/ppermute | solution.py:122
  54.1 19.7 %copy-start.5 = (bf16[384,192]{0,1:T(8,128)(2,1)S(1)}, bf16[384,192]{0,1:T(8,128)(2,1)}, u32[]{:S(2)}) copy-start(bf16[384,192]{0,1:T(8,128)(2,1)} %param.20) | copy-start | bytes 442372
  62.1 10.8 %collective-permute-start.8 = (bf16[192,1152]{1,0:T(8,128)(2,1)S(1)}, bf16[192,1152]{1,0:T(8,128)(2,1)S(1)}, u32[]{:S(2)}, u32[]{:S(2)}) collective-permute-start(bf16[192,1152]{1,0:T(8,128)(2,1)S(1)} %collective-permute-done.6), channel_id=1, source_target_pairs={{0,8},{8,16},{16,24},{24,28},{28,20},{20,12},{12,4},{4,0},{1,9},{9... | collective-permute-start | bytes 1327112 | tf_op jit(solution)/shard_map/ppermute | solution.py:119
  73.8 13.6 %collective-permute-start.9 = (bf16[384,192]{0,1:T(8,128)(2,1)S(1)}, bf16[384,192]{0,1:T(8,128)(2,1)S(1)}, u32[]{:S(2)}, u32[]{:S(2)}) collective-permute-start(bf16[384,192]{0,1:T(8,128)(2,1)S(1)} %copy-done.5), channel_id=1, source_target_pairs={{0,8},{8,16},{16,24},{24,28},{28,20},{20,12},{12,4},{4,0},{1,9},{9... | collective-permute-start | bytes 442376 | tf_op jit(solution)/shard_map/ppermute | solution.py:119
  75.3 13.7 %collective-permute-start.10 = (bf16[384,192]{0,1:T(8,128)(2,1)S(1)}, bf16[384,192]{0,1:T(8,128)(2,1)S(1)}, u32[]{:S(2)}, u32[]{:S(2)}) collective-permute-start(bf16[384,192]{0,1:T(8,128)(2,1)S(1)} %copy-done.5), channel_id=1, source_target_pairs={{0,4},{8,0},{16,8},{24,16},{28,24},{20,28},{12,20},{4,12},{1,5},{9... | collective-permute-start | bytes 442376 | tf_op jit(solution)/shard_map/ppermute | solution.py:122
  80.0 1.0 copy-start.4
  87.4 6.5 %collective-permute-start.11 = (bf16[384,192]{0,1:T(8,128)(2,1)S(1)}, bf16[384,192]{0,1:T(8,128)(2,1)S(1)}, u32[]{:S(2)}, u32[]{:S(2)}) collective-permute-start(bf16[384,192]{0,1:T(8,128)(2,1)S(1)} %collective-permute-done.9), channel_id=1, source_target_pairs={{0,8},{8,16},{16,24},{24,28},{28,20},{20,12},{12,4},{4,0},{1,9},{9... | collective-permute-start | bytes 442376 | tf_op jit(solution)/shard_map/ppermute | solution.py:119
  89.1 6.8 %collective-permute-start.12 = (bf16[384,192]{0,1:T(8,128)(2,1)S(1)}, bf16[384,192]{0,1:T(8,128)(2,1)S(1)}, u32[]{:S(2)}, u32[]{:S(2)}) collective-permute-start(bf16[384,192]{0,1:T(8,128)(2,1)S(1)} %collective-permute-done.10), channel_id=1, source_target_pairs={{0,4},{8,0},{16,8},{24,16},{28,24},{20,28},{12,20},{4,12},{1,5},{9... | collective-permute-start | bytes 442376 | tf_op jit(solution)/shard_map/ppermute | solution.py:122
  93.9 6.2 %collective-permute-start.13 = (bf16[384,192]{0,1:T(8,128)(2,1)S(1)}, bf16[384,192]{0,1:T(8,128)(2,1)S(1)}, u32[]{:S(2)}, u32[]{:S(2)}) collective-permute-start(bf16[384,192]{0,1:T(8,128)(2,1)S(1)} %collective-permute-done.11), channel_id=1, source_target_pairs={{0,8},{8,16},{16,24},{24,28},{28,20},{20,12},{12,4},{4,0},{1,9},{9... | collective-permute-start | bytes 442376 | tf_op jit(solution)/shard_map/ppermute | solution.py:119
  95.8 5.8 %collective-permute-start.14 = (bf16[384,192]{0,1:T(8,128)(2,1)S(1)}, bf16[384,192]{0,1:T(8,128)(2,1)S(1)}, u32[]{:S(2)}, u32[]{:S(2)}) collective-permute-start(bf16[384,192]{0,1:T(8,128)(2,1)S(1)} %collective-permute-done.12), channel_id=1, source_target_pairs={{0,4},{8,0},{16,8},{24,16},{28,24},{20,28},{12,20},{4,12},{1,5},{9... | collective-permute-start | bytes 442376 | tf_op jit(solution)/shard_map/ppermute | solution.py:122
  100.1 5.1 %collective-permute-start.15 = (bf16[384,192]{0,1:T(8,128)(2,1)S(1)}, bf16[384,192]{0,1:T(8,128)(2,1)S(1)}, u32[]{:S(2)}, u32[]{:S(2)}) collective-permute-start(bf16[384,192]{0,1:T(8,128)(2,1)S(1)} %collective-permute-done.13), channel_id=1, source_target_pairs={{0,8},{8,16},{16,24},{24,28},{28,20},{20,12},{12,4},{4,0},{1,9},{9... | collective-permute-start | bytes 442376 | tf_op jit(solution)/shard_map/ppermute | solution.py:119
  106.3 1.7 copy-start.7
  106.3 1.8 copy-start.6
  107.2 9.8 %collective-permute-start.18 = (bf16[128,1536]{1,0:T(8,128)(2,1)}, bf16[128,1536]{1,0:T(8,128)(2,1)}, u32[]{:S(2)}, u32[]{:S(2)}) collective-permute-start(bf16[128,1536]{1,0:T(8,128)(2,1)} %get-tuple-element.69), channel_id=1, source_target_pairs={{0,3},{1,0},{2,1},{3,2},{4,7},{5,4},{6,5},{7,6},{8,11},{9,8},{10,9... | collective-permute-start | bytes 1179656 | tf_op jit(solution)/shard_map/ppermute | solution.py:69
  107.2 18.6 %collective-permute-start.17 = (bf16[128,1536]{1,0:T(8,128)(2,1)S(1)}, bf16[128,1536]{1,0:T(8,128)(2,1)}, u32[]{:S(2)}, u32[]{:S(2)}) collective-permute-start(bf16[128,1536]{1,0:T(8,128)(2,1)S(1)} %get-tuple-element.70), channel_id=1, source_target_pairs={{0,2},{1,3},{2,0},{3,1},{4,6},{5,7},{6,4},{7,5},{8,10},{9,11},{10,... | collective-permute-start | bytes 1179656 | tf_op jit(solution)/shard_map/ppermute | solution.py:69
  107.8 18.7 %collective-permute-start.16 = (bf16[128,1536]{1,0:T(8,128)(2,1)S(1)}, bf16[128,1536]{1,0:T(8,128)(2,1)}, u32[]{:S(2)}, u32[]{:S(2)}) collective-permute-start(bf16[128,1536]{1,0:T(8,128)(2,1)S(1)} %get-tuple-element.68), channel_id=1, source_target_pairs={{0,1},{1,2},{2,3},{3,0},{4,5},{5,6},{6,7},{7,4},{8,9},{9,10},{10,1... | collective-permute-start | bytes 1179656 | tf_op jit(solution)/shard_map/ppermute | solution.py:69
  109.5 20.8 %collective-permute-start.21 = (bf16[288,768]{1,0:T(8,128)(2,1)S(1)}, bf16[288,768]{1,0:T(8,128)(2,1)S(1)}, u32[]{:S(2)}, u32[]{:S(2)}) collective-permute-start(bf16[288,768]{1,0:T(8,128)(2,1)S(1)} %pad_maximum_fusion), channel_id=1, source_target_pairs={{0,8},{8,16},{16,24},{24,28},{28,20},{20,12},{12,4},{4,0},{1,9},{9... | collective-permute-start | bytes 1327112 | tf_op jit(solution)/shard_map/ppermute | solution.py:119
  111.1 20.8 %collective-permute-start.22 = (bf16[288,768]{1,0:T(8,128)(2,1)S(1)}, bf16[288,768]{1,0:T(8,128)(2,1)S(1)}, u32[]{:S(2)}, u32[]{:S(2)}) collective-permute-start(bf16[288,768]{1,0:T(8,128)(2,1)S(1)} %pad_maximum_fusion), channel_id=1, source_target_pairs={{0,4},{8,0},{16,8},{24,16},{28,24},{20,28},{12,20},{4,12},{1,5},{9... | collective-permute-start | bytes 1327112 | tf_op jit(solution)/shard_map/ppermute | solution.py:122
  111.8 16.6 %copy-start.10 = (f32[1536]{0:T(1024)S(1)}, f32[1536]{0:T(1024)}, u32[]{:S(2)}) copy-start(f32[1536]{0:T(1024)} %param.18) | copy-start | bytes 18436
  128.7 9.9 %collective-permute-start.19 = (bf16[128,1536]{1,0:T(8,128)(2,1)S(1)}, bf16[128,1536]{1,0:T(8,128)(2,1)S(1)}, u32[]{:S(2)}, u32[]{:S(2)}) collective-permute-start(bf16[128,1536]{1,0:T(8,128)(2,1)S(1)} %get-tuple-element.62), channel_id=1, source_target_pairs={{0,2},{1,3},{2,0},{3,1},{4,6},{5,7},{6,4},{7,5},{8,10},{9,11},{10,... | collective-permute-start | bytes 1179656 | tf_op jit(solution)/shard_map/ppermute | solution.py:36
  130.3 10.0 %collective-permute-start.23 = (bf16[288,768]{1,0:T(8,128)(2,1)S(1)}, bf16[288,768]{1,0:T(8,128)(2,1)S(1)}, u32[]{:S(2)}, u32[]{:S(2)}) collective-permute-start(bf16[288,768]{1,0:T(8,128)(2,1)S(1)} %collective-permute-done.21), channel_id=1, source_target_pairs={{0,8},{8,16},{16,24},{24,28},{28,20},{20,12},{12,4},{4,0},{1,9},{9... | collective-permute-start | bytes 1327112 | tf_op jit(solution)/shard_map/ppermute | solution.py:119
  131.9 10.0 %collective-permute-start.24 = (bf16[288,768]{1,0:T(8,128)(2,1)S(1)}, bf16[288,768]{1,0:T(8,128)(2,1)S(1)}, u32[]{:S(2)}, u32[]{:S(2)}) collective-permute-start(bf16[288,768]{1,0:T(8,128)(2,1)S(1)} %collective-permute-done.22), channel_id=1, source_target_pairs={{0,4},{8,0},{16,8},{24,16},{28,24},{20,28},{12,20},{4,12},{1,5},{9... | collective-permute-start | bytes 1327112 | tf_op jit(solution)/shard_map/ppermute | solution.py:122
  138.6 14.2 %collective-permute-start.20 = (bf16[2,128,1536]{2,1,0:T(8,128)(2,1)S(1)}, bf16[2,128,1536]{2,1,0:T(8,128)(2,1)S(1)}, u32[]{:S(2)}, u32[]{:S(2)}) collective-permute-start(bf16[2,128,1536]{2,1,0:T(8,128)(2,1)S(1)} %get-tuple-element.73), channel_id=1, source_target_pairs={{0,1},{1,0},{2,3},{3,2},{4,5},{5,4},{6,7},{7,6},{8,9},{9,8},{10,11... | collective-permute-start | bytes 2359304 | tf_op jit(solution)/shard_map/ppermute | solution.py:42
  140.3 11.0 %collective-permute-start.25 = (bf16[288,768]{1,0:T(8,128)(2,1)S(1)}, bf16[288,768]{1,0:T(8,128)(2,1)S(1)}, u32[]{:S(2)}, u32[]{:S(2)}) collective-permute-start(bf16[288,768]{1,0:T(8,128)(2,1)S(1)} %collective-permute-done.23), channel_id=1, source_target_pairs={{0,8},{8,16},{16,24},{24,28},{28,20},{20,12},{12,4},{4,0},{1,9},{9... | collective-permute-start | bytes 1327112 | tf_op jit(solution)/shard_map/ppermute | solution.py:119
  141.9 10.9 %collective-permute-start.26 = (bf16[288,768]{1,0:T(8,128)(2,1)S(1)}, bf16[288,768]{1,0:T(8,128)(2,1)S(1)}, u32[]{:S(2)}, u32[]{:S(2)}) collective-permute-start(bf16[288,768]{1,0:T(8,128)(2,1)S(1)} %collective-permute-done.24), channel_id=1, source_target_pairs={{0,4},{8,0},{16,8},{24,16},{28,24},{20,28},{12,20},{4,12},{1,5},{9... | collective-permute-start | bytes 1327112 | tf_op jit(solution)/shard_map/ppermute | solution.py:122
  151.3 10.0 %collective-permute-start.27 = (bf16[288,768]{1,0:T(8,128)(2,1)S(1)}, bf16[288,768]{1,0:T(8,128)(2,1)S(1)}, u32[]{:S(2)}, u32[]{:S(2)}) collective-permute-start(bf16[288,768]{1,0:T(8,128)(2,1)S(1)} %collective-permute-done.25), channel_id=1, source_target_pairs={{0,8},{8,16},{16,24},{24,28},{28,20},{20,12},{12,4},{4,0},{1,9},{9... | collective-permute-start | bytes 1327112 | tf_op jit(solution)/shard_map/ppermute | solution.py:119
  153.0 8.4 %copy-start.3 = (bf16[4,128,1536]{2,1,0:T(8,128)(2,1)}, bf16[4,128,1536]{2,1,0:T(8,128)(2,1)S(1)}, u32[]{:S(2)}) copy-start(bf16[4,128,1536]{2,1,0:T(8,128)(2,1)S(1)} %slice_dynamic-update-slice_fusion) | copy-start | bytes 4718596
  168.7 0.7 copy-start.22
  168.8 0.7 copy-start.32
  169.0 7.2 %copy-start.1 = (bf16[8,96,768]{2,1,0:T(8,128)(2,1)S(1)}, bf16[8,96,768]{2,1,0:T(8,128)(2,1)}, u32[]{:S(2)}) copy-start(bf16[8,96,768]{2,1,0:T(8,128)(2,1)} %slice.423) | copy-start | bytes 3538948
  179.7 9.6 %collective-permute-start.30 = (bf16[128,1536]{1,0:T(8,128)(2,1)S(1)}, bf16[128,1536]{1,0:T(8,128)(2,1)S(1)}, u32[]{:S(2)}, u32[]{:S(2)}) collective-permute-start(bf16[128,1536]{1,0:T(8,128)(2,1)S(1)} %get-tuple-element.66), channel_id=1, source_target_pairs={{0,3},{1,0},{2,1},{3,2},{4,7},{5,4},{6,5},{7,6},{8,11},{9,8},{10,9... | collective-permute-start | bytes 1179656 | tf_op jit(solution)/shard_map/ppermute | solution.py:69
  179.8 17.7 %collective-permute-start.29 = (bf16[128,1536]{1,0:T(8,128)(2,1)S(1)}, bf16[128,1536]{1,0:T(8,128)(2,1)S(1)}, u32[]{:S(2)}, u32[]{:S(2)}) collective-permute-start(bf16[128,1536]{1,0:T(8,128)(2,1)S(1)} %get-tuple-element.67), channel_id=1, source_target_pairs={{0,2},{1,3},{2,0},{3,1},{4,6},{5,7},{6,4},{7,5},{8,10},{9,11},{10,... | collective-permute-start | bytes 1179656 | tf_op jit(solution)/shard_map/ppermute | solution.py:69
  180.1 18.3 %collective-permute-start.28 = (bf16[128,1536]{1,0:T(8,128)(2,1)S(1)}, bf16[128,1536]{1,0:T(8,128)(2,1)S(1)}, u32[]{:S(2)}, u32[]{:S(2)}) collective-permute-start(bf16[128,1536]{1,0:T(8,128)(2,1)S(1)} %get-tuple-element.65), channel_id=1, source_target_pairs={{0,1},{1,2},{2,3},{3,0},{4,5},{5,6},{6,7},{7,4},{8,9},{9,10},{10,1... | collective-permute-start | bytes 1179656 | tf_op jit(solution)/shard_map/ppermute | solution.py:69
  (38 other events, 25.3 us)

commit v6 on v5

--- a/solution.py
+++ b/solution.py
@@ -181,12 +181,13 @@
     kernel_reach = dw_kernel.shape[0] // 2
     qkv_parts = ring_gather(w_qkv.reshape(w_qkv.shape[0], 3 * group_width), ring)
     qkv_matrix = qkv_parts.reshape(model_width, 3 * group_width)
+    kv_start = qkv_parts
     out_parts = ring_gather(after(qkv_parts, w_out), ring)
     out_local = jnp.einsum("nrc->rnc", out_parts).reshape(w_out.shape[0], model_width)
     glu_rows = w_glu.shape[0]
     glu_local = w_glu.reshape(glu_rows, 2 * group_width)
     both_parts = ring_gather(
-        after(out_parts, jnp.concatenate([glu_local, w_proj.reshape(-1, 2 * group_width)])), ring
+        after(kv_start, jnp.concatenate([glu_local, w_proj.reshape(-1, 2 * group_width)])), ring
     )
     glu_matrix = both_parts[:, :glu_rows].reshape(model_width, 2 * group_width)
     proj_parts = both_parts[:, glu_rows:].reshape(-1, *w_proj.shape)

time: 200 us -> 213 us (1.065)
  local copies, waits for them, and re-layouts: 24.3 us -> 38.5 us
  waiting for transfers between devices: 94 us -> 87.2 us
  other arithmetic: 17.5 us -> 20.3 us
    ppermute x12, waiting for transfers between devices: 54.8 us -> 44.3 us  [ring_gather(): ahead = lax.ppermute(ahead, 'dp', forward)]
    dynamic_update_slice x4, local copies, waits for them, and re-layouts: 0.13 us -> 3.62 us  [seq_gather(): out = lax.dynamic_update_index_in_dim(out, other[k], 2 * k + partner % 2, 0)]
    ppermute x2, waiting for transfers between devices: 6.12 us -> 8.52 us  [seq_gather(): lax.ppermute(block, 'seq', [(i, (i + 2 * shift) % count) for i in range(c...]
  transfers between devices with their start and end apart: 31 -> 31, of which waited for: 17 -> 15; matrix products, arithmetic and copies ran while one was open for 17% -> 27% of each run, Pallas kernels for 0% -> 0%
where the time goes in v6:
time: 213 us; the launch traced here: 212 us
  waiting for transfers between devices  87.2 us (41%)
  local copies, waits for them, and re-layouts  38.5 us (18%)
  starting transfers between devices  30.2 us (14%)
  other arithmetic  20.3 us (10%)
  between operations  18.4 us (9%)
  matrix products  17.4 us (8%)
    ppermute x12, waiting for transfers between devices, ring_gather(): ahead = lax.ppermute(ahead, 'dp', forward)  44.3 us
    ppermute x6, waiting for transfers between devices, seq_scatter_sum(): lax.ppermute(piece, 'seq', [(i, (i + shift) % count) for i in range(count)])  33.3 us
    ppermute x12, starting transfers between devices, ring_gather(): ahead = lax.ppermute(ahead, 'dp', forward)  20.6 us
    ppermute x2, waiting for transfers between devices, seq_gather(): lax.ppermute(block, 'seq', [(i, (i + 2 * shift) % count) for i in range(c...  8.52 us
    convert_element_type x1, other arithmetic, depthwise(): return jax.nn.silu(total_acc).astype(jnp.bfloat16)  6.85 us
    dynamic_update_slice x12, local copies, waits for them, and re-layouts, ring_gather(): lax.dynamic_update_index_in_dim(out, ahead, order[(my_pos - step) % count...  5.4 us
    sub x1, matrix products, one_block(): weights = jnp.exp(scores - top_score)  4.82 us
    dynamic_update_slice x9, local copies, waits for them, and re-layouts, ring_gather(): lax.dynamic_update_index_in_dim(out, behind, order[(my_pos + step) % coun...  4.57 us
  transfers between devices with their start and end apart: 31, of which 15 were waited for; matrix products, arithmetic and copies ran while one was open for 27% of the time, Pallas kernels for 0%

profile of v6, /device:TPU:0, one launch (start us, length us, event | category | flops | bytes accessed | tf_op | source)
XLA Modules:
  0.0 212.0 jit_solution(846945412374113221)
XLA Ops:
  0.0 1.1 copy.43
  1.2 3.1 %collective-permute-start.2 = (bf16[192,1152]{1,0:T(8,128)(2,1)S(1)}, bf16[192,1152]{1,0:T(8,128)(2,1)S(1)}, u32[]{:S(2)}, u32[]{:S(2)}) collective-permute-start(bf16[192,1152]{1,0:T(8,128)(2,1)S(1)} %bitcast.160), channel_id=1, source_target_pairs={{0,8},{8,16},{16,24},{24,28},{28,20},{20,12},{12,4},{4,0},{1,9},{9... | collective-permute-start | bytes 1327112 | tf_op jit(solution)/shard_map/ppermute | solution.py:119
  4.3 1.1 convert_reduce_fusion.1
  5.4 1.2 fusion.16
  7.5 2.0 collective-permute-start
  24.3 1.6 convert_reduce_fusion.33
  26.0 1.7 convert_reduce_fusion.34
  31.4 1.0 copy.39
  33.7 2.2 %broadcast_in_dim.399 = bf16[8,192,1152]{2,1,0:T(8,128)(2,1)} broadcast(bf16[]{:T(256)} %constant.324.clone.1), dimensions={} | broadcast | bytes 3538946 | tf_op jit(solution)/shard_map/broadcast_in_dim | solution.py:115
  42.5 1.6 collective-permute-start.4
  46.2 8.9 %collective-permute-done.4 = bf16[192,1152]{1,0:T(8,128)(2,1)S(1)} collective-permute-done((bf16[192,1152]{1,0:T(8,128)(2,1)S(1)}, bf16[192,1152]{1,0:T(8,128)(2,1)S(1)}, u32[]{:S(2)}, u32[]{:S(2)}) %collective-permute-start.4) | collective-permute-done | bytes 442400 | tf_op jit(solution)/shard_map/ppermute | solution.py:119
  55.1 1.6 collective-permute-start.6
  58.8 8.0 %collective-permute-done.6 = bf16[192,1152]{1,0:T(8,128)(2,1)S(1)} collective-permute-done((bf16[192,1152]{1,0:T(8,128)(2,1)S(1)}, bf16[192,1152]{1,0:T(8,128)(2,1)S(1)}, u32[]{:S(2)}, u32[]{:S(2)}) %collective-permute-start.6) | collective-permute-done | bytes 442400 | tf_op jit(solution)/shard_map/ppermute | solution.py:119
  66.8 1.6 collective-permute-start.8
  70.0 7.6 %collective-permute-done.8 = bf16[192,1152]{1,0:T(8,128)(2,1)S(1)} collective-permute-done((bf16[192,1152]{1,0:T(8,128)(2,1)S(1)}, bf16[192,1152]{1,0:T(8,128)(2,1)S(1)}, u32[]{:S(2)}, u32[]{:S(2)}) %collective-permute-start.8) | collective-permute-done | bytes 442400 | tf_op jit(solution)/shard_map/ppermute | solution.py:119
  78.4 1.6 collective-permute-start.9
  80.5 1.6 collective-permute-start.21
  82.5 4.2 %convolution_convert_fusion = bf16[512,1152]{1,0:T(8,128)(2,1)S(1)} fusion(bf16[512,1536]{1,0:T(8,128)(2,1)S(1)} %bitcast.155, bf16[1536,1152]{1,0:T(8,128)(2,1)} %bitcast.24), kind=kOutput, calls=%fused_computation.5 | convolution fusion | flops 1812529152 | bytes 6291456 | tf_op jit(solution)/shard_map/dot_general | solution.py:200
  86.7 1.4 copy.37
  88.4 1.0 bitcast_dynamic-update-slice_fusion.7
  89.4 4.8 %fusion.39 = (f32[4,512]{1,0:T(4,128)S(1)}, f32[4,512,512]{1,2,0:T(8,128)}) fusion(pred[512,512]{0,1:T(8,128)(4,1)} %broadcast_compare_fusion, bf16[512,3,4,96]{0,3,2,1:T(8,128)(2,1)} %bitcast.158), kind=kOutput, calls=%fused_computation.172 | convolution fusion | flops 205521408 | bytes 5251072 | tf_op jit(solution)/shard_map/while/body/eval_jaxpr/sub | solution.py:151
  94.2 2.8 %fusion.6 = bf16[4,96,512]{2,1,0:T(8,128)(2,1)S(1)} fusion(f32[4,512,512]{1,2,0:T(8,128)} %get-tuple-element.116, f32[4,512]{1,0:T(4,128)S(1)} %get-tuple-element.115, bf16[512,3,4,96]{0,3,2,1:T(8,128)(2,1)} %bitcast.159), kind=kOutput, calls=%fused_computation.12 | convolution fusion | flops 203620352 | bytes 4988928 | tf_op jit(solution)/shard_map/while/body/eval_jaxpr/hqk,khe->qhe/dot_general | solution.py:153
  98.1 1.6 collective-permute-start.11
  102.2 2.9 %collective-permute-done.11 = bf16[384,192]{0,1:T(8,128)(2,1)S(1)} collective-permute-done((bf16[384,192]{0,1:T(8,128)(2,1)}, bf16[384,192]{0,1:T(8,128)(2,1)S(1)}, u32[]{:S(2)}, u32[]{:S(2)}) %collective-permute-start.11) | collective-permute-done | bytes 147488 | tf_op jit(solution)/shard_map/ppermute | solution.py:119
  105.1 1.6 collective-permute-start.13
  108.1 1.6 collective-permute-start.23
  110.2 1.0 bitcast_dynamic-update-slice_fusion.6
  111.9 1.6 collective-permute-start.15
  113.5 5.5 %collective-permute-done.15 = bf16[384,192]{0,1:T(8,128)(2,1)S(1)} collective-permute-done((bf16[384,192]{0,1:T(8,128)(2,1)S(1)}, bf16[384,192]{0,1:T(8,128)(2,1)S(1)}, u32[]{:S(2)}, u32[]{:S(2)}) %collective-permute-start.15) | collective-permute-done | bytes 147488 | tf_op jit(solution)/shard_map/ppermute | solution.py:119
  122.3 1.4 collective-permute-start.25
  124.5 5.0 %collective-permute-done.18 = bf16[128,1536]{1,0:T(8,128)(2,1)S(1)} collective-permute-done((bf16[128,1536]{1,0:T(8,128)(2,1)S(1)}, bf16[128,1536]{1,0:T(8,128)(2,1)S(1)}, u32[]{:S(2)}, u32[]{:S(2)}) %collective-permute-start.18) | collective-permute-done | bytes 393248 | tf_op jit(solution)/shard_map/ppermute | solution.py:69
  129.5 9.2 %collective-permute-done.17 = bf16[128,1536]{1,0:T(8,128)(2,1)S(1)} collective-permute-done((bf16[128,1536]{1,0:T(8,128)(2,1)S(1)}, bf16[128,1536]{1,0:T(8,128)(2,1)S(1)}, u32[]{:S(2)}, u32[]{:S(2)}) %collective-permute-start.17) | collective-permute-done | bytes 393248 | tf_op jit(solution)/shard_map/ppermute | solution.py:69
  141.1 1.1 bitcast_dynamic-update-slice_fusion.17
  142.2 1.2 collective-permute-start.19
  143.6 8.5 %collective-permute-done.19 = bf16[128,1536]{1,0:T(8,128)(2,1)S(1)} collective-permute-done((bf16[128,1536]{1,0:T(8,128)(2,1)S(1)}, bf16[128,1536]{1,0:T(8,128)(2,1)S(1)}, u32[]{:S(2)}, u32[]{:S(2)}) %collective-permute-start.19) | collective-permute-done | bytes 393248 | tf_op jit(solution)/shard_map/ppermute | solution.py:36
  153.0 1.7 collective-permute-start.27
  154.8 10.8 %collective-permute-done.27 = bf16[288,768]{1,0:T(8,128)(2,1)S(1)} collective-permute-done((bf16[288,768]{1,0:T(8,128)(2,1)S(1)}, bf16[288,768]{1,0:T(8,128)(2,1)S(1)}, u32[]{:S(2)}, u32[]{:S(2)}) %collective-permute-start.27) | collective-permute-done | bytes 442400 | tf_op jit(solution)/shard_map/ppermute | solution.py:119
  165.6 1.5 slice.420
  167.2 1.1 slice.423
  168.3 4.4 %copy.40 = bf16[768,1536]{1,0:T(8,128)(2,1)} copy(bf16[768,1536]{0,1:T(8,128)(2,1)} %bitcast.149) | data formatting | bytes 4718592 | tf_op jit(solution)/shard_map/dot_general | solution.py:211
  172.7 1.5 reshape.239
  175.0 1.8 slice_dynamic-update-slice_fusion.1
  176.8 1.8 slice_dynamic-update-slice_fusion
  178.6 3.6 %fusion.40 = f32[512,2,384]{2,0,1:T(8,128)S(1)} fusion(bf16[512,1536,1]{1,0,2:T(8,128)(2,1)} %bitcast.156, bf16[2,384,1536]{2,1,0:T(8,128)(2,1)} %bitcast.153), kind=kOutput, calls=%fused_computation.173 | convolution fusion | flops 1207959552 | bytes 5505024 | tf_op jit(solution)/shard_map/dot_general | solution.py:211
  183.2 6.9 %multiply_convert_fusion = bf16[512,384]{1,0:T(8,128)(2,1)S(1)} fusion(bf16[512,384]{1,0:T(8,128)(2,1)S(1)} %fusion.32, f32[384]{0:T(512)S(1)} %copy-done.37, f32[384]{0:T(512)S(1)} %copy-done.38, f32[384]{0:T(512)S(1)} %get-tuple-element.30, f32[384]{0:T(512)S(1)} %copy-done.10, f32[384]{0:T(512)S(1)} %copy-done.11, f32[384]{0:T(512)S(1)} %copy-done.12, ...), kind=kLoop, calls=%fused_computation.41 | loop fusion | flops 25165824 | bytes 849920 | tf_op jit(solution)/shard_map/convert_element_type | solution.py:172
  191.4 1.3 collective-permute-start.29
  192.6 8.0 %collective-permute-done.30 = bf16[128,1536]{1,0:T(8,128)(2,1)S(1)} collective-permute-done((bf16[128,1536]{1,0:T(8,128)(2,1)S(1)}, bf16[128,1536]{1,0:T(8,128)(2,1)S(1)}, u32[]{:S(2)}, u32[]{:S(2)}) %collective-permute-start.30) | collective-permute-done | bytes 393248 | tf_op jit(solution)/shard_map/ppermute | solution.py:69
  200.7 10.1 %collective-permute-done.29 = bf16[128,1536]{1,0:T(8,128)(2,1)S(1)} collective-permute-done((bf16[128,1536]{1,0:T(8,128)(2,1)S(1)}, bf16[128,1536]{1,0:T(8,128)(2,1)S(1)}, u32[]{:S(2)}, u32[]{:S(2)}) %collective-permute-start.29) | collective-permute-done | bytes 393248 | tf_op jit(solution)/shard_map/ppermute | solution.py:69
  (208 shorter events, 34.9 us)
Async XLA Ops:
  0.0 9.5 %copy-start.5 = (bf16[192,3,384]{2,0,1:T(8,128)(2,1)S(1)}, bf16[192,3,384]{2,0,1:T(8,128)(2,1)}, u32[]{:S(2)}) copy-start(bf16[192,3,384]{2,0,1:T(8,128)(2,1)} %param.19) | copy-start | bytes 1327108
  0.0 7.2 %copy-start = (bf16[1,128,1536]{2,1,0:T(8,128)(2,1)S(1)}, bf16[1,128,1536]{2,1,0:T(8,128)(2,1)}, u32[]{:S(2)}) copy-start(bf16[1,128,1536]{2,1,0:T(8,128)(2,1)} %param.15) | copy-start | bytes 1179652
  0.0 7.2 %copy-start.7 = (f32[1536]{0:T(1024)S(1)}, f32[1536]{0:T(1024)}, u32[]{:S(2)}) copy-start(f32[1536]{0:T(1024)} %param.17) | copy-start | bytes 18436
  1.1 8.7 %copy-start.54 = (s32[8]{0:T(128)S(1)}, s32[8]{0:T(128)}, u32[]{:S(2)}) copy-start(s32[8]{0:T(128)} %constant.355.clone) | copy-start | bytes 100
  1.2 14.0 %copy-start.8 = (s32[8]{0:T(128)S(1)}, s32[8]{0:T(128)}, u32[]{:S(2)}) copy-start(s32[8]{0:T(128)} %constant.356.clone) | copy-start | bytes 100
  1.2 41.3 %collective-permute-start.2 = (bf16[192,1152]{1,0:T(8,128)(2,1)S(1)}, bf16[192,1152]{1,0:T(8,128)(2,1)S(1)}, u32[]{:S(2)}, u32[]{:S(2)}) collective-permute-start(bf16[192,1152]{1,0:T(8,128)(2,1)S(1)} %bitcast.160), channel_id=1, source_target_pairs={{0,8},{8,16},{16,24},{24,28},{28,20},{20,12},{12,4},{4,0},{1,9},{9... | collective-permute-start | bytes 1327112 | tf_op jit(solution)/shard_map/ppermute | solution.py:119
  4.2 39.9 %collective-permute-start.3 = (bf16[192,1152]{1,0:T(8,128)(2,1)S(1)}, bf16[192,1152]{1,0:T(8,128)(2,1)S(1)}, u32[]{:S(2)}, u32[]{:S(2)}) collective-permute-start(bf16[192,1152]{1,0:T(8,128)(2,1)S(1)} %bitcast.161), channel_id=1, source_target_pairs={{0,4},{8,0},{16,8},{24,16},{28,24},{20,28},{12,20},{4,12},{1,5},{9... | collective-permute-start | bytes 1327112 | tf_op jit(solution)/shard_map/ppermute | solution.py:122
  5.4 1.3 copy-start.39
  7.5 34.9 %collective-permute-start = (bf16[128,1536]{1,0:T(8,128)(2,1)S(1)}, bf16[128,1536]{1,0:T(8,128)(2,1)S(1)}, u32[]{:S(2)}, u32[]{:S(2)}) collective-permute-start(bf16[128,1536]{1,0:T(8,128)(2,1)S(1)} %fusion.18), channel_id=1, source_target_pairs={{0,2},{1,3},{2,0},{3,1},{4,6},{5,7},{6,4},{7,5},{8,10},{9,11},{10,... | collective-permute-start | bytes 1179656 | tf_op jit(solution)/shard_map/ppermute | solution.py:36
  41.0 1.0 copy-start.40
  41.0 1.0 copy-start.42
  42.4 16.3 %collective-permute-start.1 = (bf16[2,128,1536]{2,1,0:T(8,128)(2,1)S(1)}, bf16[2,128,1536]{2,1,0:T(8,128)(2,1)S(1)}, u32[]{:S(2)}, u32[]{:S(2)}) collective-permute-start(bf16[2,128,1536]{2,1,0:T(8,128)(2,1)S(1)} %get-tuple-element.75), channel_id=1, source_target_pairs={{0,1},{1,0},{2,3},{3,2},{4,5},{5,4},{6,7},{7,6},{8,9},{9,8},{10,11... | collective-permute-start | bytes 2359304 | tf_op jit(solution)/shard_map/ppermute | solution.py:42
  42.5 12.6 %collective-permute-start.4 = (bf16[192,1152]{1,0:T(8,128)(2,1)S(1)}, bf16[192,1152]{1,0:T(8,128)(2,1)S(1)}, u32[]{:S(2)}, u32[]{:S(2)}) collective-permute-start(bf16[192,1152]{1,0:T(8,128)(2,1)S(1)} %collective-permute-done.2), channel_id=1, source_target_pairs={{0,8},{8,16},{16,24},{24,28},{28,20},{20,12},{12,4},{4,0},{1,9},{9... | collective-permute-start | bytes 1327112 | tf_op jit(solution)/shard_map/ppermute | solution.py:119
  44.2 12.5 %collective-permute-start.5 = (bf16[192,1152]{1,0:T(8,128)(2,1)S(1)}, bf16[192,1152]{1,0:T(8,128)(2,1)S(1)}, u32[]{:S(2)}, u32[]{:S(2)}) collective-permute-start(bf16[192,1152]{1,0:T(8,128)(2,1)S(1)} %collective-permute-done.3), channel_id=1, source_target_pairs={{0,4},{8,0},{16,8},{24,16},{28,24},{20,28},{12,20},{4,12},{1,5},{9... | collective-permute-start | bytes 1327112 | tf_op jit(solution)/shard_map/ppermute | solution.py:122
  55.1 11.7 %collective-permute-start.6 = (bf16[192,1152]{1,0:T(8,128)(2,1)S(1)}, bf16[192,1152]{1,0:T(8,128)(2,1)S(1)}, u32[]{:S(2)}, u32[]{:S(2)}) collective-permute-start(bf16[192,1152]{1,0:T(8,128)(2,1)S(1)} %collective-permute-done.4), channel_id=1, source_target_pairs={{0,8},{8,16},{16,24},{24,28},{28,20},{20,12},{12,4},{4,0},{1,9},{9... | collective-permute-start | bytes 1327112 | tf_op jit(solution)/shard_map/ppermute | solution.py:119
  56.7 12.5 %collective-permute-start.7 = (bf16[192,1152]{1,0:T(8,128)(2,1)S(1)}, bf16[192,1152]{1,0:T(8,128)(2,1)S(1)}, u32[]{:S(2)}, u32[]{:S(2)}) collective-permute-start(bf16[192,1152]{1,0:T(8,128)(2,1)S(1)} %collective-permute-done.5), channel_id=1, source_target_pairs={{0,4},{8,0},{16,8},{24,16},{28,24},{20,28},{12,20},{4,12},{1,5},{9... | collective-permute-start | bytes 1327112 | tf_op jit(solution)/shard_map/ppermute | solution.py:122
  66.8 10.8 %collective-permute-start.8 = (bf16[192,1152]{1,0:T(8,128)(2,1)S(1)}, bf16[192,1152]{1,0:T(8,128)(2,1)S(1)}, u32[]{:S(2)}, u32[]{:S(2)}) collective-permute-start(bf16[192,1152]{1,0:T(8,128)(2,1)S(1)} %collective-permute-done.6), channel_id=1, source_target_pairs={{0,8},{8,16},{16,24},{24,28},{28,20},{20,12},{12,4},{4,0},{1,9},{9... | collective-permute-start | bytes 1327112 | tf_op jit(solution)/shard_map/ppermute | solution.py:119
  78.4 19.7 %collective-permute-start.9 = (bf16[384,192]{0,1:T(8,128)(2,1)}, bf16[384,192]{0,1:T(8,128)(2,1)}, u32[]{:S(2)}, u32[]{:S(2)}) collective-permute-start(bf16[384,192]{0,1:T(8,128)(2,1)} %param.20), channel_id=1, source_target_pairs={{0,8},{8,16},{16,24},{24,28},{28,20},{20,12},{12,4},{4,0},{1,9},{9... | collective-permute-start | bytes 442376 | tf_op jit(solution)/shard_map/ppermute | solution.py:119
  80.0 20.7 %collective-permute-start.10 = (bf16[384,192]{0,1:T(8,128)(2,1)}, bf16[384,192]{0,1:T(8,128)(2,1)}, u32[]{:S(2)}, u32[]{:S(2)}) collective-permute-start(bf16[384,192]{0,1:T(8,128)(2,1)} %param.20), channel_id=1, source_target_pairs={{0,4},{8,0},{16,8},{24,16},{28,24},{20,28},{12,20},{4,12},{1,5},{9... | collective-permute-start | bytes 442376 | tf_op jit(solution)/shard_map/ppermute | solution.py:122
  80.5 27.7 %collective-permute-start.21 = (bf16[288,768]{1,0:T(8,128)(2,1)}, bf16[288,768]{1,0:T(8,128)(2,1)}, u32[]{:S(2)}, u32[]{:S(2)}) collective-permute-start(bf16[288,768]{1,0:T(8,128)(2,1)} %pad_maximum_fusion), channel_id=1, source_target_pairs={{0,8},{8,16},{16,24},{24,28},{28,20},{20,12},{12,4},{4,0},{1,9},{9... | collective-permute-start | bytes 1327112 | tf_op jit(solution)/shard_map/ppermute | solution.py:119
  82.0 27.7 %collective-permute-start.22 = (bf16[288,768]{1,0:T(8,128)(2,1)}, bf16[288,768]{1,0:T(8,128)(2,1)}, u32[]{:S(2)}, u32[]{:S(2)}) collective-permute-start(bf16[288,768]{1,0:T(8,128)(2,1)} %pad_maximum_fusion), channel_id=1, source_target_pairs={{0,4},{8,0},{16,8},{24,16},{28,24},{20,28},{12,20},{4,12},{1,5},{9... | collective-permute-start | bytes 1327112 | tf_op jit(solution)/shard_map/ppermute | solution.py:122
  98.1 7.0 %collective-permute-start.11 = (bf16[384,192]{0,1:T(8,128)(2,1)}, bf16[384,192]{0,1:T(8,128)(2,1)S(1)}, u32[]{:S(2)}, u32[]{:S(2)}) collective-permute-start(bf16[384,192]{0,1:T(8,128)(2,1)} %collective-permute-done.9), channel_id=1, source_target_pairs={{0,8},{8,16},{16,24},{24,28},{28,20},{20,12},{12,4},{4,0},{1,9},{9... | collective-permute-start | bytes 442376 | tf_op jit(solution)/shard_map/ppermute | solution.py:119
  100.7 6.9 %collective-permute-start.12 = (bf16[384,192]{0,1:T(8,128)(2,1)}, bf16[384,192]{0,1:T(8,128)(2,1)S(1)}, u32[]{:S(2)}, u32[]{:S(2)}) collective-permute-start(bf16[384,192]{0,1:T(8,128)(2,1)} %collective-permute-done.10), channel_id=1, source_target_pairs={{0,4},{8,0},{16,8},{24,16},{28,24},{20,28},{12,20},{4,12},{1,5},{9... | collective-permute-start | bytes 442376 | tf_op jit(solution)/shard_map/ppermute | solution.py:122
  105.1 6.8 %collective-permute-start.13 = (bf16[384,192]{0,1:T(8,128)(2,1)S(1)}, bf16[384,192]{0,1:T(8,128)(2,1)S(1)}, u32[]{:S(2)}, u32[]{:S(2)}) collective-permute-start(bf16[384,192]{0,1:T(8,128)(2,1)S(1)} %collective-permute-done.11), channel_id=1, source_target_pairs={{0,8},{8,16},{16,24},{24,28},{28,20},{20,12},{12,4},{4,0},{1,9},{9... | collective-permute-start | bytes 442376 | tf_op jit(solution)/shard_map/ppermute | solution.py:119
  107.6 5.8 %collective-permute-start.14 = (bf16[384,192]{0,1:T(8,128)(2,1)S(1)}, bf16[384,192]{0,1:T(8,128)(2,1)S(1)}, u32[]{:S(2)}, u32[]{:S(2)}) collective-permute-start(bf16[384,192]{0,1:T(8,128)(2,1)S(1)} %collective-permute-done.12), channel_id=1, source_target_pairs={{0,4},{8,0},{16,8},{24,16},{28,24},{20,28},{12,20},{4,12},{1,5},{9... | collective-permute-start | bytes 442376 | tf_op jit(solution)/shard_map/ppermute | solution.py:122
  108.1 14.2 %collective-permute-start.23 = (bf16[288,768]{1,0:T(8,128)(2,1)}, bf16[288,768]{1,0:T(8,128)(2,1)S(1)}, u32[]{:S(2)}, u32[]{:S(2)}) collective-permute-start(bf16[288,768]{1,0:T(8,128)(2,1)} %collective-permute-done.21), channel_id=1, source_target_pairs={{0,8},{8,16},{16,24},{24,28},{28,20},{20,12},{12,4},{4,0},{1,9},{9... | collective-permute-start | bytes 1327112 | tf_op jit(solution)/shard_map/ppermute | solution.py:119
  109.8 13.9 %collective-permute-start.24 = (bf16[288,768]{1,0:T(8,128)(2,1)}, bf16[288,768]{1,0:T(8,128)(2,1)S(1)}, u32[]{:S(2)}, u32[]{:S(2)}) collective-permute-start(bf16[288,768]{1,0:T(8,128)(2,1)} %collective-permute-done.22), channel_id=1, source_target_pairs={{0,4},{8,0},{16,8},{24,16},{28,24},{20,28},{12,20},{4,12},{1,5},{9... | collective-permute-start | bytes 1327112 | tf_op jit(solution)/shard_map/ppermute | solution.py:122
  111.9 7.2 %collective-permute-start.15 = (bf16[384,192]{0,1:T(8,128)(2,1)S(1)}, bf16[384,192]{0,1:T(8,128)(2,1)S(1)}, u32[]{:S(2)}, u32[]{:S(2)}) collective-permute-start(bf16[384,192]{0,1:T(8,128)(2,1)S(1)} %collective-permute-done.13), channel_id=1, source_target_pairs={{0,8},{8,16},{16,24},{24,28},{28,20},{20,12},{12,4},{4,0},{1,9},{9... | collective-permute-start | bytes 442376 | tf_op jit(solution)/shard_map/ppermute | solution.py:119
  120.1 19.3 %copy-start.1 = (bf16[1,128,1536]{2,1,0:T(8,128)(2,1)S(1)}, bf16[1,128,1536]{2,1,0:T(8,128)(2,1)}, u32[]{:S(2)}) copy-start(bf16[1,128,1536]{2,1,0:T(8,128)(2,1)} %param.15) | copy-start | bytes 1179652
  120.2 9.2 %collective-permute-start.18 = (bf16[128,1536]{1,0:T(8,128)(2,1)S(1)}, bf16[128,1536]{1,0:T(8,128)(2,1)S(1)}, u32[]{:S(2)}, u32[]{:S(2)}) collective-permute-start(bf16[128,1536]{1,0:T(8,128)(2,1)S(1)} %get-tuple-element.69), channel_id=1, source_target_pairs={{0,3},{1,0},{2,1},{3,2},{4,7},{5,4},{6,5},{7,6},{8,11},{9,8},{10,9... | collective-permute-start | bytes 1179656 | tf_op jit(solution)/shard_map/ppermute | solution.py:69
  120.3 18.4 %collective-permute-start.17 = (bf16[128,1536]{1,0:T(8,128)(2,1)S(1)}, bf16[128,1536]{1,0:T(8,128)(2,1)S(1)}, u32[]{:S(2)}, u32[]{:S(2)}) collective-permute-start(bf16[128,1536]{1,0:T(8,128)(2,1)S(1)} %get-tuple-element.70), channel_id=1, source_target_pairs={{0,2},{1,3},{2,0},{3,1},{4,6},{5,7},{6,4},{7,5},{8,10},{9,11},{10,... | collective-permute-start | bytes 1179656 | tf_op jit(solution)/shard_map/ppermute | solution.py:69
  121.1 18.3 %collective-permute-start.16 = (bf16[128,1536]{1,0:T(8,128)(2,1)S(1)}, bf16[128,1536]{1,0:T(8,128)(2,1)S(1)}, u32[]{:S(2)}, u32[]{:S(2)}) collective-permute-start(bf16[128,1536]{1,0:T(8,128)(2,1)S(1)} %get-tuple-element.68), channel_id=1, source_target_pairs={{0,1},{1,2},{2,3},{3,0},{4,5},{5,6},{6,7},{7,4},{8,9},{9,10},{10,1... | collective-permute-start | bytes 1179656 | tf_op jit(solution)/shard_map/ppermute | solution.py:69
  122.3 30.6 %collective-permute-start.25 = (bf16[288,768]{1,0:T(8,128)(2,1)S(1)}, bf16[288,768]{1,0:T(8,128)(2,1)S(1)}, u32[]{:S(2)}, u32[]{:S(2)}) collective-permute-start(bf16[288,768]{1,0:T(8,128)(2,1)S(1)} %collective-permute-done.23), channel_id=1, source_target_pairs={{0,8},{8,16},{16,24},{24,28},{28,20},{20,12},{12,4},{4,0},{1,9},{9... | collective-permute-start | bytes 1327112 | tf_op jit(solution)/shard_map/ppermute | solution.py:119
  123.7 31.0 %collective-permute-start.26 = (bf16[288,768]{1,0:T(8,128)(2,1)S(1)}, bf16[288,768]{1,0:T(8,128)(2,1)S(1)}, u32[]{:S(2)}, u32[]{:S(2)}) collective-permute-start(bf16[288,768]{1,0:T(8,128)(2,1)S(1)} %collective-permute-done.24), channel_id=1, source_target_pairs={{0,4},{8,0},{16,8},{24,16},{28,24},{20,28},{12,20},{4,12},{1,5},{9... | collective-permute-start | bytes 1327112 | tf_op jit(solution)/shard_map/ppermute | solution.py:122
  124.4 16.6 %copy-start.9 = (f32[1536]{0:T(1024)S(1)}, f32[1536]{0:T(1024)}, u32[]{:S(2)}) copy-start(f32[1536]{0:T(1024)} %param.18) | copy-start | bytes 18436
  139.8 3.7 %copy-start.2 = (bf16[128,1536]{1,0:T(8,128)(2,1)}, bf16[128,1536]{1,0:T(8,128)(2,1)S(1)}, u32[]{:S(2)}) copy-start(bf16[128,1536]{1,0:T(8,128)(2,1)S(1)} %get-tuple-element.64) | copy-start | bytes 1179652
  142.2 9.9 %collective-permute-start.19 = (bf16[128,1536]{1,0:T(8,128)(2,1)S(1)}, bf16[128,1536]{1,0:T(8,128)(2,1)S(1)}, u32[]{:S(2)}, u32[]{:S(2)}) collective-permute-start(bf16[128,1536]{1,0:T(8,128)(2,1)S(1)} %get-tuple-element.62), channel_id=1, source_target_pairs={{0,2},{1,3},{2,0},{3,1},{4,6},{5,7},{6,4},{7,5},{8,10},{9,11},{10,... | collective-permute-start | bytes 1179656 | tf_op jit(solution)/shard_map/ppermute | solution.py:36
  152.9 1.9 copy-start.6
  152.9 22.1 %collective-permute-start.20 = (bf16[2,128,1536]{2,1,0:T(8,128)(2,1)}, bf16[2,128,1536]{2,1,0:T(8,128)(2,1)}, u32[]{:S(2)}, u32[]{:S(2)}) collective-permute-start(bf16[2,128,1536]{2,1,0:T(8,128)(2,1)} %get-tuple-element.73), channel_id=1, source_target_pairs={{0,1},{1,0},{2,3},{3,2},{4,5},{5,4},{6,7},{7,6},{8,9},{9,8},{10,11... | collective-permute-start | bytes 2359304 | tf_op jit(solution)/shard_map/ppermute | solution.py:42
  153.0 12.6 %collective-permute-start.27 = (bf16[288,768]{1,0:T(8,128)(2,1)S(1)}, bf16[288,768]{1,0:T(8,128)(2,1)S(1)}, u32[]{:S(2)}, u32[]{:S(2)}) collective-permute-start(bf16[288,768]{1,0:T(8,128)(2,1)S(1)} %collective-permute-done.25), channel_id=1, source_target_pairs={{0,8},{8,16},{16,24},{24,28},{28,20},{20,12},{12,4},{4,0},{1,9},{9... | collective-permute-start | bytes 1327112 | tf_op jit(solution)/shard_map/ppermute | solution.py:119
  168.3 4.4 %copy-start.4 = (bf16[8,96,768]{2,1,0:T(8,128)(2,1)S(1)}, bf16[8,96,768]{2,1,0:T(8,128)(2,1)}, u32[]{:S(2)}) copy-start(bf16[8,96,768]{2,1,0:T(8,128)(2,1)} %slice.423) | copy-start | bytes 3538948
  182.2 0.7 copy-start.18
  182.3 0.7 copy-start.28
  182.3 0.7 copy-start.29
  191.1 19.9 %copy-start.3 = (bf16[128,1536]{1,0:T(8,128)(2,1)S(1)}, bf16[128,1536]{1,0:T(8,128)(2,1)}, u32[]{:S(2)}) copy-start(bf16[128,1536]{1,0:T(8,128)(2,1)} %copy-done.2) | copy-start | bytes 1179652
  191.2 9.5 %collective-permute-start.30 = (bf16[128,1536]{1,0:T(8,128)(2,1)S(1)}, bf16[128,1536]{1,0:T(8,128)(2,1)S(1)}, u32[]{:S(2)}, u32[]{:S(2)}) collective-permute-start(bf16[128,1536]{1,0:T(8,128)(2,1)S(1)} %get-tuple-element.66), channel_id=1, source_target_pairs={{0,3},{1,0},{2,1},{3,2},{4,7},{5,4},{6,5},{7,6},{8,11},{9,8},{10,9... | collective-permute-start | bytes 1179656 | tf_op jit(solution)/shard_map/ppermute | solution.py:69
  191.4 19.4 %collective-permute-start.29 = (bf16[128,1536]{1,0:T(8,128)(2,1)S(1)}, bf16[128,1536]{1,0:T(8,128)(2,1)S(1)}, u32[]{:S(2)}, u32[]{:S(2)}) collective-permute-start(bf16[128,1536]{1,0:T(8,128)(2,1)S(1)} %get-tuple-element.67), channel_id=1, source_target_pairs={{0,2},{1,3},{2,0},{3,1},{4,6},{5,7},{6,4},{7,5},{8,10},{9,11},{10,... | collective-permute-start | bytes 1179656 | tf_op jit(solution)/shard_map/ppermute | solution.py:69
  192.6 18.4 %collective-permute-start.28 = (bf16[128,1536]{1,0:T(8,128)(2,1)S(1)}, bf16[128,1536]{1,0:T(8,128)(2,1)S(1)}, u32[]{:S(2)}, u32[]{:S(2)}) collective-permute-start(bf16[128,1536]{1,0:T(8,128)(2,1)S(1)} %get-tuple-element.65), channel_id=1, source_target_pairs={{0,1},{1,2},{2,3},{3,0},{4,5},{5,6},{6,7},{7,4},{8,9},{9,10},{10,1... | collective-permute-start | bytes 1179656 | tf_op jit(solution)/shard_map/ppermute | solution.py:69
  (38 other events, 25.4 us)

commit v7 on v5

--- a/solution.py
+++ b/solution.py
@@ -181,12 +181,11 @@
     kernel_reach = dw_kernel.shape[0] // 2
     qkv_parts = ring_gather(w_qkv.reshape(w_qkv.shape[0], 3 * group_width), ring)
     qkv_matrix = qkv_parts.reshape(model_width, 3 * group_width)
-    out_parts = ring_gather(after(qkv_parts, w_out), ring)
-    out_local = jnp.einsum("nrc->rnc", out_parts).reshape(w_out.shape[0], model_width)
+    out_local = lax.all_gather(w_out, "dp", axis=1, tiled=True)
     glu_rows = w_glu.shape[0]
     glu_local = w_glu.reshape(glu_rows, 2 * group_width)
     both_parts = ring_gather(
-        after(out_parts, jnp.concatenate([glu_local, w_proj.reshape(-1, 2 * group_width)])), ring
+        after(qkv_parts, jnp.concatenate([glu_local, w_proj.reshape(-1, 2 * group_width)])), ring
     )
     glu_matrix = both_parts[:, :glu_rows].reshape(model_width, 2 * group_width)
     proj_parts = both_parts[:, glu_rows:].reshape(-1, *w_proj.shape)

time: 200 us -> 207 us (1.035)
  between operations: 18.4 us -> 31.7 us
  waiting for transfers between devices: 94 us -> 80.7 us
  local copies, waits for them, and re-layouts: 24.3 us -> 33.8 us
  starting transfers between devices: 29.2 us -> 21.7 us
  matrix products: 16.1 us -> 20.1 us
    ppermute x12 -> x8, waiting for transfers between devices: 54.8 us -> 42.1 us  [ring_gather(): ahead = lax.ppermute(ahead, 'dp', forward)]
    ppermute x12 -> x8, starting transfers between devices: 20.5 us -> 10.7 us  [ring_gather(): ahead = lax.ppermute(ahead, 'dp', forward)]
    dynamic_update_slice x4, local copies, waits for them, and re-layouts: 0.13 us -> 3.62 us  [seq_gather(): out = lax.dynamic_update_index_in_dim(out, other[k], 2 * k + partner % 2, 0)]
    ppermute x9 -> x6, starting transfers between devices: 3.78 us -> 5.6 us  [ring_gather(): behind = lax.ppermute(behind, 'dp', backward)]
    dynamic_update_slice x12 -> x8, local copies, waits for them, and re-layouts: 3.45 us -> 4.36 us  [ring_gather(): lax.dynamic_update_index_in_dim(out, ahead, order[(my_pos - step) % count...]
  transfers between devices with their start and end apart: 31 -> 25, of which waited for: 17 -> 12; matrix products, arithmetic and copies ran while one was open for 17% -> 27% of each run, Pallas kernels for 0% -> 0%
where the time goes in v7:
time: 207 us; the launch traced here: 206 us
  waiting for transfers between devices  80.7 us (39%)
  local copies, waits for them, and re-layouts  33.8 us (16%)
  between operations  31.7 us (15%)
  starting transfers between devices  21.7 us (10%)
  matrix products  20.1 us (10%)
  other arithmetic  18.6 us (9%)
    ppermute x8, waiting for transfers between devices, ring_gather(): ahead = lax.ppermute(ahead, 'dp', forward)  42.1 us
    ppermute x6, waiting for transfers between devices, seq_scatter_sum(): lax.ppermute(piece, 'seq', [(i, (i + shift) % count) for i in range(count)])  32.2 us
    ppermute x8, starting transfers between devices, ring_gather(): ahead = lax.ppermute(ahead, 'dp', forward)  10.7 us
    convert_element_type x1, other arithmetic, depthwise(): return jax.nn.silu(total_acc).astype(jnp.bfloat16)  6.81 us
    ppermute x2, waiting for transfers between devices, seq_gather(): lax.ppermute(block, 'seq', [(i, (i + 2 * shift) % count) for i in range(c...  6.39 us
    ppermute x6, starting transfers between devices, ring_gather(): behind = lax.ppermute(behind, 'dp', backward)  5.6 us
    sub x1, matrix products, one_block(): weights = jnp.exp(scores - top_score)  5.41 us
    dot_general x1, local copies, waits for them, and re-layouts, on_device(): jnp.dot(shard_piece, glu_matrix, preferred_element_type=jnp.float32)  4.37 us
  transfers between devices with their start and end apart: 25, of which 12 were waited for; matrix products, arithmetic and copies ran while one was open for 27% of the time, Pallas kernels for 0%

profile of v7, /device:TPU:0, one launch (start us, length us, event | category | flops | bytes accessed | tf_op | source)
XLA Modules:
  0.0 206.5 jit_solution(16693265884444506785)
XLA Ops:
  6.6 1.1 copy.41
  7.7 3.1 %collective-permute-start.2 = (bf16[192,1152]{1,0:T(8,128)(2,1)S(1)}, bf16[192,1152]{1,0:T(8,128)(2,1)S(1)}, u32[]{:S(2)}, u32[]{:S(2)}) collective-permute-start(bf16[192,1152]{1,0:T(8,128)(2,1)S(1)} %bitcast.140), channel_id=1, source_target_pairs={{0,8},{8,16},{16,24},{24,28},{28,20},{20,12},{12,4},{4,0},{1,9},{9... | collective-permute-start | bytes 1327112 | tf_op jit(solution)/shard_map/ppermute | solution.py:119
  10.8 1.1 convert_reduce_fusion.1
  12.0 1.2 fusion.16
  13.2 1.3 fusion.18
  14.5 2.0 collective-permute-start
  32.9 0.9 broadcast_compare_fusion
  36.1 1.0 copy.42
  37.1 2.2 %broadcast_in_dim.371 = bf16[8,192,1152]{2,1,0:T(8,128)(2,1)} broadcast(bf16[]{:T(256)} %constant.266.clone.1), dimensions={} | broadcast | bytes 3538946 | tf_op jit(solution)/shard_map/broadcast_in_dim | solution.py:115
  45.7 1.6 collective-permute-start.4
  49.4 12.7 %collective-permute-done.4 = bf16[192,1152]{1,0:T(8,128)(2,1)S(1)} collective-permute-done((bf16[192,1152]{1,0:T(8,128)(2,1)S(1)}, bf16[192,1152]{1,0:T(8,128)(2,1)S(1)}, u32[]{:S(2)}, u32[]{:S(2)}) %collective-permute-start.4) | collective-permute-done | bytes 442400 | tf_op jit(solution)/shard_map/ppermute | solution.py:119
  62.1 2.5 %collective-permute-start.6 = (bf16[192,1152]{1,0:T(8,128)(2,1)S(1)}, bf16[192,1152]{1,0:T(8,128)(2,1)S(1)}, u32[]{:S(2)}, u32[]{:S(2)}) collective-permute-start(bf16[192,1152]{1,0:T(8,128)(2,1)S(1)} %collective-permute-done.4), channel_id=1, source_target_pairs={{0,8},{8,16},{16,24},{24,28},{28,20},{20,12},{12,4},{4,0},{1,9},{9... | collective-permute-start | bytes 1327112 | tf_op jit(solution)/shard_map/ppermute | solution.py:119
  64.6 0.9 collective-permute-start.7
  67.3 8.6 %collective-permute-done.6 = bf16[192,1152]{1,0:T(8,128)(2,1)S(1)} collective-permute-done((bf16[192,1152]{1,0:T(8,128)(2,1)S(1)}, bf16[192,1152]{1,0:T(8,128)(2,1)S(1)}, u32[]{:S(2)}, u32[]{:S(2)}) %collective-permute-start.6) | collective-permute-done | bytes 442400 | tf_op jit(solution)/shard_map/ppermute | solution.py:119
  75.8 0.8 collective-permute-start.8
  78.3 9.0 %collective-permute-done.8 = bf16[192,1152]{1,0:T(8,128)(2,1)S(1)} collective-permute-done((bf16[192,1152]{1,0:T(8,128)(2,1)S(1)}, bf16[192,1152]{1,0:T(8,128)(2,1)S(1)}, u32[]{:S(2)}, u32[]{:S(2)}) %collective-permute-start.8) | collective-permute-done | bytes 442400 | tf_op jit(solution)/shard_map/ppermute | solution.py:119
  88.6 1.5 collective-permute-start.15
  90.1 4.2 %convolution_convert_fusion = bf16[512,1152]{1,0:T(8,128)(2,1)S(1)} fusion(bf16[512,1536]{1,0:T(8,128)(2,1)S(1)} %bitcast.135, bf16[1536,1152]{1,0:T(8,128)(2,1)} %bitcast.24), kind=kOutput, calls=%fused_computation.5 | convolution fusion | flops 1812529152 | bytes 6291456 | tf_op jit(solution)/shard_map/dot_general | solution.py:198
  94.3 1.5 copy.35
  96.0 1.0 bitcast_dynamic-update-slice_fusion.7
  97.1 5.4 %fusion.39 = (f32[4,512]{1,0:T(4,128)}, f32[4,512,512]{1,2,0:T(8,128)}) fusion(pred[512,512]{0,1:T(8,128)(4,1)} %broadcast_compare_fusion, bf16[512,3,4,96]{0,3,2,1:T(8,128)(2,1)} %bitcast.138), kind=kOutput, calls=%fused_computation.164 | convolution fusion | flops 205521408 | bytes 5251072 | tf_op jit(solution)/shard_map/while/body/eval_jaxpr/sub | solution.py:151
  102.5 3.5 %fusion.6 = bf16[4,96,512]{2,1,0:T(8,128)(2,1)} fusion(f32[4,512,512]{1,2,0:T(8,128)} %get-tuple-element.114, f32[4,512]{1,0:T(4,128)} %get-tuple-element.113, bf16[512,3,4,96]{0,3,2,1:T(8,128)(2,1)} %bitcast.139), kind=kOutput, calls=%fused_computation.12 | convolution fusion | flops 203620352 | bytes 4988928 | tf_op jit(solution)/shard_map/while/body/eval_jaxpr/hqk,khe->qhe/dot_general | solution.py:153
  106.0 2.4 %convolution_convert_fusion.2 = bf16[512,1536]{1,0:T(8,128)(2,1)S(1)} fusion(bf16[512,384]{0,1:T(8,128)(2,1)} %bitcast.142, bf16[384,1536]{0,1:T(8,128)(2,1)} %all-gather.2.cloned.1.call-done), kind=kOutput, calls=%fused_computation.7 | convolution fusion | flops 604766208 | bytes 3145728 | tf_op jit(solution)/shard_map/dot_general | solution.py:204
  110.3 1.3 collective-permute-start.17
  111.6 1.0 bitcast_dynamic-update-slice_fusion.6
  112.7 1.0 bitcast_dynamic-update-slice_fusion.5
  113.7 4.1 %collective-permute-done.11 = bf16[128,1536]{1,0:T(8,128)(2,1)S(1)} collective-permute-done((bf16[128,1536]{1,0:T(8,128)(2,1)S(1)}, bf16[128,1536]{1,0:T(8,128)(2,1)S(1)}, u32[]{:S(2)}, u32[]{:S(2)}) %collective-permute-start.11) | collective-permute-done | bytes 393248 | tf_op jit(solution)/shard_map/ppermute | solution.py:69
  117.8 9.1 %collective-permute-done.10 = bf16[128,1536]{1,0:T(8,128)(2,1)S(1)} collective-permute-done((bf16[128,1536]{1,0:T(8,128)(2,1)S(1)}, bf16[128,1536]{1,0:T(8,128)(2,1)S(1)}, u32[]{:S(2)}, u32[]{:S(2)}) %collective-permute-start.10) | collective-permute-done | bytes 393248 | tf_op jit(solution)/shard_map/ppermute | solution.py:69
  128.4 1.0 broadcast.155
  129.4 1.1 bitcast_dynamic-update-slice_fusion.17
  130.5 1.2 collective-permute-start.12
  132.5 1.5 collective-permute-start.19
  134.0 6.4 %collective-permute-done.12 = bf16[128,1536]{1,0:T(8,128)(2,1)S(1)} collective-permute-done((bf16[128,1536]{1,0:T(8,128)(2,1)S(1)}, bf16[128,1536]{1,0:T(8,128)(2,1)S(1)}, u32[]{:S(2)}, u32[]{:S(2)}) %collective-permute-start.12) | collective-permute-done | bytes 393248 | tf_op jit(solution)/shard_map/ppermute | solution.py:36
  141.3 0.9 collective-permute-done.18
  143.0 10.9 %collective-permute-done.20 = bf16[288,768]{1,0:T(8,128)(2,1)S(1)} collective-permute-done((bf16[288,768]{1,0:T(8,128)(2,1)S(1)}, bf16[288,768]{1,0:T(8,128)(2,1)S(1)}, u32[]{:S(2)}, u32[]{:S(2)}) %collective-permute-start.20) | collective-permute-done | bytes 442400 | tf_op jit(solution)/shard_map/ppermute | solution.py:119
  154.0 1.5 slice.420
  155.5 1.1 slice.423
  156.6 4.4 %copy.38 = bf16[768,1536]{1,0:T(8,128)(2,1)} copy(bf16[768,1536]{0,1:T(8,128)(2,1)} %bitcast.130) | data formatting | bytes 4718592 | tf_op jit(solution)/shard_map/dot_general | solution.py:209
  161.0 1.5 reshape.221
  162.5 0.8 copy.39
  163.4 1.8 slice_dynamic-update-slice_fusion.1
  165.1 1.8 slice_dynamic-update-slice_fusion
  167.3 3.6 %fusion.40 = f32[512,2,384]{2,0,1:T(8,128)S(1)} fusion(bf16[512,1536,1]{1,0,2:T(8,128)(2,1)} %bitcast.136, bf16[2,384,1536]{2,1,0:T(8,128)(2,1)} %bitcast.133), kind=kOutput, calls=%fused_computation.165 | convolution fusion | flops 1207959552 | bytes 5505024 | tf_op jit(solution)/shard_map/dot_general | solution.py:209
  171.5 6.8 %multiply_convert_fusion = bf16[512,384]{1,0:T(8,128)(2,1)S(1)} fusion(bf16[512,384]{1,0:T(8,128)(2,1)S(1)} %fusion.32, f32[384]{0:T(512)S(1)} %copy-done.37, f32[384]{0:T(512)S(1)} %copy-done.38, f32[384]{0:T(512)S(1)} %get-tuple-element.20, f32[384]{0:T(512)S(1)} %get-tuple-element.28, f32[384]{0:T(512)S(1)} %get-tuple-element.30, f32[384]{0:T(512)S(1)} %copy-done.12, ...), kind=kLoop, calls=%fused_computation.41 | loop fusion | flops 25165824 | bytes 849920 | tf_op jit(solution)/shard_map/convert_element_type | solution.py:172
  178.3 1.0 convolution_convert_fusion.1
  180.5 8.2 %collective-permute-done.23 = bf16[128,1536]{1,0:T(8,128)(2,1)S(1)} collective-permute-done((bf16[128,1536]{1,0:T(8,128)(2,1)S(1)}, bf16[128,1536]{1,0:T(8,128)(2,1)S(1)}, u32[]{:S(2)}, u32[]{:S(2)}) %collective-permute-start.23) | collective-permute-done | bytes 393248 | tf_op jit(solution)/shard_map/ppermute | solution.py:69
  188.7 9.1 %collective-permute-done.22 = bf16[128,1536]{1,0:T(8,128)(2,1)S(1)} collective-permute-done((bf16[128,1536]{1,0:T(8,128)(2,1)S(1)}, bf16[128,1536]{1,0:T(8,128)(2,1)S(1)}, u32[]{:S(2)}, u32[]{:S(2)}) %collective-permute-start.22) | collective-permute-done | bytes 393248 | tf_op jit(solution)/shard_map/ppermute | solution.py:69
  198.6 1.0 fusion.31
  (186 shorter events, 22.9 us)
Async XLA Ops:
  6.5 10.5 %copy-start.53 = (s32[8]{0:T(128)S(1)}, s32[8]{0:T(128)}, u32[]{:S(2)}) copy-start(s32[8]{0:T(128)} %constant.297.clone) | copy-start | bytes 100
  6.5 15.7 %copy-start.10 = (s32[8]{0:T(128)S(1)}, s32[8]{0:T(128)}, u32[]{:S(2)}) copy-start(s32[8]{0:T(128)} %constant.298.clone) | copy-start | bytes 100
  6.5 10.1 %copy-start.5 = (bf16[192,3,384]{2,0,1:T(8,128)(2,1)S(1)}, bf16[192,3,384]{2,0,1:T(8,128)(2,1)}, u32[]{:S(2)}) copy-start(bf16[192,3,384]{2,0,1:T(8,128)(2,1)} %param.17) | copy-start | bytes 1327108
  6.5 24.7 %copy-start.8 = (bf16[31,384]{1,0:T(8,128)(2,1)S(1)}, bf16[31,384]{1,0:T(8,128)(2,1)}, u32[]{:S(2)}) copy-start(bf16[31,384]{1,0:T(8,128)(2,1)} %param.20) | copy-start | bytes 71428
  6.5 26.1 %copy-start.52 = (s32[1,4]{1,0:T(1,128)S(1)}, s32[1,4]{1,0:T(1,128)}, u32[]{:S(2)}) copy-start(s32[1,4]{1,0:T(1,128)} %param.14) | copy-start | bytes 52
  6.5 99.4 %all-gather.2.cloned.1.call-start = ((), (), s32[]{:S(2)}) async-start(), calls=%async_computation | async-start | bytes 1327104 | tf_op jit(solution)/shard_map/all_gather | solution.py:184
  7.7 28.0 %copy-start.7 = (bf16[384,192]{0,1:T(8,128)(2,1)S(1)}, bf16[384,192]{0,1:T(8,128)(2,1)}, u32[]{:S(2)}) copy-start(bf16[384,192]{0,1:T(8,128)(2,1)} %param.21) | copy-start | bytes 442372
  7.7 38.0 %collective-permute-start.2 = (bf16[192,1152]{1,0:T(8,128)(2,1)S(1)}, bf16[192,1152]{1,0:T(8,128)(2,1)S(1)}, u32[]{:S(2)}, u32[]{:S(2)}) collective-permute-start(bf16[192,1152]{1,0:T(8,128)(2,1)S(1)} %bitcast.140), channel_id=1, source_target_pairs={{0,8},{8,16},{16,24},{24,28},{28,20},{20,12},{12,4},{4,0},{1,9},{9... | collective-permute-start | bytes 1327112 | tf_op jit(solution)/shard_map/ppermute | solution.py:119
  10.8 36.6 %collective-permute-start.3 = (bf16[192,1152]{1,0:T(8,128)(2,1)S(1)}, bf16[192,1152]{1,0:T(8,128)(2,1)S(1)}, u32[]{:S(2)}, u32[]{:S(2)}) collective-permute-start(bf16[192,1152]{1,0:T(8,128)(2,1)S(1)} %bitcast.141), channel_id=1, source_target_pairs={{0,4},{8,0},{16,8},{24,16},{28,24},{20,28},{12,20},{4,12},{1,5},{9... | collective-permute-start | bytes 1327112 | tf_op jit(solution)/shard_map/ppermute | solution.py:122
  14.5 31.1 %collective-permute-start = (bf16[128,1536]{1,0:T(8,128)(2,1)S(1)}, bf16[128,1536]{1,0:T(8,128)(2,1)S(1)}, u32[]{:S(2)}, u32[]{:S(2)}) collective-permute-start(bf16[128,1536]{1,0:T(8,128)(2,1)S(1)} %fusion.18), channel_id=1, source_target_pairs={{0,2},{1,3},{2,0},{3,1},{4,6},{5,7},{6,4},{7,5},{8,10},{9,11},{10,... | collective-permute-start | bytes 1179656 | tf_op jit(solution)/shard_map/ppermute | solution.py:36
  39.3 6.0 %copy-start = (bf16[1,128,1536]{2,1,0:T(8,128)(2,1)S(1)}, bf16[1,128,1536]{2,1,0:T(8,128)(2,1)}, u32[]{:S(2)}) copy-start(bf16[1,128,1536]{2,1,0:T(8,128)(2,1)} %param.13) | copy-start | bytes 1179652
  39.3 6.0 %copy-start.9 = (f32[1536]{0:T(1024)S(1)}, f32[1536]{0:T(1024)}, u32[]{:S(2)}) copy-start(f32[1536]{0:T(1024)} %param.15) | copy-start | bytes 18436
  45.6 21.5 %collective-permute-start.1 = (bf16[2,128,1536]{2,1,0:T(8,128)(2,1)S(1)}, bf16[2,128,1536]{2,1,0:T(8,128)(2,1)S(1)}, u32[]{:S(2)}, u32[]{:S(2)}) collective-permute-start(bf16[2,128,1536]{2,1,0:T(8,128)(2,1)S(1)} %get-tuple-element.73), channel_id=1, source_target_pairs={{0,1},{1,0},{2,3},{3,2},{4,5},{5,4},{6,7},{7,6},{8,9},{9,8},{10,11... | collective-permute-start | bytes 2359304 | tf_op jit(solution)/shard_map/ppermute | solution.py:42
  45.7 16.4 %collective-permute-start.4 = (bf16[192,1152]{1,0:T(8,128)(2,1)S(1)}, bf16[192,1152]{1,0:T(8,128)(2,1)S(1)}, u32[]{:S(2)}, u32[]{:S(2)}) collective-permute-start(bf16[192,1152]{1,0:T(8,128)(2,1)S(1)} %collective-permute-done.2), channel_id=1, source_target_pairs={{0,8},{8,16},{16,24},{24,28},{28,20},{20,12},{12,4},{4,0},{1,9},{9... | collective-permute-start | bytes 1327112 | tf_op jit(solution)/shard_map/ppermute | solution.py:119
  47.4 17.3 %collective-permute-start.5 = (bf16[192,1152]{1,0:T(8,128)(2,1)S(1)}, bf16[192,1152]{1,0:T(8,128)(2,1)S(1)}, u32[]{:S(2)}, u32[]{:S(2)}) collective-permute-start(bf16[192,1152]{1,0:T(8,128)(2,1)S(1)} %collective-permute-done.3), channel_id=1, source_target_pairs={{0,4},{8,0},{16,8},{24,16},{28,24},{20,28},{12,20},{4,12},{1,5},{9... | collective-permute-start | bytes 1327112 | tf_op jit(solution)/shard_map/ppermute | solution.py:122
  62.1 13.7 %collective-permute-start.6 = (bf16[192,1152]{1,0:T(8,128)(2,1)S(1)}, bf16[192,1152]{1,0:T(8,128)(2,1)S(1)}, u32[]{:S(2)}, u32[]{:S(2)}) collective-permute-start(bf16[192,1152]{1,0:T(8,128)(2,1)S(1)} %collective-permute-done.4), channel_id=1, source_target_pairs={{0,8},{8,16},{16,24},{24,28},{28,20},{20,12},{12,4},{4,0},{1,9},{9... | collective-permute-start | bytes 1327112 | tf_op jit(solution)/shard_map/ppermute | solution.py:119
  64.6 12.8 %collective-permute-start.7 = (bf16[192,1152]{1,0:T(8,128)(2,1)S(1)}, bf16[192,1152]{1,0:T(8,128)(2,1)S(1)}, u32[]{:S(2)}, u32[]{:S(2)}) collective-permute-start(bf16[192,1152]{1,0:T(8,128)(2,1)S(1)} %collective-permute-done.5), channel_id=1, source_target_pairs={{0,4},{8,0},{16,8},{24,16},{28,24},{20,28},{12,20},{4,12},{1,5},{9... | collective-permute-start | bytes 1327112 | tf_op jit(solution)/shard_map/ppermute | solution.py:122
  75.8 11.5 %collective-permute-start.8 = (bf16[192,1152]{1,0:T(8,128)(2,1)S(1)}, bf16[192,1152]{1,0:T(8,128)(2,1)S(1)}, u32[]{:S(2)}, u32[]{:S(2)}) collective-permute-start(bf16[192,1152]{1,0:T(8,128)(2,1)S(1)} %collective-permute-done.6), channel_id=1, source_target_pairs={{0,8},{8,16},{16,24},{24,28},{28,20},{20,12},{12,4},{4,0},{1,9},{9... | collective-permute-start | bytes 1327112 | tf_op jit(solution)/shard_map/ppermute | solution.py:119
  88.1 21.5 %collective-permute-start.14 = (bf16[288,768]{1,0:T(8,128)(2,1)}, bf16[288,768]{1,0:T(8,128)(2,1)}, u32[]{:S(2)}, u32[]{:S(2)}) collective-permute-start(bf16[288,768]{1,0:T(8,128)(2,1)} %pad_maximum_fusion), channel_id=1, source_target_pairs={{0,8},{8,16},{16,24},{24,28},{28,20},{20,12},{12,4},{4,0},{1,9},{9... | collective-permute-start | bytes 1327112 | tf_op jit(solution)/shard_map/ppermute | solution.py:119
  88.6 21.7 %collective-permute-start.15 = (bf16[288,768]{1,0:T(8,128)(2,1)}, bf16[288,768]{1,0:T(8,128)(2,1)}, u32[]{:S(2)}, u32[]{:S(2)}) collective-permute-start(bf16[288,768]{1,0:T(8,128)(2,1)} %pad_maximum_fusion), channel_id=1, source_target_pairs={{0,4},{8,0},{16,8},{24,16},{28,24},{20,28},{12,20},{4,12},{1,5},{9... | collective-permute-start | bytes 1327112 | tf_op jit(solution)/shard_map/ppermute | solution.py:122
  108.4 19.3 %copy-start.1 = (bf16[1,128,1536]{2,1,0:T(8,128)(2,1)S(1)}, bf16[1,128,1536]{2,1,0:T(8,128)(2,1)}, u32[]{:S(2)}) copy-start(bf16[1,128,1536]{2,1,0:T(8,128)(2,1)} %param.13) | copy-start | bytes 1179652
  108.5 9.3 %collective-permute-start.11 = (bf16[128,1536]{1,0:T(8,128)(2,1)S(1)}, bf16[128,1536]{1,0:T(8,128)(2,1)S(1)}, u32[]{:S(2)}, u32[]{:S(2)}) collective-permute-start(bf16[128,1536]{1,0:T(8,128)(2,1)S(1)} %get-tuple-element.67), channel_id=1, source_target_pairs={{0,3},{1,0},{2,1},{3,2},{4,7},{5,4},{6,5},{7,6},{8,11},{9,8},{10,9... | collective-permute-start | bytes 1179656 | tf_op jit(solution)/shard_map/ppermute | solution.py:69
  108.6 18.3 %collective-permute-start.10 = (bf16[128,1536]{1,0:T(8,128)(2,1)S(1)}, bf16[128,1536]{1,0:T(8,128)(2,1)S(1)}, u32[]{:S(2)}, u32[]{:S(2)}) collective-permute-start(bf16[128,1536]{1,0:T(8,128)(2,1)S(1)} %get-tuple-element.68), channel_id=1, source_target_pairs={{0,2},{1,3},{2,0},{3,1},{4,6},{5,7},{6,4},{7,5},{8,10},{9,11},{10,... | collective-permute-start | bytes 1179656 | tf_op jit(solution)/shard_map/ppermute | solution.py:69
  109.4 18.3 %collective-permute-start.9 = (bf16[128,1536]{1,0:T(8,128)(2,1)S(1)}, bf16[128,1536]{1,0:T(8,128)(2,1)S(1)}, u32[]{:S(2)}, u32[]{:S(2)}) collective-permute-start(bf16[128,1536]{1,0:T(8,128)(2,1)S(1)} %get-tuple-element.66), channel_id=1, source_target_pairs={{0,1},{1,2},{2,3},{3,0},{4,5},{5,6},{6,7},{7,4},{8,9},{9,10},{10,1... | collective-permute-start | bytes 1179656 | tf_op jit(solution)/shard_map/ppermute | solution.py:69
  109.6 22.3 %collective-permute-start.16 = (bf16[288,768]{1,0:T(8,128)(2,1)}, bf16[288,768]{1,0:T(8,128)(2,1)S(1)}, u32[]{:S(2)}, u32[]{:S(2)}) collective-permute-start(bf16[288,768]{1,0:T(8,128)(2,1)} %collective-permute-done.14), channel_id=1, source_target_pairs={{0,8},{8,16},{16,24},{24,28},{28,20},{20,12},{12,4},{4,0},{1,9},{9... | collective-permute-start | bytes 1327112 | tf_op jit(solution)/shard_map/ppermute | solution.py:119
  110.3 22.2 %collective-permute-start.17 = (bf16[288,768]{1,0:T(8,128)(2,1)}, bf16[288,768]{1,0:T(8,128)(2,1)S(1)}, u32[]{:S(2)}, u32[]{:S(2)}) collective-permute-start(bf16[288,768]{1,0:T(8,128)(2,1)} %collective-permute-done.15), channel_id=1, source_target_pairs={{0,4},{8,0},{16,8},{24,16},{28,24},{20,28},{12,20},{4,12},{1,5},{9... | collective-permute-start | bytes 1327112 | tf_op jit(solution)/shard_map/ppermute | solution.py:122
  112.7 16.7 %copy-start.11 = (f32[1536]{0:T(1024)S(1)}, f32[1536]{0:T(1024)}, u32[]{:S(2)}) copy-start(f32[1536]{0:T(1024)} %param.16) | copy-start | bytes 18436
  130.5 9.9 %collective-permute-start.12 = (bf16[128,1536]{1,0:T(8,128)(2,1)S(1)}, bf16[128,1536]{1,0:T(8,128)(2,1)S(1)}, u32[]{:S(2)}, u32[]{:S(2)}) collective-permute-start(bf16[128,1536]{1,0:T(8,128)(2,1)S(1)} %get-tuple-element.60), channel_id=1, source_target_pairs={{0,2},{1,3},{2,0},{3,1},{4,6},{5,7},{6,4},{7,5},{8,10},{9,11},{10,... | collective-permute-start | bytes 1179656 | tf_op jit(solution)/shard_map/ppermute | solution.py:36
  131.9 10.2 %collective-permute-start.18 = (bf16[288,768]{1,0:T(8,128)(2,1)S(1)}, bf16[288,768]{1,0:T(8,128)(2,1)S(1)}, u32[]{:S(2)}, u32[]{:S(2)}) collective-permute-start(bf16[288,768]{1,0:T(8,128)(2,1)S(1)} %collective-permute-done.16), channel_id=1, source_target_pairs={{0,8},{8,16},{16,24},{24,28},{28,20},{20,12},{12,4},{4,0},{1,9},{9... | collective-permute-start | bytes 1327112 | tf_op jit(solution)/shard_map/ppermute | solution.py:119
  132.5 10.4 %collective-permute-start.19 = (bf16[288,768]{1,0:T(8,128)(2,1)S(1)}, bf16[288,768]{1,0:T(8,128)(2,1)S(1)}, u32[]{:S(2)}, u32[]{:S(2)}) collective-permute-start(bf16[288,768]{1,0:T(8,128)(2,1)S(1)} %collective-permute-done.17), channel_id=1, source_target_pairs={{0,4},{8,0},{16,8},{24,16},{28,24},{20,28},{12,20},{4,12},{1,5},{9... | collective-permute-start | bytes 1327112 | tf_op jit(solution)/shard_map/ppermute | solution.py:122
  141.2 22.1 %collective-permute-start.13 = (bf16[2,128,1536]{2,1,0:T(8,128)(2,1)}, bf16[2,128,1536]{2,1,0:T(8,128)(2,1)}, u32[]{:S(2)}, u32[]{:S(2)}) collective-permute-start(bf16[2,128,1536]{2,1,0:T(8,128)(2,1)} %get-tuple-element.71), channel_id=1, source_target_pairs={{0,1},{1,0},{2,3},{3,2},{4,5},{5,4},{6,7},{7,6},{8,9},{9,8},{10,11... | collective-permute-start | bytes 2359304 | tf_op jit(solution)/shard_map/ppermute | solution.py:42
  142.1 11.8 %collective-permute-start.20 = (bf16[288,768]{1,0:T(8,128)(2,1)S(1)}, bf16[288,768]{1,0:T(8,128)(2,1)S(1)}, u32[]{:S(2)}, u32[]{:S(2)}) collective-permute-start(bf16[288,768]{1,0:T(8,128)(2,1)S(1)} %collective-permute-done.18), channel_id=1, source_target_pairs={{0,8},{8,16},{16,24},{24,28},{28,20},{20,12},{12,4},{4,0},{1,9},{9... | collective-permute-start | bytes 1327112 | tf_op jit(solution)/shard_map/ppermute | solution.py:119
  156.6 4.4 %copy-start.4 = (bf16[8,96,768]{2,1,0:T(8,128)(2,1)S(1)}, bf16[8,96,768]{2,1,0:T(8,128)(2,1)}, u32[]{:S(2)}) copy-start(bf16[8,96,768]{2,1,0:T(8,128)(2,1)} %slice.423) | copy-start | bytes 3538948
  166.9 4.2 %copy-start.16 = (f32[384]{0:T(512)S(1)}, f32[384]{0:T(512)}, u32[]{:S(2)}) copy-start(f32[384]{0:T(512)} %get-tuple-element.36) | copy-start | bytes 4612
  166.9 4.2 %copy-start.17 = (f32[384]{0:T(512)S(1)}, f32[384]{0:T(512)}, u32[]{:S(2)}) copy-start(f32[384]{0:T(512)} %get-tuple-element.37) | copy-start | bytes 4612
  166.9 4.2 %copy-start.18 = (f32[384]{0:T(512)S(1)}, f32[384]{0:T(512)}, u32[]{:S(2)}) copy-start(f32[384]{0:T(512)} %get-tuple-element.38) | copy-start | bytes 4612
  166.9 4.2 %copy-start.19 = (f32[384]{0:T(512)S(1)}, f32[384]{0:T(512)}, u32[]{:S(2)}) copy-start(f32[384]{0:T(512)} %get-tuple-element.39) | copy-start | bytes 4612
  167.0 4.2 %copy-start.20 = (f32[384]{0:T(512)S(1)}, f32[384]{0:T(512)}, u32[]{:S(2)}) copy-start(f32[384]{0:T(512)} %get-tuple-element.40) | copy-start | bytes 4612
  167.0 4.2 %copy-start.21 = (f32[384]{0:T(512)S(1)}, f32[384]{0:T(512)}, u32[]{:S(2)}) copy-start(f32[384]{0:T(512)} %get-tuple-element.41) | copy-start | bytes 4612
  167.0 4.2 %copy-start.22 = (f32[384]{0:T(512)S(1)}, f32[384]{0:T(512)}, u32[]{:S(2)}) copy-start(f32[384]{0:T(512)} %get-tuple-element.42) | copy-start | bytes 4612
  167.0 4.2 %copy-start.23 = (f32[384]{0:T(512)S(1)}, f32[384]{0:T(512)}, u32[]{:S(2)}) copy-start(f32[384]{0:T(512)} %get-tuple-element.43) | copy-start | bytes 4612
  167.0 4.2 %copy-start.24 = (f32[384]{0:T(512)S(1)}, f32[384]{0:T(512)}, u32[]{:S(2)}) copy-start(f32[384]{0:T(512)} %get-tuple-element.44) | copy-start | bytes 4612
  167.0 4.2 %copy-start.25 = (f32[384]{0:T(512)S(1)}, f32[384]{0:T(512)}, u32[]{:S(2)}) copy-start(f32[384]{0:T(512)} %get-tuple-element.45) | copy-start | bytes 4612
  167.0 4.2 %copy-start.26 = (f32[384]{0:T(512)S(1)}, f32[384]{0:T(512)}, u32[]{:S(2)}) copy-start(f32[384]{0:T(512)} %get-tuple-element.46) | copy-start | bytes 4612
  178.3 20.3 %copy-start.3 = (bf16[128,1536]{1,0:T(8,128)(2,1)S(1)}, bf16[128,1536]{1,0:T(8,128)(2,1)}, u32[]{:S(2)}) copy-start(bf16[128,1536]{1,0:T(8,128)(2,1)} %copy-done.2) | copy-start | bytes 1179652
  179.4 9.3 %collective-permute-start.23 = (bf16[128,1536]{1,0:T(8,128)(2,1)S(1)}, bf16[128,1536]{1,0:T(8,128)(2,1)S(1)}, u32[]{:S(2)}, u32[]{:S(2)}) collective-permute-start(bf16[128,1536]{1,0:T(8,128)(2,1)S(1)} %get-tuple-element.64), channel_id=1, source_target_pairs={{0,3},{1,0},{2,1},{3,2},{4,7},{5,4},{6,5},{7,6},{8,11},{9,8},{10,9... | collective-permute-start | bytes 1179656 | tf_op jit(solution)/shard_map/ppermute | solution.py:69
  179.5 18.3 %collective-permute-start.22 = (bf16[128,1536]{1,0:T(8,128)(2,1)S(1)}, bf16[128,1536]{1,0:T(8,128)(2,1)S(1)}, u32[]{:S(2)}, u32[]{:S(2)}) collective-permute-start(bf16[128,1536]{1,0:T(8,128)(2,1)S(1)} %get-tuple-element.65), channel_id=1, source_target_pairs={{0,2},{1,3},{2,0},{3,1},{4,6},{5,7},{6,4},{7,5},{8,10},{9,11},{10,... | collective-permute-start | bytes 1179656 | tf_op jit(solution)/shard_map/ppermute | solution.py:69
  180.3 18.3 %collective-permute-start.21 = (bf16[128,1536]{1,0:T(8,128)(2,1)S(1)}, bf16[128,1536]{1,0:T(8,128)(2,1)S(1)}, u32[]{:S(2)}, u32[]{:S(2)}) collective-permute-start(bf16[128,1536]{1,0:T(8,128)(2,1)S(1)} %get-tuple-element.63), channel_id=1, source_target_pairs={{0,1},{1,2},{2,3},{3,0},{4,5},{5,6},{6,7},{7,4},{8,9},{9,10},{10,1... | collective-permute-start | bytes 1179656 | tf_op jit(solution)/shard_map/ppermute | solution.py:69
  (31 other events, 127.1 us)
Sparse Core Ops, SparseCore 0:
  16.6 42.9 all-gather.1

commit v8 on v5

--- a/solution.py
+++ b/solution.py
@@ -59,14 +59,33 @@
         return False
 
 
-def seq_scatter_sum(full):
+def seq_scatter_sum(full, paired):
     count = lax.axis_size("seq")
     me = lax.axis_index("seq")
     rows = full.shape[0] // count
-    total = lax.dynamic_slice_in_dim(full, me * rows, rows, axis=0).astype(jnp.float32)
-    for shift in range(1, count):
-        piece = lax.dynamic_slice_in_dim(full, ((me + shift) % count) * rows, rows, axis=0)
-        got = lax.ppermute(piece, "seq", [(i, (i + shift) % count) for i in range(count)])
+    if not paired:
+        total = lax.dynamic_slice_in_dim(full, me * rows, rows, axis=0).astype(jnp.float32)
+        for shift in range(1, count):
+            piece = lax.dynamic_slice_in_dim(full, ((me + shift) % count) * rows, rows, axis=0)
+            got = lax.ppermute(piece, "seq", [(i, (i + shift) % count) for i in range(count)])
+            total = total + got.astype(jnp.float32)
+        return total
+    half = count // 2
+    core = me % 2
+    quads = full.reshape(half, 2, rows, full.shape[1])
+    mine = lax.dynamic_index_in_dim(quads, core, axis=1, keepdims=False)
+    theirs = lax.dynamic_index_in_dim(quads, 1 - core, axis=1, keepdims=False)
+    got = lax.ppermute(theirs, "seq", [(i, i ^ 1) for i in range(count)])
+    chip_sum = mine.astype(jnp.float32) + got.astype(jnp.float32)
+    here = me // 2
+    total = lax.dynamic_index_in_dim(chip_sum, here, axis=0, keepdims=False)
+    for shift in range(1, half):
+        piece = lax.dynamic_index_in_dim(chip_sum, (here + shift) % half, axis=0, keepdims=False)
+        got = lax.ppermute(
+            piece.astype(jnp.bfloat16),
+            "seq",
+            [(i, (i + 2 * shift) % count) for i in range(count)],
+        )
         total = total + got.astype(jnp.float32)
     return total
 
@@ -202,7 +221,8 @@
     )
     attended = attend(projected, seg_all, HD)
     attn_sum = seq_scatter_sum(
-        jnp.dot(attended, out_local, preferred_element_type=jnp.float32).astype(jnp.bfloat16)
+        jnp.dot(attended, out_local, preferred_element_type=jnp.float32).astype(jnp.bfloat16),
+        paired,
     )
     middle = (inputs + attn_sum).astype(jnp.bfloat16)
     normed2 = layer_norm(middle.astype(jnp.float32), ln2_gain)
@@ -218,7 +238,8 @@
     )
     activated = lax.optimization_barrier(activated)
     conv_out = seq_scatter_sum(
-        jnp.dot(activated, proj_local, preferred_element_type=jnp.float32).astype(jnp.bfloat16)
+        jnp.dot(activated, proj_local, preferred_element_type=jnp.float32).astype(jnp.bfloat16),
+        paired,
     )
     results = [(middle.astype(jnp.float32) + conv_out).astype(jnp.bfloat16)]
     return jnp.stack(results, axis=0)

time: 200 us -> 197 us (0.985)
  local copies, waits for them, and re-layouts: 24.3 us -> 33.9 us
  waiting for transfers between devices: 94 us -> 85 us
  other arithmetic: 17.5 us -> 13.7 us
    ppermute x6 -> x4, waiting for transfers between devices: 32.8 us -> 12.9 us  [the longest x2 10.6 us: seq_scatter_sum(): lax.ppermute(piece.astype(jnp.bfloat16), 'seq', [(i, (i + 2 * shift) % co...]
    ppermute x12, waiting for transfers between devices: 54.8 us -> 62.6 us  [ring_gather(): ahead = lax.ppermute(ahead, 'dp', forward)]
    dynamic_update_slice x4, local copies, waits for them, and re-layouts: 0.13 us -> 3.6 us  [seq_gather(): out = lax.dynamic_update_index_in_dim(out, other[k], 2 * k + partner % 2, 0)]
    ppermute x2, waiting for transfers between devices: 6.12 us -> 8.55 us  [seq_gather(): lax.ppermute(block, 'seq', [(i, (i + 2 * shift) % count) for i in range(c...]
  transfers between devices with their start and end apart: 31 -> 29, of which waited for: 17 -> 13; matrix products, arithmetic and copies ran while one was open for 17% -> 23% of each run, Pallas kernels for 0% -> 0%
where the time goes in v8:
time: 197 us; the launch traced here: 196 us
  waiting for transfers between devices  85 us (43%)
  local copies, waits for them, and re-layouts  33.9 us (17%)
  starting transfers between devices  28.4 us (14%)
  between operations  18.7 us (9%)
  matrix products  16.1 us (8%)
  other arithmetic  13.7 us (7%)
    ppermute x12, waiting for transfers between devices, ring_gather(): ahead = lax.ppermute(ahead, 'dp', forward)  62.6 us
    ppermute x12, starting transfers between devices, ring_gather(): ahead = lax.ppermute(ahead, 'dp', forward)  20.7 us
    ppermute x2, waiting for transfers between devices, seq_scatter_sum(): lax.ppermute(piece.astype(jnp.bfloat16), 'seq', [(i, (i + 2 * shift) % co...  10.6 us
    ppermute x2, waiting for transfers between devices, seq_gather(): lax.ppermute(block, 'seq', [(i, (i + 2 * shift) % count) for i in range(c...  8.55 us
    convert_element_type x1, other arithmetic, depthwise(): return jax.nn.silu(total_acc).astype(jnp.bfloat16)  5.51 us
    dynamic_update_slice x12, local copies, waits for them, and re-layouts, ring_gather(): lax.dynamic_update_index_in_dim(out, ahead, order[(my_pos - step) % count...  5.4 us
    dot_general x1, matrix products, on_device(): jnp.dot(seq_gather(normed1, paired).reshape(group_rows, model_width), qkv...  4.19 us
  transfers between devices with their start and end apart: 29, of which 13 were waited for; matrix products, arithmetic and copies ran while one was open for 23% of the time, Pallas kernels for 0%

profile of v8, /device:TPU:0, one launch (start us, length us, event | category | flops | bytes accessed | tf_op | source)
XLA Modules:
  0.0 195.8 jit_solution(17836840160521246753)
XLA Ops:
  0.0 1.9 copy.51
  1.9 3.0 %collective-permute-start.2 = (bf16[192,1152]{1,0:T(8,128)(2,1)}, bf16[192,1152]{1,0:T(8,128)(2,1)}, u32[]{:S(2)}, u32[]{:S(2)}) collective-permute-start(bf16[192,1152]{1,0:T(8,128)(2,1)} %bitcast.83), channel_id=1, source_target_pairs={{0,8},{8,16},{16,24},{24,28},{28,20},{20,12},{12,4},{4,0},{1,9},{9... | collective-permute-start | bytes 1327112 | tf_op jit(solution)/shard_map/ppermute | solution.py:138
  4.9 1.1 convert_reduce_fusion.1
  6.1 1.2 fusion.16
  7.6 2.0 %collective-permute-start = (bf16[128,1536]{1,0:T(8,128)(2,1)S(1)}, bf16[128,1536]{1,0:T(8,128)(2,1)}, u32[]{:S(2)}, u32[]{:S(2)}) collective-permute-start(bf16[128,1536]{1,0:T(8,128)(2,1)S(1)} %fusion.18), channel_id=1, source_target_pairs={{0,2},{1,3},{2,0},{3,1},{4,6},{5,7},{6,4},{7,5},{8,10},{9,11},{10,... | collective-permute-start | bytes 1179656 | tf_op jit(solution)/shard_map/ppermute | solution.py:36
  27.7 2.2 %broadcast_in_dim.399 = bf16[8,192,1152]{2,1,0:T(8,128)(2,1)} broadcast(bf16[]{:T(256)} %constant.341.clone.1), dimensions={} | broadcast | bytes 3538946 | tf_op jit(solution)/shard_map/broadcast_in_dim | solution.py:134
  35.7 1.1 bitcast_dynamic-update-slice_fusion.19
  36.8 1.6 collective-permute-start.4
  38.9 1.8 bitcast_dynamic-update-slice_fusion.14
  41.5 8.1 %collective-permute-done.4 = bf16[192,1152]{1,0:T(8,128)(2,1)S(1)} collective-permute-done((bf16[192,1152]{1,0:T(8,128)(2,1)}, bf16[192,1152]{1,0:T(8,128)(2,1)S(1)}, u32[]{:S(2)}, u32[]{:S(2)}) %collective-permute-start.4) | collective-permute-done | bytes 442400 | tf_op jit(solution)/shard_map/ppermute | solution.py:138
  49.6 1.6 collective-permute-start.6
  53.3 8.0 %collective-permute-done.6 = bf16[192,1152]{1,0:T(8,128)(2,1)S(1)} collective-permute-done((bf16[192,1152]{1,0:T(8,128)(2,1)S(1)}, bf16[192,1152]{1,0:T(8,128)(2,1)S(1)}, u32[]{:S(2)}, u32[]{:S(2)}) %collective-permute-start.6) | collective-permute-done | bytes 442400 | tf_op jit(solution)/shard_map/ppermute | solution.py:138
  61.3 1.6 collective-permute-start.8
  64.5 7.6 %collective-permute-done.8 = bf16[192,1152]{1,0:T(8,128)(2,1)S(1)} collective-permute-done((bf16[192,1152]{1,0:T(8,128)(2,1)S(1)}, bf16[192,1152]{1,0:T(8,128)(2,1)S(1)}, u32[]{:S(2)}, u32[]{:S(2)}) %collective-permute-start.8) | collective-permute-done | bytes 442400 | tf_op jit(solution)/shard_map/ppermute | solution.py:138
  72.9 1.6 collective-permute-start.9
  75.0 4.2 %convolution_convert_fusion = bf16[512,1152]{1,0:T(8,128)(2,1)S(1)} fusion(bf16[512,1536]{1,0:T(8,128)(2,1)S(1)} %bitcast.190, bf16[1536,1152]{1,0:T(8,128)(2,1)} %bitcast.24), kind=kOutput, calls=%fused_computation.5 | convolution fusion | flops 1812529152 | bytes 6291456 | tf_op jit(solution)/shard_map/dot_general | solution.py:218
  79.8 3.6 %fusion.41 = (f32[4,512]{1,0:T(4,128)S(1)}, f32[4,512,512]{1,2,0:T(8,128)}) fusion(pred[512,512]{0,1:T(8,128)(4,1)S(1)} %broadcast_compare_fusion, bf16[512,3,4,96]{0,3,2,1:T(8,128)(2,1)S(1)} %bitcast.193), kind=kOutput, calls=%fused_computation.176 | convolution fusion | flops 205521408 | bytes 5251072 | tf_op jit(solution)/shard_map/while/body/eval_jaxpr/sub | solution.py:170
  83.4 2.7 %fusion.6 = bf16[4,96,512]{2,1,0:T(8,128)(2,1)S(1)} fusion(f32[4,512,512]{1,2,0:T(8,128)} %get-tuple-element.110, f32[4,512]{1,0:T(4,128)S(1)} %get-tuple-element.109, bf16[512,3,4,96]{0,3,2,1:T(8,128)(2,1)S(1)} %bitcast.194), kind=kOutput, calls=%fused_computation.14 | convolution fusion | flops 203620352 | bytes 4988928 | tf_op jit(solution)/shard_map/while/body/eval_jaxpr/hqk,khe->qhe/dot_general | solution.py:172
  87.2 1.6 collective-permute-start.11
  88.8 1.0 bitcast_dynamic-update-slice_fusion.27
  90.3 1.0 bitcast_dynamic-update-slice_fusion.26
  91.3 2.6 %collective-permute-done.11 = bf16[384,192]{0,1:T(8,128)(2,1)S(1)} collective-permute-done((bf16[384,192]{0,1:T(8,128)(2,1)}, bf16[384,192]{0,1:T(8,128)(2,1)S(1)}, u32[]{:S(2)}, u32[]{:S(2)}) %collective-permute-start.11) | collective-permute-done | bytes 147488 | tf_op jit(solution)/shard_map/ppermute | solution.py:138
  93.9 1.6 collective-permute-start.13
  95.5 1.0 collective-permute-done.12
  97.1 3.0 %collective-permute-done.13 = bf16[384,192]{0,1:T(8,128)(2,1)S(1)} collective-permute-done((bf16[384,192]{0,1:T(8,128)(2,1)S(1)}, bf16[384,192]{0,1:T(8,128)(2,1)S(1)}, u32[]{:S(2)}, u32[]{:S(2)}) %collective-permute-start.13) | collective-permute-done | bytes 147488 | tf_op jit(solution)/shard_map/ppermute | solution.py:138
  100.0 1.6 collective-permute-start.15
  101.7 3.5 %collective-permute-done.15 = bf16[384,192]{0,1:T(8,128)(2,1)S(1)} collective-permute-done((bf16[384,192]{0,1:T(8,128)(2,1)S(1)}, bf16[384,192]{0,1:T(8,128)(2,1)S(1)}, u32[]{:S(2)}, u32[]{:S(2)}) %collective-permute-start.15) | collective-permute-done | bytes 147488 | tf_op jit(solution)/shard_map/ppermute | solution.py:138
  105.2 1.0 convolution_convert_fusion.2
  106.5 1.6 collective-permute-start.20
  108.9 10.2 %collective-permute-done.20 = bf16[288,768]{1,0:T(8,128)(2,1)S(1)} collective-permute-done((bf16[288,768]{1,0:T(8,128)(2,1)S(1)}, bf16[288,768]{1,0:T(8,128)(2,1)S(1)}, u32[]{:S(2)}, u32[]{:S(2)}) %collective-permute-start.20) | collective-permute-done | bytes 442400 | tf_op jit(solution)/shard_map/ppermute | solution.py:138
  119.1 1.6 collective-permute-start.22
  122.1 8.8 %collective-permute-done.22 = bf16[288,768]{1,0:T(8,128)(2,1)S(1)} collective-permute-done((bf16[288,768]{1,0:T(8,128)(2,1)S(1)}, bf16[288,768]{1,0:T(8,128)(2,1)S(1)}, u32[]{:S(2)}, u32[]{:S(2)}) %collective-permute-start.22) | collective-permute-done | bytes 442400 | tf_op jit(solution)/shard_map/ppermute | solution.py:138
  130.9 1.6 collective-permute-start.24
  134.4 1.0 bitcast_dynamic-update-slice_fusion.17
  136.2 8.5 %collective-permute-done.18 = bf16[128,1536]{1,0:T(8,128)(2,1)S(1)} collective-permute-done((bf16[128,1536]{1,0:T(8,128)(2,1)S(1)}, bf16[128,1536]{1,0:T(8,128)(2,1)S(1)}, u32[]{:S(2)}, u32[]{:S(2)}) %collective-permute-start.18) | collective-permute-done | bytes 393248 | tf_op jit(solution)/shard_map/ppermute | solution.py:36
  145.6 1.6 collective-permute-start.26
  147.4 10.9 %collective-permute-done.26 = bf16[288,768]{1,0:T(8,128)(2,1)S(1)} collective-permute-done((bf16[288,768]{1,0:T(8,128)(2,1)S(1)}, bf16[288,768]{1,0:T(8,128)(2,1)S(1)}, u32[]{:S(2)}, u32[]{:S(2)}) %collective-permute-start.26) | collective-permute-done | bytes 442400 | tf_op jit(solution)/shard_map/ppermute | solution.py:138
  158.5 1.1 slice.423
  159.6 2.4 %copy.45 = bf16[768,1536]{1,0:T(8,128)(2,1)} copy(bf16[768,1536]{0,1:T(8,128)(2,1)S(1)} %bitcast.180) | data formatting | bytes 4718592 | tf_op jit(solution)/shard_map/dot_general | solution.py:230
  162.0 3.0 %reshape.252 = bf16[8,384,192]{2,1,0:T(8,128)(2,1)S(1)} reshape(bf16[8,96,768]{2,1,0:T(8,128)(2,1)} %slice.423) | data formatting | bytes 2359296 | tf_op jit(solution)/shard_map/reshape | solution.py:211
  165.0 1.5 copy.46
  166.5 1.8 slice_dynamic-update-slice_fusion.1
  168.3 1.8 slice_dynamic-update-slice_fusion
  170.1 3.6 %fusion.42 = f32[512,2,384]{2,0,1:T(8,128)S(1)} fusion(bf16[512,1536,1]{1,0,2:T(8,128)(2,1)} %bitcast.191, bf16[2,384,1536]{2,1,0:T(8,128)(2,1)} %bitcast.188), kind=kOutput, calls=%fused_computation.177 | convolution fusion | flops 1207959552 | bytes 5505024 | tf_op jit(solution)/shard_map/dot_general | solution.py:230
  174.5 5.5 %multiply_convert_fusion = bf16[512,384]{1,0:T(8,128)(2,1)S(1)} fusion(bf16[512,384]{1,0:T(8,128)(2,1)S(1)} %fusion.34, f32[384]{0:T(512)S(1)} %get-tuple-element.59, f32[384]{0:T(512)S(1)} %get-tuple-element.60, f32[384]{0:T(512)S(1)} %get-tuple-element.30, f32[384]{0:T(512)S(1)} %get-tuple-element.32, f32[384]{0:T(512)S(1)} %get-tuple-element.33, ...), kind=kLoop, calls=%fused_computation.47 | loop fusion | flops 25165824 | bytes 849920 | tf_op jit(solution)/shard_map/convert_element_type | solution.py:191
  180.0 1.0 convolution_convert_fusion.1
  181.2 2.3 %collective-permute-done.27 = bf16[2,128,1536]{2,1,0:T(8,128)(2,1)S(1)} collective-permute-done((bf16[2,128,1536]{2,1,0:T(8,128)(2,1)S(1)}, bf16[2,128,1536]{2,1,0:T(8,128)(2,1)S(1)}, u32[]{:S(2)}, u32[]{:S(2)}) %collective-permute-start.27) | collective-permute-done | bytes 786464 | tf_op jit(solution)/shard_map/ppermute | solution.py:78
  184.4 10.6 %collective-permute-done.28 = bf16[128,1536]{1,0:T(8,128)(2,1)S(1)} collective-permute-done((bf16[128,1536]{1,0:T(8,128)(2,1)S(1)}, bf16[128,1536]{1,0:T(8,128)(2,1)S(1)}, u32[]{:S(2)}, u32[]{:S(2)}) %collective-permute-start.28) | collective-permute-done | bytes 393248 | tf_op jit(solution)/shard_map/ppermute | solution.py:84
  (164 shorter events, 23.9 us)
Async XLA Ops:
  0.0 9.7 %copy-start.2 = (bf16[192,3,384]{2,0,1:T(8,128)(2,1)S(1)}, bf16[192,3,384]{2,0,1:T(8,128)(2,1)}, u32[]{:S(2)}) copy-start(bf16[192,3,384]{2,0,1:T(8,128)(2,1)} %param.19) | copy-start | bytes 1327108
  0.0 7.3 %copy-start = (bf16[1,128,1536]{2,1,0:T(8,128)(2,1)S(1)}, bf16[1,128,1536]{2,1,0:T(8,128)(2,1)}, u32[]{:S(2)}) copy-start(bf16[1,128,1536]{2,1,0:T(8,128)(2,1)} %param.15) | copy-start | bytes 1179652
  0.0 7.3 %copy-start.7 = (f32[1536]{0:T(1024)S(1)}, f32[1536]{0:T(1024)}, u32[]{:S(2)}) copy-start(f32[1536]{0:T(1024)} %param.17) | copy-start | bytes 18436
  1.9 8.2 %copy-start.32 = (s32[8]{0:T(128)S(1)}, s32[8]{0:T(128)}, u32[]{:S(2)}) copy-start(s32[8]{0:T(128)} %constant.370.clone) | copy-start | bytes 100
  1.9 13.4 %copy-start.8 = (s32[8]{0:T(128)S(1)}, s32[8]{0:T(128)}, u32[]{:S(2)}) copy-start(s32[8]{0:T(128)} %constant.371.clone) | copy-start | bytes 100
  1.9 23.0 %copy-start.31 = (s32[1,4]{1,0:T(1,128)S(1)}, s32[1,4]{1,0:T(1,128)}, u32[]{:S(2)}) copy-start(s32[1,4]{1,0:T(1,128)} %param.16) | copy-start | bytes 52
  1.9 34.9 %collective-permute-start.2 = (bf16[192,1152]{1,0:T(8,128)(2,1)}, bf16[192,1152]{1,0:T(8,128)(2,1)}, u32[]{:S(2)}, u32[]{:S(2)}) collective-permute-start(bf16[192,1152]{1,0:T(8,128)(2,1)} %bitcast.83), channel_id=1, source_target_pairs={{0,8},{8,16},{16,24},{24,28},{28,20},{20,12},{12,4},{4,0},{1,9},{9... | collective-permute-start | bytes 1327112 | tf_op jit(solution)/shard_map/ppermute | solution.py:138
  4.9 33.5 %collective-permute-start.3 = (bf16[192,1152]{1,0:T(8,128)(2,1)}, bf16[192,1152]{1,0:T(8,128)(2,1)S(1)}, u32[]{:S(2)}, u32[]{:S(2)}) collective-permute-start(bf16[192,1152]{1,0:T(8,128)(2,1)} %bitcast.83), channel_id=1, source_target_pairs={{0,4},{8,0},{16,8},{24,16},{28,24},{20,28},{12,20},{4,12},{1,5},{9... | collective-permute-start | bytes 1327112 | tf_op jit(solution)/shard_map/ppermute | solution.py:141
  7.6 18.1 %copy-start.5 = (bf16[384,192]{0,1:T(8,128)(2,1)S(1)}, bf16[384,192]{0,1:T(8,128)(2,1)}, u32[]{:S(2)}) copy-start(bf16[384,192]{0,1:T(8,128)(2,1)} %param.23) | copy-start | bytes 442372
  7.6 28.0 %collective-permute-start = (bf16[128,1536]{1,0:T(8,128)(2,1)S(1)}, bf16[128,1536]{1,0:T(8,128)(2,1)}, u32[]{:S(2)}, u32[]{:S(2)}) collective-permute-start(bf16[128,1536]{1,0:T(8,128)(2,1)S(1)} %fusion.18), channel_id=1, source_target_pairs={{0,2},{1,3},{2,0},{3,1},{4,6},{5,7},{6,4},{7,5},{8,10},{9,11},{10,... | collective-permute-start | bytes 1179656 | tf_op jit(solution)/shard_map/ppermute | solution.py:36
  9.7 16.5 %copy-start.4 = (bf16[192,2,384]{2,1,0:T(2,128)(2,1)S(1)}, bf16[192,2,384]{2,1,0:T(2,128)(2,1)}, u32[]{:S(2)}) copy-start(bf16[192,2,384]{2,1,0:T(2,128)(2,1)} %param.21) | copy-start | bytes 884740
  10.0 16.1 %copy-start.6 = (bf16[31,384]{1,0:T(8,128)(2,1)S(1)}, bf16[31,384]{1,0:T(8,128)(2,1)}, u32[]{:S(2)}) copy-start(bf16[31,384]{1,0:T(8,128)(2,1)} %param.22) | copy-start | bytes 71428
  36.7 16.5 %collective-permute-start.1 = (bf16[2,128,1536]{2,1,0:T(8,128)(2,1)S(1)}, bf16[2,128,1536]{2,1,0:T(8,128)(2,1)S(1)}, u32[]{:S(2)}, u32[]{:S(2)}) collective-permute-start(bf16[2,128,1536]{2,1,0:T(8,128)(2,1)S(1)} %get-tuple-element.69), channel_id=1, source_target_pairs={{0,1},{1,0},{2,3},{3,2},{4,5},{5,4},{6,7},{7,6},{8,9},{9,8},{10,11... | collective-permute-start | bytes 2359304 | tf_op jit(solution)/shard_map/ppermute | solution.py:42
  36.8 12.8 %collective-permute-start.4 = (bf16[192,1152]{1,0:T(8,128)(2,1)}, bf16[192,1152]{1,0:T(8,128)(2,1)S(1)}, u32[]{:S(2)}, u32[]{:S(2)}) collective-permute-start(bf16[192,1152]{1,0:T(8,128)(2,1)} %collective-permute-done.2), channel_id=1, source_target_pairs={{0,8},{8,16},{16,24},{24,28},{28,20},{20,12},{12,4},{4,0},{1,9},{9... | collective-permute-start | bytes 1327112 | tf_op jit(solution)/shard_map/ppermute | solution.py:138
  38.5 12.7 %collective-permute-start.5 = (bf16[192,1152]{1,0:T(8,128)(2,1)S(1)}, bf16[192,1152]{1,0:T(8,128)(2,1)S(1)}, u32[]{:S(2)}, u32[]{:S(2)}) collective-permute-start(bf16[192,1152]{1,0:T(8,128)(2,1)S(1)} %collective-permute-done.3), channel_id=1, source_target_pairs={{0,4},{8,0},{16,8},{24,16},{28,24},{20,28},{12,20},{4,12},{1,5},{9... | collective-permute-start | bytes 1327112 | tf_op jit(solution)/shard_map/ppermute | solution.py:141
  49.6 11.7 %collective-permute-start.6 = (bf16[192,1152]{1,0:T(8,128)(2,1)S(1)}, bf16[192,1152]{1,0:T(8,128)(2,1)S(1)}, u32[]{:S(2)}, u32[]{:S(2)}) collective-permute-start(bf16[192,1152]{1,0:T(8,128)(2,1)S(1)} %collective-permute-done.4), channel_id=1, source_target_pairs={{0,8},{8,16},{16,24},{24,28},{28,20},{20,12},{12,4},{4,0},{1,9},{9... | collective-permute-start | bytes 1327112 | tf_op jit(solution)/shard_map/ppermute | solution.py:138
  51.2 12.5 %collective-permute-start.7 = (bf16[192,1152]{1,0:T(8,128)(2,1)S(1)}, bf16[192,1152]{1,0:T(8,128)(2,1)S(1)}, u32[]{:S(2)}, u32[]{:S(2)}) collective-permute-start(bf16[192,1152]{1,0:T(8,128)(2,1)S(1)} %collective-permute-done.5), channel_id=1, source_target_pairs={{0,4},{8,0},{16,8},{24,16},{28,24},{20,28},{12,20},{4,12},{1,5},{9... | collective-permute-start | bytes 1327112 | tf_op jit(solution)/shard_map/ppermute | solution.py:141
  61.3 10.8 %collective-permute-start.8 = (bf16[192,1152]{1,0:T(8,128)(2,1)S(1)}, bf16[192,1152]{1,0:T(8,128)(2,1)S(1)}, u32[]{:S(2)}, u32[]{:S(2)}) collective-permute-start(bf16[192,1152]{1,0:T(8,128)(2,1)S(1)} %collective-permute-done.6), channel_id=1, source_target_pairs={{0,8},{8,16},{16,24},{24,28},{28,20},{20,12},{12,4},{4,0},{1,9},{9... | collective-permute-start | bytes 1327112 | tf_op jit(solution)/shard_map/ppermute | solution.py:138
  72.9 14.2 %collective-permute-start.9 = (bf16[384,192]{0,1:T(8,128)(2,1)}, bf16[384,192]{0,1:T(8,128)(2,1)}, u32[]{:S(2)}, u32[]{:S(2)}) collective-permute-start(bf16[384,192]{0,1:T(8,128)(2,1)} %param.20), channel_id=1, source_target_pairs={{0,8},{8,16},{16,24},{24,28},{28,20},{20,12},{12,4},{4,0},{1,9},{9... | collective-permute-start | bytes 442376 | tf_op jit(solution)/shard_map/ppermute | solution.py:138
  74.5 15.3 %collective-permute-start.10 = (bf16[384,192]{0,1:T(8,128)(2,1)}, bf16[384,192]{0,1:T(8,128)(2,1)}, u32[]{:S(2)}, u32[]{:S(2)}) collective-permute-start(bf16[384,192]{0,1:T(8,128)(2,1)} %param.20), channel_id=1, source_target_pairs={{0,4},{8,0},{16,8},{24,16},{28,24},{20,28},{12,20},{4,12},{1,5},{9... | collective-permute-start | bytes 442376 | tf_op jit(solution)/shard_map/ppermute | solution.py:141
  87.2 6.7 %collective-permute-start.11 = (bf16[384,192]{0,1:T(8,128)(2,1)}, bf16[384,192]{0,1:T(8,128)(2,1)S(1)}, u32[]{:S(2)}, u32[]{:S(2)}) collective-permute-start(bf16[384,192]{0,1:T(8,128)(2,1)} %collective-permute-done.9), channel_id=1, source_target_pairs={{0,8},{8,16},{16,24},{24,28},{28,20},{20,12},{12,4},{4,0},{1,9},{9... | collective-permute-start | bytes 442376 | tf_op jit(solution)/shard_map/ppermute | solution.py:138
  89.8 6.7 %collective-permute-start.12 = (bf16[384,192]{0,1:T(8,128)(2,1)}, bf16[384,192]{0,1:T(8,128)(2,1)S(1)}, u32[]{:S(2)}, u32[]{:S(2)}) collective-permute-start(bf16[384,192]{0,1:T(8,128)(2,1)} %collective-permute-done.10), channel_id=1, source_target_pairs={{0,4},{8,0},{16,8},{24,16},{28,24},{20,28},{12,20},{4,12},{1,5},{9... | collective-permute-start | bytes 442376 | tf_op jit(solution)/shard_map/ppermute | solution.py:141
  93.9 6.2 %collective-permute-start.13 = (bf16[384,192]{0,1:T(8,128)(2,1)S(1)}, bf16[384,192]{0,1:T(8,128)(2,1)S(1)}, u32[]{:S(2)}, u32[]{:S(2)}) collective-permute-start(bf16[384,192]{0,1:T(8,128)(2,1)S(1)} %collective-permute-done.11), channel_id=1, source_target_pairs={{0,8},{8,16},{16,24},{24,28},{28,20},{20,12},{12,4},{4,0},{1,9},{9... | collective-permute-start | bytes 442376 | tf_op jit(solution)/shard_map/ppermute | solution.py:138
  96.5 5.2 %collective-permute-start.14 = (bf16[384,192]{0,1:T(8,128)(2,1)S(1)}, bf16[384,192]{0,1:T(8,128)(2,1)S(1)}, u32[]{:S(2)}, u32[]{:S(2)}) collective-permute-start(bf16[384,192]{0,1:T(8,128)(2,1)S(1)} %collective-permute-done.12), channel_id=1, source_target_pairs={{0,4},{8,0},{16,8},{24,16},{28,24},{20,28},{12,20},{4,12},{1,5},{9... | collective-permute-start | bytes 442376 | tf_op jit(solution)/shard_map/ppermute | solution.py:141
  100.0 5.1 %collective-permute-start.15 = (bf16[384,192]{0,1:T(8,128)(2,1)S(1)}, bf16[384,192]{0,1:T(8,128)(2,1)S(1)}, u32[]{:S(2)}, u32[]{:S(2)}) collective-permute-start(bf16[384,192]{0,1:T(8,128)(2,1)S(1)} %collective-permute-done.13), channel_id=1, source_target_pairs={{0,8},{8,16},{16,24},{24,28},{28,20},{20,12},{12,4},{4,0},{1,9},{9... | collective-permute-start | bytes 442376 | tf_op jit(solution)/shard_map/ppermute | solution.py:138
  106.3 14.8 %collective-permute-start.16 = (bf16[2,128,1536]{2,1,0:T(8,128)(2,1)S(1)}, bf16[2,128,1536]{2,1,0:T(8,128)(2,1)S(1)}, u32[]{:S(2)}, u32[]{:S(2)}) collective-permute-start(bf16[2,128,1536]{2,1,0:T(8,128)(2,1)S(1)} %dynamic-slice_bitcast_fusion.1), channel_id=1, source_target_pairs={{0,1},{1,0},{2,3},{3,2},{4,5},{5,4},{6,7},{7,6},{8,9},{9,8},{10,11... | collective-permute-start | bytes 2359304 | tf_op jit(solution)/shard_map/ppermute | solution.py:78
  106.5 12.6 %collective-permute-start.20 = (bf16[288,768]{1,0:T(8,128)(2,1)S(1)}, bf16[288,768]{1,0:T(8,128)(2,1)S(1)}, u32[]{:S(2)}, u32[]{:S(2)}) collective-permute-start(bf16[288,768]{1,0:T(8,128)(2,1)S(1)} %pad_maximum_fusion), channel_id=1, source_target_pairs={{0,8},{8,16},{16,24},{24,28},{28,20},{20,12},{12,4},{4,0},{1,9},{9... | collective-permute-start | bytes 1327112 | tf_op jit(solution)/shard_map/ppermute | solution.py:138
  108.1 12.6 %collective-permute-start.21 = (bf16[288,768]{1,0:T(8,128)(2,1)S(1)}, bf16[288,768]{1,0:T(8,128)(2,1)S(1)}, u32[]{:S(2)}, u32[]{:S(2)}) collective-permute-start(bf16[288,768]{1,0:T(8,128)(2,1)S(1)} %pad_maximum_fusion), channel_id=1, source_target_pairs={{0,4},{8,0},{16,8},{24,16},{28,24},{20,28},{12,20},{4,12},{1,5},{9... | collective-permute-start | bytes 1327112 | tf_op jit(solution)/shard_map/ppermute | solution.py:141
  119.1 11.8 %collective-permute-start.22 = (bf16[288,768]{1,0:T(8,128)(2,1)S(1)}, bf16[288,768]{1,0:T(8,128)(2,1)S(1)}, u32[]{:S(2)}, u32[]{:S(2)}) collective-permute-start(bf16[288,768]{1,0:T(8,128)(2,1)S(1)} %collective-permute-done.20), channel_id=1, source_target_pairs={{0,8},{8,16},{16,24},{24,28},{28,20},{20,12},{12,4},{4,0},{1,9},{9... | collective-permute-start | bytes 1327112 | tf_op jit(solution)/shard_map/ppermute | solution.py:138
  120.7 11.8 %collective-permute-start.23 = (bf16[288,768]{1,0:T(8,128)(2,1)S(1)}, bf16[288,768]{1,0:T(8,128)(2,1)S(1)}, u32[]{:S(2)}, u32[]{:S(2)}) collective-permute-start(bf16[288,768]{1,0:T(8,128)(2,1)S(1)} %collective-permute-done.21), channel_id=1, source_target_pairs={{0,4},{8,0},{16,8},{24,16},{28,24},{20,28},{12,20},{4,12},{1,5},{9... | collective-permute-start | bytes 1327112 | tf_op jit(solution)/shard_map/ppermute | solution.py:141
  121.5 11.5 %collective-permute-start.17 = (bf16[128,1536]{1,0:T(8,128)(2,1)S(1)}, bf16[128,1536]{1,0:T(8,128)(2,1)S(1)}, u32[]{:S(2)}, u32[]{:S(2)}) collective-permute-start(bf16[128,1536]{1,0:T(8,128)(2,1)S(1)} %fusion.31), channel_id=1, source_target_pairs={{0,2},{1,3},{2,0},{3,1},{4,6},{5,7},{6,4},{7,5},{8,10},{9,11},{10,... | collective-permute-start | bytes 1179656 | tf_op jit(solution)/shard_map/ppermute | solution.py:84
  130.9 14.8 %collective-permute-start.24 = (bf16[288,768]{1,0:T(8,128)(2,1)S(1)}, bf16[288,768]{1,0:T(8,128)(2,1)S(1)}, u32[]{:S(2)}, u32[]{:S(2)}) collective-permute-start(bf16[288,768]{1,0:T(8,128)(2,1)S(1)} %collective-permute-done.22), channel_id=1, source_target_pairs={{0,8},{8,16},{16,24},{24,28},{28,20},{20,12},{12,4},{4,0},{1,9},{9... | collective-permute-start | bytes 1327112 | tf_op jit(solution)/shard_map/ppermute | solution.py:138
  132.5 14.9 %collective-permute-start.25 = (bf16[288,768]{1,0:T(8,128)(2,1)S(1)}, bf16[288,768]{1,0:T(8,128)(2,1)S(1)}, u32[]{:S(2)}, u32[]{:S(2)}) collective-permute-start(bf16[288,768]{1,0:T(8,128)(2,1)S(1)} %collective-permute-done.23), channel_id=1, source_target_pairs={{0,4},{8,0},{16,8},{24,16},{28,24},{20,28},{12,20},{4,12},{1,5},{9... | collective-permute-start | bytes 1327112 | tf_op jit(solution)/shard_map/ppermute | solution.py:141
  132.9 1.5 copy-start.9
  135.5 9.3 %collective-permute-start.18 = (bf16[128,1536]{1,0:T(8,128)(2,1)S(1)}, bf16[128,1536]{1,0:T(8,128)(2,1)S(1)}, u32[]{:S(2)}, u32[]{:S(2)}) collective-permute-start(bf16[128,1536]{1,0:T(8,128)(2,1)S(1)} %get-tuple-element.62), channel_id=1, source_target_pairs={{0,2},{1,3},{2,0},{3,1},{4,6},{5,7},{6,4},{7,5},{8,10},{9,11},{10,... | collective-permute-start | bytes 1179656 | tf_op jit(solution)/shard_map/ppermute | solution.py:36
  145.6 12.7 %copy-start.3 = (bf16[4,128,1536]{2,1,0:T(8,128)(2,1)}, bf16[4,128,1536]{2,1,0:T(8,128)(2,1)S(1)}, u32[]{:S(2)}) copy-start(bf16[4,128,1536]{2,1,0:T(8,128)(2,1)S(1)} %get-tuple-element.68) | copy-start | bytes 4718596
  145.6 20.9 %collective-permute-start.19 = (bf16[2,128,1536]{2,1,0:T(8,128)(2,1)}, bf16[2,128,1536]{2,1,0:T(8,128)(2,1)}, u32[]{:S(2)}, u32[]{:S(2)}) collective-permute-start(bf16[2,128,1536]{2,1,0:T(8,128)(2,1)} %get-tuple-element.67), channel_id=1, source_target_pairs={{0,1},{1,0},{2,3},{3,2},{4,5},{5,4},{6,7},{7,6},{8,9},{9,8},{10,11... | collective-permute-start | bytes 2359304 | tf_op jit(solution)/shard_map/ppermute | solution.py:42
  145.6 12.6 %collective-permute-start.26 = (bf16[288,768]{1,0:T(8,128)(2,1)S(1)}, bf16[288,768]{1,0:T(8,128)(2,1)S(1)}, u32[]{:S(2)}, u32[]{:S(2)}) collective-permute-start(bf16[288,768]{1,0:T(8,128)(2,1)S(1)} %collective-permute-done.24), channel_id=1, source_target_pairs={{0,8},{8,16},{16,24},{24,28},{28,20},{20,12},{12,4},{4,0},{1,9},{9... | collective-permute-start | bytes 1327112 | tf_op jit(solution)/shard_map/ppermute | solution.py:138
  173.6 0.7 copy-start.10
  173.6 0.7 copy-start.11
  173.7 0.7 copy-start.12
  173.7 0.7 copy-start.13
  173.7 0.7 copy-start.14
  173.7 0.7 copy-start.19
  173.7 0.7 copy-start.20
  173.8 6.2 %copy-start.1 = (bf16[384,8,192]{0,2,1:T(8,128)(2,1)S(1)}, bf16[384,8,192]{0,2,1:T(8,128)(2,1)}, u32[]{:S(2)}) copy-start(bf16[384,8,192]{0,2,1:T(8,128)(2,1)} %copy.46) | copy-start | bytes 3538948
  181.1 2.4 %collective-permute-start.27 = (bf16[2,128,1536]{2,1,0:T(8,128)(2,1)S(1)}, bf16[2,128,1536]{2,1,0:T(8,128)(2,1)S(1)}, u32[]{:S(2)}, u32[]{:S(2)}) collective-permute-start(bf16[2,128,1536]{2,1,0:T(8,128)(2,1)S(1)} %dynamic-slice_bitcast_fusion), channel_id=1, source_target_pairs={{0,1},{1,0},{2,3},{3,2},{4,5},{5,4},{6,7},{7,6},{8,9},{9,8},{10,11... | collective-permute-start | bytes 2359304 | tf_op jit(solution)/shard_map/ppermute | solution.py:78
  183.8 11.2 %collective-permute-start.28 = (bf16[128,1536]{1,0:T(8,128)(2,1)S(1)}, bf16[128,1536]{1,0:T(8,128)(2,1)S(1)}, u32[]{:S(2)}, u32[]{:S(2)}) collective-permute-start(bf16[128,1536]{1,0:T(8,128)(2,1)S(1)} %fusion.32), channel_id=1, source_target_pairs={{0,2},{1,3},{2,0},{3,1},{4,6},{5,7},{6,4},{7,5},{8,10},{9,11},{10,... | collective-permute-start | bytes 1179656 | tf_op jit(solution)/shard_map/ppermute | solution.py:84
  (14 other events, 9.2 us)

commit v9 on v8

--- a/solution.py
+++ b/solution.py
@@ -200,16 +200,13 @@
     kernel_reach = dw_kernel.shape[0] // 2
     qkv_parts = ring_gather(w_qkv.reshape(w_qkv.shape[0], 3 * group_width), ring)
     qkv_matrix = qkv_parts.reshape(model_width, 3 * group_width)
-    out_parts = ring_gather(after(qkv_parts, w_out), ring)
-    out_local = jnp.einsum("nrc->rnc", out_parts).reshape(w_out.shape[0], model_width)
+    out_parts = ring_gather(after(qkv_parts, w_out.T), ring)
+    out_cols = out_parts.reshape(model_width, w_out.shape[0])
     glu_rows = w_glu.shape[0]
     glu_local = w_glu.reshape(glu_rows, 2 * group_width)
-    both_parts = ring_gather(
-        after(out_parts, jnp.concatenate([glu_local, w_proj.reshape(-1, 2 * group_width)])), ring
-    )
-    glu_matrix = both_parts[:, :glu_rows].reshape(model_width, 2 * group_width)
-    proj_parts = both_parts[:, glu_rows:].reshape(-1, *w_proj.shape)
-    proj_local = jnp.einsum("nrc->rnc", proj_parts).reshape(w_proj.shape[0], model_width)
+    both_parts = ring_gather(after(out_parts, jnp.concatenate([glu_local, w_proj.T], axis=1)), ring)
+    glu_matrix = both_parts[:, :, : 2 * group_width].reshape(model_width, 2 * group_width)
+    proj_cols = both_parts[:, :, 2 * group_width :].reshape(model_width, w_proj.shape[0])
     inputs = frames[0].astype(jnp.float32)
     record_ends = jnp.cumsum(lengths[0])
     seg_all = segment_of(record_ends, jnp.arange(group_rows, dtype=jnp.int32))
@@ -221,7 +218,7 @@
     )
     attended = attend(projected, seg_all, HD)
     attn_sum = seq_scatter_sum(
-        jnp.dot(attended, out_local, preferred_element_type=jnp.float32).astype(jnp.bfloat16),
+        jnp.dot(attended, out_cols.T, preferred_element_type=jnp.float32).astype(jnp.bfloat16),
         paired,
     )
     middle = (inputs + attn_sum).astype(jnp.bfloat16)
@@ -238,7 +235,7 @@
     )
     activated = lax.optimization_barrier(activated)
     conv_out = seq_scatter_sum(
-        jnp.dot(activated, proj_local, preferred_element_type=jnp.float32).astype(jnp.bfloat16),
+        jnp.dot(activated, proj_cols.T, preferred_element_type=jnp.float32).astype(jnp.bfloat16),
         paired,
     )
     results = [(middle.astype(jnp.float32) + conv_out).astype(jnp.bfloat16)]

time: 197 us -> 183 us (0.929)
  waiting for transfers between devices: 85 us -> 74.9 us
  local copies, waits for them, and re-layouts: 33.9 us -> 28.9 us
    ppermute x2, waiting for transfers between devices: 8.55 us -> 0.01 us  [seq_gather(): lax.ppermute(block, 'seq', [(i, (i + 2 * shift) % count) for i in range(c...]
    reshape x2 -> x0, local copies, waits for them, and re-layouts: 3.19 us -> none  [the longest x1 2.97 us: on_device(): proj_parts = both_parts[:, glu_rows:].reshape(-1, *w_proj.shape)]
    another operation x4 -> x6, local copies, waits for them, and re-layouts: 1.25 us -> 3.89 us
    broadcast_in_dim x3 -> x1, local copies, waits for them, and re-layouts: 2.54 us -> 0.1 us  [ring_gather(): out = jnp.zeros((count,) + block.shape, block.dtype)]
    ppermute x12, waiting for transfers between devices: 62.6 us -> 60.5 us  [ring_gather(): ahead = lax.ppermute(ahead, 'dp', forward)]
  transfers between devices with their start and end apart: 29 -> 29, of which waited for: 13 -> 15; matrix products, arithmetic and copies ran while one was open for 23% -> 23% of each run, Pallas kernels for 0% -> 0%
where the time goes in v9:
time: 183 us; the launch traced here: 182 us
  waiting for transfers between devices  74.9 us (41%)
  local copies, waits for them, and re-layouts  28.9 us (16%)
  starting transfers between devices  28.5 us (16%)
  between operations  18.7 us (10%)
  matrix products  16.1 us (9%)
  other arithmetic  15 us (8%)
    ppermute x12, waiting for transfers between devices, ring_gather(): ahead = lax.ppermute(ahead, 'dp', forward)  60.5 us
    ppermute x12, starting transfers between devices, ring_gather(): ahead = lax.ppermute(ahead, 'dp', forward)  20.7 us
    ppermute x2, waiting for transfers between devices, seq_scatter_sum(): lax.ppermute(piece.astype(jnp.bfloat16), 'seq', [(i, (i + 2 * shift) % co...  10.6 us
    convert_element_type x1, other arithmetic, depthwise(): return jax.nn.silu(total_acc).astype(jnp.bfloat16)  5.5 us
    dynamic_update_slice x12, local copies, waits for them, and re-layouts, ring_gather(): lax.dynamic_update_index_in_dim(out, ahead, order[(my_pos - step) % count...  4.43 us
    dot_general x1, matrix products, on_device(): jnp.dot(seq_gather(normed1, paired).reshape(group_rows, model_width), qkv...  4.19 us
    another operation x6, local copies, waits for them, and re-layouts  3.89 us
    ppermute x9, starting transfers between devices, ring_gather(): behind = lax.ppermute(behind, 'dp', backward)  3.78 us
  transfers between devices with their start and end apart: 29, of which 15 were waited for; matrix products, arithmetic and copies ran while one was open for 23% of the time, Pallas kernels for 0%

profile of v9, /device:TPU:0, one launch (start us, length us, event | category | flops | bytes accessed | tf_op | source)
XLA Modules:
  0.0 182.1 jit_solution(14810532877839939323)
XLA Ops:
  0.0 1.1 copy.53
  1.2 3.1 %collective-permute-start.2 = (bf16[192,1152]{1,0:T(8,128)(2,1)S(1)}, bf16[192,1152]{1,0:T(8,128)(2,1)S(1)}, u32[]{:S(2)}, u32[]{:S(2)}) collective-permute-start(bf16[192,1152]{1,0:T(8,128)(2,1)S(1)} %bitcast.193), channel_id=1, source_target_pairs={{0,8},{8,16},{16,24},{24,28},{28,20},{20,12},{12,4},{4,0},{1,9},{9... | collective-permute-start | bytes 1327112 | tf_op jit(solution)/shard_map/ppermute | solution.py:138
  4.3 1.1 convert_reduce_fusion.1
  5.4 1.2 fusion.16
  7.0 2.0 %collective-permute-start = (bf16[128,1536]{1,0:T(8,128)(2,1)S(1)}, bf16[128,1536]{1,0:T(8,128)(2,1)}, u32[]{:S(2)}, u32[]{:S(2)}) collective-permute-start(bf16[128,1536]{1,0:T(8,128)(2,1)S(1)} %fusion.18), channel_id=1, source_target_pairs={{0,2},{1,3},{2,0},{3,1},{4,6},{5,7},{6,4},{7,5},{8,10},{9,11},{10,... | collective-permute-start | bytes 1179656 | tf_op jit(solution)/shard_map/ppermute | solution.py:36
  27.9 1.0 copy.54
  28.9 2.2 %broadcast.165.clone = bf16[8,192,1152]{2,1,0:T(8,128)(2,1)} broadcast(bf16[]{:T(256)} %constant.338.clone.1), dimensions={} | broadcast | bytes 3538946 | tf_op jit(solution)/shard_map/broadcast.15
  36.9 1.1 bitcast_dynamic-update-slice_fusion.19
  38.0 1.6 collective-permute-start.4
  41.7 8.9 %collective-permute-done.4 = bf16[192,1152]{1,0:T(8,128)(2,1)S(1)} collective-permute-done((bf16[192,1152]{1,0:T(8,128)(2,1)S(1)}, bf16[192,1152]{1,0:T(8,128)(2,1)S(1)}, u32[]{:S(2)}, u32[]{:S(2)}) %collective-permute-start.4) | collective-permute-done | bytes 442400 | tf_op jit(solution)/shard_map/ppermute | solution.py:138
  50.6 1.6 collective-permute-start.6
  54.3 8.0 %collective-permute-done.6 = bf16[192,1152]{1,0:T(8,128)(2,1)S(1)} collective-permute-done((bf16[192,1152]{1,0:T(8,128)(2,1)S(1)}, bf16[192,1152]{1,0:T(8,128)(2,1)S(1)}, u32[]{:S(2)}, u32[]{:S(2)}) %collective-permute-start.6) | collective-permute-done | bytes 442400 | tf_op jit(solution)/shard_map/ppermute | solution.py:138
  62.3 1.6 collective-permute-start.8
  65.5 7.6 %collective-permute-done.8 = bf16[192,1152]{1,0:T(8,128)(2,1)S(1)} collective-permute-done((bf16[192,1152]{1,0:T(8,128)(2,1)S(1)}, bf16[192,1152]{1,0:T(8,128)(2,1)S(1)}, u32[]{:S(2)}, u32[]{:S(2)}) %collective-permute-start.8) | collective-permute-done | bytes 442400 | tf_op jit(solution)/shard_map/ppermute | solution.py:138
  73.9 1.6 collective-permute-start.9
  75.9 4.2 %convolution_convert_fusion = bf16[512,1152]{1,0:T(8,128)(2,1)S(1)} fusion(bf16[512,1536]{1,0:T(8,128)(2,1)S(1)} %bitcast.188, bf16[1536,1152]{1,0:T(8,128)(2,1)} %bitcast.24), kind=kOutput, calls=%fused_computation.5 | convolution fusion | flops 1812529152 | bytes 6291456 | tf_op jit(solution)/shard_map/dot_general | solution.py:215
  81.1 3.6 %fusion.41 = (f32[4,512]{1,0:T(4,128)S(1)}, f32[4,512,512]{1,2,0:T(8,128)}) fusion(pred[512,512]{0,1:T(8,128)(4,1)S(1)} %copy-done.4, bf16[512,3,4,96]{0,3,2,1:T(8,128)(2,1)S(1)} %bitcast.191), kind=kOutput, calls=%fused_computation.176 | convolution fusion | flops 205521408 | bytes 5251072 | tf_op jit(solution)/shard_map/while/body/eval_jaxpr/sub | solution.py:170
  84.7 2.7 %fusion.6 = bf16[4,96,512]{2,1,0:T(8,128)(2,1)S(1)} fusion(f32[4,512,512]{1,2,0:T(8,128)} %get-tuple-element.110, f32[4,512]{1,0:T(4,128)S(1)} %get-tuple-element.109, bf16[512,3,4,96]{0,3,2,1:T(8,128)(2,1)S(1)} %bitcast.192), kind=kOutput, calls=%fused_computation.14 | convolution fusion | flops 203620352 | bytes 4988928 | tf_op jit(solution)/shard_map/while/body/eval_jaxpr/hqk,khe->qhe/dot_general | solution.py:172
  87.5 0.9 bitcast_dynamic-update-slice_fusion.28
  88.5 1.6 collective-permute-start.11
  90.1 1.0 bitcast_dynamic-update-slice_fusion.27
  91.6 1.0 bitcast_dynamic-update-slice_fusion.26
  92.6 2.6 %collective-permute-done.11 = bf16[192,384]{1,0:T(8,128)(2,1)S(1)} collective-permute-done((bf16[192,384]{1,0:T(8,128)(2,1)}, bf16[192,384]{1,0:T(8,128)(2,1)S(1)}, u32[]{:S(2)}, u32[]{:S(2)}) %collective-permute-start.11) | collective-permute-done | bytes 147488 | tf_op jit(solution)/shard_map/ppermute | solution.py:138
  95.2 1.6 collective-permute-start.13
  96.8 1.0 collective-permute-done.12
  98.4 3.0 %collective-permute-done.13 = bf16[192,384]{1,0:T(8,128)(2,1)S(1)} collective-permute-done((bf16[192,384]{1,0:T(8,128)(2,1)S(1)}, bf16[192,384]{1,0:T(8,128)(2,1)S(1)}, u32[]{:S(2)}, u32[]{:S(2)}) %collective-permute-start.13) | collective-permute-done | bytes 147488 | tf_op jit(solution)/shard_map/ppermute | solution.py:138
  101.3 1.6 collective-permute-start.15
  103.0 5.1 %collective-permute-done.15 = bf16[192,384]{1,0:T(8,128)(2,1)S(1)} collective-permute-done((bf16[192,384]{1,0:T(8,128)(2,1)S(1)}, bf16[192,384]{1,0:T(8,128)(2,1)S(1)}, u32[]{:S(2)}, u32[]{:S(2)}) %collective-permute-start.15) | collective-permute-done | bytes 147488 | tf_op jit(solution)/shard_map/ppermute | solution.py:138
  108.1 1.6 collective-permute-start.20
  110.2 1.0 convolution_convert_fusion.2
  111.9 6.0 %collective-permute-done.20 = bf16[192,1152]{1,0:T(8,128)(2,1)S(1)} collective-permute-done((bf16[192,1152]{1,0:T(8,128)(2,1)S(1)}, bf16[192,1152]{1,0:T(8,128)(2,1)S(1)}, u32[]{:S(2)}, u32[]{:S(2)}) %collective-permute-start.20) | collective-permute-done | bytes 442400 | tf_op jit(solution)/shard_map/ppermute | solution.py:138
  117.9 1.6 collective-permute-start.22
  121.2 7.4 %collective-permute-done.22 = bf16[192,1152]{1,0:T(8,128)(2,1)S(1)} collective-permute-done((bf16[192,1152]{1,0:T(8,128)(2,1)S(1)}, bf16[192,1152]{1,0:T(8,128)(2,1)S(1)}, u32[]{:S(2)}, u32[]{:S(2)}) %collective-permute-start.22) | collective-permute-done | bytes 442400 | tf_op jit(solution)/shard_map/ppermute | solution.py:138
  128.6 1.6 collective-permute-start.24
  131.5 1.0 broadcast.164
  132.5 1.0 bitcast_dynamic-update-slice_fusion.17
  134.3 6.2 %collective-permute-done.24 = bf16[192,1152]{1,0:T(8,128)(2,1)S(1)} collective-permute-done((bf16[192,1152]{1,0:T(8,128)(2,1)S(1)}, bf16[192,1152]{1,0:T(8,128)(2,1)S(1)}, u32[]{:S(2)}, u32[]{:S(2)}) %collective-permute-start.24) | collective-permute-done | bytes 442400 | tf_op jit(solution)/shard_map/ppermute | solution.py:138
  140.5 1.6 collective-permute-start.26
  143.0 5.8 %collective-permute-done.26 = bf16[192,1152]{1,0:T(8,128)(2,1)S(1)} collective-permute-done((bf16[192,1152]{1,0:T(8,128)(2,1)S(1)}, bf16[192,1152]{1,0:T(8,128)(2,1)S(1)}, u32[]{:S(2)}, u32[]{:S(2)}) %collective-permute-start.26) | collective-permute-done | bytes 442400 | tf_op jit(solution)/shard_map/ppermute | solution.py:138
  149.0 1.2 slice.423
  150.2 2.4 %copy.48 = bf16[768,1536]{1,0:T(8,128)(2,1)} copy(bf16[768,1536]{0,1:T(8,128)(2,1)S(1)} %bitcast.179) | data formatting | bytes 4718592 | tf_op jit(solution)/shard_map/dot_general | solution.py:227
  152.6 1.8 slice_dynamic-update-slice_fusion.1
  154.4 1.8 slice_dynamic-update-slice_fusion
  156.1 3.6 %fusion.42 = f32[512,2,384]{2,0,1:T(8,128)S(1)} fusion(bf16[512,1536,1]{1,0,2:T(8,128)(2,1)} %bitcast.189, bf16[2,384,1536]{2,1,0:T(8,128)(2,1)} %bitcast.186), kind=kOutput, calls=%fused_computation.177 | convolution fusion | flops 1207959552 | bytes 5505024 | tf_op jit(solution)/shard_map/dot_general | solution.py:227
  160.8 5.5 %multiply_convert_fusion = bf16[512,384]{1,0:T(8,128)(2,1)S(1)} fusion(bf16[512,384]{1,0:T(8,128)(2,1)S(1)} %fusion.34, f32[384]{0:T(512)S(1)} %copy-done.15, f32[384]{0:T(512)S(1)} %copy-done.16, f32[384]{0:T(512)S(1)} %get-tuple-element.30, f32[384]{0:T(512)S(1)} %get-tuple-element.32, f32[384]{0:T(512)S(1)} %get-tuple-element.33, ...), kind=kLoop, calls=%fused_computation.47 | loop fusion | flops 25165824 | bytes 849920 | tf_op jit(solution)/shard_map/convert_element_type | solution.py:191
  166.3 1.0 convolution_convert_fusion.1
  167.5 2.3 %collective-permute-done.27 = bf16[2,128,1536]{2,1,0:T(8,128)(2,1)S(1)} collective-permute-done((bf16[2,128,1536]{2,1,0:T(8,128)(2,1)S(1)}, bf16[2,128,1536]{2,1,0:T(8,128)(2,1)S(1)}, u32[]{:S(2)}, u32[]{:S(2)}) %collective-permute-start.27) | collective-permute-done | bytes 786464 | tf_op jit(solution)/shard_map/ppermute | solution.py:78
  170.6 10.6 %collective-permute-done.28 = bf16[128,1536]{1,0:T(8,128)(2,1)S(1)} collective-permute-done((bf16[128,1536]{1,0:T(8,128)(2,1)S(1)}, bf16[128,1536]{1,0:T(8,128)(2,1)S(1)}, u32[]{:S(2)}, u32[]{:S(2)}) %collective-permute-start.28) | collective-permute-done | bytes 393248 | tf_op jit(solution)/shard_map/ppermute | solution.py:84
  (194 shorter events, 25.0 us)
Async XLA Ops:
  0.0 9.0 %copy-start.2 = (bf16[192,3,384]{2,0,1:T(8,128)(2,1)S(1)}, bf16[192,3,384]{2,0,1:T(8,128)(2,1)}, u32[]{:S(2)}) copy-start(bf16[192,3,384]{2,0,1:T(8,128)(2,1)} %param.19) | copy-start | bytes 1327108
  0.0 6.7 %copy-start = (bf16[1,128,1536]{2,1,0:T(8,128)(2,1)S(1)}, bf16[1,128,1536]{2,1,0:T(8,128)(2,1)}, u32[]{:S(2)}) copy-start(bf16[1,128,1536]{2,1,0:T(8,128)(2,1)} %param.15) | copy-start | bytes 1179652
  0.0 6.7 %copy-start.7 = (f32[1536]{0:T(1024)S(1)}, f32[1536]{0:T(1024)}, u32[]{:S(2)}) copy-start(f32[1536]{0:T(1024)} %param.17) | copy-start | bytes 18436
  1.1 8.2 %copy-start.49 = (s32[8]{0:T(128)S(1)}, s32[8]{0:T(128)}, u32[]{:S(2)}) copy-start(s32[8]{0:T(128)} %constant.367.clone) | copy-start | bytes 100
  1.2 13.5 %copy-start.8 = (s32[8]{0:T(128)S(1)}, s32[8]{0:T(128)}, u32[]{:S(2)}) copy-start(s32[8]{0:T(128)} %constant.368.clone) | copy-start | bytes 100
  1.2 22.9 %copy-start.6 = (bf16[31,384]{1,0:T(8,128)(2,1)S(1)}, bf16[31,384]{1,0:T(8,128)(2,1)}, u32[]{:S(2)}) copy-start(bf16[31,384]{1,0:T(8,128)(2,1)} %param.22) | copy-start | bytes 71428
  1.2 23.6 %copy-start.48 = (s32[1,4]{1,0:T(1,128)S(1)}, s32[1,4]{1,0:T(1,128)}, u32[]{:S(2)}) copy-start(s32[1,4]{1,0:T(1,128)} %param.16) | copy-start | bytes 52
  1.2 36.8 %collective-permute-start.2 = (bf16[192,1152]{1,0:T(8,128)(2,1)S(1)}, bf16[192,1152]{1,0:T(8,128)(2,1)S(1)}, u32[]{:S(2)}, u32[]{:S(2)}) collective-permute-start(bf16[192,1152]{1,0:T(8,128)(2,1)S(1)} %bitcast.193), channel_id=1, source_target_pairs={{0,8},{8,16},{16,24},{24,28},{28,20},{20,12},{12,4},{4,0},{1,9},{9... | collective-permute-start | bytes 1327112 | tf_op jit(solution)/shard_map/ppermute | solution.py:138
  4.3 35.4 %collective-permute-start.3 = (bf16[192,1152]{1,0:T(8,128)(2,1)S(1)}, bf16[192,1152]{1,0:T(8,128)(2,1)S(1)}, u32[]{:S(2)}, u32[]{:S(2)}) collective-permute-start(bf16[192,1152]{1,0:T(8,128)(2,1)S(1)} %bitcast.194), channel_id=1, source_target_pairs={{0,4},{8,0},{16,8},{24,16},{28,24},{20,28},{12,20},{4,12},{1,5},{9... | collective-permute-start | bytes 1327112 | tf_op jit(solution)/shard_map/ppermute | solution.py:141
  7.0 29.9 %collective-permute-start = (bf16[128,1536]{1,0:T(8,128)(2,1)S(1)}, bf16[128,1536]{1,0:T(8,128)(2,1)}, u32[]{:S(2)}, u32[]{:S(2)}) collective-permute-start(bf16[128,1536]{1,0:T(8,128)(2,1)S(1)} %fusion.18), channel_id=1, source_target_pairs={{0,2},{1,3},{2,0},{3,1},{4,6},{5,7},{6,4},{7,5},{8,10},{9,11},{10,... | collective-permute-start | bytes 1179656 | tf_op jit(solution)/shard_map/ppermute | solution.py:36
  28.9 7.4 %copy-start.5 = (bf16[384,192]{0,1:T(8,128)(2,1)S(1)}, bf16[384,192]{0,1:T(8,128)(2,1)}, u32[]{:S(2)}) copy-start(bf16[384,192]{0,1:T(8,128)(2,1)} %param.23) | copy-start | bytes 442372
  37.9 16.3 %collective-permute-start.1 = (bf16[2,128,1536]{2,1,0:T(8,128)(2,1)S(1)}, bf16[2,128,1536]{2,1,0:T(8,128)(2,1)S(1)}, u32[]{:S(2)}, u32[]{:S(2)}) collective-permute-start(bf16[2,128,1536]{2,1,0:T(8,128)(2,1)S(1)} %get-tuple-element.69), channel_id=1, source_target_pairs={{0,1},{1,0},{2,3},{3,2},{4,5},{5,4},{6,7},{7,6},{8,9},{9,8},{10,11... | collective-permute-start | bytes 2359304 | tf_op jit(solution)/shard_map/ppermute | solution.py:42
  38.0 12.6 %collective-permute-start.4 = (bf16[192,1152]{1,0:T(8,128)(2,1)S(1)}, bf16[192,1152]{1,0:T(8,128)(2,1)S(1)}, u32[]{:S(2)}, u32[]{:S(2)}) collective-permute-start(bf16[192,1152]{1,0:T(8,128)(2,1)S(1)} %collective-permute-done.2), channel_id=1, source_target_pairs={{0,8},{8,16},{16,24},{24,28},{28,20},{20,12},{12,4},{4,0},{1,9},{9... | collective-permute-start | bytes 1327112 | tf_op jit(solution)/shard_map/ppermute | solution.py:138
  39.6 12.5 %collective-permute-start.5 = (bf16[192,1152]{1,0:T(8,128)(2,1)S(1)}, bf16[192,1152]{1,0:T(8,128)(2,1)S(1)}, u32[]{:S(2)}, u32[]{:S(2)}) collective-permute-start(bf16[192,1152]{1,0:T(8,128)(2,1)S(1)} %collective-permute-done.3), channel_id=1, source_target_pairs={{0,4},{8,0},{16,8},{24,16},{28,24},{20,28},{12,20},{4,12},{1,5},{9... | collective-permute-start | bytes 1327112 | tf_op jit(solution)/shard_map/ppermute | solution.py:141
  50.6 11.7 %collective-permute-start.6 = (bf16[192,1152]{1,0:T(8,128)(2,1)S(1)}, bf16[192,1152]{1,0:T(8,128)(2,1)S(1)}, u32[]{:S(2)}, u32[]{:S(2)}) collective-permute-start(bf16[192,1152]{1,0:T(8,128)(2,1)S(1)} %collective-permute-done.4), channel_id=1, source_target_pairs={{0,8},{8,16},{16,24},{24,28},{28,20},{20,12},{12,4},{4,0},{1,9},{9... | collective-permute-start | bytes 1327112 | tf_op jit(solution)/shard_map/ppermute | solution.py:138
  52.2 12.5 %collective-permute-start.7 = (bf16[192,1152]{1,0:T(8,128)(2,1)S(1)}, bf16[192,1152]{1,0:T(8,128)(2,1)S(1)}, u32[]{:S(2)}, u32[]{:S(2)}) collective-permute-start(bf16[192,1152]{1,0:T(8,128)(2,1)S(1)} %collective-permute-done.5), channel_id=1, source_target_pairs={{0,4},{8,0},{16,8},{24,16},{28,24},{20,28},{12,20},{4,12},{1,5},{9... | collective-permute-start | bytes 1327112 | tf_op jit(solution)/shard_map/ppermute | solution.py:141
  62.3 10.8 %collective-permute-start.8 = (bf16[192,1152]{1,0:T(8,128)(2,1)S(1)}, bf16[192,1152]{1,0:T(8,128)(2,1)S(1)}, u32[]{:S(2)}, u32[]{:S(2)}) collective-permute-start(bf16[192,1152]{1,0:T(8,128)(2,1)S(1)} %collective-permute-done.6), channel_id=1, source_target_pairs={{0,8},{8,16},{16,24},{24,28},{28,20},{20,12},{12,4},{4,0},{1,9},{9... | collective-permute-start | bytes 1327112 | tf_op jit(solution)/shard_map/ppermute | solution.py:138
  73.9 14.5 %collective-permute-start.9 = (bf16[192,384]{1,0:T(8,128)(2,1)}, bf16[192,384]{1,0:T(8,128)(2,1)}, u32[]{:S(2)}, u32[]{:S(2)}) collective-permute-start(bf16[192,384]{1,0:T(8,128)(2,1)} %bitcast.33), channel_id=1, source_target_pairs={{0,8},{8,16},{16,24},{24,28},{28,20},{20,12},{12,4},{4,0},{1,9},{9... | collective-permute-start | bytes 442376 | tf_op jit(solution)/shard_map/ppermute | solution.py:138
  75.5 15.6 %collective-permute-start.10 = (bf16[192,384]{1,0:T(8,128)(2,1)}, bf16[192,384]{1,0:T(8,128)(2,1)}, u32[]{:S(2)}, u32[]{:S(2)}) collective-permute-start(bf16[192,384]{1,0:T(8,128)(2,1)} %bitcast.33), channel_id=1, source_target_pairs={{0,4},{8,0},{16,8},{24,16},{28,24},{20,28},{12,20},{4,12},{1,5},{9... | collective-permute-start | bytes 442376 | tf_op jit(solution)/shard_map/ppermute | solution.py:141
  80.1 1.0 copy-start.4
  88.5 6.7 %collective-permute-start.11 = (bf16[192,384]{1,0:T(8,128)(2,1)}, bf16[192,384]{1,0:T(8,128)(2,1)S(1)}, u32[]{:S(2)}, u32[]{:S(2)}) collective-permute-start(bf16[192,384]{1,0:T(8,128)(2,1)} %collective-permute-done.9), channel_id=1, source_target_pairs={{0,8},{8,16},{16,24},{24,28},{28,20},{20,12},{12,4},{4,0},{1,9},{9... | collective-permute-start | bytes 442376 | tf_op jit(solution)/shard_map/ppermute | solution.py:138
  91.1 6.7 %collective-permute-start.12 = (bf16[192,384]{1,0:T(8,128)(2,1)}, bf16[192,384]{1,0:T(8,128)(2,1)S(1)}, u32[]{:S(2)}, u32[]{:S(2)}) collective-permute-start(bf16[192,384]{1,0:T(8,128)(2,1)} %collective-permute-done.10), channel_id=1, source_target_pairs={{0,4},{8,0},{16,8},{24,16},{28,24},{20,28},{12,20},{4,12},{1,5},{9... | collective-permute-start | bytes 442376 | tf_op jit(solution)/shard_map/ppermute | solution.py:141
  95.2 6.2 %collective-permute-start.13 = (bf16[192,384]{1,0:T(8,128)(2,1)S(1)}, bf16[192,384]{1,0:T(8,128)(2,1)S(1)}, u32[]{:S(2)}, u32[]{:S(2)}) collective-permute-start(bf16[192,384]{1,0:T(8,128)(2,1)S(1)} %collective-permute-done.11), channel_id=1, source_target_pairs={{0,8},{8,16},{16,24},{24,28},{28,20},{20,12},{12,4},{4,0},{1,9},{9... | collective-permute-start | bytes 442376 | tf_op jit(solution)/shard_map/ppermute | solution.py:138
  97.8 5.2 %collective-permute-start.14 = (bf16[192,384]{1,0:T(8,128)(2,1)S(1)}, bf16[192,384]{1,0:T(8,128)(2,1)S(1)}, u32[]{:S(2)}, u32[]{:S(2)}) collective-permute-start(bf16[192,384]{1,0:T(8,128)(2,1)S(1)} %collective-permute-done.12), channel_id=1, source_target_pairs={{0,4},{8,0},{16,8},{24,16},{28,24},{20,28},{12,20},{4,12},{1,5},{9... | collective-permute-start | bytes 442376 | tf_op jit(solution)/shard_map/ppermute | solution.py:141
  101.3 6.8 %collective-permute-start.15 = (bf16[192,384]{1,0:T(8,128)(2,1)S(1)}, bf16[192,384]{1,0:T(8,128)(2,1)S(1)}, u32[]{:S(2)}, u32[]{:S(2)}) collective-permute-start(bf16[192,384]{1,0:T(8,128)(2,1)S(1)} %collective-permute-done.13), channel_id=1, source_target_pairs={{0,8},{8,16},{16,24},{24,28},{28,20},{20,12},{12,4},{4,0},{1,9},{9... | collective-permute-start | bytes 442376 | tf_op jit(solution)/shard_map/ppermute | solution.py:138
  108.1 9.7 %collective-permute-start.20 = (bf16[192,1152]{1,0:T(8,128)(2,1)S(1)}, bf16[192,1152]{1,0:T(8,128)(2,1)S(1)}, u32[]{:S(2)}, u32[]{:S(2)}) collective-permute-start(bf16[192,1152]{1,0:T(8,128)(2,1)S(1)} %pad_maximum_fusion), channel_id=1, source_target_pairs={{0,8},{8,16},{16,24},{24,28},{28,20},{20,12},{12,4},{4,0},{1,9},{9... | collective-permute-start | bytes 1327112 | tf_op jit(solution)/shard_map/ppermute | solution.py:138
  109.8 9.9 %collective-permute-start.21 = (bf16[192,1152]{1,0:T(8,128)(2,1)S(1)}, bf16[192,1152]{1,0:T(8,128)(2,1)S(1)}, u32[]{:S(2)}, u32[]{:S(2)}) collective-permute-start(bf16[192,1152]{1,0:T(8,128)(2,1)S(1)} %pad_maximum_fusion), channel_id=1, source_target_pairs={{0,4},{8,0},{16,8},{24,16},{28,24},{20,28},{12,20},{4,12},{1,5},{9... | collective-permute-start | bytes 1327112 | tf_op jit(solution)/shard_map/ppermute | solution.py:141
  111.3 9.0 %collective-permute-start.16 = (bf16[2,128,1536]{2,1,0:T(8,128)(2,1)S(1)}, bf16[2,128,1536]{2,1,0:T(8,128)(2,1)S(1)}, u32[]{:S(2)}, u32[]{:S(2)}) collective-permute-start(bf16[2,128,1536]{2,1,0:T(8,128)(2,1)S(1)} %dynamic-slice_bitcast_fusion.1), channel_id=1, source_target_pairs={{0,1},{1,0},{2,3},{3,2},{4,5},{5,4},{6,7},{7,6},{8,9},{9,8},{10,11... | collective-permute-start | bytes 2359304 | tf_op jit(solution)/shard_map/ppermute | solution.py:78
  117.9 10.8 %collective-permute-start.22 = (bf16[192,1152]{1,0:T(8,128)(2,1)S(1)}, bf16[192,1152]{1,0:T(8,128)(2,1)S(1)}, u32[]{:S(2)}, u32[]{:S(2)}) collective-permute-start(bf16[192,1152]{1,0:T(8,128)(2,1)S(1)} %collective-permute-done.20), channel_id=1, source_target_pairs={{0,8},{8,16},{16,24},{24,28},{28,20},{20,12},{12,4},{4,0},{1,9},{9... | collective-permute-start | bytes 1327112 | tf_op jit(solution)/shard_map/ppermute | solution.py:138
  119.7 10.7 %collective-permute-start.23 = (bf16[192,1152]{1,0:T(8,128)(2,1)S(1)}, bf16[192,1152]{1,0:T(8,128)(2,1)S(1)}, u32[]{:S(2)}, u32[]{:S(2)}) collective-permute-start(bf16[192,1152]{1,0:T(8,128)(2,1)S(1)} %collective-permute-done.21), channel_id=1, source_target_pairs={{0,4},{8,0},{16,8},{24,16},{28,24},{20,28},{12,20},{4,12},{1,5},{9... | collective-permute-start | bytes 1327112 | tf_op jit(solution)/shard_map/ppermute | solution.py:141
  120.6 10.4 %collective-permute-start.17 = (bf16[128,1536]{1,0:T(8,128)(2,1)S(1)}, bf16[128,1536]{1,0:T(8,128)(2,1)S(1)}, u32[]{:S(2)}, u32[]{:S(2)}) collective-permute-start(bf16[128,1536]{1,0:T(8,128)(2,1)S(1)} %fusion.31), channel_id=1, source_target_pairs={{0,2},{1,3},{2,0},{3,1},{4,6},{5,7},{6,4},{7,5},{8,10},{9,11},{10,... | collective-permute-start | bytes 1179656 | tf_op jit(solution)/shard_map/ppermute | solution.py:84
  128.6 11.9 %collective-permute-start.24 = (bf16[192,1152]{1,0:T(8,128)(2,1)S(1)}, bf16[192,1152]{1,0:T(8,128)(2,1)S(1)}, u32[]{:S(2)}, u32[]{:S(2)}) collective-permute-start(bf16[192,1152]{1,0:T(8,128)(2,1)S(1)} %collective-permute-done.22), channel_id=1, source_target_pairs={{0,8},{8,16},{16,24},{24,28},{28,20},{20,12},{12,4},{4,0},{1,9},{9... | collective-permute-start | bytes 1327112 | tf_op jit(solution)/shard_map/ppermute | solution.py:138
  130.5 12.5 %collective-permute-start.25 = (bf16[192,1152]{1,0:T(8,128)(2,1)S(1)}, bf16[192,1152]{1,0:T(8,128)(2,1)S(1)}, u32[]{:S(2)}, u32[]{:S(2)}) collective-permute-start(bf16[192,1152]{1,0:T(8,128)(2,1)S(1)} %collective-permute-done.23), channel_id=1, source_target_pairs={{0,4},{8,0},{16,8},{24,16},{28,24},{20,28},{12,20},{4,12},{1,5},{9... | collective-permute-start | bytes 1327112 | tf_op jit(solution)/shard_map/ppermute | solution.py:141
  131.0 1.5 copy-start.9
  133.5 8.6 %collective-permute-start.18 = (bf16[128,1536]{1,0:T(8,128)(2,1)S(1)}, bf16[128,1536]{1,0:T(8,128)(2,1)S(1)}, u32[]{:S(2)}, u32[]{:S(2)}) collective-permute-start(bf16[128,1536]{1,0:T(8,128)(2,1)S(1)} %get-tuple-element.62), channel_id=1, source_target_pairs={{0,2},{1,3},{2,0},{3,1},{4,6},{5,7},{6,4},{7,5},{8,10},{9,11},{10,... | collective-permute-start | bytes 1179656 | tf_op jit(solution)/shard_map/ppermute | solution.py:36
  140.5 8.3 %collective-permute-start.26 = (bf16[192,1152]{1,0:T(8,128)(2,1)S(1)}, bf16[192,1152]{1,0:T(8,128)(2,1)S(1)}, u32[]{:S(2)}, u32[]{:S(2)}) collective-permute-start(bf16[192,1152]{1,0:T(8,128)(2,1)S(1)} %collective-permute-done.24), channel_id=1, source_target_pairs={{0,8},{8,16},{16,24},{24,28},{28,20},{20,12},{12,4},{4,0},{1,9},{9... | collective-permute-start | bytes 1327112 | tf_op jit(solution)/shard_map/ppermute | solution.py:138
  143.0 5.8 %copy-start.3 = (bf16[4,128,1536]{2,1,0:T(8,128)(2,1)}, bf16[4,128,1536]{2,1,0:T(8,128)(2,1)S(1)}, u32[]{:S(2)}) copy-start(bf16[4,128,1536]{2,1,0:T(8,128)(2,1)S(1)} %get-tuple-element.68) | copy-start | bytes 4718596
  143.0 9.6 %collective-permute-start.19 = (bf16[2,128,1536]{2,1,0:T(8,128)(2,1)}, bf16[2,128,1536]{2,1,0:T(8,128)(2,1)}, u32[]{:S(2)}, u32[]{:S(2)}) collective-permute-start(bf16[2,128,1536]{2,1,0:T(8,128)(2,1)} %get-tuple-element.67), channel_id=1, source_target_pairs={{0,1},{1,0},{2,3},{3,2},{4,5},{5,4},{6,7},{7,6},{8,9},{9,8},{10,11... | collective-permute-start | bytes 2359304 | tf_op jit(solution)/shard_map/ppermute | solution.py:42
  159.7 0.7 copy-start.10
  159.7 0.7 copy-start.13
  159.8 0.7 copy-start.18
  159.8 0.7 copy-start.19
  159.9 0.7 copy-start.33
  160.0 0.7 copy-start.37
  160.0 0.7 copy-start.38
  160.1 6.2 %copy-start.1 = (bf16[8,192,384]{2,1,0:T(8,128)(2,1)S(1)}, bf16[8,192,384]{2,1,0:T(8,128)(2,1)}, u32[]{:S(2)}) copy-start(bf16[8,192,384]{2,1,0:T(8,128)(2,1)} %slice.423) | copy-start | bytes 3538948
  167.4 2.4 %collective-permute-start.27 = (bf16[2,128,1536]{2,1,0:T(8,128)(2,1)S(1)}, bf16[2,128,1536]{2,1,0:T(8,128)(2,1)S(1)}, u32[]{:S(2)}, u32[]{:S(2)}) collective-permute-start(bf16[2,128,1536]{2,1,0:T(8,128)(2,1)S(1)} %dynamic-slice_bitcast_fusion), channel_id=1, source_target_pairs={{0,1},{1,0},{2,3},{3,2},{4,5},{5,4},{6,7},{7,6},{8,9},{9,8},{10,11... | collective-permute-start | bytes 2359304 | tf_op jit(solution)/shard_map/ppermute | solution.py:78
  170.0 11.2 %collective-permute-start.28 = (bf16[128,1536]{1,0:T(8,128)(2,1)S(1)}, bf16[128,1536]{1,0:T(8,128)(2,1)S(1)}, u32[]{:S(2)}, u32[]{:S(2)}) collective-permute-start(bf16[128,1536]{1,0:T(8,128)(2,1)S(1)} %fusion.32), channel_id=1, source_target_pairs={{0,2},{1,3},{2,0},{3,1},{4,6},{5,7},{6,4},{7,5},{8,10},{9,11},{10,... | collective-permute-start | bytes 1179656 | tf_op jit(solution)/shard_map/ppermute | solution.py:84
  (31 other events, 20.5 us)

commit v10 on v9

--- a/solution.py
+++ b/solution.py
@@ -198,10 +198,10 @@
     group_rows = frame_rows * seq_count
     group_width = model_width // seq_count
     kernel_reach = dw_kernel.shape[0] // 2
-    qkv_parts = ring_gather(w_qkv.reshape(w_qkv.shape[0], 3 * group_width), ring)
-    qkv_matrix = qkv_parts.reshape(model_width, 3 * group_width)
-    out_parts = ring_gather(after(qkv_parts, w_out.T), ring)
-    out_cols = out_parts.reshape(model_width, w_out.shape[0])
+    qkv_local = w_qkv.reshape(w_qkv.shape[0], 3 * group_width)
+    out_parts = ring_gather(jnp.concatenate([qkv_local, w_out.T], axis=1), ring)
+    qkv_matrix = out_parts[:, :, : 3 * group_width].reshape(model_width, 3 * group_width)
+    out_cols = out_parts[:, :, 3 * group_width :].reshape(model_width, w_out.shape[0])
     glu_rows = w_glu.shape[0]
     glu_local = w_glu.reshape(glu_rows, 2 * group_width)
     both_parts = ring_gather(after(out_parts, jnp.concatenate([glu_local, w_proj.T], axis=1)), ring)

time: 183 us -> 177 us (0.967)
  starting transfers between devices: 28.5 us -> 20.7 us
  waiting for transfers between devices: 74.9 us -> 67.4 us
  local copies, waits for them, and re-layouts: 28.9 us -> 33.5 us
  other arithmetic: 15 us -> 18.9 us
    ppermute x12 -> x8, waiting for transfers between devices: 60.5 us -> 52.3 us  [ring_gather(): ahead = lax.ppermute(ahead, 'dp', forward)]
    ppermute x12 -> x8, starting transfers between devices: 20.7 us -> 14.5 us  [ring_gather(): ahead = lax.ppermute(ahead, 'dp', forward)]
    slice x0 -> x2, local copies, waits for them, and re-layouts: none -> 3.66 us  [the longest x1 2.27 us: on_device(): out_parts[:, :, :3 * group_width].reshape(model_width, 3 * group_width)]
    broadcast_in_dim x1 -> x2, local copies, waits for them, and re-layouts: 0.1 us -> 2.97 us  [ring_gather(): out = jnp.zeros((count,) + block.shape, block.dtype)]
    unnamed x102 -> x103, local copies, waits for them, and re-layouts: 2.2 us -> 0.25 us
    ppermute x2, waiting for transfers between devices: 0.01 us -> 1.84 us  [seq_gather(): lax.ppermute(block, 'seq', [(i, (i + 2 * shift) % count) for i in range(c...]
    ppermute x9 -> x6, starting transfers between devices: 3.78 us -> 2.09 us  [ring_gather(): behind = lax.ppermute(behind, 'dp', backward)]
    another operation x6 -> x4, local copies, waits for them, and re-layouts: 3.89 us -> 2.43 us
  transfers between devices with their start and end apart: 29 -> 22, of which waited for: 15 -> 10; matrix products, arithmetic and copies ran while one was open for 23% -> 26% of each run, Pallas kernels for 0% -> 0%
where the time goes in v10:
time: 177 us; the launch traced here: 176 us
  waiting for transfers between devices  67.4 us (38%)
  local copies, waits for them, and re-layouts  33.5 us (19%)
  starting transfers between devices  20.7 us (12%)
  other arithmetic  18.9 us (11%)
  between operations  18.9 us (11%)
  matrix products  16.6 us (9%)
    ppermute x8, waiting for transfers between devices, ring_gather(): ahead = lax.ppermute(ahead, 'dp', forward)  52.3 us
    ppermute x8, starting transfers between devices, ring_gather(): ahead = lax.ppermute(ahead, 'dp', forward)  14.5 us
    ppermute x2, waiting for transfers between devices, seq_scatter_sum(): lax.ppermute(piece.astype(jnp.bfloat16), 'seq', [(i, (i + 2 * shift) % co...  11 us
    convert_element_type x1, other arithmetic, depthwise(): return jax.nn.silu(total_acc).astype(jnp.bfloat16)  6.53 us
    dynamic_update_slice x4, local copies, waits for them, and re-layouts, seq_gather(): out = lax.dynamic_update_index_in_dim(out, other[k], 2 * k + partner % 2, 0)  5.09 us
    dot_general x1, matrix products, on_device(): jnp.dot(seq_gather(normed1, paired).reshape(group_rows, model_width), qkv...  4.65 us
    dynamic_update_slice x8, local copies, waits for them, and re-layouts, ring_gather(): lax.dynamic_update_index_in_dim(out, ahead, order[(my_pos - step) % count...  4.61 us
    dynamic_update_slice x6, local copies, waits for them, and re-layouts, ring_gather(): lax.dynamic_update_index_in_dim(out, behind, order[(my_pos + step) % coun...  3.76 us
  transfers between devices with their start and end apart: 22, of which 10 were waited for; matrix products, arithmetic and copies ran while one was open for 26% of the time, Pallas kernels for 0%

profile of v10, /device:TPU:0, one launch (start us, length us, event | category | flops | bytes accessed | tf_op | source)
XLA Modules:
  0.0 176.0 jit_solution(6691898514873650622)
XLA Ops:
  0.0 1.1 copy.43
  1.1 1.8 %pad_maximum_fusion = bf16[192,1536]{1,0:T(8,128)(2,1)} fusion(bf16[192,384]{1,0:T(8,128)(2,1)} %bitcast.180, bf16[192,1152]{1,0:T(8,128)(2,1)S(1)} %bitcast.172), kind=kLoop, calls=%fused_computation.51 | loop fusion | flops 1179648 | bytes 1179648 | tf_op jit(solution)/shard_map/concatenate | solution.py:202
  2.9 3.0 %collective-permute-start.2 = (bf16[192,1536]{1,0:T(8,128)(2,1)}, bf16[192,1536]{1,0:T(8,128)(2,1)S(1)}, u32[]{:S(2)}, u32[]{:S(2)}) collective-permute-start(bf16[192,1536]{1,0:T(8,128)(2,1)} %pad_maximum_fusion), channel_id=1, source_target_pairs={{0,8},{8,16},{16,24},{24,28},{28,20},{20,12},{12,4},{4,0},{1,9},{9... | collective-permute-start | bytes 1769480 | tf_op jit(solution)/shard_map/ppermute | solution.py:138
  6.6 2.0 %collective-permute-start = (bf16[128,1536]{1,0:T(8,128)(2,1)S(1)}, bf16[128,1536]{1,0:T(8,128)(2,1)}, u32[]{:S(2)}, u32[]{:S(2)}) collective-permute-start(bf16[128,1536]{1,0:T(8,128)(2,1)S(1)} %fusion.18), channel_id=1, source_target_pairs={{0,2},{1,3},{2,0},{3,1},{4,6},{5,7},{6,4},{7,5},{8,10},{9,11},{10,... | collective-permute-start | bytes 1179656 | tf_op jit(solution)/shard_map/ppermute | solution.py:36
  8.9 0.9 broadcast_compare_fusion
  11.4 2.5 %broadcast_in_dim.371 = bf16[8,192,1536]{2,1,0:T(8,128)(2,1)} broadcast(bf16[]{:T(256)} %constant.283.clone.1), dimensions={} | broadcast | bytes 4718594 | tf_op jit(solution)/shard_map/broadcast_in_dim | solution.py:134
  14.8 1.3 broadcast.151.clone
  16.1 1.0 constant_dynamic-update-slice_fusion
  37.1 0.9 pad_maximum_fusion.1
  38.7 1.8 %bitcast_dynamic-update-slice_fusion.20 = (bf16[2,128,1536]{2,1,0:T(8,128)(2,1)S(1)}, bf16[4,128,1536]{2,1,0:T(8,128)(2,1)}) fusion(bf16[2,128,1536]{2,1,0:T(8,128)(2,1)S(1)} %get-tuple-element.63, s32[]{:T(128)S(6)} %select_n.337, bf16[128,1536]{1,0:T(8,128)(2,1)} %collective-permute-done, bf16[4,128,1536]{2,1,0:T(8,128)(2,1)} %get-tuple-element.64, ...), kind=kLoop, calls=%fused_computation.85 | loop fusion | bytes 1179656 | tf_op jit(solution)/shard_map/jit(dynamic_update_index_in_dim)/dynamic_update_slice | solution.py:40
  40.6 1.6 collective-permute-start.4
  43.4 0.9 bitcast_dynamic-update-slice_fusion.5
  44.3 12.0 %collective-permute-done.4 = bf16[192,1536]{1,0:T(8,128)(2,1)S(1)} collective-permute-done((bf16[192,1536]{1,0:T(8,128)(2,1)S(1)}, bf16[192,1536]{1,0:T(8,128)(2,1)S(1)}, u32[]{:S(2)}, u32[]{:S(2)}) %collective-permute-start.4) | collective-permute-done | bytes 589856 | tf_op jit(solution)/shard_map/ppermute | solution.py:138
  56.3 1.6 collective-permute-start.6
  58.3 0.9 bitcast_dynamic-update-slice_fusion.4
  59.2 0.9 bitcast_dynamic-update-slice_fusion.3
  61.6 9.6 %collective-permute-done.6 = bf16[192,1536]{1,0:T(8,128)(2,1)S(1)} collective-permute-done((bf16[192,1536]{1,0:T(8,128)(2,1)S(1)}, bf16[192,1536]{1,0:T(8,128)(2,1)S(1)}, u32[]{:S(2)}, u32[]{:S(2)}) %collective-permute-start.6) | collective-permute-done | bytes 589856 | tf_op jit(solution)/shard_map/ppermute | solution.py:138
  71.3 1.6 collective-permute-start.8
  74.6 10.7 %collective-permute-done.8 = bf16[192,1536]{1,0:T(8,128)(2,1)S(1)} collective-permute-done((bf16[192,1536]{1,0:T(8,128)(2,1)S(1)}, bf16[192,1536]{1,0:T(8,128)(2,1)S(1)}, u32[]{:S(2)}, u32[]{:S(2)}) %collective-permute-start.8) | collective-permute-done | bytes 589856 | tf_op jit(solution)/shard_map/ppermute | solution.py:138
  86.2 2.3 %slice.423 = bf16[8,192,1152]{2,1,0:T(8,128)(2,1)S(1)} slice(bf16[8,192,1536]{2,1,0:T(8,128)(2,1)} %bitcast_dynamic-update-slice_fusion), slice={[0:8], [0:192], [0:1152]} | slice | bytes 7077888 | tf_op jit(solution)/shard_map/slice | solution.py:203
  88.5 1.4 slice.427
  89.9 1.7 collective-permute-start.13
  91.9 4.7 %convolution_convert_fusion = bf16[512,1152]{1,0:T(8,128)(2,1)} fusion(bf16[512,1536]{1,0:T(8,128)(2,1)} %bitcast.2, bf16[1536,1152]{1,0:T(8,128)(2,1)S(1)} %bitcast.174), kind=kOutput, calls=%fused_computation.5 | convolution fusion | flops 1812529152 | bytes 6291456 | tf_op jit(solution)/shard_map/dot_general | solution.py:215
  96.6 1.6 copy.35
  98.2 3.6 %fusion.41 = (f32[4,512]{1,0:T(4,128)S(1)}, f32[4,512,512]{1,2,0:T(8,128)}) fusion(pred[512,512]{0,1:T(8,128)(4,1)S(1)} %copy-done.5, bf16[512,3,4,96]{0,3,2,1:T(8,128)(2,1)S(1)} %bitcast.178), kind=kOutput, calls=%fused_computation.169 | convolution fusion | flops 205521408 | bytes 5251072 | tf_op jit(solution)/shard_map/while/body/eval_jaxpr/sub | solution.py:170
  101.9 2.7 %fusion.6 = bf16[4,96,512]{2,1,0:T(8,128)(2,1)S(1)} fusion(f32[4,512,512]{1,2,0:T(8,128)} %get-tuple-element.108, f32[4,512]{1,0:T(4,128)S(1)} %get-tuple-element.107, bf16[512,3,4,96]{0,3,2,1:T(8,128)(2,1)S(1)} %bitcast.179), kind=kOutput, calls=%fused_computation.14 | convolution fusion | flops 203620352 | bytes 4988928 | tf_op jit(solution)/shard_map/while/body/eval_jaxpr/hqk,khe->qhe/dot_general | solution.py:172
  104.5 1.0 convolution_convert_fusion.2
  106.2 1.7 collective-permute-start.15
  108.3 1.1 bitcast_dynamic-update-slice_fusion.14
  109.4 1.1 bitcast_dynamic-update-slice_fusion.13
  111.5 7.6 %collective-permute-done.15 = bf16[192,1152]{1,0:T(8,128)(2,1)S(1)} collective-permute-done((bf16[192,1152]{1,0:T(8,128)(2,1)}, bf16[192,1152]{1,0:T(8,128)(2,1)S(1)}, u32[]{:S(2)}, u32[]{:S(2)}) %collective-permute-start.15) | collective-permute-done | bytes 442400 | tf_op jit(solution)/shard_map/ppermute | solution.py:138
  119.1 1.6 collective-permute-start.17
  122.3 1.0 broadcast.154
  123.2 1.0 bitcast_dynamic-update-slice_fusion.18
  125.1 5.8 %collective-permute-done.17 = bf16[192,1152]{1,0:T(8,128)(2,1)S(1)} collective-permute-done((bf16[192,1152]{1,0:T(8,128)(2,1)S(1)}, bf16[192,1152]{1,0:T(8,128)(2,1)S(1)}, u32[]{:S(2)}, u32[]{:S(2)}) %collective-permute-start.17) | collective-permute-done | bytes 442400 | tf_op jit(solution)/shard_map/ppermute | solution.py:138
  130.9 1.6 collective-permute-start.19
  132.5 1.8 %collective-permute-done.11 = bf16[128,1536]{1,0:T(8,128)(2,1)S(1)} collective-permute-done((bf16[128,1536]{1,0:T(8,128)(2,1)S(1)}, bf16[128,1536]{1,0:T(8,128)(2,1)S(1)}, u32[]{:S(2)}, u32[]{:S(2)}) %collective-permute-start.11) | collective-permute-done | bytes 393248 | tf_op jit(solution)/shard_map/ppermute | solution.py:36
  135.3 6.5 %collective-permute-done.19 = bf16[192,1152]{1,0:T(8,128)(2,1)S(1)} collective-permute-done((bf16[192,1152]{1,0:T(8,128)(2,1)S(1)}, bf16[192,1152]{1,0:T(8,128)(2,1)S(1)}, u32[]{:S(2)}, u32[]{:S(2)}) %collective-permute-start.19) | collective-permute-done | bytes 442400 | tf_op jit(solution)/shard_map/ppermute | solution.py:138
  142.0 1.2 slice.433
  143.1 2.4 %copy.38 = bf16[768,1536]{1,0:T(8,128)(2,1)} copy(bf16[768,1536]{0,1:T(8,128)(2,1)S(1)} %bitcast.165) | data formatting | bytes 4718592 | tf_op jit(solution)/shard_map/dot_general | solution.py:227
  145.6 1.8 %slice_dynamic-update-slice_fusion.1 = bf16[4,128,1536]{2,1,0:T(8,128)(2,1)} fusion(bf16[4,128,1536]{2,1,0:T(8,128)(2,1)} %copy-done.2, s32[]{:T(128)S(6)} %select_n.339, bf16[2,128,1536]{2,1,0:T(8,128)(2,1)} %collective-permute-done.12), kind=kLoop, calls=%fused_computation.75 | loop fusion | bytes 786436 | tf_op jit(solution)/shard_map/jit(dynamic_update_index_in_dim)/dynamic_update_slice | solution.py:45
  147.4 1.8 slice_dynamic-update-slice_fusion
  149.5 3.5 %fusion.42 = f32[512,2,384]{2,0,1:T(8,128)S(1)} fusion(bf16[512,1536,1]{1,0,2:T(8,128)(2,1)} %bitcast.176, bf16[2,384,1536]{2,1,0:T(8,128)(2,1)} %bitcast.175), kind=kOutput, calls=%fused_computation.170 | convolution fusion | flops 1207959552 | bytes 5505024 | tf_op jit(solution)/shard_map/dot_general | solution.py:227
  153.6 6.5 %multiply_convert_fusion = bf16[512,384]{1,0:T(8,128)(2,1)S(1)} fusion(bf16[512,384]{1,0:T(8,128)(2,1)S(1)} %fusion.34, f32[384]{0:T(512)S(1)} %copy-done.21, f32[384]{0:T(512)S(1)} %copy-done.22, f32[384]{0:T(512)S(1)} %get-tuple-element.20, f32[384]{0:T(512)S(1)} %get-tuple-element.28, f32[384]{0:T(512)S(1)} %get-tuple-element.30, ...), kind=kLoop, calls=%fused_computation.47 | loop fusion | flops 25165824 | bytes 849920 | tf_op jit(solution)/shard_map/convert_element_type | solution.py:191
  160.2 1.0 convolution_convert_fusion.1
  161.4 2.3 %collective-permute-done.20 = bf16[2,128,1536]{2,1,0:T(8,128)(2,1)S(1)} collective-permute-done((bf16[2,128,1536]{2,1,0:T(8,128)(2,1)S(1)}, bf16[2,128,1536]{2,1,0:T(8,128)(2,1)S(1)}, u32[]{:S(2)}, u32[]{:S(2)}) %collective-permute-start.20) | collective-permute-done | bytes 786464 | tf_op jit(solution)/shard_map/ppermute | solution.py:78
  164.6 10.5 %collective-permute-done.21 = bf16[128,1536]{1,0:T(8,128)(2,1)S(1)} collective-permute-done((bf16[128,1536]{1,0:T(8,128)(2,1)S(1)}, bf16[128,1536]{1,0:T(8,128)(2,1)S(1)}, u32[]{:S(2)}, u32[]{:S(2)}) %collective-permute-start.21) | collective-permute-done | bytes 393248 | tf_op jit(solution)/shard_map/ppermute | solution.py:84
  175.1 0.9 fusion.33
  (174 shorter events, 19.2 us)
Async XLA Ops:
  0.0 5.9 %copy-start = (bf16[1,128,1536]{2,1,0:T(8,128)(2,1)S(1)}, bf16[1,128,1536]{2,1,0:T(8,128)(2,1)}, u32[]{:S(2)}) copy-start(bf16[1,128,1536]{2,1,0:T(8,128)(2,1)} %param.13) | copy-start | bytes 1179652
  0.0 6.3 %copy-start.7 = (f32[1536]{0:T(1024)S(1)}, f32[1536]{0:T(1024)}, u32[]{:S(2)}) copy-start(f32[1536]{0:T(1024)} %param.15) | copy-start | bytes 18436
  0.0 8.6 %copy-start.49 = (s32[1,4]{1,0:T(1,128)S(1)}, s32[1,4]{1,0:T(1,128)}, u32[]{:S(2)}) copy-start(s32[1,4]{1,0:T(1,128)} %param.14) | copy-start | bytes 52
  2.9 37.7 %collective-permute-start.2 = (bf16[192,1536]{1,0:T(8,128)(2,1)}, bf16[192,1536]{1,0:T(8,128)(2,1)S(1)}, u32[]{:S(2)}, u32[]{:S(2)}) collective-permute-start(bf16[192,1536]{1,0:T(8,128)(2,1)} %pad_maximum_fusion), channel_id=1, source_target_pairs={{0,8},{8,16},{16,24},{24,28},{28,20},{20,12},{12,4},{4,0},{1,9},{9... | collective-permute-start | bytes 1769480 | tf_op jit(solution)/shard_map/ppermute | solution.py:138
  5.9 36.3 %collective-permute-start.3 = (bf16[192,1536]{1,0:T(8,128)(2,1)}, bf16[192,1536]{1,0:T(8,128)(2,1)S(1)}, u32[]{:S(2)}, u32[]{:S(2)}) collective-permute-start(bf16[192,1536]{1,0:T(8,128)(2,1)} %pad_maximum_fusion), channel_id=1, source_target_pairs={{0,4},{8,0},{16,8},{24,16},{28,24},{20,28},{12,20},{4,12},{1,5},{9... | collective-permute-start | bytes 1769480 | tf_op jit(solution)/shard_map/ppermute | solution.py:141
  6.6 32.1 %collective-permute-start = (bf16[128,1536]{1,0:T(8,128)(2,1)S(1)}, bf16[128,1536]{1,0:T(8,128)(2,1)}, u32[]{:S(2)}, u32[]{:S(2)}) collective-permute-start(bf16[128,1536]{1,0:T(8,128)(2,1)S(1)} %fusion.18), channel_id=1, source_target_pairs={{0,2},{1,3},{2,0},{3,1},{4,6},{5,7},{6,4},{7,5},{8,10},{9,11},{10,... | collective-permute-start | bytes 1179656 | tf_op jit(solution)/shard_map/ppermute | solution.py:36
  14.7 8.3 %copy-start.8 = (s32[8]{0:T(128)S(1)}, s32[8]{0:T(128)}, u32[]{:S(2)}) copy-start(s32[8]{0:T(128)} %constant.313.clone) | copy-start | bytes 100
  14.7 17.9 %copy-start.4 = (bf16[192,2,384]{2,1,0:T(2,128)(2,1)S(1)}, bf16[192,2,384]{2,1,0:T(2,128)(2,1)}, u32[]{:S(2)}) copy-start(bf16[192,2,384]{2,1,0:T(2,128)(2,1)} %param.19) | copy-start | bytes 884740
  40.6 19.5 %collective-permute-start.1 = (bf16[2,128,1536]{2,1,0:T(8,128)(2,1)S(1)}, bf16[2,128,1536]{2,1,0:T(8,128)(2,1)S(1)}, u32[]{:S(2)}, u32[]{:S(2)}) collective-permute-start(bf16[2,128,1536]{2,1,0:T(8,128)(2,1)S(1)} %get-tuple-element.67), channel_id=1, source_target_pairs={{0,1},{1,0},{2,3},{3,2},{4,5},{5,4},{6,7},{7,6},{8,9},{9,8},{10,11... | collective-permute-start | bytes 2359304 | tf_op jit(solution)/shard_map/ppermute | solution.py:42
  40.6 15.7 %collective-permute-start.4 = (bf16[192,1536]{1,0:T(8,128)(2,1)S(1)}, bf16[192,1536]{1,0:T(8,128)(2,1)S(1)}, u32[]{:S(2)}, u32[]{:S(2)}) collective-permute-start(bf16[192,1536]{1,0:T(8,128)(2,1)S(1)} %collective-permute-done.2), channel_id=1, source_target_pairs={{0,8},{8,16},{16,24},{24,28},{28,20},{20,12},{12,4},{4,0},{1,9},{9... | collective-permute-start | bytes 1769480 | tf_op jit(solution)/shard_map/ppermute | solution.py:138
  42.2 15.7 %collective-permute-start.5 = (bf16[192,1536]{1,0:T(8,128)(2,1)S(1)}, bf16[192,1536]{1,0:T(8,128)(2,1)S(1)}, u32[]{:S(2)}, u32[]{:S(2)}) collective-permute-start(bf16[192,1536]{1,0:T(8,128)(2,1)S(1)} %collective-permute-done.3), channel_id=1, source_target_pairs={{0,4},{8,0},{16,8},{24,16},{28,24},{20,28},{12,20},{4,12},{1,5},{9... | collective-permute-start | bytes 1769480 | tf_op jit(solution)/shard_map/ppermute | solution.py:141
  56.3 15.0 %collective-permute-start.6 = (bf16[192,1536]{1,0:T(8,128)(2,1)S(1)}, bf16[192,1536]{1,0:T(8,128)(2,1)S(1)}, u32[]{:S(2)}, u32[]{:S(2)}) collective-permute-start(bf16[192,1536]{1,0:T(8,128)(2,1)S(1)} %collective-permute-done.4), channel_id=1, source_target_pairs={{0,8},{8,16},{16,24},{24,28},{28,20},{20,12},{12,4},{4,0},{1,9},{9... | collective-permute-start | bytes 1769480 | tf_op jit(solution)/shard_map/ppermute | solution.py:138
  57.9 15.8 %collective-permute-start.7 = (bf16[192,1536]{1,0:T(8,128)(2,1)S(1)}, bf16[192,1536]{1,0:T(8,128)(2,1)S(1)}, u32[]{:S(2)}, u32[]{:S(2)}) collective-permute-start(bf16[192,1536]{1,0:T(8,128)(2,1)S(1)} %collective-permute-done.5), channel_id=1, source_target_pairs={{0,4},{8,0},{16,8},{24,16},{28,24},{20,28},{12,20},{4,12},{1,5},{9... | collective-permute-start | bytes 1769480 | tf_op jit(solution)/shard_map/ppermute | solution.py:141
  71.3 14.1 %collective-permute-start.8 = (bf16[192,1536]{1,0:T(8,128)(2,1)S(1)}, bf16[192,1536]{1,0:T(8,128)(2,1)S(1)}, u32[]{:S(2)}, u32[]{:S(2)}) collective-permute-start(bf16[192,1536]{1,0:T(8,128)(2,1)S(1)} %collective-permute-done.6), channel_id=1, source_target_pairs={{0,8},{8,16},{16,24},{24,28},{28,20},{20,12},{12,4},{4,0},{1,9},{9... | collective-permute-start | bytes 1769480 | tf_op jit(solution)/shard_map/ppermute | solution.py:138
  89.9 16.4 %collective-permute-start.13 = (bf16[192,1152]{1,0:T(8,128)(2,1)S(1)}, bf16[192,1152]{1,0:T(8,128)(2,1)}, u32[]{:S(2)}, u32[]{:S(2)}) collective-permute-start(bf16[192,1152]{1,0:T(8,128)(2,1)S(1)} %pad_maximum_fusion.1), channel_id=1, source_target_pairs={{0,8},{8,16},{16,24},{24,28},{28,20},{20,12},{12,4},{4,0},{1,9},{9... | collective-permute-start | bytes 1327112 | tf_op jit(solution)/shard_map/ppermute | solution.py:138
  91.5 16.4 %collective-permute-start.14 = (bf16[192,1152]{1,0:T(8,128)(2,1)S(1)}, bf16[192,1152]{1,0:T(8,128)(2,1)}, u32[]{:S(2)}, u32[]{:S(2)}) collective-permute-start(bf16[192,1152]{1,0:T(8,128)(2,1)S(1)} %pad_maximum_fusion.1), channel_id=1, source_target_pairs={{0,4},{8,0},{16,8},{24,16},{28,24},{20,28},{12,20},{4,12},{1,5},{9... | collective-permute-start | bytes 1327112 | tf_op jit(solution)/shard_map/ppermute | solution.py:141
  105.7 4.8 %collective-permute-start.9 = (bf16[2,128,1536]{2,1,0:T(8,128)(2,1)S(1)}, bf16[2,128,1536]{2,1,0:T(8,128)(2,1)S(1)}, u32[]{:S(2)}, u32[]{:S(2)}) collective-permute-start(bf16[2,128,1536]{2,1,0:T(8,128)(2,1)S(1)} %dynamic-slice_bitcast_fusion.1), channel_id=1, source_target_pairs={{0,1},{1,0},{2,3},{3,2},{4,5},{5,4},{6,7},{7,6},{8,9},{9,8},{10,11... | collective-permute-start | bytes 2359304 | tf_op jit(solution)/shard_map/ppermute | solution.py:78
  106.2 12.8 %collective-permute-start.15 = (bf16[192,1152]{1,0:T(8,128)(2,1)}, bf16[192,1152]{1,0:T(8,128)(2,1)S(1)}, u32[]{:S(2)}, u32[]{:S(2)}) collective-permute-start(bf16[192,1152]{1,0:T(8,128)(2,1)} %collective-permute-done.13), channel_id=1, source_target_pairs={{0,8},{8,16},{16,24},{24,28},{28,20},{20,12},{12,4},{4,0},{1,9},{9... | collective-permute-start | bytes 1327112 | tf_op jit(solution)/shard_map/ppermute | solution.py:138
  107.9 12.8 %collective-permute-start.16 = (bf16[192,1152]{1,0:T(8,128)(2,1)}, bf16[192,1152]{1,0:T(8,128)(2,1)S(1)}, u32[]{:S(2)}, u32[]{:S(2)}) collective-permute-start(bf16[192,1152]{1,0:T(8,128)(2,1)} %collective-permute-done.14), channel_id=1, source_target_pairs={{0,4},{8,0},{16,8},{24,16},{28,24},{20,28},{12,20},{4,12},{1,5},{9... | collective-permute-start | bytes 1327112 | tf_op jit(solution)/shard_map/ppermute | solution.py:141
  110.8 11.0 %collective-permute-start.10 = (bf16[128,1536]{1,0:T(8,128)(2,1)S(1)}, bf16[128,1536]{1,0:T(8,128)(2,1)S(1)}, u32[]{:S(2)}, u32[]{:S(2)}) collective-permute-start(bf16[128,1536]{1,0:T(8,128)(2,1)S(1)} %fusion.31), channel_id=1, source_target_pairs={{0,2},{1,3},{2,0},{3,1},{4,6},{5,7},{6,4},{7,5},{8,10},{9,11},{10,... | collective-permute-start | bytes 1179656 | tf_op jit(solution)/shard_map/ppermute | solution.py:84
  119.1 11.8 %collective-permute-start.17 = (bf16[192,1152]{1,0:T(8,128)(2,1)S(1)}, bf16[192,1152]{1,0:T(8,128)(2,1)S(1)}, u32[]{:S(2)}, u32[]{:S(2)}) collective-permute-start(bf16[192,1152]{1,0:T(8,128)(2,1)S(1)} %collective-permute-done.15), channel_id=1, source_target_pairs={{0,8},{8,16},{16,24},{24,28},{28,20},{20,12},{12,4},{4,0},{1,9},{9... | collective-permute-start | bytes 1327112 | tf_op jit(solution)/shard_map/ppermute | solution.py:138
  120.8 14.4 %collective-permute-start.18 = (bf16[192,1152]{1,0:T(8,128)(2,1)S(1)}, bf16[192,1152]{1,0:T(8,128)(2,1)S(1)}, u32[]{:S(2)}, u32[]{:S(2)}) collective-permute-start(bf16[192,1152]{1,0:T(8,128)(2,1)S(1)} %collective-permute-done.16), channel_id=1, source_target_pairs={{0,4},{8,0},{16,8},{24,16},{28,24},{20,28},{12,20},{4,12},{1,5},{9... | collective-permute-start | bytes 1327112 | tf_op jit(solution)/shard_map/ppermute | solution.py:141
  124.3 10.1 %collective-permute-start.11 = (bf16[128,1536]{1,0:T(8,128)(2,1)S(1)}, bf16[128,1536]{1,0:T(8,128)(2,1)S(1)}, u32[]{:S(2)}, u32[]{:S(2)}) collective-permute-start(bf16[128,1536]{1,0:T(8,128)(2,1)S(1)} %get-tuple-element.60), channel_id=1, source_target_pairs={{0,2},{1,3},{2,0},{3,1},{4,6},{5,7},{6,4},{7,5},{8,10},{9,11},{10,... | collective-permute-start | bytes 1179656 | tf_op jit(solution)/shard_map/ppermute | solution.py:36
  130.9 10.9 %collective-permute-start.19 = (bf16[192,1152]{1,0:T(8,128)(2,1)S(1)}, bf16[192,1152]{1,0:T(8,128)(2,1)S(1)}, u32[]{:S(2)}, u32[]{:S(2)}) collective-permute-start(bf16[192,1152]{1,0:T(8,128)(2,1)S(1)} %collective-permute-done.17), channel_id=1, source_target_pairs={{0,8},{8,16},{16,24},{24,28},{28,20},{20,12},{12,4},{4,0},{1,9},{9... | collective-permute-start | bytes 1327112 | tf_op jit(solution)/shard_map/ppermute | solution.py:138
  135.2 6.6 %copy-start.2 = (bf16[4,128,1536]{2,1,0:T(8,128)(2,1)}, bf16[4,128,1536]{2,1,0:T(8,128)(2,1)S(1)}, u32[]{:S(2)}) copy-start(bf16[4,128,1536]{2,1,0:T(8,128)(2,1)S(1)} %get-tuple-element.66) | copy-start | bytes 4718596
  135.2 10.4 %collective-permute-start.12 = (bf16[2,128,1536]{2,1,0:T(8,128)(2,1)}, bf16[2,128,1536]{2,1,0:T(8,128)(2,1)}, u32[]{:S(2)}, u32[]{:S(2)}) collective-permute-start(bf16[2,128,1536]{2,1,0:T(8,128)(2,1)} %get-tuple-element.65), channel_id=1, source_target_pairs={{0,1},{1,0},{2,3},{3,2},{4,5},{5,4},{6,7},{7,6},{8,9},{9,8},{10,11... | collective-permute-start | bytes 2359304 | tf_op jit(solution)/shard_map/ppermute | solution.py:42
  149.1 4.2 %copy-start.14 = (f32[384]{0:T(512)S(1)}, f32[384]{0:T(512)}, u32[]{:S(2)}) copy-start(f32[384]{0:T(512)} %get-tuple-element.42) | copy-start | bytes 4612
  149.1 4.2 %copy-start.15 = (f32[384]{0:T(512)S(1)}, f32[384]{0:T(512)}, u32[]{:S(2)}) copy-start(f32[384]{0:T(512)} %get-tuple-element.43) | copy-start | bytes 4612
  149.1 4.2 %copy-start.16 = (f32[384]{0:T(512)S(1)}, f32[384]{0:T(512)}, u32[]{:S(2)}) copy-start(f32[384]{0:T(512)} %get-tuple-element.44) | copy-start | bytes 4612
  149.2 4.2 %copy-start.17 = (f32[384]{0:T(512)S(1)}, f32[384]{0:T(512)}, u32[]{:S(2)}) copy-start(f32[384]{0:T(512)} %get-tuple-element.45) | copy-start | bytes 4612
  149.2 4.2 %copy-start.18 = (f32[384]{0:T(512)S(1)}, f32[384]{0:T(512)}, u32[]{:S(2)}) copy-start(f32[384]{0:T(512)} %get-tuple-element.46) | copy-start | bytes 4612
  149.2 4.2 %copy-start.19 = (f32[384]{0:T(512)S(1)}, f32[384]{0:T(512)}, u32[]{:S(2)}) copy-start(f32[384]{0:T(512)} %get-tuple-element.55) | copy-start | bytes 4612
  149.2 4.2 %copy-start.20 = (f32[384]{0:T(512)S(1)}, f32[384]{0:T(512)}, u32[]{:S(2)}) copy-start(f32[384]{0:T(512)} %get-tuple-element.56) | copy-start | bytes 4612
  149.2 4.2 %copy-start.21 = (f32[384]{0:T(512)S(1)}, f32[384]{0:T(512)}, u32[]{:S(2)}) copy-start(f32[384]{0:T(512)} %get-tuple-element.57) | copy-start | bytes 4612
  149.2 4.2 %copy-start.22 = (f32[384]{0:T(512)S(1)}, f32[384]{0:T(512)}, u32[]{:S(2)}) copy-start(f32[384]{0:T(512)} %get-tuple-element.58) | copy-start | bytes 4612
  149.2 4.2 %copy-start.23 = (pred[512]{0:T(512)(128)(4,1)S(1)}, pred[512]{0:T(512)(128)(4,1)}, u32[]{:S(2)}) copy-start(pred[512]{0:T(512)(128)(4,1)} %get-tuple-element.87) | copy-start | bytes 1540
  149.2 4.2 %copy-start.24 = (pred[512]{0:T(512)(128)(4,1)S(1)}, pred[512]{0:T(512)(128)(4,1)}, u32[]{:S(2)}) copy-start(pred[512]{0:T(512)(128)(4,1)} %get-tuple-element.88) | copy-start | bytes 1540
  149.2 4.2 %copy-start.25 = (pred[512]{0:T(512)(128)(4,1)S(1)}, pred[512]{0:T(512)(128)(4,1)}, u32[]{:S(2)}) copy-start(pred[512]{0:T(512)(128)(4,1)} %get-tuple-element.89) | copy-start | bytes 1540
  149.2 4.2 %copy-start.26 = (pred[512]{0:T(512)(128)(4,1)S(1)}, pred[512]{0:T(512)(128)(4,1)}, u32[]{:S(2)}) copy-start(pred[512]{0:T(512)(128)(4,1)} %get-tuple-element.90) | copy-start | bytes 1540
  149.3 4.2 %copy-start.27 = (pred[512]{0:T(512)(128)(4,1)S(1)}, pred[512]{0:T(512)(128)(4,1)}, u32[]{:S(2)}) copy-start(pred[512]{0:T(512)(128)(4,1)} %get-tuple-element.91) | copy-start | bytes 1540
  149.3 4.2 %copy-start.28 = (pred[512]{0:T(512)(128)(4,1)S(1)}, pred[512]{0:T(512)(128)(4,1)}, u32[]{:S(2)}) copy-start(pred[512]{0:T(512)(128)(4,1)} %get-tuple-element.92) | copy-start | bytes 1540
  149.3 4.2 %copy-start.29 = (pred[512]{0:T(512)(128)(4,1)S(1)}, pred[512]{0:T(512)(128)(4,1)}, u32[]{:S(2)}) copy-start(pred[512]{0:T(512)(128)(4,1)} %get-tuple-element.93) | copy-start | bytes 1540
  149.3 4.2 %copy-start.30 = (pred[512]{0:T(512)(128)(4,1)S(1)}, pred[512]{0:T(512)(128)(4,1)}, u32[]{:S(2)}) copy-start(pred[512]{0:T(512)(128)(4,1)} %get-tuple-element.94) | copy-start | bytes 1540
  149.3 4.2 %copy-start.31 = (pred[512]{0:T(512)(128)(4,1)S(1)}, pred[512]{0:T(512)(128)(4,1)}, u32[]{:S(2)}) copy-start(pred[512]{0:T(512)(128)(4,1)} %get-tuple-element.95) | copy-start | bytes 1540
  149.3 4.2 %copy-start.32 = (pred[512]{0:T(512)(128)(4,1)S(1)}, pred[512]{0:T(512)(128)(4,1)}, u32[]{:S(2)}) copy-start(pred[512]{0:T(512)(128)(4,1)} %get-tuple-element.96) | copy-start | bytes 1540
  153.0 7.2 %copy-start.1 = (bf16[8,192,384]{2,1,0:T(8,128)(2,1)S(1)}, bf16[8,192,384]{2,1,0:T(8,128)(2,1)}, u32[]{:S(2)}) copy-start(bf16[8,192,384]{2,1,0:T(8,128)(2,1)} %slice.433) | copy-start | bytes 3538948
  161.3 2.4 %collective-permute-start.20 = (bf16[2,128,1536]{2,1,0:T(8,128)(2,1)S(1)}, bf16[2,128,1536]{2,1,0:T(8,128)(2,1)S(1)}, u32[]{:S(2)}, u32[]{:S(2)}) collective-permute-start(bf16[2,128,1536]{2,1,0:T(8,128)(2,1)S(1)} %dynamic-slice_bitcast_fusion), channel_id=1, source_target_pairs={{0,1},{1,0},{2,3},{3,2},{4,5},{5,4},{6,7},{7,6},{8,9},{9,8},{10,11... | collective-permute-start | bytes 2359304 | tf_op jit(solution)/shard_map/ppermute | solution.py:78
  163.9 11.2 %collective-permute-start.21 = (bf16[128,1536]{1,0:T(8,128)(2,1)S(1)}, bf16[128,1536]{1,0:T(8,128)(2,1)S(1)}, u32[]{:S(2)}, u32[]{:S(2)}) collective-permute-start(bf16[128,1536]{1,0:T(8,128)(2,1)S(1)} %fusion.32), channel_id=1, source_target_pairs={{0,2},{1,3},{2,0},{3,1},{4,6},{5,7},{6,4},{7,5},{8,10},{9,11},{10,... | collective-permute-start | bytes 1179656 | tf_op jit(solution)/shard_map/ppermute | solution.py:84
  (25 other events, 96.5 us)

commit v11 on v9

--- a/solution.py
+++ b/solution.py
@@ -124,23 +124,32 @@
     return cycle
 
 
-def ring_gather(block, ring):
+def ring_gather(block, ring, cuts):
     count = len(ring)
     me = lax.axis_index("dp")
     my_pos = jnp.asarray([ring.index(i) for i in range(count)], jnp.int32)[me]
     order = jnp.asarray(ring, jnp.int32)
     forward = [(ring[p], ring[(p + 1) % count]) for p in range(count)]
     backward = [(ring[p], ring[(p - 1) % count]) for p in range(count)]
-    out = jnp.zeros((count,) + block.shape, block.dtype)
-    out = lax.dynamic_update_index_in_dim(out, block, me, 0)
+    edges = [0] + list(cuts) + [block.shape[-1]]
+    spans = list(zip(edges[:-1], edges[1:]))
+    outs = [jnp.zeros((count,) + block.shape[:-1] + (hi - lo,), block.dtype) for lo, hi in spans]
+
+    def place(outs, piece, where):
+        return [
+            lax.dynamic_update_index_in_dim(out, piece[..., lo:hi], where, 0)
+            for out, (lo, hi) in zip(outs, spans)
+        ]
+
+    outs = place(outs, block, me)
     ahead = behind = block
     for step in range(1, count // 2 + 1):
         ahead = lax.ppermute(ahead, "dp", forward)
-        out = lax.dynamic_update_index_in_dim(out, ahead, order[(my_pos - step) % count], 0)
+        outs = place(outs, ahead, order[(my_pos - step) % count])
         if step <= count - 1 - count // 2:
             behind = lax.ppermute(behind, "dp", backward)
-            out = lax.dynamic_update_index_in_dim(out, behind, order[(my_pos + step) % count], 0)
-    return out
+            outs = place(outs, behind, order[(my_pos + step) % count])
+    return outs
 
 
 def after(token, value):
@@ -198,15 +207,19 @@
     group_rows = frame_rows * seq_count
     group_width = model_width // seq_count
     kernel_reach = dw_kernel.shape[0] // 2
-    qkv_parts = ring_gather(w_qkv.reshape(w_qkv.shape[0], 3 * group_width), ring)
+    qkv_local = w_qkv.reshape(w_qkv.shape[0], 3 * group_width)
+    qkv_parts, out_parts = ring_gather(
+        jnp.concatenate([qkv_local, w_out.T], axis=1), ring, [3 * group_width]
+    )
     qkv_matrix = qkv_parts.reshape(model_width, 3 * group_width)
-    out_parts = ring_gather(after(qkv_parts, w_out.T), ring)
     out_cols = out_parts.reshape(model_width, w_out.shape[0])
     glu_rows = w_glu.shape[0]
     glu_local = w_glu.reshape(glu_rows, 2 * group_width)
-    both_parts = ring_gather(after(out_parts, jnp.concatenate([glu_local, w_proj.T], axis=1)), ring)
-    glu_matrix = both_parts[:, :, : 2 * group_width].reshape(model_width, 2 * group_width)
-    proj_cols = both_parts[:, :, 2 * group_width :].reshape(model_width, w_proj.shape[0])
+    glu_parts, proj_parts = ring_gather(
+        after(out_parts, jnp.concatenate([glu_local, w_proj.T], axis=1)), ring, [2 * group_width]
+    )
+    glu_matrix = glu_parts.reshape(model_width, 2 * group_width)
+    proj_cols = proj_parts.reshape(model_width, w_proj.shape[0])
     inputs = frames[0].astype(jnp.float32)
     record_ends = jnp.cumsum(lengths[0])
     seg_all = segment_of(record_ends, jnp.arange(group_rows, dtype=jnp.int32))

time: 183 us -> 175 us (0.956)
  waiting for transfers between devices: 74.9 us -> 63.5 us
  local copies, waits for them, and re-layouts: 28.9 us -> 37.5 us
  starting transfers between devices: 28.5 us -> 20.8 us
    ppermute x12 -> x8, waiting for transfers between devices: 60.5 us -> 45 us  [ring_gather(): ahead = lax.ppermute(ahead, 'dp', forward)]
    dynamic_update_slice x24 -> x32, local copies, waits for them, and re-layouts: 9.82 us -> 17.4 us  [place(): lax.dynamic_update_index_in_dim(out, piece[..., lo:hi], where, 0)]
    ppermute x12 -> x8, starting transfers between devices: 20.7 us -> 14.2 us  [ring_gather(): ahead = lax.ppermute(ahead, 'dp', forward)]
    ppermute x2, waiting for transfers between devices: 0.01 us -> 3.6 us  [seq_gather(): lax.ppermute(block, 'seq', [(i, (i + 2 * shift) % count) for i in range(c...]
    unnamed x102 -> x90, local copies, waits for them, and re-layouts: 2.2 us -> 4.73 us
    another operation x6, local copies, waits for them, and re-layouts: 3.89 us -> 1.46 us
    ppermute x2, waiting for transfers between devices: 10.6 us -> 12.6 us  [seq_scatter_sum(): lax.ppermute(piece.astype(jnp.bfloat16), 'seq', [(i, (i + 2 * shift) % co...]
    concatenate x0 -> x1, other arithmetic: none -> 1.87 us  [on_device(): jnp.concatenate([qkv_local, w_out.T], axis=1)]
  transfers between devices with their start and end apart: 29 -> 22, of which waited for: 15 -> 10; matrix products, arithmetic and copies ran while one was open for 23% -> 29% of each run, Pallas kernels for 0% -> 0%
where the time goes in v11:
time: 175 us; the launch traced here: 174 us
  waiting for transfers between devices  63.5 us (36%)
  local copies, waits for them, and re-layouts  37.5 us (21%)
  starting transfers between devices  20.8 us (12%)
  between operations  18.1 us (10%)
  matrix products  17.1 us (10%)
  other arithmetic  16.8 us (10%)
    ppermute x8, waiting for transfers between devices, ring_gather(): ahead = lax.ppermute(ahead, 'dp', forward)  45 us
    dynamic_update_slice x32, local copies, waits for them, and re-layouts, place(): lax.dynamic_update_index_in_dim(out, piece[..., lo:hi], where, 0)  17.4 us
    ppermute x8, starting transfers between devices, ring_gather(): ahead = lax.ppermute(ahead, 'dp', forward)  14.2 us
    ppermute x2, waiting for transfers between devices, seq_scatter_sum(): lax.ppermute(piece.astype(jnp.bfloat16), 'seq', [(i, (i + 2 * shift) % co...  12.6 us
    convert_element_type x1, other arithmetic, depthwise(): return jax.nn.silu(total_acc).astype(jnp.bfloat16)  5.53 us
    dot_general x1, matrix products, on_device(): jnp.dot(seq_gather(normed1, paired).reshape(group_rows, model_width), qkv...  5.2 us
    unnamed x90, local copies, waits for them, and re-layouts  4.73 us
    sub x1, matrix products, one_block(): weights = jnp.exp(scores - top_score)  3.65 us
  transfers between devices with their start and end apart: 22, of which 10 were waited for; matrix products, arithmetic and copies ran while one was open for 29% of the time, Pallas kernels for 0%

profile of v11, /device:TPU:0, one launch (start us, length us, event | category | flops | bytes accessed | tf_op | source)
XLA Modules:
  0.0 173.7 jit_solution(5115962161508815903)
XLA Ops:
  0.0 1.1 copy.41
  1.1 1.9 %pad_maximum_fusion = bf16[192,1536]{1,0:T(8,128)(2,1)} fusion(bf16[192,384]{1,0:T(8,128)(2,1)} %bitcast.268, bf16[192,1152]{1,0:T(8,128)(2,1)S(1)} %bitcast.261), kind=kLoop, calls=%fused_computation.51 | loop fusion | flops 1179648 | bytes 1179648 | tf_op jit(solution)/shard_map/concatenate | solution.py:212
  3.0 3.0 %collective-permute-start.2 = (bf16[192,1536]{1,0:T(8,128)(2,1)}, bf16[192,1536]{1,0:T(8,128)(2,1)}, u32[]{:S(2)}, u32[]{:S(2)}) collective-permute-start(bf16[192,1536]{1,0:T(8,128)(2,1)} %pad_maximum_fusion), channel_id=1, source_target_pairs={{0,8},{8,16},{16,24},{24,28},{28,20},{20,12},{12,4},{4,0},{1,9},{9... | collective-permute-start | bytes 1769480 | tf_op jit(solution)/shard_map/ppermute | solution.py:147
  6.4 1.0 fusion.18
  7.5 1.9 %collective-permute-start = (bf16[128,1536]{1,0:T(8,128)(2,1)}, bf16[128,1536]{1,0:T(8,128)(2,1)}, u32[]{:S(2)}, u32[]{:S(2)}) collective-permute-start(bf16[128,1536]{1,0:T(8,128)(2,1)} %fusion.18), channel_id=1, source_target_pairs={{0,2},{1,3},{2,0},{3,1},{4,6},{5,7},{6,4},{7,5},{8,10},{9,11},{10,... | collective-permute-start | bytes 1179656 | tf_op jit(solution)/shard_map/ppermute | solution.py:36
  14.1 1.2 copy-done.3
  30.7 1.0 copy.42
  36.0 1.7 pad_maximum_fusion.1
  37.8 1.8 %bitcast_dynamic-update-slice_fusion.4 = (bf16[2,128,1536]{2,1,0:T(8,128)(2,1)}, bf16[4,128,1536]{2,1,0:T(8,128)(2,1)S(1)}) fusion(bf16[2,128,1536]{2,1,0:T(8,128)(2,1)} %copy-done.6, s32[]{:T(128)S(6)} %select_n.354, bf16[128,1536]{1,0:T(8,128)(2,1)} %collective-permute-done, bf16[4,128,1536]{2,1,0:T(8,128)(2,1)S(1)} %get-tuple-element.64, s32[]{:T(128)S(6)} %select_n.350), kind=kLoop, calls=%fused_computation.83 | loop fusion | bytes 1179656 | tf_op jit(solution)/shard_map/jit(dynamic_update_index_in_dim)/dynamic_update_slice | solution.py:40
  39.6 1.6 collective-permute-start.4
  41.6 1.8 %fusion.35 = bf16[8,192,1152]{2,1,0:T(8,128)(2,1)} fusion(bf16[8,192,1152]{2,1,0:T(8,128)(2,1)} %copy-done.3, s32[]{:T(128)S(6)} %select_n.361, bf16[192,1536]{1,0:T(8,128)(2,1)} %collective-permute-done.2), kind=kLoop, calls=%fused_computation.66 | loop fusion | bytes 884740 | tf_op jit(solution)/shard_map/jit(dynamic_update_index_in_dim)/dynamic_update_slice | solution.py:140
  43.4 1.8 %fusion.34 = bf16[8,192,1152]{2,1,0:T(8,128)(2,1)} fusion(bf16[8,192,1152]{2,1,0:T(8,128)(2,1)} %fusion.35, s32[]{:T(128)S(6)} %select_n.364, bf16[192,1536]{1,0:T(8,128)(2,1)} %collective-permute-done.3), kind=kLoop, calls=%fused_computation.64 | loop fusion | bytes 884740 | tf_op jit(solution)/shard_map/jit(dynamic_update_index_in_dim)/dynamic_update_slice | solution.py:140
  46.2 0.9 fusion.62
  47.1 8.4 %collective-permute-done.4 = bf16[192,1536]{1,0:T(8,128)(2,1)S(1)} collective-permute-done((bf16[192,1536]{1,0:T(8,128)(2,1)}, bf16[192,1536]{1,0:T(8,128)(2,1)S(1)}, u32[]{:S(2)}, u32[]{:S(2)}) %collective-permute-start.4) | collective-permute-done | bytes 589856 | tf_op jit(solution)/shard_map/ppermute | solution.py:147
  55.5 1.6 collective-permute-start.6
  59.3 11.1 %collective-permute-done.6 = bf16[192,1536]{1,0:T(8,128)(2,1)S(1)} collective-permute-done((bf16[192,1536]{1,0:T(8,128)(2,1)S(1)}, bf16[192,1536]{1,0:T(8,128)(2,1)S(1)}, u32[]{:S(2)}, u32[]{:S(2)}) %collective-permute-start.6) | collective-permute-done | bytes 589856 | tf_op jit(solution)/shard_map/ppermute | solution.py:147
  70.5 1.6 collective-permute-start.8
  73.8 10.8 %collective-permute-done.8 = bf16[192,1536]{1,0:T(8,128)(2,1)S(1)} collective-permute-done((bf16[192,1536]{1,0:T(8,128)(2,1)S(1)}, bf16[192,1536]{1,0:T(8,128)(2,1)S(1)}, u32[]{:S(2)}, u32[]{:S(2)}) %collective-permute-start.8) | collective-permute-done | bytes 589856 | tf_op jit(solution)/shard_map/ppermute | solution.py:147
  84.6 1.6 collective-permute-start.13
  87.5 5.2 %convolution_convert_fusion = bf16[512,1152]{1,0:T(8,128)(2,1)} fusion(bf16[512,1536]{1,0:T(8,128)(2,1)S(1)} %bitcast.263, bf16[1536,1152]{1,0:T(8,128)(2,1)} %bitcast.259), kind=kOutput, calls=%fused_computation.5 | convolution fusion | flops 1812529152 | bytes 6291456 | tf_op jit(solution)/shard_map/dot_general | solution.py:228
  92.7 1.6 copy.32
  94.3 3.6 %fusion.69 = (f32[4,512]{1,0:T(4,128)S(1)}, f32[4,512,512]{1,2,0:T(8,128)}) fusion(pred[512,512]{0,1:T(8,128)(4,1)S(1)} %copy-done.9, bf16[512,3,4,96]{0,3,2,1:T(8,128)(2,1)S(1)} %bitcast.266), kind=kOutput, calls=%fused_computation.213 | convolution fusion | flops 205521408 | bytes 5251072 | tf_op jit(solution)/shard_map/while/body/eval_jaxpr/sub | solution.py:179
  97.9 2.7 %fusion.6 = bf16[4,96,512]{2,1,0:T(8,128)(2,1)S(1)} fusion(f32[4,512,512]{1,2,0:T(8,128)} %get-tuple-element.108, f32[4,512]{1,0:T(4,128)S(1)} %get-tuple-element.107, bf16[512,3,4,96]{0,3,2,1:T(8,128)(2,1)S(1)} %bitcast.267), kind=kOutput, calls=%fused_computation.14 | convolution fusion | flops 203620352 | bytes 4988928 | tf_op jit(solution)/shard_map/while/body/eval_jaxpr/hqk,khe->qhe/dot_general | solution.py:181
  100.6 1.0 convolution_convert_fusion.2
  101.9 0.9 bitcast_dynamic-update-slice_fusion.8
  103.0 1.0 bitcast_dynamic-update-slice_fusion.6
  104.0 1.6 collective-permute-start.15
  107.0 0.9 fusion.55
  108.0 1.0 fusion.49
  109.0 1.0 fusion.48
  111.0 5.9 %collective-permute-done.15 = bf16[192,1152]{1,0:T(8,128)(2,1)S(1)} collective-permute-done((bf16[192,1152]{1,0:T(8,128)(2,1)}, bf16[192,1152]{1,0:T(8,128)(2,1)S(1)}, u32[]{:S(2)}, u32[]{:S(2)}) %collective-permute-start.15) | collective-permute-done | bytes 442400 | tf_op jit(solution)/shard_map/ppermute | solution.py:147
  116.9 1.6 collective-permute-start.17
  119.3 2.0 %collective-permute-done.10 = bf16[128,1536]{1,0:T(8,128)(2,1)S(1)} collective-permute-done((bf16[128,1536]{1,0:T(8,128)(2,1)S(1)}, bf16[128,1536]{1,0:T(8,128)(2,1)S(1)}, u32[]{:S(2)}, u32[]{:S(2)}) %collective-permute-start.10) | collective-permute-done | bytes 393248 | tf_op jit(solution)/shard_map/ppermute | solution.py:84
  121.8 1.0 broadcast.157
  122.7 1.0 bitcast_dynamic-update-slice_fusion.2
  124.6 4.0 %collective-permute-done.17 = bf16[192,1152]{1,0:T(8,128)(2,1)S(1)} collective-permute-done((bf16[192,1152]{1,0:T(8,128)(2,1)S(1)}, bf16[192,1152]{1,0:T(8,128)(2,1)S(1)}, u32[]{:S(2)}, u32[]{:S(2)}) %collective-permute-start.17) | collective-permute-done | bytes 442400 | tf_op jit(solution)/shard_map/ppermute | solution.py:147
  128.6 1.6 collective-permute-start.19
  130.3 3.6 %collective-permute-done.11 = bf16[128,1536]{1,0:T(8,128)(2,1)S(1)} collective-permute-done((bf16[128,1536]{1,0:T(8,128)(2,1)S(1)}, bf16[128,1536]{1,0:T(8,128)(2,1)S(1)}, u32[]{:S(2)}, u32[]{:S(2)}) %collective-permute-start.11) | collective-permute-done | bytes 393248 | tf_op jit(solution)/shard_map/ppermute | solution.py:36
  134.8 4.7 %collective-permute-done.19 = bf16[192,1152]{1,0:T(8,128)(2,1)S(1)} collective-permute-done((bf16[192,1152]{1,0:T(8,128)(2,1)S(1)}, bf16[192,1152]{1,0:T(8,128)(2,1)S(1)}, u32[]{:S(2)}, u32[]{:S(2)}) %collective-permute-start.19) | collective-permute-done | bytes 442400 | tf_op jit(solution)/shard_map/ppermute | solution.py:147
  140.3 2.4 %copy.38 = bf16[768,1536]{1,0:T(8,128)(2,1)} copy(bf16[768,1536]{0,1:T(8,128)(2,1)S(1)} %bitcast.252) | data formatting | bytes 4718592 | tf_op jit(solution)/shard_map/dot_general | solution.py:240
  142.7 1.6 fusion.50
  144.3 1.8 %slice_dynamic-update-slice_fusion.1 = bf16[4,128,1536]{2,1,0:T(8,128)(2,1)} fusion(bf16[4,128,1536]{2,1,0:T(8,128)(2,1)} %copy-done.5, s32[]{:T(128)S(6)} %select_n.356, bf16[2,128,1536]{2,1,0:T(8,128)(2,1)} %collective-permute-done.12), kind=kLoop, calls=%fused_computation.73 | loop fusion | bytes 786436 | tf_op jit(solution)/shard_map/jit(dynamic_update_index_in_dim)/dynamic_update_slice | solution.py:45
  146.1 1.8 %slice_dynamic-update-slice_fusion = bf16[4,128,1536]{2,1,0:T(8,128)(2,1)} fusion(bf16[4,128,1536]{2,1,0:T(8,128)(2,1)} %slice_dynamic-update-slice_fusion.1, s32[]{:T(128)S(6)} %select_n.357, bf16[2,128,1536]{2,1,0:T(8,128)(2,1)} %collective-permute-done.12), kind=kLoop, calls=%fused_computation.72 | loop fusion | bytes 786436 | tf_op jit(solution)/shard_map/jit(dynamic_update_index_in_dim)/dynamic_update_slice | solution.py:45
  147.9 3.5 %fusion.70 = f32[512,2,384]{2,0,1:T(8,128)S(1)} fusion(bf16[512,1536,1]{1,0,2:T(8,128)(2,1)} %bitcast.264, bf16[2,384,1536]{2,1,0:T(8,128)(2,1)} %bitcast.260), kind=kOutput, calls=%fused_computation.214 | convolution fusion | flops 1207959552 | bytes 5505024 | tf_op jit(solution)/shard_map/dot_general | solution.py:240
  152.3 5.5 %multiply_convert_fusion = bf16[512,384]{1,0:T(8,128)(2,1)S(1)} fusion(bf16[512,384]{1,0:T(8,128)(2,1)S(1)} %fusion.41, f32[384]{0:T(512)S(1)} %get-tuple-element.57, f32[384]{0:T(512)S(1)} %get-tuple-element.58, f32[384]{0:T(512)S(1)} %get-tuple-element.20, f32[384]{0:T(512)S(1)} %get-tuple-element.28, f32[384]{0:T(512)S(1)} %get-tuple-element.30, ...), kind=kLoop, calls=%fused_computation.47 | loop fusion | flops 25165824 | bytes 849920 | tf_op jit(solution)/shard_map/convert_element_type | solution.py:200
  157.9 1.0 convolution_convert_fusion.1
  159.1 2.3 %collective-permute-done.20 = bf16[2,128,1536]{2,1,0:T(8,128)(2,1)S(1)} collective-permute-done((bf16[2,128,1536]{2,1,0:T(8,128)(2,1)S(1)}, bf16[2,128,1536]{2,1,0:T(8,128)(2,1)S(1)}, u32[]{:S(2)}, u32[]{:S(2)}) %collective-permute-start.20) | collective-permute-done | bytes 786464 | tf_op jit(solution)/shard_map/ppermute | solution.py:78
  162.3 10.5 %collective-permute-done.21 = bf16[128,1536]{1,0:T(8,128)(2,1)S(1)} collective-permute-done((bf16[128,1536]{1,0:T(8,128)(2,1)S(1)}, bf16[128,1536]{1,0:T(8,128)(2,1)S(1)}, u32[]{:S(2)}, u32[]{:S(2)}) %collective-permute-start.21) | collective-permute-done | bytes 393248 | tf_op jit(solution)/shard_map/ppermute | solution.py:84
  (176 shorter events, 23.0 us)
Async XLA Ops:
  0.0 6.0 %copy-start = (bf16[1,128,1536]{2,1,0:T(8,128)(2,1)S(1)}, bf16[1,128,1536]{2,1,0:T(8,128)(2,1)}, u32[]{:S(2)}) copy-start(bf16[1,128,1536]{2,1,0:T(8,128)(2,1)} %param.13) | copy-start | bytes 1179652
  0.0 6.4 %copy-start.11 = (f32[1536]{0:T(1024)S(1)}, f32[1536]{0:T(1024)}, u32[]{:S(2)}) copy-start(f32[1536]{0:T(1024)} %param.15) | copy-start | bytes 18436
  1.1 8.3 %copy-start.4 = (bf16[192,3,384]{2,0,1:T(8,128)(2,1)S(1)}, bf16[192,3,384]{2,0,1:T(8,128)(2,1)}, u32[]{:S(2)}) copy-start(bf16[192,3,384]{2,0,1:T(8,128)(2,1)} %param.17) | copy-start | bytes 1327108
  3.0 6.8 %copy-start.42 = (s32[1,4]{1,0:T(1,128)S(1)}, s32[1,4]{1,0:T(1,128)}, u32[]{:S(2)}) copy-start(s32[1,4]{1,0:T(1,128)} %param.14) | copy-start | bytes 52
  3.0 36.6 %collective-permute-start.2 = (bf16[192,1536]{1,0:T(8,128)(2,1)}, bf16[192,1536]{1,0:T(8,128)(2,1)}, u32[]{:S(2)}, u32[]{:S(2)}) collective-permute-start(bf16[192,1536]{1,0:T(8,128)(2,1)} %pad_maximum_fusion), channel_id=1, source_target_pairs={{0,8},{8,16},{16,24},{24,28},{28,20},{20,12},{12,4},{4,0},{1,9},{9... | collective-permute-start | bytes 1769480 | tf_op jit(solution)/shard_map/ppermute | solution.py:147
  6.0 35.1 %collective-permute-start.3 = (bf16[192,1536]{1,0:T(8,128)(2,1)}, bf16[192,1536]{1,0:T(8,128)(2,1)}, u32[]{:S(2)}, u32[]{:S(2)}) collective-permute-start(bf16[192,1536]{1,0:T(8,128)(2,1)} %pad_maximum_fusion), channel_id=1, source_target_pairs={{0,4},{8,0},{16,8},{24,16},{28,24},{20,28},{12,20},{4,12},{1,5},{9... | collective-permute-start | bytes 1769480 | tf_op jit(solution)/shard_map/ppermute | solution.py:150
  7.5 30.3 %collective-permute-start = (bf16[128,1536]{1,0:T(8,128)(2,1)}, bf16[128,1536]{1,0:T(8,128)(2,1)}, u32[]{:S(2)}, u32[]{:S(2)}) collective-permute-start(bf16[128,1536]{1,0:T(8,128)(2,1)} %fusion.18), channel_id=1, source_target_pairs={{0,2},{1,3},{2,0},{3,1},{4,6},{5,7},{6,4},{7,5},{8,10},{9,11},{10,... | collective-permute-start | bytes 1179656 | tf_op jit(solution)/shard_map/ppermute | solution.py:36
  9.4 3.6 %copy-start.7 = (bf16[384,192]{0,1:T(8,128)(2,1)S(1)}, bf16[384,192]{0,1:T(8,128)(2,1)}, u32[]{:S(2)}) copy-start(bf16[384,192]{0,1:T(8,128)(2,1)} %param.18) | copy-start | bytes 442372
  13.6 1.8 %copy-start.3 = (bf16[8,192,1152]{2,1,0:T(8,128)(2,1)}, bf16[8,192,1152]{2,1,0:T(8,128)(2,1)S(1)}, u32[]{:S(2)}) copy-start(bf16[8,192,1152]{2,1,0:T(8,128)(2,1)S(1)} %constant_dynamic-update-slice_fusion) | copy-start | bytes 10616836
  13.6 2.6 %copy-start.10 = (bf16[31,384]{1,0:T(8,128)(2,1)S(1)}, bf16[31,384]{1,0:T(8,128)(2,1)}, u32[]{:S(2)}) copy-start(bf16[31,384]{1,0:T(8,128)(2,1)} %param.20) | copy-start | bytes 71428
  13.7 2.7 %copy-start.43 = (s32[8]{0:T(128)S(1)}, s32[8]{0:T(128)}, u32[]{:S(2)}) copy-start(s32[8]{0:T(128)} %constant.347.clone) | copy-start | bytes 100
  13.7 7.8 %copy-start.12 = (s32[8]{0:T(128)S(1)}, s32[8]{0:T(128)}, u32[]{:S(2)}) copy-start(s32[8]{0:T(128)} %constant.348.clone) | copy-start | bytes 100
  15.3 0.9 copy-start.6
  39.6 18.8 %collective-permute-start.1 = (bf16[2,128,1536]{2,1,0:T(8,128)(2,1)}, bf16[2,128,1536]{2,1,0:T(8,128)(2,1)S(1)}, u32[]{:S(2)}, u32[]{:S(2)}) collective-permute-start(bf16[2,128,1536]{2,1,0:T(8,128)(2,1)} %get-tuple-element.67), channel_id=1, source_target_pairs={{0,1},{1,0},{2,3},{3,2},{4,5},{5,4},{6,7},{7,6},{8,9},{9,8},{10,11... | collective-permute-start | bytes 2359304 | tf_op jit(solution)/shard_map/ppermute | solution.py:42
  39.6 16.0 %collective-permute-start.4 = (bf16[192,1536]{1,0:T(8,128)(2,1)}, bf16[192,1536]{1,0:T(8,128)(2,1)S(1)}, u32[]{:S(2)}, u32[]{:S(2)}) collective-permute-start(bf16[192,1536]{1,0:T(8,128)(2,1)} %collective-permute-done.2), channel_id=1, source_target_pairs={{0,8},{8,16},{16,24},{24,28},{28,20},{20,12},{12,4},{4,0},{1,9},{9... | collective-permute-start | bytes 1769480 | tf_op jit(solution)/shard_map/ppermute | solution.py:147
  41.2 16.0 %collective-permute-start.5 = (bf16[192,1536]{1,0:T(8,128)(2,1)}, bf16[192,1536]{1,0:T(8,128)(2,1)S(1)}, u32[]{:S(2)}, u32[]{:S(2)}) collective-permute-start(bf16[192,1536]{1,0:T(8,128)(2,1)} %collective-permute-done.3), channel_id=1, source_target_pairs={{0,4},{8,0},{16,8},{24,16},{28,24},{20,28},{12,20},{4,12},{1,5},{9... | collective-permute-start | bytes 1769480 | tf_op jit(solution)/shard_map/ppermute | solution.py:150
  55.5 15.0 %collective-permute-start.6 = (bf16[192,1536]{1,0:T(8,128)(2,1)S(1)}, bf16[192,1536]{1,0:T(8,128)(2,1)S(1)}, u32[]{:S(2)}, u32[]{:S(2)}) collective-permute-start(bf16[192,1536]{1,0:T(8,128)(2,1)S(1)} %collective-permute-done.4), channel_id=1, source_target_pairs={{0,8},{8,16},{16,24},{24,28},{28,20},{20,12},{12,4},{4,0},{1,9},{9... | collective-permute-start | bytes 1769480 | tf_op jit(solution)/shard_map/ppermute | solution.py:147
  57.1 15.8 %collective-permute-start.7 = (bf16[192,1536]{1,0:T(8,128)(2,1)S(1)}, bf16[192,1536]{1,0:T(8,128)(2,1)S(1)}, u32[]{:S(2)}, u32[]{:S(2)}) collective-permute-start(bf16[192,1536]{1,0:T(8,128)(2,1)S(1)} %collective-permute-done.5), channel_id=1, source_target_pairs={{0,4},{8,0},{16,8},{24,16},{28,24},{20,28},{12,20},{4,12},{1,5},{9... | collective-permute-start | bytes 1769480 | tf_op jit(solution)/shard_map/ppermute | solution.py:150
  70.5 14.1 %collective-permute-start.8 = (bf16[192,1536]{1,0:T(8,128)(2,1)S(1)}, bf16[192,1536]{1,0:T(8,128)(2,1)S(1)}, u32[]{:S(2)}, u32[]{:S(2)}) collective-permute-start(bf16[192,1536]{1,0:T(8,128)(2,1)S(1)} %collective-permute-done.6), channel_id=1, source_target_pairs={{0,8},{8,16},{16,24},{24,28},{28,20},{20,12},{12,4},{4,0},{1,9},{9... | collective-permute-start | bytes 1769480 | tf_op jit(solution)/shard_map/ppermute | solution.py:147
  84.6 19.4 %collective-permute-start.13 = (bf16[192,1152]{1,0:T(8,128)(2,1)}, bf16[192,1152]{1,0:T(8,128)(2,1)}, u32[]{:S(2)}, u32[]{:S(2)}) collective-permute-start(bf16[192,1152]{1,0:T(8,128)(2,1)} %pad_maximum_fusion.1), channel_id=1, source_target_pairs={{0,8},{8,16},{16,24},{24,28},{28,20},{20,12},{12,4},{4,0},{1,9},{9... | collective-permute-start | bytes 1327112 | tf_op jit(solution)/shard_map/ppermute | solution.py:147
  86.2 19.4 %collective-permute-start.14 = (bf16[192,1152]{1,0:T(8,128)(2,1)}, bf16[192,1152]{1,0:T(8,128)(2,1)}, u32[]{:S(2)}, u32[]{:S(2)}) collective-permute-start(bf16[192,1152]{1,0:T(8,128)(2,1)} %pad_maximum_fusion.1), channel_id=1, source_target_pairs={{0,4},{8,0},{16,8},{24,16},{28,24},{20,28},{12,20},{4,12},{1,5},{9... | collective-permute-start | bytes 1327112 | tf_op jit(solution)/shard_map/ppermute | solution.py:150
  92.7 1.6 copy-start.9
  101.7 8.3 %collective-permute-start.9 = (bf16[2,128,1536]{2,1,0:T(8,128)(2,1)S(1)}, bf16[2,128,1536]{2,1,0:T(8,128)(2,1)S(1)}, u32[]{:S(2)}, u32[]{:S(2)}) collective-permute-start(bf16[2,128,1536]{2,1,0:T(8,128)(2,1)S(1)} %dynamic-slice_bitcast_fusion.1), channel_id=1, source_target_pairs={{0,1},{1,0},{2,3},{3,2},{4,5},{5,4},{6,7},{7,6},{8,9},{9,8},{10,11... | collective-permute-start | bytes 2359304 | tf_op jit(solution)/shard_map/ppermute | solution.py:78
  104.0 12.8 %collective-permute-start.15 = (bf16[192,1152]{1,0:T(8,128)(2,1)}, bf16[192,1152]{1,0:T(8,128)(2,1)S(1)}, u32[]{:S(2)}, u32[]{:S(2)}) collective-permute-start(bf16[192,1152]{1,0:T(8,128)(2,1)} %collective-permute-done.13), channel_id=1, source_target_pairs={{0,8},{8,16},{16,24},{24,28},{28,20},{20,12},{12,4},{4,0},{1,9},{9... | collective-permute-start | bytes 1327112 | tf_op jit(solution)/shard_map/ppermute | solution.py:147
  105.7 12.8 %collective-permute-start.16 = (bf16[192,1152]{1,0:T(8,128)(2,1)}, bf16[192,1152]{1,0:T(8,128)(2,1)S(1)}, u32[]{:S(2)}, u32[]{:S(2)}) collective-permute-start(bf16[192,1152]{1,0:T(8,128)(2,1)} %collective-permute-done.14), channel_id=1, source_target_pairs={{0,4},{8,0},{16,8},{24,16},{28,24},{20,28},{12,20},{4,12},{1,5},{9... | collective-permute-start | bytes 1327112 | tf_op jit(solution)/shard_map/ppermute | solution.py:150
  110.3 11.0 %collective-permute-start.10 = (bf16[128,1536]{1,0:T(8,128)(2,1)S(1)}, bf16[128,1536]{1,0:T(8,128)(2,1)S(1)}, u32[]{:S(2)}, u32[]{:S(2)}) collective-permute-start(bf16[128,1536]{1,0:T(8,128)(2,1)S(1)} %fusion.38), channel_id=1, source_target_pairs={{0,2},{1,3},{2,0},{3,1},{4,6},{5,7},{6,4},{7,5},{8,10},{9,11},{10,... | collective-permute-start | bytes 1179656 | tf_op jit(solution)/shard_map/ppermute | solution.py:84
  116.9 11.8 %collective-permute-start.17 = (bf16[192,1152]{1,0:T(8,128)(2,1)S(1)}, bf16[192,1152]{1,0:T(8,128)(2,1)S(1)}, u32[]{:S(2)}, u32[]{:S(2)}) collective-permute-start(bf16[192,1152]{1,0:T(8,128)(2,1)S(1)} %collective-permute-done.15), channel_id=1, source_target_pairs={{0,8},{8,16},{16,24},{24,28},{28,20},{20,12},{12,4},{4,0},{1,9},{9... | collective-permute-start | bytes 1327112 | tf_op jit(solution)/shard_map/ppermute | solution.py:147
  118.5 16.2 %collective-permute-start.18 = (bf16[192,1152]{1,0:T(8,128)(2,1)S(1)}, bf16[192,1152]{1,0:T(8,128)(2,1)S(1)}, u32[]{:S(2)}, u32[]{:S(2)}) collective-permute-start(bf16[192,1152]{1,0:T(8,128)(2,1)S(1)} %collective-permute-done.16), channel_id=1, source_target_pairs={{0,4},{8,0},{16,8},{24,16},{28,24},{20,28},{12,20},{4,12},{1,5},{9... | collective-permute-start | bytes 1327112 | tf_op jit(solution)/shard_map/ppermute | solution.py:150
  119.2 3.5 %copy-start.13 = (f32[1536]{0:T(1024)S(1)}, f32[1536]{0:T(1024)}, u32[]{:S(2)}) copy-start(f32[1536]{0:T(1024)} %param.16) | copy-start | bytes 18436
  123.8 10.1 %collective-permute-start.11 = (bf16[128,1536]{1,0:T(8,128)(2,1)S(1)}, bf16[128,1536]{1,0:T(8,128)(2,1)S(1)}, u32[]{:S(2)}, u32[]{:S(2)}) collective-permute-start(bf16[128,1536]{1,0:T(8,128)(2,1)S(1)} %get-tuple-element.60), channel_id=1, source_target_pairs={{0,2},{1,3},{2,0},{3,1},{4,6},{5,7},{6,4},{7,5},{8,10},{9,11},{10,... | collective-permute-start | bytes 1179656 | tf_op jit(solution)/shard_map/ppermute | solution.py:36
  128.6 10.9 %collective-permute-start.19 = (bf16[192,1152]{1,0:T(8,128)(2,1)S(1)}, bf16[192,1152]{1,0:T(8,128)(2,1)S(1)}, u32[]{:S(2)}, u32[]{:S(2)}) collective-permute-start(bf16[192,1152]{1,0:T(8,128)(2,1)S(1)} %collective-permute-done.17), channel_id=1, source_target_pairs={{0,8},{8,16},{16,24},{24,28},{28,20},{20,12},{12,4},{4,0},{1,9},{9... | collective-permute-start | bytes 1327112 | tf_op jit(solution)/shard_map/ppermute | solution.py:147
  134.7 4.9 %copy-start.5 = (bf16[4,128,1536]{2,1,0:T(8,128)(2,1)}, bf16[4,128,1536]{2,1,0:T(8,128)(2,1)S(1)}, u32[]{:S(2)}) copy-start(bf16[4,128,1536]{2,1,0:T(8,128)(2,1)S(1)} %get-tuple-element.66) | copy-start | bytes 4718596
  134.7 9.6 %collective-permute-start.12 = (bf16[2,128,1536]{2,1,0:T(8,128)(2,1)}, bf16[2,128,1536]{2,1,0:T(8,128)(2,1)}, u32[]{:S(2)}, u32[]{:S(2)}) collective-permute-start(bf16[2,128,1536]{2,1,0:T(8,128)(2,1)} %get-tuple-element.65), channel_id=1, source_target_pairs={{0,1},{1,0},{2,3},{3,2},{4,5},{5,4},{6,7},{7,6},{8,9},{9,8},{10,11... | collective-permute-start | bytes 2359304 | tf_op jit(solution)/shard_map/ppermute | solution.py:42
  134.8 4.8 %copy-start.1 = (bf16[8,192,384]{2,1,0:T(8,128)(2,1)}, bf16[8,192,384]{2,1,0:T(8,128)(2,1)S(1)}, u32[]{:S(2)}) copy-start(bf16[8,192,384]{2,1,0:T(8,128)(2,1)S(1)} %fusion.51) | copy-start | bytes 3538948
  139.5 0.8 copy-start.8
  151.4 0.7 copy-start.14
  151.5 0.7 copy-start.19
  151.5 0.7 copy-start.20
  151.5 0.7 copy-start.21
  151.5 0.7 copy-start.23
  151.5 0.7 copy-start.24
  151.5 0.7 copy-start.25
  151.5 0.7 copy-start.27
  151.6 0.7 copy-start.37
  151.7 0.7 copy-start.38
  151.7 6.2 %copy-start.2 = (bf16[8,192,384]{2,1,0:T(8,128)(2,1)S(1)}, bf16[8,192,384]{2,1,0:T(8,128)(2,1)}, u32[]{:S(2)}) copy-start(bf16[8,192,384]{2,1,0:T(8,128)(2,1)} %fusion.50) | copy-start | bytes 3538948
  159.0 2.4 %collective-permute-start.20 = (bf16[2,128,1536]{2,1,0:T(8,128)(2,1)S(1)}, bf16[2,128,1536]{2,1,0:T(8,128)(2,1)S(1)}, u32[]{:S(2)}, u32[]{:S(2)}) collective-permute-start(bf16[2,128,1536]{2,1,0:T(8,128)(2,1)S(1)} %dynamic-slice_bitcast_fusion), channel_id=1, source_target_pairs={{0,1},{1,0},{2,3},{3,2},{4,5},{5,4},{6,7},{7,6},{8,9},{9,8},{10,11... | collective-permute-start | bytes 2359304 | tf_op jit(solution)/shard_map/ppermute | solution.py:78
  161.6 11.2 %collective-permute-start.21 = (bf16[128,1536]{1,0:T(8,128)(2,1)S(1)}, bf16[128,1536]{1,0:T(8,128)(2,1)S(1)}, u32[]{:S(2)}, u32[]{:S(2)}) collective-permute-start(bf16[128,1536]{1,0:T(8,128)(2,1)S(1)} %fusion.39), channel_id=1, source_target_pairs={{0,2},{1,3},{2,0},{3,1},{4,6},{5,7},{6,4},{7,5},{8,10},{9,11},{10,... | collective-permute-start | bytes 1179656 | tf_op jit(solution)/shard_map/ppermute | solution.py:84
  (18 other events, 11.9 us)

commit v12 on v11

--- a/solution.py
+++ b/solution.py
@@ -143,10 +143,25 @@
 
     outs = place(outs, block, me)
     ahead = behind = block
-    for step in range(1, count // 2 + 1):
+    far = count // 2
+    for step in range(1, far + 1):
+        if step == far and count % 2 == 0:
+            rows = block.shape[0] // 2
+            where = order[(my_pos - step) % count]
+            front = lax.ppermute(ahead[:rows], "dp", forward)
+            back = lax.ppermute(behind[rows:], "dp", backward)
+            outs = [
+                lax.dynamic_update_slice(
+                    lax.dynamic_update_slice(out, front[None, :, lo:hi], (where, 0, 0)),
+                    back[None, :, lo:hi],
+                    (where, rows, 0),
+                )
+                for out, (lo, hi) in zip(outs, spans)
+            ]
+            break
         ahead = lax.ppermute(ahead, "dp", forward)
         outs = place(outs, ahead, order[(my_pos - step) % count])
-        if step <= count - 1 - count // 2:
+        if step < far or count % 2 == 1:
             behind = lax.ppermute(behind, "dp", backward)
             outs = place(outs, behind, order[(my_pos + step) % count])
     return outs

time: 175 us -> 167 us (0.954)
  waiting for transfers between devices: 63.5 us -> 52.7 us
    ppermute x8 -> x6, waiting for transfers between devices: 45 us -> 28.1 us  [ring_gather(): ahead = lax.ppermute(ahead, 'dp', forward)]
    ppermute x0 -> x4, waiting for transfers between devices: none -> 6.74 us  [the longest x2 3.98 us: ring_gather(): front = lax.ppermute(ahead[:rows], 'dp', forward)]
    dynamic_update_slice x32 -> x28, local copies, waits for them, and re-layouts: 17.4 us -> 11.9 us  [place(): lax.dynamic_update_index_in_dim(out, piece[..., lo:hi], where, 0)]
    ppermute x0 -> x4, starting transfers between devices: none -> 4.26 us  [the longest x2 3.25 us: ring_gather(): front = lax.ppermute(ahead[:rows], 'dp', forward)]
    unnamed x90 -> x104, local copies, waits for them, and re-layouts: 4.73 us -> 0.8 us
    another operation x6, local copies, waits for them, and re-layouts: 1.46 us -> 4.68 us
    ppermute x8 -> x6, starting transfers between devices: 14.2 us -> 11 us  [ring_gather(): ahead = lax.ppermute(ahead, 'dp', forward)]
    dynamic_update_slice x0 -> x8, local copies, waits for them, and re-layouts: none -> 2.75 us  [the longest x4 1.38 us: ring_gather(): lax.dynamic_update_slice(out, front[None, :, lo:hi], (where, 0, 0))]
  transfers between devices with their start and end apart: 22 -> 24, of which waited for: 10 -> 11; matrix products, arithmetic and copies ran while one was open for 29% -> 33% of each run, Pallas kernels for 0% -> 0%
where the time goes in v12:
time: 167 us
  waiting for transfers between devices  52.7 us (32%)
  local copies, waits for them, and re-layouts  38.3 us (23%)
  starting transfers between devices  21.7 us (13%)
  other arithmetic  18.3 us (11%)
  between operations  18 us (11%)
  matrix products  17.6 us (11%)
    ppermute x6, waiting for transfers between devices, ring_gather(): ahead = lax.ppermute(ahead, 'dp', forward)  28.1 us
    ppermute x2, waiting for transfers between devices, seq_scatter_sum(): lax.ppermute(piece.astype(jnp.bfloat16), 'seq', [(i, (i + 2 * shift) % co...  12.6 us
    dynamic_update_slice x28, local copies, waits for them, and re-layouts, place(): lax.dynamic_update_index_in_dim(out, piece[..., lo:hi], where, 0)  11.9 us
    ppermute x6, starting transfers between devices, ring_gather(): ahead = lax.ppermute(ahead, 'dp', forward)  11 us
    convert_element_type x1, other arithmetic, depthwise(): return jax.nn.silu(total_acc).astype(jnp.bfloat16)  6.51 us
    dot_general x1, matrix products, on_device(): jnp.dot(seq_gather(normed1, paired).reshape(group_rows, model_width), qkv...  5.73 us
    dynamic_update_slice x4, local copies, waits for them, and re-layouts, seq_gather(): out = lax.dynamic_update_index_in_dim(out, other[k], 2 * k + partner % 2, 0)  5.09 us
    another operation x6, local copies, waits for them, and re-layouts  4.68 us
  transfers between devices with their start and end apart: 24, of which 11 were waited for; matrix products, arithmetic and copies ran while one was open for 33% of the time, Pallas kernels for 0%

profile of v12, /device:TPU:0, one launch (start us, length us, event | category | flops | bytes accessed | tf_op | source)
XLA Modules:
  0.0 166.6 jit_solution(11591819326074085520)
XLA Ops:
  0.0 1.1 copy.40
  1.1 1.8 %pad_maximum_fusion = bf16[192,1536]{1,0:T(8,128)(2,1)} fusion(bf16[192,384]{1,0:T(8,128)(2,1)} %bitcast.281, bf16[192,1152]{1,0:T(8,128)(2,1)S(1)} %bitcast.276), kind=kLoop, calls=%fused_computation.51 | loop fusion | flops 1179648 | bytes 1179648 | tf_op jit(solution)/shard_map/concatenate | solution.py:227
  3.0 3.0 %collective-permute-start.2 = (bf16[192,1536]{1,0:T(8,128)(2,1)}, bf16[192,1536]{1,0:T(8,128)(2,1)}, u32[]{:S(2)}, u32[]{:S(2)}) collective-permute-start(bf16[192,1536]{1,0:T(8,128)(2,1)} %pad_maximum_fusion), channel_id=1, source_target_pairs={{0,8},{8,16},{16,24},{24,28},{28,20},{20,12},{12,4},{4,0},{1,9},{9... | collective-permute-start | bytes 1769480 | tf_op jit(solution)/shard_map/ppermute | solution.py:162
  6.4 1.0 fusion.18
  7.4 1.9 %collective-permute-start = (bf16[128,1536]{1,0:T(8,128)(2,1)}, bf16[128,1536]{1,0:T(8,128)(2,1)}, u32[]{:S(2)}, u32[]{:S(2)}) collective-permute-start(bf16[128,1536]{1,0:T(8,128)(2,1)} %fusion.18), channel_id=1, source_target_pairs={{0,2},{1,3},{2,0},{3,1},{4,6},{5,7},{6,4},{7,5},{8,10},{9,11},{10,... | collective-permute-start | bytes 1179656 | tf_op jit(solution)/shard_map/ppermute | solution.py:36
  12.4 2.2 %broadcast_in_dim.432 = bf16[8,192,1152]{2,1,0:T(8,128)(2,1)} broadcast(bf16[]{:T(256)} %constant.311.clone.1), dimensions={} | broadcast | bytes 3538946 | tf_op jit(solution)/shard_map/broadcast_in_dim | solution.py:136
  15.4 0.9 broadcast.157.clone
  16.3 1.3 broadcast.154.clone
  17.6 1.2 constant_dynamic-update-slice_fusion.1
  37.8 0.9 pad_maximum_fusion.1
  39.4 1.9 %bitcast_dynamic-update-slice_fusion.4 = (bf16[2,128,1536]{2,1,0:T(8,128)(2,1)}, bf16[4,128,1536]{2,1,0:T(8,128)(2,1)}) fusion(bf16[2,128,1536]{2,1,0:T(8,128)(2,1)} %get-tuple-element.63, s32[]{:T(128)S(6)} %select_n.358, bf16[128,1536]{1,0:T(8,128)(2,1)} %collective-permute-done, bf16[4,128,1536]{2,1,0:T(8,128)(2,1)} %get-tuple-element.64, s32[]{:T(128)S(6)} %select_n.354), kind=kLoop, calls=%fused_computation.81 | loop fusion | bytes 1179656 | tf_op jit(solution)/shard_map/jit(dynamic_update_index_in_dim)/dynamic_update_slice | solution.py:40
  41.4 1.6 collective-permute-start.4
  43.4 1.8 %fusion.34 = bf16[8,192,1152]{2,1,0:T(8,128)(2,1)} fusion(bf16[8,192,1152]{2,1,0:T(8,128)(2,1)} %constant_dynamic-update-slice_fusion, s32[]{:T(128)S(6)} %select_n.365, bf16[192,1536]{1,0:T(8,128)(2,1)} %collective-permute-done.2), kind=kLoop, calls=%fused_computation.64 | loop fusion | bytes 884740 | tf_op jit(solution)/shard_map/jit(dynamic_update_index_in_dim)/dynamic_update_slice | solution.py:140
  47.0 10.3 %collective-permute-done.4 = bf16[192,1536]{1,0:T(8,128)(2,1)S(1)} collective-permute-done((bf16[192,1536]{1,0:T(8,128)(2,1)}, bf16[192,1536]{1,0:T(8,128)(2,1)S(1)}, u32[]{:S(2)}, u32[]{:S(2)}) %collective-permute-start.4) | collective-permute-done | bytes 589856 | tf_op jit(solution)/shard_map/ppermute | solution.py:162
  57.3 1.6 collective-permute-start.6
  62.6 9.7 %collective-permute-done.6 = bf16[192,1536]{1,0:T(8,128)(2,1)S(1)} collective-permute-done((bf16[192,1536]{1,0:T(8,128)(2,1)S(1)}, bf16[192,1536]{1,0:T(8,128)(2,1)S(1)}, u32[]{:S(2)}, u32[]{:S(2)}) %collective-permute-start.6) | collective-permute-done | bytes 589856 | tf_op jit(solution)/shard_map/ppermute | solution.py:162
  72.3 1.6 collective-permute-start.8
  76.1 3.9 %collective-permute-done.8 = bf16[96,1536]{1,0:T(8,128)(2,1)S(1)} collective-permute-done((bf16[96,1536]{1,0:T(8,128)(2,1)S(1)}, bf16[96,1536]{1,0:T(8,128)(2,1)S(1)}, u32[]{:S(2)}, u32[]{:S(2)}) %collective-permute-start.8) | collective-permute-done | bytes 294944 | tf_op jit(solution)/shard_map/ppermute | solution.py:151
  80.1 1.4 collective-permute-done.9
  81.5 1.6 collective-permute-start.14
  85.0 5.7 %convolution_convert_fusion = bf16[512,1152]{1,0:T(8,128)(2,1)} fusion(bf16[512,1536]{1,0:T(8,128)(2,1)} %bitcast.2, bf16[1536,1152]{1,0:T(8,128)(2,1)} %bitcast.26), kind=kOutput, calls=%fused_computation.5 | convolution fusion | flops 1812529152 | bytes 6291456 | tf_op jit(solution)/shard_map/dot_general | solution.py:243
  90.7 1.6 copy.31
  92.3 3.6 %fusion.73 = (f32[4,512]{1,0:T(4,128)S(1)}, f32[4,512,512]{1,2,0:T(8,128)}) fusion(pred[512,512]{0,1:T(8,128)(4,1)S(1)} %broadcast_compare_fusion, bf16[512,3,4,96]{0,3,2,1:T(8,128)(2,1)S(1)} %bitcast.279), kind=kOutput, calls=%fused_computation.221 | convolution fusion | flops 205521408 | bytes 5251072 | tf_op jit(solution)/shard_map/while/body/eval_jaxpr/sub | solution.py:194
  95.9 2.7 %fusion.6 = bf16[4,96,512]{2,1,0:T(8,128)(2,1)S(1)} fusion(f32[4,512,512]{1,2,0:T(8,128)} %get-tuple-element.108, f32[4,512]{1,0:T(4,128)S(1)} %get-tuple-element.107, bf16[512,3,4,96]{0,3,2,1:T(8,128)(2,1)S(1)} %bitcast.280), kind=kOutput, calls=%fused_computation.14 | convolution fusion | flops 203620352 | bytes 4988928 | tf_op jit(solution)/shard_map/while/body/eval_jaxpr/hqk,khe->qhe/dot_general | solution.py:196
  98.6 1.0 convolution_convert_fusion.2
  100.1 1.6 collective-permute-start.16
  102.2 0.9 fusion.55
  103.2 0.9 fusion.54
  104.1 1.0 fusion.47
  105.1 1.0 fusion.46
  107.0 6.0 %collective-permute-done.16 = bf16[192,1152]{1,0:T(8,128)(2,1)S(1)} collective-permute-done((bf16[192,1152]{1,0:T(8,128)(2,1)}, bf16[192,1152]{1,0:T(8,128)(2,1)S(1)}, u32[]{:S(2)}, u32[]{:S(2)}) %collective-permute-start.16) | collective-permute-done | bytes 442400 | tf_op jit(solution)/shard_map/ppermute | solution.py:162
  113.0 1.6 collective-permute-start.18
  115.4 2.0 %collective-permute-done.11 = bf16[128,1536]{1,0:T(8,128)(2,1)S(1)} collective-permute-done((bf16[128,1536]{1,0:T(8,128)(2,1)S(1)}, bf16[128,1536]{1,0:T(8,128)(2,1)S(1)}, u32[]{:S(2)}, u32[]{:S(2)}) %collective-permute-start.11) | collective-permute-done | bytes 393248 | tf_op jit(solution)/shard_map/ppermute | solution.py:84
  117.9 1.0 broadcast.157
  118.9 1.0 bitcast_dynamic-update-slice_fusion.2
  120.5 1.3 broadcast.154
  122.5 2.2 %collective-permute-done.18 = bf16[192,1152]{1,0:T(8,128)(2,1)S(1)} collective-permute-done((bf16[192,1152]{1,0:T(8,128)(2,1)S(1)}, bf16[192,1152]{1,0:T(8,128)(2,1)S(1)}, u32[]{:S(2)}, u32[]{:S(2)}) %collective-permute-start.18) | collective-permute-done | bytes 442400 | tf_op jit(solution)/shard_map/ppermute | solution.py:162
  124.8 1.6 collective-permute-start.20
  127.1 2.9 %collective-permute-done.12 = bf16[128,1536]{1,0:T(8,128)(2,1)S(1)} collective-permute-done((bf16[128,1536]{1,0:T(8,128)(2,1)S(1)}, bf16[128,1536]{1,0:T(8,128)(2,1)S(1)}, u32[]{:S(2)}, u32[]{:S(2)}) %collective-permute-start.12) | collective-permute-done | bytes 393248 | tf_op jit(solution)/shard_map/ppermute | solution.py:36
  131.0 1.4 collective-permute-done.21
  132.4 2.4 %copy.37 = bf16[768,1536]{1,0:T(8,128)(2,1)} copy(bf16[768,1536]{0,1:T(8,128)(2,1)S(1)} %bitcast.268) | data formatting | bytes 4718592 | tf_op jit(solution)/shard_map/dot_general | solution.py:255
  136.1 1.8 %slice_dynamic-update-slice_fusion.1 = bf16[4,128,1536]{2,1,0:T(8,128)(2,1)} fusion(bf16[4,128,1536]{2,1,0:T(8,128)(2,1)} %get-tuple-element.66, s32[]{:T(128)S(6)} %select_n.360, bf16[2,128,1536]{2,1,0:T(8,128)(2,1)} %collective-permute-done.13), kind=kLoop, calls=%fused_computation.71 | loop fusion | bytes 786436 | tf_op jit(solution)/shard_map/jit(dynamic_update_index_in_dim)/dynamic_update_slice | solution.py:45
  137.9 1.8 %slice_dynamic-update-slice_fusion = bf16[4,128,1536]{2,1,0:T(8,128)(2,1)} fusion(bf16[4,128,1536]{2,1,0:T(8,128)(2,1)} %slice_dynamic-update-slice_fusion.1, s32[]{:T(128)S(6)} %select_n.361, bf16[2,128,1536]{2,1,0:T(8,128)(2,1)} %collective-permute-done.13), kind=kLoop, calls=%fused_computation.70 | loop fusion | bytes 786436 | tf_op jit(solution)/shard_map/jit(dynamic_update_index_in_dim)/dynamic_update_slice | solution.py:45
  139.7 3.6 %fusion.74 = f32[512,2,384]{2,0,1:T(8,128)S(1)} fusion(bf16[512,1536,1]{1,0,2:T(8,128)(2,1)} %bitcast.53, bf16[2,384,1536]{2,1,0:T(8,128)(2,1)} %bitcast.275), kind=kOutput, calls=%fused_computation.222 | convolution fusion | flops 1207959552 | bytes 5505024 | tf_op jit(solution)/shard_map/dot_general | solution.py:255
  144.3 6.5 %multiply_convert_fusion = bf16[512,384]{1,0:T(8,128)(2,1)S(1)} fusion(bf16[512,384]{1,0:T(8,128)(2,1)S(1)} %fusion.40, f32[384]{0:T(512)S(1)} %copy-done.21, f32[384]{0:T(512)S(1)} %copy-done.22, f32[384]{0:T(512)S(1)} %get-tuple-element.20, f32[384]{0:T(512)S(1)} %get-tuple-element.28, f32[384]{0:T(512)S(1)} %get-tuple-element.30, ...), kind=kLoop, calls=%fused_computation.47 | loop fusion | flops 25165824 | bytes 849920 | tf_op jit(solution)/shard_map/convert_element_type | solution.py:215
  150.8 1.0 convolution_convert_fusion.1
  152.0 2.3 %collective-permute-done.22 = bf16[2,128,1536]{2,1,0:T(8,128)(2,1)S(1)} collective-permute-done((bf16[2,128,1536]{2,1,0:T(8,128)(2,1)S(1)}, bf16[2,128,1536]{2,1,0:T(8,128)(2,1)S(1)}, u32[]{:S(2)}, u32[]{:S(2)}) %collective-permute-start.22) | collective-permute-done | bytes 786464 | tf_op jit(solution)/shard_map/ppermute | solution.py:78
  155.2 10.6 %collective-permute-done.23 = bf16[128,1536]{1,0:T(8,128)(2,1)S(1)} collective-permute-done((bf16[128,1536]{1,0:T(8,128)(2,1)S(1)}, bf16[128,1536]{1,0:T(8,128)(2,1)S(1)}, u32[]{:S(2)}, u32[]{:S(2)}) %collective-permute-start.23) | collective-permute-done | bytes 393248 | tf_op jit(solution)/shard_map/ppermute | solution.py:84
  (202 shorter events, 26.7 us)
Async XLA Ops:
  0.0 6.0 %copy-start = (bf16[1,128,1536]{2,1,0:T(8,128)(2,1)S(1)}, bf16[1,128,1536]{2,1,0:T(8,128)(2,1)}, u32[]{:S(2)}) copy-start(bf16[1,128,1536]{2,1,0:T(8,128)(2,1)} %param.13) | copy-start | bytes 1179652
  0.0 6.4 %copy-start.7 = (f32[1536]{0:T(1024)S(1)}, f32[1536]{0:T(1024)}, u32[]{:S(2)}) copy-start(f32[1536]{0:T(1024)} %param.15) | copy-start | bytes 18436
  1.1 8.3 %copy-start.3 = (bf16[192,3,384]{2,0,1:T(8,128)(2,1)S(1)}, bf16[192,3,384]{2,0,1:T(8,128)(2,1)}, u32[]{:S(2)}) copy-start(bf16[192,3,384]{2,0,1:T(8,128)(2,1)} %param.17) | copy-start | bytes 1327108
  3.0 6.8 %copy-start.49 = (s32[1,4]{1,0:T(1,128)S(1)}, s32[1,4]{1,0:T(1,128)}, u32[]{:S(2)}) copy-start(s32[1,4]{1,0:T(1,128)} %param.14) | copy-start | bytes 52
  3.0 38.4 %collective-permute-start.2 = (bf16[192,1536]{1,0:T(8,128)(2,1)}, bf16[192,1536]{1,0:T(8,128)(2,1)}, u32[]{:S(2)}, u32[]{:S(2)}) collective-permute-start(bf16[192,1536]{1,0:T(8,128)(2,1)} %pad_maximum_fusion), channel_id=1, source_target_pairs={{0,8},{8,16},{16,24},{24,28},{28,20},{20,12},{12,4},{4,0},{1,9},{9... | collective-permute-start | bytes 1769480 | tf_op jit(solution)/shard_map/ppermute | solution.py:162
  6.0 37.0 %collective-permute-start.3 = (bf16[192,1536]{1,0:T(8,128)(2,1)}, bf16[192,1536]{1,0:T(8,128)(2,1)S(1)}, u32[]{:S(2)}, u32[]{:S(2)}) collective-permute-start(bf16[192,1536]{1,0:T(8,128)(2,1)} %pad_maximum_fusion), channel_id=1, source_target_pairs={{0,4},{8,0},{16,8},{24,16},{28,24},{20,28},{12,20},{4,12},{1,5},{9... | collective-permute-start | bytes 1769480 | tf_op jit(solution)/shard_map/ppermute | solution.py:165
  7.4 32.0 %collective-permute-start = (bf16[128,1536]{1,0:T(8,128)(2,1)}, bf16[128,1536]{1,0:T(8,128)(2,1)}, u32[]{:S(2)}, u32[]{:S(2)}) collective-permute-start(bf16[128,1536]{1,0:T(8,128)(2,1)} %fusion.18), channel_id=1, source_target_pairs={{0,2},{1,3},{2,0},{3,1},{4,6},{5,7},{6,4},{7,5},{8,10},{9,11},{10,... | collective-permute-start | bytes 1179656 | tf_op jit(solution)/shard_map/ppermute | solution.py:36
  9.4 2.9 %copy-start.4 = (bf16[384,192]{0,1:T(8,128)(2,1)S(1)}, bf16[384,192]{0,1:T(8,128)(2,1)}, u32[]{:S(2)}) copy-start(bf16[384,192]{0,1:T(8,128)(2,1)} %param.18) | copy-start | bytes 442372
  16.3 2.5 %copy-start.6 = (bf16[31,384]{1,0:T(8,128)(2,1)S(1)}, bf16[31,384]{1,0:T(8,128)(2,1)}, u32[]{:S(2)}) copy-start(bf16[31,384]{1,0:T(8,128)(2,1)} %param.20) | copy-start | bytes 71428
  16.3 3.2 %copy-start.50 = (s32[8]{0:T(128)S(1)}, s32[8]{0:T(128)}, u32[]{:S(2)}) copy-start(s32[8]{0:T(128)} %constant.341.clone) | copy-start | bytes 100
  16.3 7.8 %copy-start.8 = (s32[8]{0:T(128)S(1)}, s32[8]{0:T(128)}, u32[]{:S(2)}) copy-start(s32[8]{0:T(128)} %constant.342.clone) | copy-start | bytes 100
  16.3 17.1 %copy-start.5 = (bf16[192,2,384]{2,1,0:T(2,128)(2,1)S(1)}, bf16[192,2,384]{2,1,0:T(2,128)(2,1)}, u32[]{:S(2)}) copy-start(bf16[192,2,384]{2,1,0:T(2,128)(2,1)} %param.19) | copy-start | bytes 884740
  41.4 18.8 %collective-permute-start.1 = (bf16[2,128,1536]{2,1,0:T(8,128)(2,1)}, bf16[2,128,1536]{2,1,0:T(8,128)(2,1)S(1)}, u32[]{:S(2)}, u32[]{:S(2)}) collective-permute-start(bf16[2,128,1536]{2,1,0:T(8,128)(2,1)} %get-tuple-element.67), channel_id=1, source_target_pairs={{0,1},{1,0},{2,3},{3,2},{4,5},{5,4},{6,7},{7,6},{8,9},{9,8},{10,11... | collective-permute-start | bytes 2359304 | tf_op jit(solution)/shard_map/ppermute | solution.py:42
  41.4 16.0 %collective-permute-start.4 = (bf16[192,1536]{1,0:T(8,128)(2,1)}, bf16[192,1536]{1,0:T(8,128)(2,1)S(1)}, u32[]{:S(2)}, u32[]{:S(2)}) collective-permute-start(bf16[192,1536]{1,0:T(8,128)(2,1)} %collective-permute-done.2), channel_id=1, source_target_pairs={{0,8},{8,16},{16,24},{24,28},{28,20},{20,12},{12,4},{4,0},{1,9},{9... | collective-permute-start | bytes 1769480 | tf_op jit(solution)/shard_map/ppermute | solution.py:162
  43.0 15.9 %collective-permute-start.5 = (bf16[192,1536]{1,0:T(8,128)(2,1)S(1)}, bf16[192,1536]{1,0:T(8,128)(2,1)S(1)}, u32[]{:S(2)}, u32[]{:S(2)}) collective-permute-start(bf16[192,1536]{1,0:T(8,128)(2,1)S(1)} %collective-permute-done.3), channel_id=1, source_target_pairs={{0,4},{8,0},{16,8},{24,16},{28,24},{20,28},{12,20},{4,12},{1,5},{9... | collective-permute-start | bytes 1769480 | tf_op jit(solution)/shard_map/ppermute | solution.py:165
  57.3 14.9 %collective-permute-start.6 = (bf16[192,1536]{1,0:T(8,128)(2,1)S(1)}, bf16[192,1536]{1,0:T(8,128)(2,1)S(1)}, u32[]{:S(2)}, u32[]{:S(2)}) collective-permute-start(bf16[192,1536]{1,0:T(8,128)(2,1)S(1)} %collective-permute-done.4), channel_id=1, source_target_pairs={{0,8},{8,16},{16,24},{24,28},{28,20},{20,12},{12,4},{4,0},{1,9},{9... | collective-permute-start | bytes 1769480 | tf_op jit(solution)/shard_map/ppermute | solution.py:162
  58.9 15.0 %collective-permute-start.7 = (bf16[192,1536]{1,0:T(8,128)(2,1)S(1)}, bf16[192,1536]{1,0:T(8,128)(2,1)S(1)}, u32[]{:S(2)}, u32[]{:S(2)}) collective-permute-start(bf16[192,1536]{1,0:T(8,128)(2,1)S(1)} %collective-permute-done.5), channel_id=1, source_target_pairs={{0,4},{8,0},{16,8},{24,16},{28,24},{20,28},{12,20},{4,12},{1,5},{9... | collective-permute-start | bytes 1769480 | tf_op jit(solution)/shard_map/ppermute | solution.py:165
  72.3 7.8 %collective-permute-start.8 = (bf16[96,1536]{1,0:T(8,128)(2,1)S(1)}, bf16[96,1536]{1,0:T(8,128)(2,1)S(1)}, u32[]{:S(2)}, u32[]{:S(2)}) collective-permute-start(bf16[96,1536]{1,0:T(8,128)(2,1)S(1)} %slice.565), channel_id=1, source_target_pairs={{0,8},{8,16},{16,24},{24,28},{28,20},{20,12},{12,4},{4,0},{1,9},{9... | collective-permute-start | bytes 884744 | tf_op jit(solution)/shard_map/ppermute | solution.py:151
  73.9 7.5 %collective-permute-start.9 = (bf16[96,1536]{1,0:T(8,128)(2,1)S(1)}, bf16[96,1536]{1,0:T(8,128)(2,1)S(1)}, u32[]{:S(2)}, u32[]{:S(2)}) collective-permute-start(bf16[96,1536]{1,0:T(8,128)(2,1)S(1)} %slice.567), channel_id=1, source_target_pairs={{0,4},{8,0},{16,8},{24,16},{28,24},{20,28},{12,20},{4,12},{1,5},{9... | collective-permute-start | bytes 884744 | tf_op jit(solution)/shard_map/ppermute | solution.py:152
  81.5 18.7 %collective-permute-start.14 = (bf16[192,1152]{1,0:T(8,128)(2,1)S(1)}, bf16[192,1152]{1,0:T(8,128)(2,1)}, u32[]{:S(2)}, u32[]{:S(2)}) collective-permute-start(bf16[192,1152]{1,0:T(8,128)(2,1)S(1)} %pad_maximum_fusion.1), channel_id=1, source_target_pairs={{0,8},{8,16},{16,24},{24,28},{28,20},{20,12},{12,4},{4,0},{1,9},{9... | collective-permute-start | bytes 1327112 | tf_op jit(solution)/shard_map/ppermute | solution.py:162
  83.1 18.7 %collective-permute-start.15 = (bf16[192,1152]{1,0:T(8,128)(2,1)S(1)}, bf16[192,1152]{1,0:T(8,128)(2,1)}, u32[]{:S(2)}, u32[]{:S(2)}) collective-permute-start(bf16[192,1152]{1,0:T(8,128)(2,1)S(1)} %pad_maximum_fusion.1), channel_id=1, source_target_pairs={{0,4},{8,0},{16,8},{24,16},{28,24},{20,28},{12,20},{4,12},{1,5},{9... | collective-permute-start | bytes 1327112 | tf_op jit(solution)/shard_map/ppermute | solution.py:165
  99.7 6.4 %collective-permute-start.10 = (bf16[2,128,1536]{2,1,0:T(8,128)(2,1)S(1)}, bf16[2,128,1536]{2,1,0:T(8,128)(2,1)S(1)}, u32[]{:S(2)}, u32[]{:S(2)}) collective-permute-start(bf16[2,128,1536]{2,1,0:T(8,128)(2,1)S(1)} %dynamic-slice_bitcast_fusion.1), channel_id=1, source_target_pairs={{0,1},{1,0},{2,3},{3,2},{4,5},{5,4},{6,7},{7,6},{8,9},{9,8},{10,11... | collective-permute-start | bytes 2359304 | tf_op jit(solution)/shard_map/ppermute | solution.py:78
  100.1 12.8 %collective-permute-start.16 = (bf16[192,1152]{1,0:T(8,128)(2,1)}, bf16[192,1152]{1,0:T(8,128)(2,1)S(1)}, u32[]{:S(2)}, u32[]{:S(2)}) collective-permute-start(bf16[192,1152]{1,0:T(8,128)(2,1)} %collective-permute-done.14), channel_id=1, source_target_pairs={{0,8},{8,16},{16,24},{24,28},{28,20},{20,12},{12,4},{4,0},{1,9},{9... | collective-permute-start | bytes 1327112 | tf_op jit(solution)/shard_map/ppermute | solution.py:162
  101.7 12.8 %collective-permute-start.17 = (bf16[192,1152]{1,0:T(8,128)(2,1)}, bf16[192,1152]{1,0:T(8,128)(2,1)S(1)}, u32[]{:S(2)}, u32[]{:S(2)}) collective-permute-start(bf16[192,1152]{1,0:T(8,128)(2,1)} %collective-permute-done.15), channel_id=1, source_target_pairs={{0,4},{8,0},{16,8},{24,16},{28,24},{20,28},{12,20},{4,12},{1,5},{9... | collective-permute-start | bytes 1327112 | tf_op jit(solution)/shard_map/ppermute | solution.py:165
  106.4 11.0 %collective-permute-start.11 = (bf16[128,1536]{1,0:T(8,128)(2,1)S(1)}, bf16[128,1536]{1,0:T(8,128)(2,1)S(1)}, u32[]{:S(2)}, u32[]{:S(2)}) collective-permute-start(bf16[128,1536]{1,0:T(8,128)(2,1)S(1)} %fusion.37), channel_id=1, source_target_pairs={{0,2},{1,3},{2,0},{3,1},{4,6},{5,7},{6,4},{7,5},{8,10},{9,11},{10,... | collective-permute-start | bytes 1179656 | tf_op jit(solution)/shard_map/ppermute | solution.py:84
  113.0 11.8 %collective-permute-start.18 = (bf16[192,1152]{1,0:T(8,128)(2,1)S(1)}, bf16[192,1152]{1,0:T(8,128)(2,1)S(1)}, u32[]{:S(2)}, u32[]{:S(2)}) collective-permute-start(bf16[192,1152]{1,0:T(8,128)(2,1)S(1)} %collective-permute-done.16), channel_id=1, source_target_pairs={{0,8},{8,16},{16,24},{24,28},{28,20},{20,12},{12,4},{4,0},{1,9},{9... | collective-permute-start | bytes 1327112 | tf_op jit(solution)/shard_map/ppermute | solution.py:162
  114.6 11.8 %collective-permute-start.19 = (bf16[192,1152]{1,0:T(8,128)(2,1)S(1)}, bf16[192,1152]{1,0:T(8,128)(2,1)S(1)}, u32[]{:S(2)}, u32[]{:S(2)}) collective-permute-start(bf16[192,1152]{1,0:T(8,128)(2,1)S(1)} %collective-permute-done.17), channel_id=1, source_target_pairs={{0,4},{8,0},{16,8},{24,16},{28,24},{20,28},{12,20},{4,12},{1,5},{9... | collective-permute-start | bytes 1327112 | tf_op jit(solution)/shard_map/ppermute | solution.py:165
  115.4 3.5 %copy-start.9 = (f32[1536]{0:T(1024)S(1)}, f32[1536]{0:T(1024)}, u32[]{:S(2)}) copy-start(f32[1536]{0:T(1024)} %param.16) | copy-start | bytes 18436
  119.9 10.1 %collective-permute-start.12 = (bf16[128,1536]{1,0:T(8,128)(2,1)S(1)}, bf16[128,1536]{1,0:T(8,128)(2,1)S(1)}, u32[]{:S(2)}, u32[]{:S(2)}) collective-permute-start(bf16[128,1536]{1,0:T(8,128)(2,1)S(1)} %get-tuple-element.60), channel_id=1, source_target_pairs={{0,2},{1,3},{2,0},{3,1},{4,6},{5,7},{6,4},{7,5},{8,10},{9,11},{10,... | collective-permute-start | bytes 1179656 | tf_op jit(solution)/shard_map/ppermute | solution.py:36
  124.8 6.2 %collective-permute-start.20 = (bf16[96,1152]{1,0:T(8,128)(2,1)S(1)}, bf16[96,1152]{1,0:T(8,128)(2,1)S(1)}, u32[]{:S(2)}, u32[]{:S(2)}) collective-permute-start(bf16[96,1152]{1,0:T(8,128)(2,1)S(1)} %slice.588), channel_id=1, source_target_pairs={{0,8},{8,16},{16,24},{24,28},{28,20},{20,12},{12,4},{4,0},{1,9},{9... | collective-permute-start | bytes 663560 | tf_op jit(solution)/shard_map/ppermute | solution.py:151
  126.4 6.0 %collective-permute-start.21 = (bf16[96,1152]{1,0:T(8,128)(2,1)S(1)}, bf16[96,1152]{1,0:T(8,128)(2,1)S(1)}, u32[]{:S(2)}, u32[]{:S(2)}) collective-permute-start(bf16[96,1152]{1,0:T(8,128)(2,1)S(1)} %slice.590), channel_id=1, source_target_pairs={{0,4},{8,0},{16,8},{24,16},{28,24},{20,28},{12,20},{4,12},{1,5},{9... | collective-permute-start | bytes 663560 | tf_op jit(solution)/shard_map/ppermute | solution.py:152
  127.0 5.4 %copy-start.1 = (bf16[8,192,384]{2,1,0:T(8,128)(2,1)}, bf16[8,192,384]{2,1,0:T(8,128)(2,1)S(1)}, u32[]{:S(2)}) copy-start(bf16[8,192,384]{2,1,0:T(8,128)(2,1)S(1)} %fusion.50) | copy-start | bytes 3538948
  130.9 5.2 %collective-permute-start.13 = (bf16[2,128,1536]{2,1,0:T(8,128)(2,1)}, bf16[2,128,1536]{2,1,0:T(8,128)(2,1)}, u32[]{:S(2)}, u32[]{:S(2)}) collective-permute-start(bf16[2,128,1536]{2,1,0:T(8,128)(2,1)} %get-tuple-element.65), channel_id=1, source_target_pairs={{0,1},{1,0},{2,3},{3,2},{4,5},{5,4},{6,7},{7,6},{8,9},{9,8},{10,11... | collective-permute-start | bytes 2359304 | tf_op jit(solution)/shard_map/ppermute | solution.py:42
  143.2 0.7 copy-start.10
  143.3 0.7 copy-start.11
  143.3 0.7 copy-start.12
  143.3 0.7 copy-start.13
  143.3 0.7 copy-start.14
  143.3 0.7 copy-start.15
  143.3 0.7 copy-start.16
  143.4 0.7 copy-start.26
  143.5 0.7 copy-start.40
  143.6 0.7 copy-start.41
  143.6 0.7 copy-start.43
  143.6 0.7 copy-start.47
  143.6 7.2 %copy-start.2 = (bf16[8,192,384]{2,1,0:T(8,128)(2,1)S(1)}, bf16[8,192,384]{2,1,0:T(8,128)(2,1)}, u32[]{:S(2)}) copy-start(bf16[8,192,384]{2,1,0:T(8,128)(2,1)} %fusion.64) | copy-start | bytes 3538948
  151.9 2.4 %collective-permute-start.22 = (bf16[2,128,1536]{2,1,0:T(8,128)(2,1)S(1)}, bf16[2,128,1536]{2,1,0:T(8,128)(2,1)S(1)}, u32[]{:S(2)}, u32[]{:S(2)}) collective-permute-start(bf16[2,128,1536]{2,1,0:T(8,128)(2,1)S(1)} %dynamic-slice_bitcast_fusion), channel_id=1, source_target_pairs={{0,1},{1,0},{2,3},{3,2},{4,5},{5,4},{6,7},{7,6},{8,9},{9,8},{10,11... | collective-permute-start | bytes 2359304 | tf_op jit(solution)/shard_map/ppermute | solution.py:78
  154.5 11.2 %collective-permute-start.23 = (bf16[128,1536]{1,0:T(8,128)(2,1)S(1)}, bf16[128,1536]{1,0:T(8,128)(2,1)S(1)}, u32[]{:S(2)}, u32[]{:S(2)}) collective-permute-start(bf16[128,1536]{1,0:T(8,128)(2,1)S(1)} %fusion.38), channel_id=1, source_target_pairs={{0,2},{1,3},{2,0},{3,1},{4,6},{5,7},{6,4},{7,5},{8,10},{9,11},{10,... | collective-permute-start | bytes 1179656 | tf_op jit(solution)/shard_map/ppermute | solution.py:84
  (27 other events, 18.1 us)

commit v13 on v12

--- a/solution.py
+++ b/solution.py
@@ -258,14 +258,41 @@
     gated = (glu_pair[:, 0] * jax.nn.sigmoid(glu_pair[:, 1])).astype(jnp.bfloat16)
     padded = jnp.pad(gated, ((kernel_reach, kernel_reach), (0, 0)))
     near_positions = jnp.arange(-kernel_reach, group_rows + kernel_reach, dtype=jnp.int32)
-    activated = depthwise(
-        padded, dw_kernel, seg_all, segment_of(record_ends, near_positions), group_rows
-    )
-    activated = lax.optimization_barrier(activated)
-    conv_out = seq_scatter_sum(
-        jnp.dot(activated, proj_cols.T, preferred_element_type=jnp.float32).astype(jnp.bfloat16),
-        paired,
-    )
+    near_segments = segment_of(record_ends, near_positions)
+    if paired and seq_count == 4:
+        chip_rows = group_rows // 2
+        here = lax.axis_index("seq") // 2
+        core = lax.axis_index("seq") % 2
+
+        def conv_rows(first, source):
+            window = lax.dynamic_slice_in_dim(source, first, chip_rows + 2 * kernel_reach, 0)
+            near = lax.dynamic_slice_in_dim(near_segments, first, chip_rows + 2 * kernel_reach, 0)
+            own = lax.dynamic_slice_in_dim(seg_all, first, chip_rows, 0)
+            rows_out = depthwise(window, dw_kernel, own, near, chip_rows)
+            rows_out = lax.optimization_barrier(rows_out)
+            part = jnp.dot(rows_out, proj_cols.T, preferred_element_type=jnp.float32)
+            part = part.astype(jnp.bfloat16).reshape(2, frame_rows, model_width)
+            mine = lax.dynamic_index_in_dim(part, core, axis=0, keepdims=False)
+            theirs = lax.dynamic_index_in_dim(part, 1 - core, axis=0, keepdims=False)
+            got = lax.ppermute(theirs, "seq", [(i, i ^ 1) for i in range(seq_count)])
+            return mine.astype(jnp.float32) + got.astype(jnp.float32)
+
+        far_sum = conv_rows((1 - here) * chip_rows, padded)
+        crossed = lax.ppermute(
+            far_sum.astype(jnp.bfloat16), "seq", [(i, (i + 2) % seq_count) for i in range(seq_count)]
+        )
+        conv_out = conv_rows(here * chip_rows, after(far_sum, padded)) + crossed.astype(
+            jnp.float32
+        )
+    else:
+        activated = depthwise(padded, dw_kernel, seg_all, near_segments, group_rows)
+        activated = lax.optimization_barrier(activated)
+        conv_out = seq_scatter_sum(
+            jnp.dot(activated, proj_cols.T, preferred_element_type=jnp.float32).astype(
+                jnp.bfloat16
+            ),
+            paired,
+        )
     results = [(middle.astype(jnp.float32) + conv_out).astype(jnp.bfloat16)]
     return jnp.stack(results, axis=0)
 

time: 167 us -> 169 us (1.012)
  waiting for transfers between devices: 52.7 us -> 41.7 us
  other arithmetic: 18.3 us -> 24.9 us
  local copies, waits for them, and re-layouts: 38.3 us -> 43.6 us
    ppermute x2 -> x1, waiting for transfers between devices: 12.6 us -> 2.28 us  [seq_scatter_sum(): lax.ppermute(piece.astype(jnp.bfloat16), 'seq', [(i, (i + 2 * shift) % co...]
    dynamic_update_slice x28, local copies, waits for them, and re-layouts: 11.9 us -> 18 us  [place(): lax.dynamic_update_index_in_dim(out, piece[..., lo:hi], where, 0)]
    convert_element_type x1 -> x2, other arithmetic: 6.51 us -> 12.4 us  [depthwise(): return jax.nn.silu(total_acc).astype(jnp.bfloat16)]
    ppermute x0 -> x3, waiting for transfers between devices: none -> 5.69 us  [the longest x1 4.64 us: on_device(): lax.ppermute(far_sum.astype(jnp.bfloat16), 'seq', [(i, (i + 2) % seq_coun...]
    ppermute x6, waiting for transfers between devices: 28.1 us -> 25.4 us  [ring_gather(): ahead = lax.ppermute(ahead, 'dp', forward)]
    ppermute x2 -> x1, waiting for transfers between devices: 2.27 us -> 0.01 us  [seq_scatter_sum(): got = lax.ppermute(theirs, 'seq', [(i, i ^ 1) for i in range(count)])]
    another operation x6, local copies, waits for them, and re-layouts: 4.68 us -> 2.67 us
    dot_general x1, local copies, waits for them, and re-layouts: 2.44 us -> 4.28 us  [on_device(): jnp.dot(shard_piece, glu_matrix, preferred_element_type=jnp.float32)]
  transfers between devices with their start and end apart: 24 -> 25, of which waited for: 11 -> 11; matrix products, arithmetic and copies ran while one was open for 33% -> 41% of each run, Pallas kernels for 0% -> 0%
where the time goes in v13:
time: 169 us; the launch traced here: 168 us
  local copies, waits for them, and re-layouts  43.6 us (26%)
  waiting for transfers between devices  41.7 us (25%)
  other arithmetic  24.9 us (15%)
  starting transfers between devices  22.1 us (13%)
  between operations  18.1 us (11%)
  matrix products  17.4 us (10%)
    ppermute x6, waiting for transfers between devices, ring_gather(): ahead = lax.ppermute(ahead, 'dp', forward)  25.4 us
    dynamic_update_slice x28, local copies, waits for them, and re-layouts, place(): lax.dynamic_update_index_in_dim(out, piece[..., lo:hi], where, 0)  18 us
    convert_element_type x2, other arithmetic, depthwise(): return jax.nn.silu(total_acc).astype(jnp.bfloat16)  12.4 us
    ppermute x6, starting transfers between devices, ring_gather(): ahead = lax.ppermute(ahead, 'dp', forward)  11 us
    dot_general x1, matrix products, on_device(): jnp.dot(seq_gather(normed1, paired).reshape(group_rows, model_width), qkv...  5.73 us
    ppermute x1, waiting for transfers between devices, on_device(): lax.ppermute(far_sum.astype(jnp.bfloat16), 'seq', [(i, (i + 2) % seq_coun...  4.64 us
    dot_general x1, local copies, waits for them, and re-layouts, on_device(): jnp.dot(shard_piece, glu_matrix, preferred_element_type=jnp.float32)  4.28 us
    ppermute x2, waiting for transfers between devices, ring_gather(): front = lax.ppermute(ahead[:rows], 'dp', forward)  3.96 us
  transfers between devices with their start and end apart: 25, of which 11 were waited for; matrix products, arithmetic and copies ran while one was open for 41% of the time, Pallas kernels for 0%

profile of v13, /device:TPU:0, one launch (start us, length us, event | category | flops | bytes accessed | tf_op | source)
XLA Modules:
  0.0 167.8 jit_solution(5170779391886207002)
XLA Ops:
  0.0 1.1 copy.36
  1.1 1.8 %pad_maximum_fusion = bf16[192,1536]{1,0:T(8,128)(2,1)} fusion(bf16[192,384]{1,0:T(8,128)(2,1)} %bitcast.283, bf16[192,1152]{1,0:T(8,128)(2,1)S(1)} %bitcast.277), kind=kLoop, calls=%fused_computation.50 | loop fusion | flops 1179648 | bytes 1179648 | tf_op jit(solution)/shard_map/concatenate | solution.py:227
  3.0 3.0 %collective-permute-start.2 = (bf16[192,1536]{1,0:T(8,128)(2,1)}, bf16[192,1536]{1,0:T(8,128)(2,1)}, u32[]{:S(2)}, u32[]{:S(2)}) collective-permute-start(bf16[192,1536]{1,0:T(8,128)(2,1)} %pad_maximum_fusion), channel_id=1, source_target_pairs={{0,8},{8,16},{16,24},{24,28},{28,20},{20,12},{12,4},{4,0},{1,9},{9... | collective-permute-start | bytes 1769480 | tf_op jit(solution)/shard_map/ppermute | solution.py:162
  6.7 2.0 %collective-permute-start = (bf16[128,1536]{1,0:T(8,128)(2,1)S(1)}, bf16[128,1536]{1,0:T(8,128)(2,1)}, u32[]{:S(2)}, u32[]{:S(2)}) collective-permute-start(bf16[128,1536]{1,0:T(8,128)(2,1)S(1)} %fusion.18), channel_id=1, source_target_pairs={{0,2},{1,3},{2,0},{3,1},{4,6},{5,7},{6,4},{7,5},{8,10},{9,11},{10,... | collective-permute-start | bytes 1179656 | tf_op jit(solution)/shard_map/ppermute | solution.py:36
  13.7 1.3 broadcast.184.clone
  15.0 1.0 constant_dynamic-update-slice_fusion.1
  35.3 0.9 pad_maximum_fusion.1
  36.9 1.8 %bitcast_dynamic-update-slice_fusion.4 = (bf16[2,128,1536]{2,1,0:T(8,128)(2,1)S(1)}, bf16[4,128,1536]{2,1,0:T(8,128)(2,1)}) fusion(bf16[2,128,1536]{2,1,0:T(8,128)(2,1)S(1)} %get-tuple-element.69, s32[]{:T(128)S(6)} %select_n.464, bf16[128,1536]{1,0:T(8,128)(2,1)} %collective-permute-done, bf16[4,128,1536]{2,1,0:T(8,128)(2,1)} %get-tuple-element.70, ...), kind=kLoop, calls=%fused_computation.79 | loop fusion | bytes 1179656 | tf_op jit(solution)/shard_map/jit(dynamic_update_index_in_dim)/dynamic_update_slice | solution.py:40
  38.7 1.6 collective-permute-start.4
  40.7 1.8 %fusion.35 = bf16[8,192,1152]{2,1,0:T(8,128)(2,1)} fusion(bf16[8,192,1152]{2,1,0:T(8,128)(2,1)} %copy-done.1, s32[]{:T(128)S(6)} %select_n.471, bf16[192,1536]{1,0:T(8,128)(2,1)} %collective-permute-done.2), kind=kLoop, calls=%fused_computation.63 | loop fusion | bytes 884740 | tf_op jit(solution)/shard_map/jit(dynamic_update_index_in_dim)/dynamic_update_slice | solution.py:140
  42.5 1.8 %fusion.34 = bf16[8,192,1152]{2,1,0:T(8,128)(2,1)} fusion(bf16[8,192,1152]{2,1,0:T(8,128)(2,1)} %fusion.35, s32[]{:T(128)S(6)} %select_n.474, bf16[192,1536]{1,0:T(8,128)(2,1)} %collective-permute-done.3), kind=kLoop, calls=%fused_computation.61 | loop fusion | bytes 884740 | tf_op jit(solution)/shard_map/jit(dynamic_update_index_in_dim)/dynamic_update_slice | solution.py:140
  44.4 0.9 fusion.63
  45.3 0.9 fusion.62
  46.2 8.4 %collective-permute-done.4 = bf16[192,1536]{1,0:T(8,128)(2,1)S(1)} collective-permute-done((bf16[192,1536]{1,0:T(8,128)(2,1)}, bf16[192,1536]{1,0:T(8,128)(2,1)S(1)}, u32[]{:S(2)}, u32[]{:S(2)}) %collective-permute-start.4) | collective-permute-done | bytes 589856 | tf_op jit(solution)/shard_map/ppermute | solution.py:162
  54.6 1.6 collective-permute-start.6
  59.9 9.7 %collective-permute-done.6 = bf16[192,1536]{1,0:T(8,128)(2,1)S(1)} collective-permute-done((bf16[192,1536]{1,0:T(8,128)(2,1)S(1)}, bf16[192,1536]{1,0:T(8,128)(2,1)S(1)}, u32[]{:S(2)}, u32[]{:S(2)}) %collective-permute-start.6) | collective-permute-done | bytes 589856 | tf_op jit(solution)/shard_map/ppermute | solution.py:162
  69.6 1.6 collective-permute-start.8
  73.5 4.0 %collective-permute-done.8 = bf16[96,1536]{1,0:T(8,128)(2,1)S(1)} collective-permute-done((bf16[96,1536]{1,0:T(8,128)(2,1)S(1)}, bf16[96,1536]{1,0:T(8,128)(2,1)S(1)}, u32[]{:S(2)}, u32[]{:S(2)}) %collective-permute-start.8) | collective-permute-done | bytes 294944 | tf_op jit(solution)/shard_map/ppermute | solution.py:151
  77.4 1.4 collective-permute-done.9
  78.8 1.6 collective-permute-start.14
  82.3 5.7 %convolution_convert_fusion = bf16[512,1152]{1,0:T(8,128)(2,1)} fusion(bf16[512,1536]{1,0:T(8,128)(2,1)} %bitcast.2, bf16[1536,1152]{1,0:T(8,128)(2,1)} %bitcast.271), kind=kOutput, calls=%fused_computation.5 | convolution fusion | flops 1812529152 | bytes 6291456 | tf_op jit(solution)/shard_map/dot_general | solution.py:243
  88.1 1.6 copy.29
  89.7 3.6 %fusion.74 = (f32[4,512]{1,0:T(4,128)S(1)}, f32[4,512,512]{1,2,0:T(8,128)}) fusion(pred[512,512]{0,1:T(8,128)(4,1)S(1)} %copy-done.5, bf16[512,3,4,96]{0,3,2,1:T(8,128)(2,1)S(1)} %bitcast.281), kind=kOutput, calls=%fused_computation.250 | convolution fusion | flops 205521408 | bytes 5251072 | tf_op jit(solution)/shard_map/while/body/eval_jaxpr/sub | solution.py:194
  93.3 2.7 %fusion.6 = bf16[4,96,512]{2,1,0:T(8,128)(2,1)S(1)} fusion(f32[4,512,512]{1,2,0:T(8,128)} %get-tuple-element.147, f32[4,512]{1,0:T(4,128)S(1)} %get-tuple-element.146, bf16[512,3,4,96]{0,3,2,1:T(8,128)(2,1)S(1)} %bitcast.282), kind=kOutput, calls=%fused_computation.14 | convolution fusion | flops 203620352 | bytes 4988928 | tf_op jit(solution)/shard_map/while/body/eval_jaxpr/hqk,khe->qhe/dot_general | solution.py:196
  96.0 1.0 convolution_convert_fusion.1
  97.3 1.6 broadcast_in_dim.705
  99.6 1.6 collective-permute-start.16
  101.7 0.9 fusion.55
  102.6 0.9 fusion.54
  103.5 1.7 %fusion.47 = bf16[8,192,768]{2,1,0:T(8,128)(2,1)} fusion(bf16[8,192,768]{2,1,0:T(8,128)(2,1)} %bitcast_dynamic-update-slice_fusion.6, s32[]{:T(128)S(6)} %select_n.471, bf16[192,1152]{1,0:T(8,128)(2,1)} %collective-permute-done.14), kind=kLoop, calls=%fused_computation.98 | loop fusion | bytes 589828 | tf_op jit(solution)/shard_map/jit(dynamic_update_index_in_dim)/dynamic_update_slice | solution.py:140
  105.2 1.7 %fusion.46 = bf16[8,192,768]{2,1,0:T(8,128)(2,1)} fusion(bf16[8,192,768]{2,1,0:T(8,128)(2,1)} %fusion.47, s32[]{:T(128)S(6)} %select_n.474, bf16[192,1152]{1,0:T(8,128)(2,1)} %collective-permute-done.15), kind=kLoop, calls=%fused_computation.96 | loop fusion | bytes 589828 | tf_op jit(solution)/shard_map/jit(dynamic_update_index_in_dim)/dynamic_update_slice | solution.py:140
  107.8 4.6 %collective-permute-done.16 = bf16[192,1152]{1,0:T(8,128)(2,1)S(1)} collective-permute-done((bf16[192,1152]{1,0:T(8,128)(2,1)}, bf16[192,1152]{1,0:T(8,128)(2,1)S(1)}, u32[]{:S(2)}, u32[]{:S(2)}) %collective-permute-start.16) | collective-permute-done | bytes 442400 | tf_op jit(solution)/shard_map/ppermute | solution.py:162
  112.4 1.6 collective-permute-start.18
  116.0 2.3 %collective-permute-done.11 = bf16[128,1536]{1,0:T(8,128)(2,1)S(1)} collective-permute-done((bf16[128,1536]{1,0:T(8,128)(2,1)S(1)}, bf16[128,1536]{1,0:T(8,128)(2,1)S(1)}, u32[]{:S(2)}, u32[]{:S(2)}) %collective-permute-start.11) | collective-permute-done | bytes 393248 | tf_op jit(solution)/shard_map/ppermute | solution.py:84
  118.8 1.0 broadcast.187
  119.8 1.1 bitcast_dynamic-update-slice_fusion.2
  121.5 2.7 %collective-permute-done.18 = bf16[192,1152]{1,0:T(8,128)(2,1)S(1)} collective-permute-done((bf16[192,1152]{1,0:T(8,128)(2,1)S(1)}, bf16[192,1152]{1,0:T(8,128)(2,1)S(1)}, u32[]{:S(2)}, u32[]{:S(2)}) %collective-permute-start.18) | collective-permute-done | bytes 442400 | tf_op jit(solution)/shard_map/ppermute | solution.py:162
  124.2 1.6 collective-permute-start.20
  128.3 2.6 %collective-permute-done.12 = bf16[128,1536]{1,0:T(8,128)(2,1)S(1)} collective-permute-done((bf16[128,1536]{1,0:T(8,128)(2,1)S(1)}, bf16[128,1536]{1,0:T(8,128)(2,1)S(1)}, u32[]{:S(2)}, u32[]{:S(2)}) %collective-permute-start.12) | collective-permute-done | bytes 393248 | tf_op jit(solution)/shard_map/ppermute | solution.py:36
  133.2 4.3 %copy.34 = bf16[768,1536]{1,0:T(8,128)(2,1)} copy(bf16[768,1536]{0,1:T(8,128)(2,1)} %bitcast.65) | data formatting | bytes 4718592 | tf_op jit(solution)/shard_map/dot_general | solution.py:255
  139.3 1.0 slice_dynamic-update-slice_fusion.1
  140.3 1.0 slice_dynamic-update-slice_fusion
  141.4 3.1 %fusion.75 = f32[512,2,384]{2,0,1:T(8,128)S(1)} fusion(bf16[512,1536,1]{1,0,2:T(8,128)(2,1)S(1)} %bitcast.279, bf16[2,384,1536]{2,1,0:T(8,128)(2,1)} %bitcast.276), kind=kOutput, calls=%fused_computation.251 | convolution fusion | flops 1207959552 | bytes 5505024 | tf_op jit(solution)/shard_map/dot_general | solution.py:255
  145.5 7.1 %multiply_convert_fusion.1 = bf16[256,384]{1,0:T(8,128)(2,1)S(1)} fusion(s32[]{:T(128)S(6)} %add.745, s32[]{:T(128)S(6)} %add.744, s32[]{:T(128)S(6)} %add.743, s32[]{:T(128)S(6)} %add.742, s32[]{:T(128)S(6)} %add.741, s32[]{:T(128)S(6)} %add.740, s32[]{:T(128)S(6)} %add.739, s32[]{:T(128)S(6)} %add.738, s32[]{:T(128)S(6)} %add.737, s32[]{:T(128)S(6)} %add.736, ...), kind=kLoop, calls=%fused_computation.84 | loop fusion | flops 12582912 | bytes 645500 | tf_op jit(solution)/shard_map/convert_element_type | solution.py:215
  154.2 1.1 collective-permute-done.22
  156.0 5.3 %multiply_convert_fusion = bf16[256,384]{1,0:T(8,128)(2,1)S(1)} fusion(bf16[542,384]{1,0:T(8,128)(2,1)S(1)} %pad.4, s32[]{:T(128)S(6)} %add.775, s32[]{:T(128)S(6)} %add.774, s32[]{:T(128)S(6)} %add.773, s32[]{:T(128)S(6)} %add.772, s32[]{:T(128)S(6)} %add.771, s32[]{:T(128)S(6)} %add.770, s32[]{:T(128)S(6)} %add.769, s32[]{:T(128)S(6)} %add.768, ...), kind=kLoop, calls=%fused_computation.82 | loop fusion | flops 12582912 | bytes 6347132 | tf_op jit(solution)/shard_map/convert_element_type | solution.py:215
  162.2 4.6 %collective-permute-done.24 = bf16[128,1536]{1,0:T(8,128)(2,1)S(1)} collective-permute-done((bf16[128,1536]{1,0:T(8,128)(2,1)S(1)}, bf16[128,1536]{1,0:T(8,128)(2,1)S(1)}, u32[]{:S(2)}, u32[]{:S(2)}) %collective-permute-start.24) | collective-permute-done | bytes 393248 | tf_op jit(solution)/shard_map/ppermute | solution.py:281
  166.8 0.9 fusion.39
  (221 shorter events, 32.3 us)
Async XLA Ops:
  0.0 6.0 %copy-start = (bf16[1,128,1536]{2,1,0:T(8,128)(2,1)S(1)}, bf16[1,128,1536]{2,1,0:T(8,128)(2,1)}, u32[]{:S(2)}) copy-start(bf16[1,128,1536]{2,1,0:T(8,128)(2,1)} %param.13) | copy-start | bytes 1179652
  0.0 6.4 %copy-start.9 = (f32[1536]{0:T(1024)S(1)}, f32[1536]{0:T(1024)}, u32[]{:S(2)}) copy-start(f32[1536]{0:T(1024)} %param.15) | copy-start | bytes 18436
  1.1 7.6 %copy-start.54 = (s32[1,4]{1,0:T(1,128)S(1)}, s32[1,4]{1,0:T(1,128)}, u32[]{:S(2)}) copy-start(s32[1,4]{1,0:T(1,128)} %param.14) | copy-start | bytes 52
  1.1 11.1 %copy-start.2 = (bf16[192,3,384]{2,0,1:T(8,128)(2,1)S(1)}, bf16[192,3,384]{2,0,1:T(8,128)(2,1)}, u32[]{:S(2)}) copy-start(bf16[192,3,384]{2,0,1:T(8,128)(2,1)} %param.17) | copy-start | bytes 1327108
  3.0 35.7 %collective-permute-start.2 = (bf16[192,1536]{1,0:T(8,128)(2,1)}, bf16[192,1536]{1,0:T(8,128)(2,1)}, u32[]{:S(2)}, u32[]{:S(2)}) collective-permute-start(bf16[192,1536]{1,0:T(8,128)(2,1)} %pad_maximum_fusion), channel_id=1, source_target_pairs={{0,8},{8,16},{16,24},{24,28},{28,20},{20,12},{12,4},{4,0},{1,9},{9... | collective-permute-start | bytes 1769480 | tf_op jit(solution)/shard_map/ppermute | solution.py:162
  6.0 34.3 %collective-permute-start.3 = (bf16[192,1536]{1,0:T(8,128)(2,1)}, bf16[192,1536]{1,0:T(8,128)(2,1)}, u32[]{:S(2)}, u32[]{:S(2)}) collective-permute-start(bf16[192,1536]{1,0:T(8,128)(2,1)} %pad_maximum_fusion), channel_id=1, source_target_pairs={{0,4},{8,0},{16,8},{24,16},{28,24},{20,28},{12,20},{4,12},{1,5},{9... | collective-permute-start | bytes 1769480 | tf_op jit(solution)/shard_map/ppermute | solution.py:165
  6.7 30.2 %collective-permute-start = (bf16[128,1536]{1,0:T(8,128)(2,1)S(1)}, bf16[128,1536]{1,0:T(8,128)(2,1)}, u32[]{:S(2)}, u32[]{:S(2)}) collective-permute-start(bf16[128,1536]{1,0:T(8,128)(2,1)S(1)} %fusion.18), channel_id=1, source_target_pairs={{0,2},{1,3},{2,0},{3,1},{4,6},{5,7},{6,4},{7,5},{8,10},{9,11},{10,... | collective-permute-start | bytes 1179656 | tf_op jit(solution)/shard_map/ppermute | solution.py:36
  12.2 0.9 copy-start.3
  13.6 2.4 %copy-start.1 = (bf16[8,192,1152]{2,1,0:T(8,128)(2,1)}, bf16[8,192,1152]{2,1,0:T(8,128)(2,1)S(1)}, u32[]{:S(2)}) copy-start(bf16[8,192,1152]{2,1,0:T(8,128)(2,1)S(1)} %constant_dynamic-update-slice_fusion) | copy-start | bytes 10616836
  13.7 2.4 %copy-start.8 = (bf16[31,384]{1,0:T(8,128)(2,1)S(1)}, bf16[31,384]{1,0:T(8,128)(2,1)}, u32[]{:S(2)}) copy-start(bf16[31,384]{1,0:T(8,128)(2,1)} %param.20) | copy-start | bytes 71428
  13.7 3.1 %copy-start.55 = (s32[8]{0:T(128)S(1)}, s32[8]{0:T(128)}, u32[]{:S(2)}) copy-start(s32[8]{0:T(128)} %constant.348.clone) | copy-start | bytes 100
  13.7 7.5 %copy-start.10 = (s32[8]{0:T(128)S(1)}, s32[8]{0:T(128)}, u32[]{:S(2)}) copy-start(s32[8]{0:T(128)} %constant.349.clone) | copy-start | bytes 100
  13.7 17.1 %copy-start.4 = (bf16[192,2,384]{2,1,0:T(2,128)(2,1)S(1)}, bf16[192,2,384]{2,1,0:T(2,128)(2,1)}, u32[]{:S(2)}) copy-start(bf16[192,2,384]{2,1,0:T(2,128)(2,1)} %param.19) | copy-start | bytes 884740
  38.7 18.8 %collective-permute-start.1 = (bf16[2,128,1536]{2,1,0:T(8,128)(2,1)S(1)}, bf16[2,128,1536]{2,1,0:T(8,128)(2,1)S(1)}, u32[]{:S(2)}, u32[]{:S(2)}) collective-permute-start(bf16[2,128,1536]{2,1,0:T(8,128)(2,1)S(1)} %get-tuple-element.73), channel_id=1, source_target_pairs={{0,1},{1,0},{2,3},{3,2},{4,5},{5,4},{6,7},{7,6},{8,9},{9,8},{10,11... | collective-permute-start | bytes 2359304 | tf_op jit(solution)/shard_map/ppermute | solution.py:42
  38.7 16.0 %collective-permute-start.4 = (bf16[192,1536]{1,0:T(8,128)(2,1)}, bf16[192,1536]{1,0:T(8,128)(2,1)S(1)}, u32[]{:S(2)}, u32[]{:S(2)}) collective-permute-start(bf16[192,1536]{1,0:T(8,128)(2,1)} %collective-permute-done.2), channel_id=1, source_target_pairs={{0,8},{8,16},{16,24},{24,28},{28,20},{20,12},{12,4},{4,0},{1,9},{9... | collective-permute-start | bytes 1769480 | tf_op jit(solution)/shard_map/ppermute | solution.py:162
  40.3 16.0 %collective-permute-start.5 = (bf16[192,1536]{1,0:T(8,128)(2,1)}, bf16[192,1536]{1,0:T(8,128)(2,1)S(1)}, u32[]{:S(2)}, u32[]{:S(2)}) collective-permute-start(bf16[192,1536]{1,0:T(8,128)(2,1)} %collective-permute-done.3), channel_id=1, source_target_pairs={{0,4},{8,0},{16,8},{24,16},{28,24},{20,28},{12,20},{4,12},{1,5},{9... | collective-permute-start | bytes 1769480 | tf_op jit(solution)/shard_map/ppermute | solution.py:165
  54.6 15.0 %collective-permute-start.6 = (bf16[192,1536]{1,0:T(8,128)(2,1)S(1)}, bf16[192,1536]{1,0:T(8,128)(2,1)S(1)}, u32[]{:S(2)}, u32[]{:S(2)}) collective-permute-start(bf16[192,1536]{1,0:T(8,128)(2,1)S(1)} %collective-permute-done.4), channel_id=1, source_target_pairs={{0,8},{8,16},{16,24},{24,28},{28,20},{20,12},{12,4},{4,0},{1,9},{9... | collective-permute-start | bytes 1769480 | tf_op jit(solution)/shard_map/ppermute | solution.py:162
  56.2 15.0 %collective-permute-start.7 = (bf16[192,1536]{1,0:T(8,128)(2,1)S(1)}, bf16[192,1536]{1,0:T(8,128)(2,1)S(1)}, u32[]{:S(2)}, u32[]{:S(2)}) collective-permute-start(bf16[192,1536]{1,0:T(8,128)(2,1)S(1)} %collective-permute-done.5), channel_id=1, source_target_pairs={{0,4},{8,0},{16,8},{24,16},{28,24},{20,28},{12,20},{4,12},{1,5},{9... | collective-permute-start | bytes 1769480 | tf_op jit(solution)/shard_map/ppermute | solution.py:165
  69.6 7.8 %collective-permute-start.8 = (bf16[96,1536]{1,0:T(8,128)(2,1)S(1)}, bf16[96,1536]{1,0:T(8,128)(2,1)S(1)}, u32[]{:S(2)}, u32[]{:S(2)}) collective-permute-start(bf16[96,1536]{1,0:T(8,128)(2,1)S(1)} %slice.847), channel_id=1, source_target_pairs={{0,8},{8,16},{16,24},{24,28},{28,20},{20,12},{12,4},{4,0},{1,9},{9... | collective-permute-start | bytes 884744 | tf_op jit(solution)/shard_map/ppermute | solution.py:151
  71.3 7.5 %collective-permute-start.9 = (bf16[96,1536]{1,0:T(8,128)(2,1)S(1)}, bf16[96,1536]{1,0:T(8,128)(2,1)S(1)}, u32[]{:S(2)}, u32[]{:S(2)}) collective-permute-start(bf16[96,1536]{1,0:T(8,128)(2,1)S(1)} %slice.849), channel_id=1, source_target_pairs={{0,4},{8,0},{16,8},{24,16},{28,24},{20,28},{12,20},{4,12},{1,5},{9... | collective-permute-start | bytes 884744 | tf_op jit(solution)/shard_map/ppermute | solution.py:152
  78.8 20.8 %collective-permute-start.14 = (bf16[192,1152]{1,0:T(8,128)(2,1)S(1)}, bf16[192,1152]{1,0:T(8,128)(2,1)}, u32[]{:S(2)}, u32[]{:S(2)}) collective-permute-start(bf16[192,1152]{1,0:T(8,128)(2,1)S(1)} %pad_maximum_fusion.1), channel_id=1, source_target_pairs={{0,8},{8,16},{16,24},{24,28},{28,20},{20,12},{12,4},{4,0},{1,9},{9... | collective-permute-start | bytes 1327112 | tf_op jit(solution)/shard_map/ppermute | solution.py:162
  80.5 20.8 %collective-permute-start.15 = (bf16[192,1152]{1,0:T(8,128)(2,1)S(1)}, bf16[192,1152]{1,0:T(8,128)(2,1)}, u32[]{:S(2)}, u32[]{:S(2)}) collective-permute-start(bf16[192,1152]{1,0:T(8,128)(2,1)S(1)} %pad_maximum_fusion.1), channel_id=1, source_target_pairs={{0,4},{8,0},{16,8},{24,16},{28,24},{20,28},{12,20},{4,12},{1,5},{9... | collective-permute-start | bytes 1327112 | tf_op jit(solution)/shard_map/ppermute | solution.py:165
  88.1 1.6 copy-start.5
  97.1 9.8 %collective-permute-start.10 = (bf16[2,128,1536]{2,1,0:T(8,128)(2,1)S(1)}, bf16[2,128,1536]{2,1,0:T(8,128)(2,1)S(1)}, u32[]{:S(2)}, u32[]{:S(2)}) collective-permute-start(bf16[2,128,1536]{2,1,0:T(8,128)(2,1)S(1)} %dynamic-slice_bitcast_fusion), channel_id=1, source_target_pairs={{0,1},{1,0},{2,3},{3,2},{4,5},{5,4},{6,7},{7,6},{8,9},{9,8},{10,11... | collective-permute-start | bytes 2359304 | tf_op jit(solution)/shard_map/ppermute | solution.py:78
  99.6 12.8 %collective-permute-start.16 = (bf16[192,1152]{1,0:T(8,128)(2,1)}, bf16[192,1152]{1,0:T(8,128)(2,1)S(1)}, u32[]{:S(2)}, u32[]{:S(2)}) collective-permute-start(bf16[192,1152]{1,0:T(8,128)(2,1)} %collective-permute-done.14), channel_id=1, source_target_pairs={{0,8},{8,16},{16,24},{24,28},{28,20},{20,12},{12,4},{4,0},{1,9},{9... | collective-permute-start | bytes 1327112 | tf_op jit(solution)/shard_map/ppermute | solution.py:162
  101.2 13.5 %collective-permute-start.17 = (bf16[192,1152]{1,0:T(8,128)(2,1)}, bf16[192,1152]{1,0:T(8,128)(2,1)S(1)}, u32[]{:S(2)}, u32[]{:S(2)}) collective-permute-start(bf16[192,1152]{1,0:T(8,128)(2,1)} %collective-permute-done.15), channel_id=1, source_target_pairs={{0,4},{8,0},{16,8},{24,16},{28,24},{20,28},{12,20},{4,12},{1,5},{9... | collective-permute-start | bytes 1327112 | tf_op jit(solution)/shard_map/ppermute | solution.py:165
  107.2 11.0 %collective-permute-start.11 = (bf16[128,1536]{1,0:T(8,128)(2,1)S(1)}, bf16[128,1536]{1,0:T(8,128)(2,1)S(1)}, u32[]{:S(2)}, u32[]{:S(2)}) collective-permute-start(bf16[128,1536]{1,0:T(8,128)(2,1)S(1)} %fusion.38), channel_id=1, source_target_pairs={{0,2},{1,3},{2,0},{3,1},{4,6},{5,7},{6,4},{7,5},{8,10},{9,11},{10,... | collective-permute-start | bytes 1179656 | tf_op jit(solution)/shard_map/ppermute | solution.py:84
  112.4 11.8 %collective-permute-start.18 = (bf16[192,1152]{1,0:T(8,128)(2,1)S(1)}, bf16[192,1152]{1,0:T(8,128)(2,1)S(1)}, u32[]{:S(2)}, u32[]{:S(2)}) collective-permute-start(bf16[192,1152]{1,0:T(8,128)(2,1)S(1)} %collective-permute-done.16), channel_id=1, source_target_pairs={{0,8},{8,16},{16,24},{24,28},{28,20},{20,12},{12,4},{4,0},{1,9},{9... | collective-permute-start | bytes 1327112 | tf_op jit(solution)/shard_map/ppermute | solution.py:162
  114.7 11.5 %collective-permute-start.19 = (bf16[192,1152]{1,0:T(8,128)(2,1)S(1)}, bf16[192,1152]{1,0:T(8,128)(2,1)S(1)}, u32[]{:S(2)}, u32[]{:S(2)}) collective-permute-start(bf16[192,1152]{1,0:T(8,128)(2,1)S(1)} %collective-permute-done.17), channel_id=1, source_target_pairs={{0,4},{8,0},{16,8},{24,16},{28,24},{20,28},{12,20},{4,12},{1,5},{9... | collective-permute-start | bytes 1327112 | tf_op jit(solution)/shard_map/ppermute | solution.py:165
  116.0 3.8 %copy-start.40 = (f32[1536]{0:T(1024)S(1)}, f32[1536]{0:T(1024)}, u32[]{:S(2)}) copy-start(f32[1536]{0:T(1024)} %param.16) | copy-start | bytes 18436
  120.8 10.1 %collective-permute-start.12 = (bf16[128,1536]{1,0:T(8,128)(2,1)S(1)}, bf16[128,1536]{1,0:T(8,128)(2,1)S(1)}, u32[]{:S(2)}, u32[]{:S(2)}) collective-permute-start(bf16[128,1536]{1,0:T(8,128)(2,1)S(1)} %get-tuple-element.64), channel_id=1, source_target_pairs={{0,2},{1,3},{2,0},{3,1},{4,6},{5,7},{6,4},{7,5},{8,10},{9,11},{10,... | collective-permute-start | bytes 1179656 | tf_op jit(solution)/shard_map/ppermute | solution.py:36
  124.2 7.5 %collective-permute-start.20 = (bf16[96,1152]{1,0:T(8,128)(2,1)S(1)}, bf16[96,1152]{1,0:T(8,128)(2,1)S(1)}, u32[]{:S(2)}, u32[]{:S(2)}) collective-permute-start(bf16[96,1152]{1,0:T(8,128)(2,1)S(1)} %slice.870), channel_id=1, source_target_pairs={{0,8},{8,16},{16,24},{24,28},{28,20},{20,12},{12,4},{4,0},{1,9},{9... | collective-permute-start | bytes 663560 | tf_op jit(solution)/shard_map/ppermute | solution.py:151
  126.2 6.2 %collective-permute-start.21 = (bf16[96,1152]{1,0:T(8,128)(2,1)S(1)}, bf16[96,1152]{1,0:T(8,128)(2,1)S(1)}, u32[]{:S(2)}, u32[]{:S(2)}) collective-permute-start(bf16[96,1152]{1,0:T(8,128)(2,1)S(1)} %slice.872), channel_id=1, source_target_pairs={{0,4},{8,0},{16,8},{24,16},{28,24},{20,28},{12,20},{4,12},{1,5},{9... | collective-permute-start | bytes 663560 | tf_op jit(solution)/shard_map/ppermute | solution.py:152
  131.7 7.6 %collective-permute-start.13 = (bf16[2,128,1536]{2,1,0:T(8,128)(2,1)}, bf16[2,128,1536]{2,1,0:T(8,128)(2,1)}, u32[]{:S(2)}, u32[]{:S(2)}) collective-permute-start(bf16[2,128,1536]{2,1,0:T(8,128)(2,1)} %get-tuple-element.71), channel_id=1, source_target_pairs={{0,1},{1,0},{2,3},{3,2},{4,5},{5,4},{6,7},{7,6},{8,9},{9,8},{10,11... | collective-permute-start | bytes 2359304 | tf_op jit(solution)/shard_map/ppermute | solution.py:42
  131.7 0.7 copy-start.6
  132.5 0.7 copy-start.7
  144.5 0.7 copy-start.15
  144.6 0.7 copy-start.23
  144.6 0.7 copy-start.25
  144.6 0.7 copy-start.26
  144.6 0.7 copy-start.27
  144.7 0.7 copy-start.38
  144.7 0.7 copy-start.42
  152.6 1.2 copy-start.39
  153.3 2.7 %copy-start.41 = (pred[256]{0:T(512)(128)(4,1)S(1)}, pred[256]{0:T(512)(128)(4,1)}, u32[]{:S(2)}) copy-start(pred[256]{0:T(512)(128)(4,1)} %get-tuple-element.61) | copy-start | bytes 772
  153.3 1.9 %collective-permute-start.22 = (bf16[128,1536]{1,0:T(8,128)(2,1)S(1)}, bf16[128,1536]{1,0:T(8,128)(2,1)S(1)}, u32[]{:S(2)}, u32[]{:S(2)}) collective-permute-start(bf16[128,1536]{1,0:T(8,128)(2,1)S(1)} %dynamic-slice_bitcast_fusion.2), channel_id=1, source_target_pairs={{0,1},{1,0},{2,3},{3,2},{4,5},{5,4},{6,7},{7,6},{8,9},{9,8},{10,11... | collective-permute-start | bytes 1179656 | tf_op jit(solution)/shard_map/ppermute | solution.py:277
  155.3 11.5 %collective-permute-start.24 = (bf16[128,1536]{1,0:T(8,128)(2,1)S(1)}, bf16[128,1536]{1,0:T(8,128)(2,1)S(1)}, u32[]{:S(2)}, u32[]{:S(2)}) collective-permute-start(bf16[128,1536]{1,0:T(8,128)(2,1)S(1)} %convert_add_fusion.3), channel_id=1, source_target_pairs={{0,2},{1,3},{2,0},{3,1},{4,6},{5,7},{6,4},{7,5},{8,10},{9,11},{10,... | collective-permute-start | bytes 1179656 | tf_op jit(solution)/shard_map/ppermute | solution.py:281
  161.9 4.9 %collective-permute-start.23 = (bf16[128,1536]{1,0:T(8,128)(2,1)S(1)}, bf16[128,1536]{1,0:T(8,128)(2,1)S(1)}, u32[]{:S(2)}, u32[]{:S(2)}) collective-permute-start(bf16[128,1536]{1,0:T(8,128)(2,1)S(1)} %dynamic-slice_bitcast_fusion.1), channel_id=1, source_target_pairs={{0,1},{1,0},{2,3},{3,2},{4,5},{5,4},{6,7},{7,6},{8,9},{9,8},{10,11... | collective-permute-start | bytes 1179656 | tf_op jit(solution)/shard_map/ppermute | solution.py:277
  (33 other events, 22.1 us)

commit v14 on v12

--- a/solution.py
+++ b/solution.py
@@ -256,7 +256,9 @@
         shard_piece.shape[0], 2, group_width
     )
     gated = (glu_pair[:, 0] * jax.nn.sigmoid(glu_pair[:, 1])).astype(jnp.bfloat16)
-    padded = jnp.pad(gated, ((kernel_reach, kernel_reach), (0, 0)))
+    padded = lax.optimization_barrier(
+        jnp.pad(gated, ((kernel_reach, kernel_reach), (0, 0))).astype(jnp.float32)
+    )
     near_positions = jnp.arange(-kernel_reach, group_rows + kernel_reach, dtype=jnp.int32)
     activated = depthwise(
         padded, dw_kernel, seg_all, segment_of(record_ends, near_positions), group_rows

time: 167 us -> 167 us (level)
  no operation moved by 1% of the time
where the time goes in v14:
time: 167 us; the launch traced here: 166 us
  waiting for transfers between devices  52.7 us (32%)
  local copies, waits for them, and re-layouts  38.1 us (23%)
  starting transfers between devices  21.7 us (13%)
  between operations  18.2 us (11%)
  other arithmetic  18.1 us (11%)
  matrix products  17.6 us (11%)
    ppermute x6, waiting for transfers between devices, ring_gather(): ahead = lax.ppermute(ahead, 'dp', forward)  28.1 us
    ppermute x2, waiting for transfers between devices, seq_scatter_sum(): lax.ppermute(piece.astype(jnp.bfloat16), 'seq', [(i, (i + 2 * shift) % co...  12.6 us
    dynamic_update_slice x28, local copies, waits for them, and re-layouts, place(): lax.dynamic_update_index_in_dim(out, piece[..., lo:hi], where, 0)  11.9 us
    ppermute x6, starting transfers between devices, ring_gather(): ahead = lax.ppermute(ahead, 'dp', forward)  11 us
    convert_element_type x1, other arithmetic, depthwise(): return jax.nn.silu(total_acc).astype(jnp.bfloat16)  6.24 us
    dot_general x1, matrix products, on_device(): jnp.dot(seq_gather(normed1, paired).reshape(group_rows, model_width), qkv...  5.73 us
    dynamic_update_slice x4, local copies, waits for them, and re-layouts, seq_gather(): out = lax.dynamic_update_index_in_dim(out, other[k], 2 * k + partner % 2, 0)  5.09 us
    another operation x6, local copies, waits for them, and re-layouts  4.68 us
  transfers between devices with their start and end apart: 24, of which 11 were waited for; matrix products, arithmetic and copies ran while one was open for 33% of the time, Pallas kernels for 0%

profile of v14, /device:TPU:0, one launch (start us, length us, event | category | flops | bytes accessed | tf_op | source)
XLA Modules:
  0.0 166.4 jit_solution(10669929236525060785)
XLA Ops:
  0.0 1.1 copy.40
  1.1 1.8 %pad_maximum_fusion = bf16[192,1536]{1,0:T(8,128)(2,1)} fusion(bf16[192,384]{1,0:T(8,128)(2,1)} %bitcast.281, bf16[192,1152]{1,0:T(8,128)(2,1)S(1)} %bitcast.276), kind=kLoop, calls=%fused_computation.143 | loop fusion | flops 1179648 | bytes 1179648 | tf_op jit(solution)/shard_map/concatenate | solution.py:227
  3.0 3.0 %collective-permute-start.2 = (bf16[192,1536]{1,0:T(8,128)(2,1)}, bf16[192,1536]{1,0:T(8,128)(2,1)}, u32[]{:S(2)}, u32[]{:S(2)}) collective-permute-start(bf16[192,1536]{1,0:T(8,128)(2,1)} %pad_maximum_fusion), channel_id=1, source_target_pairs={{0,8},{8,16},{16,24},{24,28},{28,20},{20,12},{12,4},{4,0},{1,9},{9... | collective-permute-start | bytes 1769480 | tf_op jit(solution)/shard_map/ppermute | solution.py:162
  6.4 1.0 fusion.18
  7.4 1.9 %collective-permute-start = (bf16[128,1536]{1,0:T(8,128)(2,1)}, bf16[128,1536]{1,0:T(8,128)(2,1)}, u32[]{:S(2)}, u32[]{:S(2)}) collective-permute-start(bf16[128,1536]{1,0:T(8,128)(2,1)} %fusion.18), channel_id=1, source_target_pairs={{0,2},{1,3},{2,0},{3,1},{4,6},{5,7},{6,4},{7,5},{8,10},{9,11},{10,... | collective-permute-start | bytes 1179656 | tf_op jit(solution)/shard_map/ppermute | solution.py:36
  12.4 2.2 %broadcast_in_dim.432 = bf16[8,192,1152]{2,1,0:T(8,128)(2,1)} broadcast(bf16[]{:T(256)} %constant.311.clone.1), dimensions={} | broadcast | bytes 3538946 | tf_op jit(solution)/shard_map/broadcast_in_dim | solution.py:136
  15.4 0.9 broadcast.157.clone
  16.3 1.3 broadcast.154.clone
  17.6 1.2 constant_dynamic-update-slice_fusion.1
  37.8 0.9 pad_maximum_fusion.1
  39.4 1.9 %bitcast_dynamic-update-slice_fusion.4 = (bf16[2,128,1536]{2,1,0:T(8,128)(2,1)}, bf16[4,128,1536]{2,1,0:T(8,128)(2,1)}) fusion(bf16[2,128,1536]{2,1,0:T(8,128)(2,1)} %get-tuple-element.63, s32[]{:T(128)S(6)} %select_n.358, bf16[128,1536]{1,0:T(8,128)(2,1)} %collective-permute-done, bf16[4,128,1536]{2,1,0:T(8,128)(2,1)} %get-tuple-element.64, s32[]{:T(128)S(6)} %select_n.354), kind=kLoop, calls=%fused_computation.174 | loop fusion | bytes 1179656 | tf_op jit(solution)/shard_map/jit(dynamic_update_index_in_dim)/dynamic_update_slice | solution.py:40
  41.4 1.6 collective-permute-start.4
  43.4 1.8 %fusion.95 = bf16[8,192,1152]{2,1,0:T(8,128)(2,1)} fusion(bf16[8,192,1152]{2,1,0:T(8,128)(2,1)} %constant_dynamic-update-slice_fusion, s32[]{:T(128)S(6)} %select_n.365, bf16[192,1536]{1,0:T(8,128)(2,1)} %collective-permute-done.2), kind=kLoop, calls=%fused_computation.156 | loop fusion | bytes 884740 | tf_op jit(solution)/shard_map/jit(dynamic_update_index_in_dim)/dynamic_update_slice | solution.py:140
  46.1 0.9 fusion.124
  47.0 10.3 %collective-permute-done.4 = bf16[192,1536]{1,0:T(8,128)(2,1)S(1)} collective-permute-done((bf16[192,1536]{1,0:T(8,128)(2,1)}, bf16[192,1536]{1,0:T(8,128)(2,1)S(1)}, u32[]{:S(2)}, u32[]{:S(2)}) %collective-permute-start.4) | collective-permute-done | bytes 589856 | tf_op jit(solution)/shard_map/ppermute | solution.py:162
  57.3 1.6 collective-permute-start.6
  62.6 9.7 %collective-permute-done.6 = bf16[192,1536]{1,0:T(8,128)(2,1)S(1)} collective-permute-done((bf16[192,1536]{1,0:T(8,128)(2,1)S(1)}, bf16[192,1536]{1,0:T(8,128)(2,1)S(1)}, u32[]{:S(2)}, u32[]{:S(2)}) %collective-permute-start.6) | collective-permute-done | bytes 589856 | tf_op jit(solution)/shard_map/ppermute | solution.py:162
  72.3 1.6 collective-permute-start.8
  76.1 3.9 %collective-permute-done.8 = bf16[96,1536]{1,0:T(8,128)(2,1)S(1)} collective-permute-done((bf16[96,1536]{1,0:T(8,128)(2,1)S(1)}, bf16[96,1536]{1,0:T(8,128)(2,1)S(1)}, u32[]{:S(2)}, u32[]{:S(2)}) %collective-permute-start.8) | collective-permute-done | bytes 294944 | tf_op jit(solution)/shard_map/ppermute | solution.py:151
  80.1 1.4 collective-permute-done.9
  81.5 1.6 collective-permute-start.14
  85.0 5.7 %convolution_convert_fusion = bf16[512,1152]{1,0:T(8,128)(2,1)} fusion(bf16[512,1536]{1,0:T(8,128)(2,1)} %bitcast.2, bf16[1536,1152]{1,0:T(8,128)(2,1)} %bitcast.26), kind=kOutput, calls=%fused_computation.5 | convolution fusion | flops 1812529152 | bytes 6291456 | tf_op jit(solution)/shard_map/dot_general | solution.py:243
  90.7 1.6 copy.31
  92.3 3.6 %fusion.134 = (f32[4,512]{1,0:T(4,128)S(1)}, f32[4,512,512]{1,2,0:T(8,128)}) fusion(pred[512,512]{0,1:T(8,128)(4,1)S(1)} %broadcast_compare_fusion, bf16[512,3,4,96]{0,3,2,1:T(8,128)(2,1)S(1)} %bitcast.279), kind=kOutput, calls=%fused_computation.309 | convolution fusion | flops 205521408 | bytes 5251072 | tf_op jit(solution)/shard_map/while/body/eval_jaxpr/sub | solution.py:194
  95.9 2.7 %fusion.6 = bf16[4,96,512]{2,1,0:T(8,128)(2,1)S(1)} fusion(f32[4,512,512]{1,2,0:T(8,128)} %get-tuple-element.108, f32[4,512]{1,0:T(4,128)S(1)} %get-tuple-element.107, bf16[512,3,4,96]{0,3,2,1:T(8,128)(2,1)S(1)} %bitcast.280), kind=kOutput, calls=%fused_computation.14 | convolution fusion | flops 203620352 | bytes 4988928 | tf_op jit(solution)/shard_map/while/body/eval_jaxpr/hqk,khe->qhe/dot_general | solution.py:196
  98.6 1.0 convolution_convert_fusion.2
  100.1 1.6 collective-permute-start.16
  103.2 0.9 fusion.115
  104.1 1.0 fusion.108
  105.1 1.0 fusion.107
  107.0 6.0 %collective-permute-done.16 = bf16[192,1152]{1,0:T(8,128)(2,1)S(1)} collective-permute-done((bf16[192,1152]{1,0:T(8,128)(2,1)}, bf16[192,1152]{1,0:T(8,128)(2,1)S(1)}, u32[]{:S(2)}, u32[]{:S(2)}) %collective-permute-start.16) | collective-permute-done | bytes 442400 | tf_op jit(solution)/shard_map/ppermute | solution.py:162
  113.0 1.6 collective-permute-start.18
  115.4 2.0 %collective-permute-done.11 = bf16[128,1536]{1,0:T(8,128)(2,1)S(1)} collective-permute-done((bf16[128,1536]{1,0:T(8,128)(2,1)S(1)}, bf16[128,1536]{1,0:T(8,128)(2,1)S(1)}, u32[]{:S(2)}, u32[]{:S(2)}) %collective-permute-start.11) | collective-permute-done | bytes 393248 | tf_op jit(solution)/shard_map/ppermute | solution.py:84
  117.9 1.0 broadcast.157
  118.9 1.0 bitcast_dynamic-update-slice_fusion.2
  120.5 1.3 broadcast.154
  122.5 2.2 %collective-permute-done.18 = bf16[192,1152]{1,0:T(8,128)(2,1)S(1)} collective-permute-done((bf16[192,1152]{1,0:T(8,128)(2,1)S(1)}, bf16[192,1152]{1,0:T(8,128)(2,1)S(1)}, u32[]{:S(2)}, u32[]{:S(2)}) %collective-permute-start.18) | collective-permute-done | bytes 442400 | tf_op jit(solution)/shard_map/ppermute | solution.py:162
  124.8 1.6 collective-permute-start.20
  127.1 2.9 %collective-permute-done.12 = bf16[128,1536]{1,0:T(8,128)(2,1)S(1)} collective-permute-done((bf16[128,1536]{1,0:T(8,128)(2,1)S(1)}, bf16[128,1536]{1,0:T(8,128)(2,1)S(1)}, u32[]{:S(2)}, u32[]{:S(2)}) %collective-permute-start.12) | collective-permute-done | bytes 393248 | tf_op jit(solution)/shard_map/ppermute | solution.py:36
  131.0 1.4 collective-permute-done.21
  132.4 2.4 %copy.37 = bf16[768,1536]{1,0:T(8,128)(2,1)} copy(bf16[768,1536]{0,1:T(8,128)(2,1)S(1)} %bitcast.268) | data formatting | bytes 4718592 | tf_op jit(solution)/shard_map/dot_general | solution.py:255
  136.1 1.8 %slice_dynamic-update-slice_fusion.1 = bf16[4,128,1536]{2,1,0:T(8,128)(2,1)} fusion(bf16[4,128,1536]{2,1,0:T(8,128)(2,1)} %get-tuple-element.66, s32[]{:T(128)S(6)} %select_n.360, bf16[2,128,1536]{2,1,0:T(8,128)(2,1)} %collective-permute-done.13), kind=kLoop, calls=%fused_computation.164 | loop fusion | bytes 786436 | tf_op jit(solution)/shard_map/jit(dynamic_update_index_in_dim)/dynamic_update_slice | solution.py:45
  137.9 1.8 %slice_dynamic-update-slice_fusion = bf16[4,128,1536]{2,1,0:T(8,128)(2,1)} fusion(bf16[4,128,1536]{2,1,0:T(8,128)(2,1)} %slice_dynamic-update-slice_fusion.1, s32[]{:T(128)S(6)} %select_n.361, bf16[2,128,1536]{2,1,0:T(8,128)(2,1)} %collective-permute-done.13), kind=kLoop, calls=%fused_computation.163 | loop fusion | bytes 786436 | tf_op jit(solution)/shard_map/jit(dynamic_update_index_in_dim)/dynamic_update_slice | solution.py:45
  139.7 3.6 %fusion.135 = f32[512,2,384]{2,0,1:T(8,128)S(1)} fusion(bf16[512,1536,1]{1,0,2:T(8,128)(2,1)} %bitcast.53, bf16[2,384,1536]{2,1,0:T(8,128)(2,1)} %bitcast.275), kind=kOutput, calls=%fused_computation.310 | convolution fusion | flops 1207959552 | bytes 5505024 | tf_op jit(solution)/shard_map/dot_general | solution.py:255
  144.3 6.2 %multiply_convert_fusion = bf16[512,384]{1,0:T(8,128)(2,1)S(1)} fusion(f32[542,384]{1,0:T(8,128)S(1)} %pad_convert_fusion, f32[384]{0:T(512)S(1)} %copy-done.21, f32[384]{0:T(512)S(1)} %copy-done.22, f32[384]{0:T(512)S(1)} %get-tuple-element.20, f32[384]{0:T(512)S(1)} %get-tuple-element.28, f32[384]{0:T(512)S(1)} %get-tuple-element.30, ...), kind=kLoop, calls=%fused_computation.139 | loop fusion | flops 19070976 | bytes 24836096 | tf_op jit(solution)/shard_map/convert_element_type | solution.py:215
  150.6 1.0 convolution_convert_fusion.1
  151.8 2.3 %collective-permute-done.22 = bf16[2,128,1536]{2,1,0:T(8,128)(2,1)S(1)} collective-permute-done((bf16[2,128,1536]{2,1,0:T(8,128)(2,1)S(1)}, bf16[2,128,1536]{2,1,0:T(8,128)(2,1)S(1)}, u32[]{:S(2)}, u32[]{:S(2)}) %collective-permute-start.22) | collective-permute-done | bytes 786464 | tf_op jit(solution)/shard_map/ppermute | solution.py:78
  155.0 10.6 %collective-permute-done.23 = bf16[128,1536]{1,0:T(8,128)(2,1)S(1)} collective-permute-done((bf16[128,1536]{1,0:T(8,128)(2,1)S(1)}, bf16[128,1536]{1,0:T(8,128)(2,1)S(1)}, u32[]{:S(2)}, u32[]{:S(2)}) %collective-permute-start.23) | collective-permute-done | bytes 393248 | tf_op jit(solution)/shard_map/ppermute | solution.py:84
  (203 shorter events, 26.6 us)
Async XLA Ops:
  0.0 6.0 %copy-start = (bf16[1,128,1536]{2,1,0:T(8,128)(2,1)S(1)}, bf16[1,128,1536]{2,1,0:T(8,128)(2,1)}, u32[]{:S(2)}) copy-start(bf16[1,128,1536]{2,1,0:T(8,128)(2,1)} %param.13) | copy-start | bytes 1179652
  0.0 6.4 %copy-start.7 = (f32[1536]{0:T(1024)S(1)}, f32[1536]{0:T(1024)}, u32[]{:S(2)}) copy-start(f32[1536]{0:T(1024)} %param.15) | copy-start | bytes 18436
  1.1 8.3 %copy-start.3 = (bf16[192,3,384]{2,0,1:T(8,128)(2,1)S(1)}, bf16[192,3,384]{2,0,1:T(8,128)(2,1)}, u32[]{:S(2)}) copy-start(bf16[192,3,384]{2,0,1:T(8,128)(2,1)} %param.17) | copy-start | bytes 1327108
  3.0 6.8 %copy-start.49 = (s32[1,4]{1,0:T(1,128)S(1)}, s32[1,4]{1,0:T(1,128)}, u32[]{:S(2)}) copy-start(s32[1,4]{1,0:T(1,128)} %param.14) | copy-start | bytes 52
  3.0 38.4 %collective-permute-start.2 = (bf16[192,1536]{1,0:T(8,128)(2,1)}, bf16[192,1536]{1,0:T(8,128)(2,1)}, u32[]{:S(2)}, u32[]{:S(2)}) collective-permute-start(bf16[192,1536]{1,0:T(8,128)(2,1)} %pad_maximum_fusion), channel_id=1, source_target_pairs={{0,8},{8,16},{16,24},{24,28},{28,20},{20,12},{12,4},{4,0},{1,9},{9... | collective-permute-start | bytes 1769480 | tf_op jit(solution)/shard_map/ppermute | solution.py:162
  6.0 37.0 %collective-permute-start.3 = (bf16[192,1536]{1,0:T(8,128)(2,1)}, bf16[192,1536]{1,0:T(8,128)(2,1)S(1)}, u32[]{:S(2)}, u32[]{:S(2)}) collective-permute-start(bf16[192,1536]{1,0:T(8,128)(2,1)} %pad_maximum_fusion), channel_id=1, source_target_pairs={{0,4},{8,0},{16,8},{24,16},{28,24},{20,28},{12,20},{4,12},{1,5},{9... | collective-permute-start | bytes 1769480 | tf_op jit(solution)/shard_map/ppermute | solution.py:165
  7.4 32.0 %collective-permute-start = (bf16[128,1536]{1,0:T(8,128)(2,1)}, bf16[128,1536]{1,0:T(8,128)(2,1)}, u32[]{:S(2)}, u32[]{:S(2)}) collective-permute-start(bf16[128,1536]{1,0:T(8,128)(2,1)} %fusion.18), channel_id=1, source_target_pairs={{0,2},{1,3},{2,0},{3,1},{4,6},{5,7},{6,4},{7,5},{8,10},{9,11},{10,... | collective-permute-start | bytes 1179656 | tf_op jit(solution)/shard_map/ppermute | solution.py:36
  9.4 2.9 %copy-start.4 = (bf16[384,192]{0,1:T(8,128)(2,1)S(1)}, bf16[384,192]{0,1:T(8,128)(2,1)}, u32[]{:S(2)}) copy-start(bf16[384,192]{0,1:T(8,128)(2,1)} %param.18) | copy-start | bytes 442372
  16.3 2.5 %copy-start.6 = (bf16[31,384]{1,0:T(8,128)(2,1)S(1)}, bf16[31,384]{1,0:T(8,128)(2,1)}, u32[]{:S(2)}) copy-start(bf16[31,384]{1,0:T(8,128)(2,1)} %param.20) | copy-start | bytes 71428
  16.3 3.2 %copy-start.50 = (s32[8]{0:T(128)S(1)}, s32[8]{0:T(128)}, u32[]{:S(2)}) copy-start(s32[8]{0:T(128)} %constant.341.clone) | copy-start | bytes 100
  16.3 7.8 %copy-start.8 = (s32[8]{0:T(128)S(1)}, s32[8]{0:T(128)}, u32[]{:S(2)}) copy-start(s32[8]{0:T(128)} %constant.342.clone) | copy-start | bytes 100
  16.3 17.1 %copy-start.5 = (bf16[192,2,384]{2,1,0:T(2,128)(2,1)S(1)}, bf16[192,2,384]{2,1,0:T(2,128)(2,1)}, u32[]{:S(2)}) copy-start(bf16[192,2,384]{2,1,0:T(2,128)(2,1)} %param.19) | copy-start | bytes 884740
  41.4 18.8 %collective-permute-start.1 = (bf16[2,128,1536]{2,1,0:T(8,128)(2,1)}, bf16[2,128,1536]{2,1,0:T(8,128)(2,1)S(1)}, u32[]{:S(2)}, u32[]{:S(2)}) collective-permute-start(bf16[2,128,1536]{2,1,0:T(8,128)(2,1)} %get-tuple-element.67), channel_id=1, source_target_pairs={{0,1},{1,0},{2,3},{3,2},{4,5},{5,4},{6,7},{7,6},{8,9},{9,8},{10,11... | collective-permute-start | bytes 2359304 | tf_op jit(solution)/shard_map/ppermute | solution.py:42
  41.4 16.0 %collective-permute-start.4 = (bf16[192,1536]{1,0:T(8,128)(2,1)}, bf16[192,1536]{1,0:T(8,128)(2,1)S(1)}, u32[]{:S(2)}, u32[]{:S(2)}) collective-permute-start(bf16[192,1536]{1,0:T(8,128)(2,1)} %collective-permute-done.2), channel_id=1, source_target_pairs={{0,8},{8,16},{16,24},{24,28},{28,20},{20,12},{12,4},{4,0},{1,9},{9... | collective-permute-start | bytes 1769480 | tf_op jit(solution)/shard_map/ppermute | solution.py:162
  43.0 15.9 %collective-permute-start.5 = (bf16[192,1536]{1,0:T(8,128)(2,1)S(1)}, bf16[192,1536]{1,0:T(8,128)(2,1)S(1)}, u32[]{:S(2)}, u32[]{:S(2)}) collective-permute-start(bf16[192,1536]{1,0:T(8,128)(2,1)S(1)} %collective-permute-done.3), channel_id=1, source_target_pairs={{0,4},{8,0},{16,8},{24,16},{28,24},{20,28},{12,20},{4,12},{1,5},{9... | collective-permute-start | bytes 1769480 | tf_op jit(solution)/shard_map/ppermute | solution.py:165
  57.3 14.9 %collective-permute-start.6 = (bf16[192,1536]{1,0:T(8,128)(2,1)S(1)}, bf16[192,1536]{1,0:T(8,128)(2,1)S(1)}, u32[]{:S(2)}, u32[]{:S(2)}) collective-permute-start(bf16[192,1536]{1,0:T(8,128)(2,1)S(1)} %collective-permute-done.4), channel_id=1, source_target_pairs={{0,8},{8,16},{16,24},{24,28},{28,20},{20,12},{12,4},{4,0},{1,9},{9... | collective-permute-start | bytes 1769480 | tf_op jit(solution)/shard_map/ppermute | solution.py:162
  58.9 15.0 %collective-permute-start.7 = (bf16[192,1536]{1,0:T(8,128)(2,1)S(1)}, bf16[192,1536]{1,0:T(8,128)(2,1)S(1)}, u32[]{:S(2)}, u32[]{:S(2)}) collective-permute-start(bf16[192,1536]{1,0:T(8,128)(2,1)S(1)} %collective-permute-done.5), channel_id=1, source_target_pairs={{0,4},{8,0},{16,8},{24,16},{28,24},{20,28},{12,20},{4,12},{1,5},{9... | collective-permute-start | bytes 1769480 | tf_op jit(solution)/shard_map/ppermute | solution.py:165
  72.3 7.8 %collective-permute-start.8 = (bf16[96,1536]{1,0:T(8,128)(2,1)S(1)}, bf16[96,1536]{1,0:T(8,128)(2,1)S(1)}, u32[]{:S(2)}, u32[]{:S(2)}) collective-permute-start(bf16[96,1536]{1,0:T(8,128)(2,1)S(1)} %slice.568), channel_id=1, source_target_pairs={{0,8},{8,16},{16,24},{24,28},{28,20},{20,12},{12,4},{4,0},{1,9},{9... | collective-permute-start | bytes 884744 | tf_op jit(solution)/shard_map/ppermute | solution.py:151
  73.9 7.5 %collective-permute-start.9 = (bf16[96,1536]{1,0:T(8,128)(2,1)S(1)}, bf16[96,1536]{1,0:T(8,128)(2,1)S(1)}, u32[]{:S(2)}, u32[]{:S(2)}) collective-permute-start(bf16[96,1536]{1,0:T(8,128)(2,1)S(1)} %slice.570), channel_id=1, source_target_pairs={{0,4},{8,0},{16,8},{24,16},{28,24},{20,28},{12,20},{4,12},{1,5},{9... | collective-permute-start | bytes 884744 | tf_op jit(solution)/shard_map/ppermute | solution.py:152
  81.5 18.7 %collective-permute-start.14 = (bf16[192,1152]{1,0:T(8,128)(2,1)S(1)}, bf16[192,1152]{1,0:T(8,128)(2,1)}, u32[]{:S(2)}, u32[]{:S(2)}) collective-permute-start(bf16[192,1152]{1,0:T(8,128)(2,1)S(1)} %pad_maximum_fusion.1), channel_id=1, source_target_pairs={{0,8},{8,16},{16,24},{24,28},{28,20},{20,12},{12,4},{4,0},{1,9},{9... | collective-permute-start | bytes 1327112 | tf_op jit(solution)/shard_map/ppermute | solution.py:162
  83.1 18.7 %collective-permute-start.15 = (bf16[192,1152]{1,0:T(8,128)(2,1)S(1)}, bf16[192,1152]{1,0:T(8,128)(2,1)}, u32[]{:S(2)}, u32[]{:S(2)}) collective-permute-start(bf16[192,1152]{1,0:T(8,128)(2,1)S(1)} %pad_maximum_fusion.1), channel_id=1, source_target_pairs={{0,4},{8,0},{16,8},{24,16},{28,24},{20,28},{12,20},{4,12},{1,5},{9... | collective-permute-start | bytes 1327112 | tf_op jit(solution)/shard_map/ppermute | solution.py:165
  99.7 6.4 %collective-permute-start.10 = (bf16[2,128,1536]{2,1,0:T(8,128)(2,1)S(1)}, bf16[2,128,1536]{2,1,0:T(8,128)(2,1)S(1)}, u32[]{:S(2)}, u32[]{:S(2)}) collective-permute-start(bf16[2,128,1536]{2,1,0:T(8,128)(2,1)S(1)} %dynamic-slice_bitcast_fusion.1), channel_id=1, source_target_pairs={{0,1},{1,0},{2,3},{3,2},{4,5},{5,4},{6,7},{7,6},{8,9},{9,8},{10,11... | collective-permute-start | bytes 2359304 | tf_op jit(solution)/shard_map/ppermute | solution.py:78
  100.1 12.8 %collective-permute-start.16 = (bf16[192,1152]{1,0:T(8,128)(2,1)}, bf16[192,1152]{1,0:T(8,128)(2,1)S(1)}, u32[]{:S(2)}, u32[]{:S(2)}) collective-permute-start(bf16[192,1152]{1,0:T(8,128)(2,1)} %collective-permute-done.14), channel_id=1, source_target_pairs={{0,8},{8,16},{16,24},{24,28},{28,20},{20,12},{12,4},{4,0},{1,9},{9... | collective-permute-start | bytes 1327112 | tf_op jit(solution)/shard_map/ppermute | solution.py:162
  101.7 12.8 %collective-permute-start.17 = (bf16[192,1152]{1,0:T(8,128)(2,1)}, bf16[192,1152]{1,0:T(8,128)(2,1)S(1)}, u32[]{:S(2)}, u32[]{:S(2)}) collective-permute-start(bf16[192,1152]{1,0:T(8,128)(2,1)} %collective-permute-done.15), channel_id=1, source_target_pairs={{0,4},{8,0},{16,8},{24,16},{28,24},{20,28},{12,20},{4,12},{1,5},{9... | collective-permute-start | bytes 1327112 | tf_op jit(solution)/shard_map/ppermute | solution.py:165
  106.4 11.0 %collective-permute-start.11 = (bf16[128,1536]{1,0:T(8,128)(2,1)S(1)}, bf16[128,1536]{1,0:T(8,128)(2,1)S(1)}, u32[]{:S(2)}, u32[]{:S(2)}) collective-permute-start(bf16[128,1536]{1,0:T(8,128)(2,1)S(1)} %fusion.98), channel_id=1, source_target_pairs={{0,2},{1,3},{2,0},{3,1},{4,6},{5,7},{6,4},{7,5},{8,10},{9,11},{10,... | collective-permute-start | bytes 1179656 | tf_op jit(solution)/shard_map/ppermute | solution.py:84
  113.0 11.8 %collective-permute-start.18 = (bf16[192,1152]{1,0:T(8,128)(2,1)S(1)}, bf16[192,1152]{1,0:T(8,128)(2,1)S(1)}, u32[]{:S(2)}, u32[]{:S(2)}) collective-permute-start(bf16[192,1152]{1,0:T(8,128)(2,1)S(1)} %collective-permute-done.16), channel_id=1, source_target_pairs={{0,8},{8,16},{16,24},{24,28},{28,20},{20,12},{12,4},{4,0},{1,9},{9... | collective-permute-start | bytes 1327112 | tf_op jit(solution)/shard_map/ppermute | solution.py:162
  114.6 11.8 %collective-permute-start.19 = (bf16[192,1152]{1,0:T(8,128)(2,1)S(1)}, bf16[192,1152]{1,0:T(8,128)(2,1)S(1)}, u32[]{:S(2)}, u32[]{:S(2)}) collective-permute-start(bf16[192,1152]{1,0:T(8,128)(2,1)S(1)} %collective-permute-done.17), channel_id=1, source_target_pairs={{0,4},{8,0},{16,8},{24,16},{28,24},{20,28},{12,20},{4,12},{1,5},{9... | collective-permute-start | bytes 1327112 | tf_op jit(solution)/shard_map/ppermute | solution.py:165
  115.4 3.5 %copy-start.9 = (f32[1536]{0:T(1024)S(1)}, f32[1536]{0:T(1024)}, u32[]{:S(2)}) copy-start(f32[1536]{0:T(1024)} %param.16) | copy-start | bytes 18436
  119.9 10.1 %collective-permute-start.12 = (bf16[128,1536]{1,0:T(8,128)(2,1)S(1)}, bf16[128,1536]{1,0:T(8,128)(2,1)S(1)}, u32[]{:S(2)}, u32[]{:S(2)}) collective-permute-start(bf16[128,1536]{1,0:T(8,128)(2,1)S(1)} %get-tuple-element.60), channel_id=1, source_target_pairs={{0,2},{1,3},{2,0},{3,1},{4,6},{5,7},{6,4},{7,5},{8,10},{9,11},{10,... | collective-permute-start | bytes 1179656 | tf_op jit(solution)/shard_map/ppermute | solution.py:36
  124.8 6.2 %collective-permute-start.20 = (bf16[96,1152]{1,0:T(8,128)(2,1)S(1)}, bf16[96,1152]{1,0:T(8,128)(2,1)S(1)}, u32[]{:S(2)}, u32[]{:S(2)}) collective-permute-start(bf16[96,1152]{1,0:T(8,128)(2,1)S(1)} %slice.591), channel_id=1, source_target_pairs={{0,8},{8,16},{16,24},{24,28},{28,20},{20,12},{12,4},{4,0},{1,9},{9... | collective-permute-start | bytes 663560 | tf_op jit(solution)/shard_map/ppermute | solution.py:151
  126.4 6.0 %collective-permute-start.21 = (bf16[96,1152]{1,0:T(8,128)(2,1)S(1)}, bf16[96,1152]{1,0:T(8,128)(2,1)S(1)}, u32[]{:S(2)}, u32[]{:S(2)}) collective-permute-start(bf16[96,1152]{1,0:T(8,128)(2,1)S(1)} %slice.593), channel_id=1, source_target_pairs={{0,4},{8,0},{16,8},{24,16},{28,24},{20,28},{12,20},{4,12},{1,5},{9... | collective-permute-start | bytes 663560 | tf_op jit(solution)/shard_map/ppermute | solution.py:152
  127.0 5.4 %copy-start.1 = (bf16[8,192,384]{2,1,0:T(8,128)(2,1)}, bf16[8,192,384]{2,1,0:T(8,128)(2,1)S(1)}, u32[]{:S(2)}) copy-start(bf16[8,192,384]{2,1,0:T(8,128)(2,1)S(1)} %fusion.111) | copy-start | bytes 3538948
  130.9 5.2 %collective-permute-start.13 = (bf16[2,128,1536]{2,1,0:T(8,128)(2,1)}, bf16[2,128,1536]{2,1,0:T(8,128)(2,1)}, u32[]{:S(2)}, u32[]{:S(2)}) collective-permute-start(bf16[2,128,1536]{2,1,0:T(8,128)(2,1)} %get-tuple-element.65), channel_id=1, source_target_pairs={{0,1},{1,0},{2,3},{3,2},{4,5},{5,4},{6,7},{7,6},{8,9},{9,8},{10,11... | collective-permute-start | bytes 2359304 | tf_op jit(solution)/shard_map/ppermute | solution.py:42
  143.2 0.7 copy-start.10
  143.3 0.7 copy-start.11
  143.3 0.7 copy-start.12
  143.3 0.7 copy-start.13
  143.3 0.7 copy-start.14
  143.3 0.7 copy-start.15
  143.3 0.7 copy-start.16
  143.3 0.7 copy-start.17
  143.3 0.7 copy-start.18
  143.3 0.7 copy-start.19
  143.3 0.7 copy-start.20
  143.4 0.7 copy-start.21
  144.3 6.3 %copy-start.2 = (bf16[8,192,384]{2,1,0:T(8,128)(2,1)S(1)}, bf16[8,192,384]{2,1,0:T(8,128)(2,1)}, u32[]{:S(2)}) copy-start(bf16[8,192,384]{2,1,0:T(8,128)(2,1)} %fusion.125) | copy-start | bytes 3538948
  151.7 2.4 %collective-permute-start.22 = (bf16[2,128,1536]{2,1,0:T(8,128)(2,1)S(1)}, bf16[2,128,1536]{2,1,0:T(8,128)(2,1)S(1)}, u32[]{:S(2)}, u32[]{:S(2)}) collective-permute-start(bf16[2,128,1536]{2,1,0:T(8,128)(2,1)S(1)} %dynamic-slice_bitcast_fusion), channel_id=1, source_target_pairs={{0,1},{1,0},{2,3},{3,2},{4,5},{5,4},{6,7},{7,6},{8,9},{9,8},{10,11... | collective-permute-start | bytes 2359304 | tf_op jit(solution)/shard_map/ppermute | solution.py:78
  154.3 11.2 %collective-permute-start.23 = (bf16[128,1536]{1,0:T(8,128)(2,1)S(1)}, bf16[128,1536]{1,0:T(8,128)(2,1)S(1)}, u32[]{:S(2)}, u32[]{:S(2)}) collective-permute-start(bf16[128,1536]{1,0:T(8,128)(2,1)S(1)} %fusion.99), channel_id=1, source_target_pairs={{0,2},{1,3},{2,0},{3,1},{4,6},{5,7},{6,4},{7,5},{8,10},{9,11},{10,... | collective-permute-start | bytes 1179656 | tf_op jit(solution)/shard_map/ppermute | solution.py:84
  (27 other events, 19.0 us)

commit v15 on v12

--- a/solution.py
+++ b/solution.py
@@ -230,10 +230,13 @@
     out_cols = out_parts.reshape(model_width, w_out.shape[0])
     glu_rows = w_glu.shape[0]
     glu_local = w_glu.reshape(glu_rows, 2 * group_width)
-    glu_parts, proj_parts = ring_gather(
-        after(out_parts, jnp.concatenate([glu_local, w_proj.T], axis=1)), ring, [2 * group_width]
-    )
-    glu_matrix = glu_parts.reshape(model_width, 2 * group_width)
+    value_parts, gate_parts, proj_parts = ring_gather(
+        after(out_parts, jnp.concatenate([glu_local, w_proj.T], axis=1)),
+        ring,
+        [group_width, 2 * group_width],
+    )
+    value_matrix = value_parts.reshape(model_width, group_width)
+    gate_matrix = gate_parts.reshape(model_width, group_width)
     proj_cols = proj_parts.reshape(model_width, w_proj.shape[0])
     inputs = frames[0].astype(jnp.float32)
     record_ends = jnp.cumsum(lengths[0])
@@ -252,10 +255,9 @@
     middle = (inputs + attn_sum).astype(jnp.bfloat16)
     normed2 = layer_norm(middle.astype(jnp.float32), ln2_gain)
     shard_piece = seq_gather(normed2, paired).reshape(group_rows, model_width)
-    glu_pair = jnp.dot(shard_piece, glu_matrix, preferred_element_type=jnp.float32).reshape(
-        shard_piece.shape[0], 2, group_width
-    )
-    gated = (glu_pair[:, 0] * jax.nn.sigmoid(glu_pair[:, 1])).astype(jnp.bfloat16)
+    glu_value = jnp.dot(shard_piece, value_matrix, preferred_element_type=jnp.float32)
+    glu_gate = jnp.dot(shard_piece, gate_matrix, preferred_element_type=jnp.float32)
+    gated = (glu_value * jax.nn.sigmoid(glu_gate)).astype(jnp.bfloat16)
     padded = jnp.pad(gated, ((kernel_reach, kernel_reach), (0, 0)))
     near_positions = jnp.arange(-kernel_reach, group_rows + kernel_reach, dtype=jnp.int32)
     activated = depthwise(

time: 167 us -> 159 us (0.952)
  local copies, waits for them, and re-layouts: 38.3 us -> 26.8 us
  waiting for transfers between devices: 52.7 us -> 57 us
    ppermute x6, waiting for transfers between devices: 28.1 us -> 33 us  [ring_gather(): ahead = lax.ppermute(ahead, 'dp', forward)]
    ppermute x2, waiting for transfers between devices: 3.98 us -> 7.7 us  [ring_gather(): front = lax.ppermute(ahead[:rows], 'dp', forward)]
    dynamic_update_slice x4, local copies, waits for them, and re-layouts: 5.09 us -> 1.62 us  [seq_gather(): out = lax.dynamic_update_index_in_dim(out, other[k], 2 * k + partner % 2, 0)]
    ppermute x2, waiting for transfers between devices: 2.93 us -> 0.01 us  [seq_gather(): lax.ppermute(block, 'seq', [(i, (i + 2 * shift) % count) for i in range(c...]
    another operation x6 -> x8, local copies, waits for them, and re-layouts: 4.68 us -> 1.93 us
    dot_general x1 -> x0, local copies, waits for them, and re-layouts: 2.44 us -> none  [on_device(): jnp.dot(shard_piece, glu_matrix, preferred_element_type=jnp.float32)]
    dot_general x1 -> x2, matrix products: 3.56 us -> 2.04 us  [the longest x1 1.06 us: on_device(): jnp.dot(shard_piece, gate_matrix, preferred_element_type=jnp.float32)]
    dynamic_update_slice x28 -> x23, local copies, waits for them, and re-layouts: 11.9 us -> 12.4 us  [place(): lax.dynamic_update_index_in_dim(out, piece[..., lo:hi], where, 0)]
  transfers between devices with their start and end apart: 24 -> 24, of which waited for: 11 -> 11; matrix products, arithmetic and copies ran while one was open for 33% -> 29% of each run, Pallas kernels for 0% -> 0%
where the time goes in v15:
time: 159 us; the launch traced here: 158 us
  waiting for transfers between devices  57 us (36%)
  local copies, waits for them, and re-layouts  26.8 us (17%)
  starting transfers between devices  21.5 us (14%)
  between operations  19 us (12%)
  other arithmetic  17.3 us (11%)
  matrix products  16.1 us (10%)
    ppermute x6, waiting for transfers between devices, ring_gather(): ahead = lax.ppermute(ahead, 'dp', forward)  33 us
    dynamic_update_slice x23, local copies, waits for them, and re-layouts, place(): lax.dynamic_update_index_in_dim(out, piece[..., lo:hi], where, 0)  12.4 us
    ppermute x2, waiting for transfers between devices, seq_scatter_sum(): lax.ppermute(piece.astype(jnp.bfloat16), 'seq', [(i, (i + 2 * shift) % co...  11.3 us
    ppermute x6, starting transfers between devices, ring_gather(): ahead = lax.ppermute(ahead, 'dp', forward)  11 us
    ppermute x2, waiting for transfers between devices, ring_gather(): front = lax.ppermute(ahead[:rows], 'dp', forward)  7.7 us
    convert_element_type x1, other arithmetic, depthwise(): return jax.nn.silu(total_acc).astype(jnp.bfloat16)  6.67 us
    dot_general x1, matrix products, on_device(): jnp.dot(seq_gather(normed1, paired).reshape(group_rows, model_width), qkv...  5.73 us
    sub x1, matrix products, one_block(): weights = jnp.exp(scores - top_score)  3.65 us
  transfers between devices with their start and end apart: 24, of which 11 were waited for; matrix products, arithmetic and copies ran while one was open for 29% of the time, Pallas kernels for 0%

profile of v15, /device:TPU:0, one launch (start us, length us, event | category | flops | bytes accessed | tf_op | source)
XLA Modules:
  0.0 157.8 jit_solution(15438574973242520822)
XLA Ops:
  0.0 1.1 copy.35
  1.1 1.8 %pad_maximum_fusion = bf16[192,1536]{1,0:T(8,128)(2,1)} fusion(bf16[192,384]{1,0:T(8,128)(2,1)} %bitcast.313, bf16[192,1152]{1,0:T(8,128)(2,1)S(1)} %bitcast.304), kind=kLoop, calls=%fused_computation.51 | loop fusion | flops 1179648 | bytes 1179648 | tf_op jit(solution)/shard_map/concatenate | solution.py:227
  3.0 3.0 %collective-permute-start.2 = (bf16[192,1536]{1,0:T(8,128)(2,1)}, bf16[192,1536]{1,0:T(8,128)(2,1)}, u32[]{:S(2)}, u32[]{:S(2)}) collective-permute-start(bf16[192,1536]{1,0:T(8,128)(2,1)} %pad_maximum_fusion), channel_id=1, source_target_pairs={{0,8},{8,16},{16,24},{24,28},{28,20},{20,12},{12,4},{4,0},{1,9},{9... | collective-permute-start | bytes 1769480 | tf_op jit(solution)/shard_map/ppermute | solution.py:162
  6.7 2.0 %collective-permute-start = (bf16[128,1536]{1,0:T(8,128)(2,1)S(1)}, bf16[128,1536]{1,0:T(8,128)(2,1)}, u32[]{:S(2)}, u32[]{:S(2)}) collective-permute-start(bf16[128,1536]{1,0:T(8,128)(2,1)S(1)} %fusion.22), channel_id=1, source_target_pairs={{0,2},{1,3},{2,0},{3,1},{4,6},{5,7},{6,4},{7,5},{8,10},{9,11},{10,... | collective-permute-start | bytes 1179656 | tf_op jit(solution)/shard_map/ppermute | solution.py:36
  9.4 0.9 broadcast_compare_fusion
  12.4 2.2 %broadcast_in_dim.455 = bf16[8,192,1152]{2,1,0:T(8,128)(2,1)} broadcast(bf16[]{:T(256)} %constant.322.clone.1), dimensions={} | broadcast | bytes 3538946 | tf_op jit(solution)/shard_map/broadcast_in_dim | solution.py:136
  14.6 0.8 constant_dynamic-update-slice_fusion
  15.5 1.3 broadcast.148.clone
  16.8 1.0 constant_dynamic-update-slice_fusion.1
  37.7 0.9 pad_maximum_fusion.1
  39.3 1.8 %bitcast_dynamic-update-slice_fusion.4 = (bf16[2,128,1536]{2,1,0:T(8,128)(2,1)S(1)}, bf16[4,128,1536]{2,1,0:T(8,128)(2,1)}) fusion(bf16[2,128,1536]{2,1,0:T(8,128)(2,1)S(1)} %get-tuple-element.81, s32[]{:T(128)S(6)} %select_n.366, bf16[128,1536]{1,0:T(8,128)(2,1)} %collective-permute-done, bf16[4,128,1536]{2,1,0:T(8,128)(2,1)} %get-tuple-element.82, ...), kind=kLoop, calls=%fused_computation.81 | loop fusion | bytes 1179656 | tf_op jit(solution)/shard_map/jit(dynamic_update_index_in_dim)/dynamic_update_slice | solution.py:40
  41.1 1.6 %collective-permute-start.4 = (bf16[192,1536]{1,0:T(8,128)(2,1)}, bf16[192,1536]{1,0:T(8,128)(2,1)S(1)}, u32[]{:S(2)}, u32[]{:S(2)}) collective-permute-start(bf16[192,1536]{1,0:T(8,128)(2,1)} %collective-permute-done.2), channel_id=1, source_target_pairs={{0,8},{8,16},{16,24},{24,28},{28,20},{20,12},{12,4},{4,0},{1,9},{9... | collective-permute-start | bytes 1769480 | tf_op jit(solution)/shard_map/ppermute | solution.py:162
  43.1 1.8 %fusion.33 = bf16[8,192,1152]{2,1,0:T(8,128)(2,1)} fusion(bf16[8,192,1152]{2,1,0:T(8,128)(2,1)} %constant_dynamic-update-slice_fusion, s32[]{:T(128)S(6)} %select_n.373, bf16[192,1536]{1,0:T(8,128)(2,1)} %collective-permute-done.2), kind=kLoop, calls=%fused_computation.64 | loop fusion | bytes 884740 | tf_op jit(solution)/shard_map/jit(dynamic_update_index_in_dim)/dynamic_update_slice | solution.py:140
  45.0 1.8 %fusion.32 = bf16[8,192,1152]{2,1,0:T(8,128)(2,1)} fusion(bf16[8,192,1152]{2,1,0:T(8,128)(2,1)} %fusion.33, s32[]{:T(128)S(6)} %select_n.376, bf16[192,1536]{1,0:T(8,128)(2,1)} %collective-permute-done.3), kind=kLoop, calls=%fused_computation.62 | loop fusion | bytes 884740 | tf_op jit(solution)/shard_map/jit(dynamic_update_index_in_dim)/dynamic_update_slice | solution.py:140
  46.8 0.9 fusion.65
  47.7 0.9 fusion.64
  48.7 8.4 %collective-permute-done.4 = bf16[192,1536]{1,0:T(8,128)(2,1)S(1)} collective-permute-done((bf16[192,1536]{1,0:T(8,128)(2,1)}, bf16[192,1536]{1,0:T(8,128)(2,1)S(1)}, u32[]{:S(2)}, u32[]{:S(2)}) %collective-permute-start.4) | collective-permute-done | bytes 589856 | tf_op jit(solution)/shard_map/ppermute | solution.py:162
  57.1 1.6 %collective-permute-start.6 = (bf16[192,1536]{1,0:T(8,128)(2,1)S(1)}, bf16[192,1536]{1,0:T(8,128)(2,1)S(1)}, u32[]{:S(2)}, u32[]{:S(2)}) collective-permute-start(bf16[192,1536]{1,0:T(8,128)(2,1)S(1)} %collective-permute-done.4), channel_id=1, source_target_pairs={{0,8},{8,16},{16,24},{24,28},{28,20},{20,12},{12,4},{4,0},{1,9},{9... | collective-permute-start | bytes 1769480 | tf_op jit(solution)/shard_map/ppermute | solution.py:162
  59.1 0.8 fusion.31
  61.5 0.8 fusion.30
  62.3 9.7 %collective-permute-done.6 = bf16[192,1536]{1,0:T(8,128)(2,1)S(1)} collective-permute-done((bf16[192,1536]{1,0:T(8,128)(2,1)S(1)}, bf16[192,1536]{1,0:T(8,128)(2,1)S(1)}, u32[]{:S(2)}, u32[]{:S(2)}) %collective-permute-start.6) | collective-permute-done | bytes 589856 | tf_op jit(solution)/shard_map/ppermute | solution.py:162
  72.0 1.6 %collective-permute-start.8 = (bf16[96,1536]{1,0:T(8,128)(2,1)S(1)}, bf16[96,1536]{1,0:T(8,128)(2,1)S(1)}, u32[]{:S(2)}, u32[]{:S(2)}) collective-permute-start(bf16[96,1536]{1,0:T(8,128)(2,1)S(1)} %slice.593), channel_id=1, source_target_pairs={{0,8},{8,16},{16,24},{24,28},{28,20},{20,12},{12,4},{4,0},{1,9},{9... | collective-permute-start | bytes 884744 | tf_op jit(solution)/shard_map/ppermute | solution.py:151
  74.2 0.8 fusion.29
  75.0 0.8 fusion.28
  75.9 4.0 %collective-permute-done.8 = bf16[96,1536]{1,0:T(8,128)(2,1)S(1)} collective-permute-done((bf16[96,1536]{1,0:T(8,128)(2,1)S(1)}, bf16[96,1536]{1,0:T(8,128)(2,1)S(1)}, u32[]{:S(2)}, u32[]{:S(2)}) %collective-permute-start.8) | collective-permute-done | bytes 294944 | tf_op jit(solution)/shard_map/ppermute | solution.py:151
  79.9 1.4 collective-permute-done.9
  81.2 1.6 %collective-permute-start.14 = (bf16[192,1152]{1,0:T(8,128)(2,1)S(1)}, bf16[192,1152]{1,0:T(8,128)(2,1)}, u32[]{:S(2)}, u32[]{:S(2)}) collective-permute-start(bf16[192,1152]{1,0:T(8,128)(2,1)S(1)} %pad_maximum_fusion.1), channel_id=1, source_target_pairs={{0,8},{8,16},{16,24},{24,28},{28,20},{20,12},{12,4},{4,0},{1,9},{9... | collective-permute-start | bytes 1327112 | tf_op jit(solution)/shard_map/ppermute | solution.py:162
  84.7 5.7 %convolution_convert_fusion = bf16[512,1152]{1,0:T(8,128)(2,1)} fusion(bf16[512,1536]{1,0:T(8,128)(2,1)} %bitcast.2, bf16[1536,1152]{1,0:T(8,128)(2,1)} %bitcast.26), kind=kOutput, calls=%fused_computation.5 | convolution fusion | flops 1812529152 | bytes 6291456 | tf_op jit(solution)/shard_map/dot_general | solution.py:246
  90.5 1.6 %copy.28 = bf16[512,1152]{0,1:T(8,128)(2,1)S(1)} copy(bf16[512,1152]{1,0:T(8,128)(2,1)} %convolution_convert_fusion) | data formatting | bytes 2359296 | tf_op jit(solution)/shard_map/convert_element_type | solution.py:247
  92.1 3.6 %fusion.79 = (f32[4,512]{1,0:T(4,128)S(1)}, f32[4,512,512]{1,2,0:T(8,128)}) fusion(pred[512,512]{0,1:T(8,128)(4,1)S(1)} %copy-done.4, bf16[512,3,4,96]{0,3,2,1:T(8,128)(2,1)S(1)} %bitcast.309), kind=kOutput, calls=%fused_computation.237 | convolution fusion | flops 205521408 | bytes 5251072 | tf_op jit(solution)/shard_map/while/body/eval_jaxpr/sub | solution.py:194
  95.7 2.7 %fusion.10 = bf16[4,96,512]{2,1,0:T(8,128)(2,1)S(1)} fusion(f32[4,512,512]{1,2,0:T(8,128)} %get-tuple-element.132, f32[4,512]{1,0:T(4,128)S(1)} %get-tuple-element.131, bf16[512,3,4,96]{0,3,2,1:T(8,128)(2,1)S(1)} %bitcast.310), kind=kOutput, calls=%fused_computation.20 | convolution fusion | flops 203620352 | bytes 4988928 | tf_op jit(solution)/shard_map/while/body/eval_jaxpr/hqk,khe->qhe/dot_general | solution.py:196
  98.4 1.0 convolution_convert_fusion.2
  100.1 1.6 %collective-permute-start.16 = (bf16[192,1152]{1,0:T(8,128)(2,1)}, bf16[192,1152]{1,0:T(8,128)(2,1)S(1)}, u32[]{:S(2)}, u32[]{:S(2)}) collective-permute-start(bf16[192,1152]{1,0:T(8,128)(2,1)} %collective-permute-done.14), channel_id=1, source_target_pairs={{0,8},{8,16},{16,24},{24,28},{28,20},{20,12},{12,4},{4,0},{1,9},{9... | collective-permute-start | bytes 1327112 | tf_op jit(solution)/shard_map/ppermute | solution.py:162
  102.1 1.1 fusion.47
  103.3 1.1 fusion.46
  105.3 7.6 %collective-permute-done.16 = bf16[192,1152]{1,0:T(8,128)(2,1)S(1)} collective-permute-done((bf16[192,1152]{1,0:T(8,128)(2,1)}, bf16[192,1152]{1,0:T(8,128)(2,1)S(1)}, u32[]{:S(2)}, u32[]{:S(2)}) %collective-permute-start.16) | collective-permute-done | bytes 442400 | tf_op jit(solution)/shard_map/ppermute | solution.py:162
  112.9 1.6 collective-permute-start.18
  117.4 7.3 %collective-permute-done.18 = bf16[192,1152]{1,0:T(8,128)(2,1)S(1)} collective-permute-done((bf16[192,1152]{1,0:T(8,128)(2,1)S(1)}, bf16[192,1152]{1,0:T(8,128)(2,1)S(1)}, u32[]{:S(2)}, u32[]{:S(2)}) %collective-permute-start.18) | collective-permute-done | bytes 442400 | tf_op jit(solution)/shard_map/ppermute | solution.py:162
  124.7 1.6 %collective-permute-start.20 = (bf16[96,1152]{1,0:T(8,128)(2,1)S(1)}, bf16[96,1152]{1,0:T(8,128)(2,1)S(1)}, u32[]{:S(2)}, u32[]{:S(2)}) collective-permute-start(bf16[96,1152]{1,0:T(8,128)(2,1)S(1)} %slice.616), channel_id=1, source_target_pairs={{0,8},{8,16},{16,24},{24,28},{28,20},{20,12},{12,4},{4,0},{1,9},{9... | collective-permute-start | bytes 663560 | tf_op jit(solution)/shard_map/ppermute | solution.py:151
  127.2 3.7 %collective-permute-done.20 = bf16[96,1152]{1,0:T(8,128)(2,1)S(1)} collective-permute-done((bf16[96,1152]{1,0:T(8,128)(2,1)S(1)}, bf16[96,1152]{1,0:T(8,128)(2,1)S(1)}, u32[]{:S(2)}, u32[]{:S(2)}) %collective-permute-start.20) | collective-permute-done | bytes 221216 | tf_op jit(solution)/shard_map/ppermute | solution.py:151
  130.9 1.4 collective-permute-done.21
  132.5 1.1 fusion.8
  133.9 1.0 fusion.9
  135.3 6.7 %multiply_convert_fusion = bf16[512,384]{1,0:T(8,128)(2,1)S(1)} fusion(bf16[512,384]{1,0:T(8,128)(2,1)S(1)} %fusion.9, f32[384]{0:T(512)S(1)} %copy-done.28, f32[384]{0:T(512)S(1)} %copy-done.29, f32[384]{0:T(512)S(1)} %get-tuple-element.20, f32[384]{0:T(512)S(1)} %get-tuple-element.28, f32[384]{0:T(512)S(1)} %get-tuple-element.30, ...), kind=kLoop, calls=%fused_computation.48 | loop fusion | flops 25165824 | bytes 849920 | tf_op jit(solution)/shard_map/convert_element_type | solution.py:215
  142.0 1.0 convolution_convert_fusion.1
  143.2 2.3 %collective-permute-done.22 = bf16[2,128,1536]{2,1,0:T(8,128)(2,1)S(1)} collective-permute-done((bf16[2,128,1536]{2,1,0:T(8,128)(2,1)S(1)}, bf16[2,128,1536]{2,1,0:T(8,128)(2,1)S(1)}, u32[]{:S(2)}, u32[]{:S(2)}) %collective-permute-start.22) | collective-permute-done | bytes 786464 | tf_op jit(solution)/shard_map/ppermute | solution.py:78
  146.3 10.6 %collective-permute-done.23 = bf16[128,1536]{1,0:T(8,128)(2,1)S(1)} collective-permute-done((bf16[128,1536]{1,0:T(8,128)(2,1)S(1)}, bf16[128,1536]{1,0:T(8,128)(2,1)S(1)}, u32[]{:S(2)}, u32[]{:S(2)}) %collective-permute-start.23) | collective-permute-done | bytes 393248 | tf_op jit(solution)/shard_map/ppermute | solution.py:84
  156.9 0.9 fusion.38
  (195 shorter events, 18.0 us)
Async XLA Ops:
  0.0 6.0 %copy-start = (bf16[1,128,1536]{2,1,0:T(8,128)(2,1)S(1)}, bf16[1,128,1536]{2,1,0:T(8,128)(2,1)}, u32[]{:S(2)}) copy-start(bf16[1,128,1536]{2,1,0:T(8,128)(2,1)} %param.13) | copy-start | bytes 1179652
  1.1 5.3 %copy-start.6 = (f32[1536]{0:T(1024)S(1)}, f32[1536]{0:T(1024)}, u32[]{:S(2)}) copy-start(f32[1536]{0:T(1024)} %param.15) | copy-start | bytes 18436
  1.1 7.6 %copy-start.1 = (bf16[192,3,384]{2,0,1:T(8,128)(2,1)S(1)}, bf16[192,3,384]{2,0,1:T(8,128)(2,1)}, u32[]{:S(2)}) copy-start(bf16[192,3,384]{2,0,1:T(8,128)(2,1)} %param.17) | copy-start | bytes 1327108
  3.0 38.1 %collective-permute-start.2 = (bf16[192,1536]{1,0:T(8,128)(2,1)}, bf16[192,1536]{1,0:T(8,128)(2,1)}, u32[]{:S(2)}, u32[]{:S(2)}) collective-permute-start(bf16[192,1536]{1,0:T(8,128)(2,1)} %pad_maximum_fusion), channel_id=1, source_target_pairs={{0,8},{8,16},{16,24},{24,28},{28,20},{20,12},{12,4},{4,0},{1,9},{9... | collective-permute-start | bytes 1769480 | tf_op jit(solution)/shard_map/ppermute | solution.py:162
  6.0 36.7 %collective-permute-start.3 = (bf16[192,1536]{1,0:T(8,128)(2,1)}, bf16[192,1536]{1,0:T(8,128)(2,1)}, u32[]{:S(2)}, u32[]{:S(2)}) collective-permute-start(bf16[192,1536]{1,0:T(8,128)(2,1)} %pad_maximum_fusion), channel_id=1, source_target_pairs={{0,4},{8,0},{16,8},{24,16},{28,24},{20,28},{12,20},{4,12},{1,5},{9... | collective-permute-start | bytes 1769480 | tf_op jit(solution)/shard_map/ppermute | solution.py:165
  6.1 3.0 %copy-start.49 = (s32[1,4]{1,0:T(1,128)S(1)}, s32[1,4]{1,0:T(1,128)}, u32[]{:S(2)}) copy-start(s32[1,4]{1,0:T(1,128)} %param.14) | copy-start | bytes 52
  6.7 32.6 %collective-permute-start = (bf16[128,1536]{1,0:T(8,128)(2,1)S(1)}, bf16[128,1536]{1,0:T(8,128)(2,1)}, u32[]{:S(2)}, u32[]{:S(2)}) collective-permute-start(bf16[128,1536]{1,0:T(8,128)(2,1)S(1)} %fusion.22), channel_id=1, source_target_pairs={{0,2},{1,3},{2,0},{3,1},{4,6},{5,7},{6,4},{7,5},{8,10},{9,11},{10,... | collective-permute-start | bytes 1179656 | tf_op jit(solution)/shard_map/ppermute | solution.py:36
  10.3 2.0 %copy-start.2 = (bf16[384,192]{0,1:T(8,128)(2,1)S(1)}, bf16[384,192]{0,1:T(8,128)(2,1)}, u32[]{:S(2)}) copy-start(bf16[384,192]{0,1:T(8,128)(2,1)} %param.18) | copy-start | bytes 442372
  15.4 2.4 %copy-start.5 = (bf16[31,384]{1,0:T(8,128)(2,1)S(1)}, bf16[31,384]{1,0:T(8,128)(2,1)}, u32[]{:S(2)}) copy-start(bf16[31,384]{1,0:T(8,128)(2,1)} %param.20) | copy-start | bytes 71428
  15.5 3.0 %copy-start.50 = (s32[8]{0:T(128)S(1)}, s32[8]{0:T(128)}, u32[]{:S(2)}) copy-start(s32[8]{0:T(128)} %constant.352.clone) | copy-start | bytes 100
  15.5 8.2 %copy-start.7 = (s32[8]{0:T(128)S(1)}, s32[8]{0:T(128)}, u32[]{:S(2)}) copy-start(s32[8]{0:T(128)} %constant.353.clone) | copy-start | bytes 100
  16.8 16.4 %copy-start.3 = (bf16[192,2,384]{2,1,0:T(2,128)(2,1)S(1)}, bf16[192,2,384]{2,1,0:T(2,128)(2,1)}, u32[]{:S(2)}) copy-start(bf16[192,2,384]{2,1,0:T(2,128)(2,1)} %param.19) | copy-start | bytes 884740
  41.1 18.8 %collective-permute-start.1 = (bf16[2,128,1536]{2,1,0:T(8,128)(2,1)S(1)}, bf16[2,128,1536]{2,1,0:T(8,128)(2,1)S(1)}, u32[]{:S(2)}, u32[]{:S(2)}) collective-permute-start(bf16[2,128,1536]{2,1,0:T(8,128)(2,1)S(1)} %get-tuple-element.85), channel_id=1, source_target_pairs={{0,1},{1,0},{2,3},{3,2},{4,5},{5,4},{6,7},{7,6},{8,9},{9,8},{10,11... | collective-permute-start | bytes 2359304 | tf_op jit(solution)/shard_map/ppermute | solution.py:42
  41.1 16.0 %collective-permute-start.4 = (bf16[192,1536]{1,0:T(8,128)(2,1)}, bf16[192,1536]{1,0:T(8,128)(2,1)S(1)}, u32[]{:S(2)}, u32[]{:S(2)}) collective-permute-start(bf16[192,1536]{1,0:T(8,128)(2,1)} %collective-permute-done.2), channel_id=1, source_target_pairs={{0,8},{8,16},{16,24},{24,28},{28,20},{20,12},{12,4},{4,0},{1,9},{9... | collective-permute-start | bytes 1769480 | tf_op jit(solution)/shard_map/ppermute | solution.py:162
  42.7 16.0 %collective-permute-start.5 = (bf16[192,1536]{1,0:T(8,128)(2,1)}, bf16[192,1536]{1,0:T(8,128)(2,1)S(1)}, u32[]{:S(2)}, u32[]{:S(2)}) collective-permute-start(bf16[192,1536]{1,0:T(8,128)(2,1)} %collective-permute-done.3), channel_id=1, source_target_pairs={{0,4},{8,0},{16,8},{24,16},{28,24},{20,28},{12,20},{4,12},{1,5},{9... | collective-permute-start | bytes 1769480 | tf_op jit(solution)/shard_map/ppermute | solution.py:165
  57.1 15.0 %collective-permute-start.6 = (bf16[192,1536]{1,0:T(8,128)(2,1)S(1)}, bf16[192,1536]{1,0:T(8,128)(2,1)S(1)}, u32[]{:S(2)}, u32[]{:S(2)}) collective-permute-start(bf16[192,1536]{1,0:T(8,128)(2,1)S(1)} %collective-permute-done.4), channel_id=1, source_target_pairs={{0,8},{8,16},{16,24},{24,28},{28,20},{20,12},{12,4},{4,0},{1,9},{9... | collective-permute-start | bytes 1769480 | tf_op jit(solution)/shard_map/ppermute | solution.py:162
  58.6 15.0 %collective-permute-start.7 = (bf16[192,1536]{1,0:T(8,128)(2,1)S(1)}, bf16[192,1536]{1,0:T(8,128)(2,1)S(1)}, u32[]{:S(2)}, u32[]{:S(2)}) collective-permute-start(bf16[192,1536]{1,0:T(8,128)(2,1)S(1)} %collective-permute-done.5), channel_id=1, source_target_pairs={{0,4},{8,0},{16,8},{24,16},{28,24},{20,28},{12,20},{4,12},{1,5},{9... | collective-permute-start | bytes 1769480 | tf_op jit(solution)/shard_map/ppermute | solution.py:165
  72.0 7.8 %collective-permute-start.8 = (bf16[96,1536]{1,0:T(8,128)(2,1)S(1)}, bf16[96,1536]{1,0:T(8,128)(2,1)S(1)}, u32[]{:S(2)}, u32[]{:S(2)}) collective-permute-start(bf16[96,1536]{1,0:T(8,128)(2,1)S(1)} %slice.593), channel_id=1, source_target_pairs={{0,8},{8,16},{16,24},{24,28},{28,20},{20,12},{12,4},{4,0},{1,9},{9... | collective-permute-start | bytes 884744 | tf_op jit(solution)/shard_map/ppermute | solution.py:151
  73.7 7.5 %collective-permute-start.9 = (bf16[96,1536]{1,0:T(8,128)(2,1)S(1)}, bf16[96,1536]{1,0:T(8,128)(2,1)S(1)}, u32[]{:S(2)}, u32[]{:S(2)}) collective-permute-start(bf16[96,1536]{1,0:T(8,128)(2,1)S(1)} %slice.595), channel_id=1, source_target_pairs={{0,4},{8,0},{16,8},{24,16},{28,24},{20,28},{12,20},{4,12},{1,5},{9... | collective-permute-start | bytes 884744 | tf_op jit(solution)/shard_map/ppermute | solution.py:152
  81.2 18.8 %collective-permute-start.14 = (bf16[192,1152]{1,0:T(8,128)(2,1)S(1)}, bf16[192,1152]{1,0:T(8,128)(2,1)}, u32[]{:S(2)}, u32[]{:S(2)}) collective-permute-start(bf16[192,1152]{1,0:T(8,128)(2,1)S(1)} %pad_maximum_fusion.1), channel_id=1, source_target_pairs={{0,8},{8,16},{16,24},{24,28},{28,20},{20,12},{12,4},{4,0},{1,9},{9... | collective-permute-start | bytes 1327112 | tf_op jit(solution)/shard_map/ppermute | solution.py:162
  82.9 18.8 %collective-permute-start.15 = (bf16[192,1152]{1,0:T(8,128)(2,1)S(1)}, bf16[192,1152]{1,0:T(8,128)(2,1)}, u32[]{:S(2)}, u32[]{:S(2)}) collective-permute-start(bf16[192,1152]{1,0:T(8,128)(2,1)S(1)} %pad_maximum_fusion.1), channel_id=1, source_target_pairs={{0,4},{8,0},{16,8},{24,16},{28,24},{20,28},{12,20},{4,12},{1,5},{9... | collective-permute-start | bytes 1327112 | tf_op jit(solution)/shard_map/ppermute | solution.py:165
  90.5 1.6 %copy-start.4 = (pred[512,512]{0,1:T(8,128)(4,1)S(1)}, pred[512,512]{0,1:T(8,128)(4,1)}, u32[]{:S(2)}) copy-start(pred[512,512]{0,1:T(8,128)(4,1)} %broadcast_compare_fusion) | copy-start | bytes 786436
  99.5 4.9 %collective-permute-start.10 = (bf16[2,128,1536]{2,1,0:T(8,128)(2,1)S(1)}, bf16[2,128,1536]{2,1,0:T(8,128)(2,1)S(1)}, u32[]{:S(2)}, u32[]{:S(2)}) collective-permute-start(bf16[2,128,1536]{2,1,0:T(8,128)(2,1)S(1)} %dynamic-slice_bitcast_fusion.1), channel_id=1, source_target_pairs={{0,1},{1,0},{2,3},{3,2},{4,5},{5,4},{6,7},{7,6},{8,9},{9,8},{10,11... | collective-permute-start | bytes 2359304 | tf_op jit(solution)/shard_map/ppermute | solution.py:78
  100.1 12.8 %collective-permute-start.16 = (bf16[192,1152]{1,0:T(8,128)(2,1)}, bf16[192,1152]{1,0:T(8,128)(2,1)S(1)}, u32[]{:S(2)}, u32[]{:S(2)}) collective-permute-start(bf16[192,1152]{1,0:T(8,128)(2,1)} %collective-permute-done.14), channel_id=1, source_target_pairs={{0,8},{8,16},{16,24},{24,28},{28,20},{20,12},{12,4},{4,0},{1,9},{9... | collective-permute-start | bytes 1327112 | tf_op jit(solution)/shard_map/ppermute | solution.py:162
  101.7 12.8 %collective-permute-start.17 = (bf16[192,1152]{1,0:T(8,128)(2,1)}, bf16[192,1152]{1,0:T(8,128)(2,1)S(1)}, u32[]{:S(2)}, u32[]{:S(2)}) collective-permute-start(bf16[192,1152]{1,0:T(8,128)(2,1)} %collective-permute-done.15), channel_id=1, source_target_pairs={{0,4},{8,0},{16,8},{24,16},{28,24},{20,28},{12,20},{4,12},{1,5},{9... | collective-permute-start | bytes 1327112 | tf_op jit(solution)/shard_map/ppermute | solution.py:165
  104.7 11.0 %collective-permute-start.11 = (bf16[128,1536]{1,0:T(8,128)(2,1)S(1)}, bf16[128,1536]{1,0:T(8,128)(2,1)S(1)}, u32[]{:S(2)}, u32[]{:S(2)}) collective-permute-start(bf16[128,1536]{1,0:T(8,128)(2,1)S(1)} %fusion.36), channel_id=1, source_target_pairs={{0,2},{1,3},{2,0},{3,1},{4,6},{5,7},{6,4},{7,5},{8,10},{9,11},{10,... | collective-permute-start | bytes 1179656 | tf_op jit(solution)/shard_map/ppermute | solution.py:84
  112.9 11.8 %collective-permute-start.18 = (bf16[192,1152]{1,0:T(8,128)(2,1)S(1)}, bf16[192,1152]{1,0:T(8,128)(2,1)S(1)}, u32[]{:S(2)}, u32[]{:S(2)}) collective-permute-start(bf16[192,1152]{1,0:T(8,128)(2,1)S(1)} %collective-permute-done.16), channel_id=1, source_target_pairs={{0,8},{8,16},{16,24},{24,28},{28,20},{20,12},{12,4},{4,0},{1,9},{9... | collective-permute-start | bytes 1327112 | tf_op jit(solution)/shard_map/ppermute | solution.py:162
  114.5 11.9 %collective-permute-start.19 = (bf16[192,1152]{1,0:T(8,128)(2,1)S(1)}, bf16[192,1152]{1,0:T(8,128)(2,1)S(1)}, u32[]{:S(2)}, u32[]{:S(2)}) collective-permute-start(bf16[192,1152]{1,0:T(8,128)(2,1)S(1)} %collective-permute-done.17), channel_id=1, source_target_pairs={{0,4},{8,0},{16,8},{24,16},{28,24},{20,28},{12,20},{4,12},{1,5},{9... | collective-permute-start | bytes 1327112 | tf_op jit(solution)/shard_map/ppermute | solution.py:165
  116.6 10.2 %collective-permute-start.12 = (bf16[128,1536]{1,0:T(8,128)(2,1)S(1)}, bf16[128,1536]{1,0:T(8,128)(2,1)S(1)}, u32[]{:S(2)}, u32[]{:S(2)}) collective-permute-start(bf16[128,1536]{1,0:T(8,128)(2,1)S(1)} %get-tuple-element.60), channel_id=1, source_target_pairs={{0,2},{1,3},{2,0},{3,1},{4,6},{5,7},{6,4},{7,5},{8,10},{9,11},{10,... | collective-permute-start | bytes 1179656 | tf_op jit(solution)/shard_map/ppermute | solution.py:36
  124.7 6.2 %collective-permute-start.20 = (bf16[96,1152]{1,0:T(8,128)(2,1)S(1)}, bf16[96,1152]{1,0:T(8,128)(2,1)S(1)}, u32[]{:S(2)}, u32[]{:S(2)}) collective-permute-start(bf16[96,1152]{1,0:T(8,128)(2,1)S(1)} %slice.616), channel_id=1, source_target_pairs={{0,8},{8,16},{16,24},{24,28},{28,20},{20,12},{12,4},{4,0},{1,9},{9... | collective-permute-start | bytes 663560 | tf_op jit(solution)/shard_map/ppermute | solution.py:151
  126.3 6.0 %collective-permute-start.21 = (bf16[96,1152]{1,0:T(8,128)(2,1)S(1)}, bf16[96,1152]{1,0:T(8,128)(2,1)S(1)}, u32[]{:S(2)}, u32[]{:S(2)}) collective-permute-start(bf16[96,1152]{1,0:T(8,128)(2,1)S(1)} %slice.618), channel_id=1, source_target_pairs={{0,4},{8,0},{16,8},{24,16},{28,24},{20,28},{12,20},{4,12},{1,5},{9... | collective-permute-start | bytes 663560 | tf_op jit(solution)/shard_map/ppermute | solution.py:152
  126.9 5.4 %collective-permute-start.13 = (bf16[2,128,1536]{2,1,0:T(8,128)(2,1)S(1)}, bf16[2,128,1536]{2,1,0:T(8,128)(2,1)S(1)}, u32[]{:S(2)}, u32[]{:S(2)}) collective-permute-start(bf16[2,128,1536]{2,1,0:T(8,128)(2,1)S(1)} %get-tuple-element.83), channel_id=1, source_target_pairs={{0,1},{1,0},{2,3},{3,2},{4,5},{5,4},{6,7},{7,6},{8,9},{9,8},{10,11... | collective-permute-start | bytes 2359304 | tf_op jit(solution)/shard_map/ppermute | solution.py:42
  133.5 1.4 copy-start.9
  133.5 1.4 copy-start.10
  133.5 1.4 copy-start.11
  133.6 1.4 copy-start.12
  133.6 1.4 copy-start.13
  133.6 1.4 copy-start.14
  133.6 1.4 copy-start.15
  133.6 1.4 copy-start.16
  133.6 1.4 copy-start.17
  133.6 1.4 copy-start.18
  133.6 1.4 copy-start.19
  133.6 1.4 copy-start.20
  133.6 1.4 copy-start.21
  133.7 1.4 copy-start.22
  143.1 2.4 %collective-permute-start.22 = (bf16[2,128,1536]{2,1,0:T(8,128)(2,1)S(1)}, bf16[2,128,1536]{2,1,0:T(8,128)(2,1)S(1)}, u32[]{:S(2)}, u32[]{:S(2)}) collective-permute-start(bf16[2,128,1536]{2,1,0:T(8,128)(2,1)S(1)} %dynamic-slice_bitcast_fusion), channel_id=1, source_target_pairs={{0,1},{1,0},{2,3},{3,2},{4,5},{5,4},{6,7},{7,6},{8,9},{9,8},{10,11... | collective-permute-start | bytes 2359304 | tf_op jit(solution)/shard_map/ppermute | solution.py:78
  145.7 11.2 %collective-permute-start.23 = (bf16[128,1536]{1,0:T(8,128)(2,1)S(1)}, bf16[128,1536]{1,0:T(8,128)(2,1)S(1)}, u32[]{:S(2)}, u32[]{:S(2)}) collective-permute-start(bf16[128,1536]{1,0:T(8,128)(2,1)S(1)} %fusion.37), channel_id=1, source_target_pairs={{0,2},{1,3},{2,0},{3,1},{4,6},{5,7},{6,4},{7,5},{8,10},{9,11},{10,... | collective-permute-start | bytes 1179656 | tf_op jit(solution)/shard_map/ppermute | solution.py:84
  (27 other events, 37.2 us)

commit v16 on v15

--- a/solution.py
+++ b/solution.py
@@ -171,14 +171,13 @@
     return lax.optimization_barrier((token, value))[1]
 
 
-def attend(projected, seg_all, head_size):
-    group_rows = projected.shape[0]
+def attend(query_rows, key_rows, value_rows, seg_all, head_size):
+    group_rows = query_rows.shape[0]
     block_rows = 512
-    heads_here = projected.shape[2] // head_size
-    split = projected.reshape(group_rows, 3, heads_here, head_size)
-    queries = split[:, 0]
-    keys = split[:, 1]
-    values = split[:, 2]
+    heads_here = query_rows.shape[1] // head_size
+    queries = query_rows.reshape(group_rows, heads_here, head_size)
+    keys = key_rows.reshape(group_rows, heads_here, head_size)
+    values = value_rows.reshape(group_rows, heads_here, head_size)
     blocks = group_rows // block_rows
     scale = 1.0 / head_size**0.5
 
@@ -223,10 +222,13 @@
     group_width = model_width // seq_count
     kernel_reach = dw_kernel.shape[0] // 2
     qkv_local = w_qkv.reshape(w_qkv.shape[0], 3 * group_width)
-    qkv_parts, out_parts = ring_gather(
-        jnp.concatenate([qkv_local, w_out.T], axis=1), ring, [3 * group_width]
-    )
-    qkv_matrix = qkv_parts.reshape(model_width, 3 * group_width)
+    query_parts, key_parts, value_parts_a, out_parts = ring_gather(
+        jnp.concatenate([qkv_local, w_out.T], axis=1),
+        ring,
+        [group_width, 2 * group_width, 3 * group_width],
+    )
+    query_matrix = query_parts.reshape(model_width, group_width)
+    kv_matrices = [p.reshape(model_width, group_width) for p in (key_parts, value_parts_a)]
     out_cols = out_parts.reshape(model_width, w_out.shape[0])
     glu_rows = w_glu.shape[0]
     glu_local = w_glu.reshape(glu_rows, 2 * group_width)
@@ -242,12 +244,12 @@
     record_ends = jnp.cumsum(lengths[0])
     seg_all = segment_of(record_ends, jnp.arange(group_rows, dtype=jnp.int32))
     normed1 = layer_norm(inputs, ln1_gain)
-    projected = (
-        jnp.dot(seq_gather(normed1, paired).reshape(group_rows, model_width), qkv_matrix, preferred_element_type=jnp.float32)
-        .astype(jnp.bfloat16)
-        .reshape(group_rows, 3, group_width)
-    )
-    attended = attend(projected, seg_all, HD)
+    group_normed = seq_gather(normed1, paired).reshape(group_rows, model_width)
+    query_rows, key_rows, value_rows = [
+        jnp.dot(group_normed, m, preferred_element_type=jnp.float32).astype(jnp.bfloat16)
+        for m in [query_matrix] + kv_matrices
+    ]
+    attended = attend(query_rows, key_rows, value_rows, seg_all, HD)
     attn_sum = seq_scatter_sum(
         jnp.dot(attended, out_cols.T, preferred_element_type=jnp.float32).astype(jnp.bfloat16),
         paired,

time: 159 us -> 150 us (0.943)
  local copies, waits for them, and re-layouts: 26.8 us -> 14 us
  waiting for transfers between devices: 57 us -> 63.7 us
  matrix products: 16.1 us -> 13.6 us
    dynamic_update_slice x23 -> x19, local copies, waits for them, and re-layouts: 12.4 us -> 5.69 us  [place(): lax.dynamic_update_index_in_dim(out, piece[..., lo:hi], where, 0)]
    ppermute x6, waiting for transfers between devices: 33 us -> 38.2 us  [ring_gather(): ahead = lax.ppermute(ahead, 'dp', forward)]
    broadcast_in_dim x2 -> x0, local copies, waits for them, and re-layouts: 2.58 us -> none  [the longest x1 2.21 us: ring_gather(): jnp.zeros((count,) + block.shape[:-1] + (hi - lo,), block.dtype)]
    dot_general x1 -> x3, matrix products: 5.73 us -> 3.23 us  [on_device(): jnp.dot(group_normed, m, preferred_element_type=jnp.float32)]
    unnamed x104 -> x117, local copies, waits for them, and re-layouts: 0.64 us -> 2.91 us
    convert_element_type x1 -> x0, local copies, waits for them, and re-layouts: 1.61 us -> none  [on_device(): projected = jnp.dot(seq_gather(normed1, paired).reshape(group_rows, model...]
  transfers between devices with their start and end apart: 24 -> 24, of which waited for: 11 -> 11; matrix products, arithmetic and copies ran while one was open for 29% -> 19% of each run, Pallas kernels for 0% -> 0%
where the time goes in v16:
time: 150 us; the launch traced here: 149 us
  waiting for transfers between devices  63.7 us (42%)
  starting transfers between devices  21.6 us (14%)
  between operations  19.3 us (13%)
  other arithmetic  17.3 us (12%)
  local copies, waits for them, and re-layouts  14 us (9%)
  matrix products  13.6 us (9%)
    ppermute x6, waiting for transfers between devices, ring_gather(): ahead = lax.ppermute(ahead, 'dp', forward)  38.2 us
    ppermute x2, waiting for transfers between devices, seq_scatter_sum(): lax.ppermute(piece.astype(jnp.bfloat16), 'seq', [(i, (i + 2 * shift) % co...  11.3 us
    ppermute x6, starting transfers between devices, ring_gather(): ahead = lax.ppermute(ahead, 'dp', forward)  11.1 us
    ppermute x2, waiting for transfers between devices, ring_gather(): front = lax.ppermute(ahead[:rows], 'dp', forward)  9.13 us
    convert_element_type x1, other arithmetic, depthwise(): return jax.nn.silu(total_acc).astype(jnp.bfloat16)  6.68 us
    dynamic_update_slice x19, local copies, waits for them, and re-layouts, place(): lax.dynamic_update_index_in_dim(out, piece[..., lo:hi], where, 0)  5.69 us
    sub x1, matrix products, one_block(): weights = jnp.exp(scores - top_score)  3.65 us
    ppermute x2, starting transfers between devices, ring_gather(): front = lax.ppermute(ahead[:rows], 'dp', forward)  3.26 us
  transfers between devices with their start and end apart: 24, of which 11 were waited for; matrix products, arithmetic and copies ran while one was open for 19% of the time, Pallas kernels for 0%

profile of v16, /device:TPU:0, one launch (start us, length us, event | category | flops | bytes accessed | tf_op | source)
XLA Modules:
  0.0 149.5 jit_solution(72933379683853860)
XLA Ops:
  0.0 1.1 copy.28
  1.1 1.8 %pad_maximum_fusion = bf16[192,1536]{1,0:T(8,128)(2,1)} fusion(bf16[192,384]{1,0:T(8,128)(2,1)} %bitcast.383, bf16[192,1152]{1,0:T(8,128)(2,1)S(1)} %bitcast.368), kind=kLoop, calls=%fused_computation.53 | loop fusion | flops 1179648 | bytes 1179648 | tf_op jit(solution)/shard_map/concatenate | solution.py:226
  2.9 3.0 %collective-permute-start.2 = (bf16[192,1536]{1,0:T(8,128)(2,1)}, bf16[192,1536]{1,0:T(8,128)(2,1)}, u32[]{:S(2)}, u32[]{:S(2)}) collective-permute-start(bf16[192,1536]{1,0:T(8,128)(2,1)} %pad_maximum_fusion), channel_id=1, source_target_pairs={{0,8},{8,16},{16,24},{24,28},{28,20},{20,12},{12,4},{4,0},{1,9},{9... | collective-permute-start | bytes 1769480 | tf_op jit(solution)/shard_map/ppermute | solution.py:162
  6.4 1.0 fusion.22
  7.4 1.9 %collective-permute-start = (bf16[128,1536]{1,0:T(8,128)(2,1)}, bf16[128,1536]{1,0:T(8,128)(2,1)}, u32[]{:S(2)}, u32[]{:S(2)}) collective-permute-start(bf16[128,1536]{1,0:T(8,128)(2,1)} %fusion.22), channel_id=1, source_target_pairs={{0,2},{1,3},{2,0},{3,1},{4,6},{5,7},{6,4},{7,5},{8,10},{9,11},{10,... | collective-permute-start | bytes 1179656 | tf_op jit(solution)/shard_map/ppermute | solution.py:36
  14.5 0.7 fusion.96
  24.8 0.7 copy-done.1
  26.2 0.9 broadcast_compare_fusion
  27.1 1.0 copy.29
  28.1 0.7 convert_reduce_fusion.34
  28.9 0.7 slice_compare_fusion.30
  34.1 0.9 pad_maximum_fusion.1
  36.1 1.2 bitcast_dynamic-update-slice_fusion.4
  37.4 0.7 slice_compare_fusion.29
  38.1 1.6 %collective-permute-start.4 = (bf16[192,1536]{1,0:T(8,128)(2,1)}, bf16[192,1536]{1,0:T(8,128)(2,1)S(1)}, u32[]{:S(2)}, u32[]{:S(2)}) collective-permute-start(bf16[192,1536]{1,0:T(8,128)(2,1)} %collective-permute-done.2), channel_id=1, source_target_pairs={{0,8},{8,16},{16,24},{24,28},{28,20},{20,12},{12,4},{4,0},{1,9},{9... | collective-permute-start | bytes 1769480 | tf_op jit(solution)/shard_map/ppermute | solution.py:162
  40.2 0.7 convert_reduce_fusion.33
  40.8 1.2 fusion.56
  42.1 1.2 fusion.55
  43.3 10.8 %collective-permute-done.4 = bf16[192,1536]{1,0:T(8,128)(2,1)S(1)} collective-permute-done((bf16[192,1536]{1,0:T(8,128)(2,1)}, bf16[192,1536]{1,0:T(8,128)(2,1)S(1)}, u32[]{:S(2)}, u32[]{:S(2)}) %collective-permute-start.4) | collective-permute-done | bytes 589856 | tf_op jit(solution)/shard_map/ppermute | solution.py:162
  54.1 1.6 %collective-permute-start.6 = (bf16[192,1536]{1,0:T(8,128)(2,1)S(1)}, bf16[192,1536]{1,0:T(8,128)(2,1)S(1)}, u32[]{:S(2)}, u32[]{:S(2)}) collective-permute-start(bf16[192,1536]{1,0:T(8,128)(2,1)S(1)} %collective-permute-done.4), channel_id=1, source_target_pairs={{0,8},{8,16},{16,24},{24,28},{28,20},{20,12},{12,4},{4,0},{1,9},{9... | collective-permute-start | bytes 1769480 | tf_op jit(solution)/shard_map/ppermute | solution.py:162
  56.4 12.6 %collective-permute-done.6 = bf16[192,1536]{1,0:T(8,128)(2,1)S(1)} collective-permute-done((bf16[192,1536]{1,0:T(8,128)(2,1)S(1)}, bf16[192,1536]{1,0:T(8,128)(2,1)S(1)}, u32[]{:S(2)}, u32[]{:S(2)}) %collective-permute-start.6) | collective-permute-done | bytes 589856 | tf_op jit(solution)/shard_map/ppermute | solution.py:162
  69.0 1.6 %collective-permute-start.8 = (bf16[96,1536]{1,0:T(8,128)(2,1)S(1)}, bf16[96,1536]{1,0:T(8,128)(2,1)S(1)}, u32[]{:S(2)}, u32[]{:S(2)}) collective-permute-start(bf16[96,1536]{1,0:T(8,128)(2,1)S(1)} %slice.658), channel_id=1, source_target_pairs={{0,8},{8,16},{16,24},{24,28},{28,20},{20,12},{12,4},{4,0},{1,9},{9... | collective-permute-start | bytes 884744 | tf_op jit(solution)/shard_map/ppermute | solution.py:151
  71.4 5.4 %collective-permute-done.8 = bf16[96,1536]{1,0:T(8,128)(2,1)S(1)} collective-permute-done((bf16[96,1536]{1,0:T(8,128)(2,1)S(1)}, bf16[96,1536]{1,0:T(8,128)(2,1)S(1)}, u32[]{:S(2)}, u32[]{:S(2)}) %collective-permute-start.8) | collective-permute-done | bytes 294944 | tf_op jit(solution)/shard_map/ppermute | solution.py:151
  76.9 1.3 collective-permute-done.9
  78.2 1.6 %collective-permute-start.14 = (bf16[192,1152]{1,0:T(8,128)(2,1)S(1)}, bf16[192,1152]{1,0:T(8,128)(2,1)}, u32[]{:S(2)}, u32[]{:S(2)}) collective-permute-start(bf16[192,1152]{1,0:T(8,128)(2,1)S(1)} %pad_maximum_fusion.1), channel_id=1, source_target_pairs={{0,8},{8,16},{16,24},{24,28},{28,20},{20,12},{12,4},{4,0},{1,9},{9... | collective-permute-start | bytes 1327112 | tf_op jit(solution)/shard_map/ppermute | solution.py:162
  80.3 1.6 %convolution_convert_fusion.4 = bf16[512,384]{0,1:T(8,128)(2,1)} fusion(bf16[512,1536]{1,0:T(8,128)(2,1)S(1)} %bitcast.372, bf16[1536,384]{1,0:T(8,128)(2,1)S(1)} %bitcast.378), kind=kOutput, calls=%fused_computation.22 | convolution fusion | flops 604176384 | bytes 3145728 | tf_op jit(solution)/shard_map/dot_general | solution.py:249
  81.9 0.8 convolution_convert_fusion.3
  82.8 0.8 convolution_convert_fusion.2
  83.7 3.6 %fusion.97 = (f32[4,512]{1,0:T(4,128)S(1)}, f32[4,512,512]{1,2,0:T(8,128)}) fusion(pred[512,512]{0,1:T(8,128)(4,1)S(1)} %copy-done.6, bf16[512,4,96]{0,2,1:T(8,128)(2,1)S(1)} %bitcast.392, bf16[512,4,96]{0,2,1:T(8,128)(2,1)S(1)} %bitcast.393), kind=kOutput, calls=%fused_computation.272 | convolution fusion | flops 205521408 | bytes 5251072 | tf_op jit(solution)/shard_map/while/body/eval_jaxpr/sub | solution.py:193
  87.3 2.7 %fusion.10 = bf16[4,96,512]{2,1,0:T(8,128)(2,1)S(1)} fusion(bf16[512,4,96]{0,2,1:T(8,128)(2,1)S(1)} %bitcast.391, f32[4,512,512]{1,2,0:T(8,128)} %get-tuple-element.164, f32[4,512]{1,0:T(4,128)S(1)} %get-tuple-element.163), kind=kOutput, calls=%fused_computation.19 | convolution fusion | flops 203620352 | bytes 4988928 | tf_op jit(solution)/shard_map/while/body/eval_jaxpr/hqk,khe->qhe/dot_general | solution.py:195
  90.0 1.0 convolution_convert_fusion.1
  91.7 1.6 %collective-permute-start.16 = (bf16[192,1152]{1,0:T(8,128)(2,1)}, bf16[192,1152]{1,0:T(8,128)(2,1)S(1)}, u32[]{:S(2)}, u32[]{:S(2)}) collective-permute-start(bf16[192,1152]{1,0:T(8,128)(2,1)} %collective-permute-done.14), channel_id=1, source_target_pairs={{0,8},{8,16},{16,24},{24,28},{28,20},{20,12},{12,4},{4,0},{1,9},{9... | collective-permute-start | bytes 1327112 | tf_op jit(solution)/shard_map/ppermute | solution.py:162
  93.8 1.1 fusion.38
  94.9 1.1 fusion.37
  96.9 7.6 %collective-permute-done.16 = bf16[192,1152]{1,0:T(8,128)(2,1)S(1)} collective-permute-done((bf16[192,1152]{1,0:T(8,128)(2,1)}, bf16[192,1152]{1,0:T(8,128)(2,1)S(1)}, u32[]{:S(2)}, u32[]{:S(2)}) %collective-permute-start.16) | collective-permute-done | bytes 442400 | tf_op jit(solution)/shard_map/ppermute | solution.py:162
  104.5 1.6 %collective-permute-start.18 = (bf16[192,1152]{1,0:T(8,128)(2,1)S(1)}, bf16[192,1152]{1,0:T(8,128)(2,1)S(1)}, u32[]{:S(2)}, u32[]{:S(2)}) collective-permute-start(bf16[192,1152]{1,0:T(8,128)(2,1)S(1)} %collective-permute-done.16), channel_id=1, source_target_pairs={{0,8},{8,16},{16,24},{24,28},{28,20},{20,12},{12,4},{4,0},{1,9},{9... | collective-permute-start | bytes 1327112 | tf_op jit(solution)/shard_map/ppermute | solution.py:162
  106.7 0.6 collective-permute-done.11
  109.0 7.3 %collective-permute-done.18 = bf16[192,1152]{1,0:T(8,128)(2,1)S(1)} collective-permute-done((bf16[192,1152]{1,0:T(8,128)(2,1)S(1)}, bf16[192,1152]{1,0:T(8,128)(2,1)S(1)}, u32[]{:S(2)}, u32[]{:S(2)}) %collective-permute-start.18) | collective-permute-done | bytes 442400 | tf_op jit(solution)/shard_map/ppermute | solution.py:162
  116.3 1.6 %collective-permute-start.20 = (bf16[96,1152]{1,0:T(8,128)(2,1)S(1)}, bf16[96,1152]{1,0:T(8,128)(2,1)S(1)}, u32[]{:S(2)}, u32[]{:S(2)}) collective-permute-start(bf16[96,1152]{1,0:T(8,128)(2,1)S(1)} %slice.696), channel_id=1, source_target_pairs={{0,8},{8,16},{16,24},{24,28},{28,20},{20,12},{12,4},{4,0},{1,9},{9... | collective-permute-start | bytes 663560 | tf_op jit(solution)/shard_map/ppermute | solution.py:151
  118.8 3.7 %collective-permute-done.20 = bf16[96,1152]{1,0:T(8,128)(2,1)S(1)} collective-permute-done((bf16[96,1152]{1,0:T(8,128)(2,1)S(1)}, bf16[96,1152]{1,0:T(8,128)(2,1)S(1)}, u32[]{:S(2)}, u32[]{:S(2)}) %collective-permute-start.20) | collective-permute-done | bytes 221216 | tf_op jit(solution)/shard_map/ppermute | solution.py:151
  122.6 1.4 collective-permute-done.21
  124.1 1.1 fusion.8
  125.6 1.0 fusion.9
  126.9 6.7 %multiply_convert_fusion = bf16[512,384]{1,0:T(8,128)(2,1)S(1)} fusion(bf16[512,384]{1,0:T(8,128)(2,1)S(1)} %fusion.9, f32[384]{0:T(512)S(1)} %copy-done.30, f32[384]{0:T(512)S(1)} %copy-done.31, f32[384]{0:T(512)S(1)} %get-tuple-element.20, f32[384]{0:T(512)S(1)} %get-tuple-element.28, f32[384]{0:T(512)S(1)} %get-tuple-element.30, ...), kind=kLoop, calls=%fused_computation.50 | loop fusion | flops 25165824 | bytes 849920 | tf_op jit(solution)/shard_map/convert_element_type | solution.py:214
  133.6 1.0 convolution_convert_fusion
  134.8 2.3 %collective-permute-done.22 = bf16[2,128,1536]{2,1,0:T(8,128)(2,1)S(1)} collective-permute-done((bf16[2,128,1536]{2,1,0:T(8,128)(2,1)S(1)}, bf16[2,128,1536]{2,1,0:T(8,128)(2,1)S(1)}, u32[]{:S(2)}, u32[]{:S(2)}) %collective-permute-start.22) | collective-permute-done | bytes 786464 | tf_op jit(solution)/shard_map/ppermute | solution.py:78
  138.0 10.6 %collective-permute-done.23 = bf16[128,1536]{1,0:T(8,128)(2,1)S(1)} collective-permute-done((bf16[128,1536]{1,0:T(8,128)(2,1)S(1)}, bf16[128,1536]{1,0:T(8,128)(2,1)S(1)}, u32[]{:S(2)}, u32[]{:S(2)}) %collective-permute-start.23) | collective-permute-done | bytes 393248 | tf_op jit(solution)/shard_map/ppermute | solution.py:84
  148.6 0.9 fusion.32
  (204 shorter events, 12.2 us)
Async XLA Ops:
  0.0 5.9 %copy-start = (bf16[1,128,1536]{2,1,0:T(8,128)(2,1)S(1)}, bf16[1,128,1536]{2,1,0:T(8,128)(2,1)}, u32[]{:S(2)}) copy-start(bf16[1,128,1536]{2,1,0:T(8,128)(2,1)} %param.13) | copy-start | bytes 1179652
  1.1 5.2 %copy-start.8 = (f32[1536]{0:T(1024)S(1)}, f32[1536]{0:T(1024)}, u32[]{:S(2)}) copy-start(f32[1536]{0:T(1024)} %param.15) | copy-start | bytes 18436
  1.1 8.2 %copy-start.57 = (s32[8]{0:T(128)S(1)}, s32[8]{0:T(128)}, u32[]{:S(2)}) copy-start(s32[8]{0:T(128)} %constant.377.clone) | copy-start | bytes 100
  2.9 11.6 %copy-start.9 = (s32[8]{0:T(128)S(1)}, s32[8]{0:T(128)}, u32[]{:S(2)}) copy-start(s32[8]{0:T(128)} %constant.378.clone) | copy-start | bytes 100
  2.9 35.2 %collective-permute-start.2 = (bf16[192,1536]{1,0:T(8,128)(2,1)}, bf16[192,1536]{1,0:T(8,128)(2,1)}, u32[]{:S(2)}, u32[]{:S(2)}) collective-permute-start(bf16[192,1536]{1,0:T(8,128)(2,1)} %pad_maximum_fusion), channel_id=1, source_target_pairs={{0,8},{8,16},{16,24},{24,28},{28,20},{20,12},{12,4},{4,0},{1,9},{9... | collective-permute-start | bytes 1769480 | tf_op jit(solution)/shard_map/ppermute | solution.py:162
  5.9 33.8 %collective-permute-start.3 = (bf16[192,1536]{1,0:T(8,128)(2,1)}, bf16[192,1536]{1,0:T(8,128)(2,1)}, u32[]{:S(2)}, u32[]{:S(2)}) collective-permute-start(bf16[192,1536]{1,0:T(8,128)(2,1)} %pad_maximum_fusion), channel_id=1, source_target_pairs={{0,4},{8,0},{16,8},{24,16},{28,24},{20,28},{12,20},{4,12},{1,5},{9... | collective-permute-start | bytes 1769480 | tf_op jit(solution)/shard_map/ppermute | solution.py:165
  6.1 18.1 %copy-start.32 = (f32[128]{0:T(128)}, f32[128]{0:T(128)S(1)}, u32[]{:S(2)}) copy-start(f32[128]{0:T(128)S(1)} %broadcast_multiply_fusion.1) | copy-start | bytes 1540
  6.4 17.8 %copy-start.34 = (f32[128]{0:T(128)}, f32[128]{0:T(128)S(1)}, u32[]{:S(2)}) copy-start(f32[128]{0:T(128)S(1)} %add_rsqrt_fusion.1) | copy-start | bytes 1540
  6.4 18.0 %copy-start.5 = (bf16[384,192]{0,1:T(8,128)(2,1)S(1)}, bf16[384,192]{0,1:T(8,128)(2,1)}, u32[]{:S(2)}) copy-start(bf16[384,192]{0,1:T(8,128)(2,1)} %param.18) | copy-start | bytes 442372
  7.4 28.6 %collective-permute-start = (bf16[128,1536]{1,0:T(8,128)(2,1)}, bf16[128,1536]{1,0:T(8,128)(2,1)}, u32[]{:S(2)}, u32[]{:S(2)}) collective-permute-start(bf16[128,1536]{1,0:T(8,128)(2,1)} %fusion.22), channel_id=1, source_target_pairs={{0,2},{1,3},{2,0},{3,1},{4,6},{5,7},{6,4},{7,5},{8,10},{9,11},{10,... | collective-permute-start | bytes 1179656 | tf_op jit(solution)/shard_map/ppermute | solution.py:36
  24.7 3.4 %copy-start.7 = (bf16[31,384]{1,0:T(8,128)(2,1)S(1)}, bf16[31,384]{1,0:T(8,128)(2,1)}, u32[]{:S(2)}) copy-start(bf16[31,384]{1,0:T(8,128)(2,1)} %param.20) | copy-start | bytes 71428
  35.8 5.1 %copy-start.2 = (bf16[8,192,384]{2,1,0:T(8,128)(2,1)S(1)}, bf16[8,192,384]{2,1,0:T(8,128)(2,1)}, u32[]{:S(2)}) copy-start(bf16[8,192,384]{2,1,0:T(8,128)(2,1)} %copy-done.1) | copy-start | bytes 3538948
  35.8 5.1 %copy-start.4 = (bf16[8,192,384]{2,1,0:T(8,128)(2,1)S(1)}, bf16[8,192,384]{2,1,0:T(8,128)(2,1)}, u32[]{:S(2)}) copy-start(bf16[8,192,384]{2,1,0:T(8,128)(2,1)} %copy-done.3) | copy-start | bytes 3538948
  37.3 18.8 %collective-permute-start.1 = (bf16[2,128,1536]{2,1,0:T(8,128)(2,1)S(1)}, bf16[2,128,1536]{2,1,0:T(8,128)(2,1)S(1)}, u32[]{:S(2)}, u32[]{:S(2)}) collective-permute-start(bf16[2,128,1536]{2,1,0:T(8,128)(2,1)S(1)} %get-tuple-element.109), channel_id=1, source_target_pairs={{0,1},{1,0},{2,3},{3,2},{4,5},{5,4},{6,7},{7,6},{8,9},{9,8},{10,11... | collective-permute-start | bytes 2359304 | tf_op jit(solution)/shard_map/ppermute | solution.py:42
  38.1 16.0 %collective-permute-start.4 = (bf16[192,1536]{1,0:T(8,128)(2,1)}, bf16[192,1536]{1,0:T(8,128)(2,1)S(1)}, u32[]{:S(2)}, u32[]{:S(2)}) collective-permute-start(bf16[192,1536]{1,0:T(8,128)(2,1)} %collective-permute-done.2), channel_id=1, source_target_pairs={{0,8},{8,16},{16,24},{24,28},{28,20},{20,12},{12,4},{4,0},{1,9},{9... | collective-permute-start | bytes 1769480 | tf_op jit(solution)/shard_map/ppermute | solution.py:162
  39.7 15.9 %collective-permute-start.5 = (bf16[192,1536]{1,0:T(8,128)(2,1)}, bf16[192,1536]{1,0:T(8,128)(2,1)S(1)}, u32[]{:S(2)}, u32[]{:S(2)}) collective-permute-start(bf16[192,1536]{1,0:T(8,128)(2,1)} %collective-permute-done.3), channel_id=1, source_target_pairs={{0,4},{8,0},{16,8},{24,16},{28,24},{20,28},{12,20},{4,12},{1,5},{9... | collective-permute-start | bytes 1769480 | tf_op jit(solution)/shard_map/ppermute | solution.py:165
  54.1 14.9 %collective-permute-start.6 = (bf16[192,1536]{1,0:T(8,128)(2,1)S(1)}, bf16[192,1536]{1,0:T(8,128)(2,1)S(1)}, u32[]{:S(2)}, u32[]{:S(2)}) collective-permute-start(bf16[192,1536]{1,0:T(8,128)(2,1)S(1)} %collective-permute-done.4), channel_id=1, source_target_pairs={{0,8},{8,16},{16,24},{24,28},{28,20},{20,12},{12,4},{4,0},{1,9},{9... | collective-permute-start | bytes 1769480 | tf_op jit(solution)/shard_map/ppermute | solution.py:162
  55.6 15.0 %collective-permute-start.7 = (bf16[192,1536]{1,0:T(8,128)(2,1)S(1)}, bf16[192,1536]{1,0:T(8,128)(2,1)S(1)}, u32[]{:S(2)}, u32[]{:S(2)}) collective-permute-start(bf16[192,1536]{1,0:T(8,128)(2,1)S(1)} %collective-permute-done.5), channel_id=1, source_target_pairs={{0,4},{8,0},{16,8},{24,16},{28,24},{20,28},{12,20},{4,12},{1,5},{9... | collective-permute-start | bytes 1769480 | tf_op jit(solution)/shard_map/ppermute | solution.py:165
  69.0 7.8 %collective-permute-start.8 = (bf16[96,1536]{1,0:T(8,128)(2,1)S(1)}, bf16[96,1536]{1,0:T(8,128)(2,1)S(1)}, u32[]{:S(2)}, u32[]{:S(2)}) collective-permute-start(bf16[96,1536]{1,0:T(8,128)(2,1)S(1)} %slice.658), channel_id=1, source_target_pairs={{0,8},{8,16},{16,24},{24,28},{28,20},{20,12},{12,4},{4,0},{1,9},{9... | collective-permute-start | bytes 884744 | tf_op jit(solution)/shard_map/ppermute | solution.py:151
  70.7 7.5 %collective-permute-start.9 = (bf16[96,1536]{1,0:T(8,128)(2,1)S(1)}, bf16[96,1536]{1,0:T(8,128)(2,1)S(1)}, u32[]{:S(2)}, u32[]{:S(2)}) collective-permute-start(bf16[96,1536]{1,0:T(8,128)(2,1)S(1)} %slice.660), channel_id=1, source_target_pairs={{0,4},{8,0},{16,8},{24,16},{28,24},{20,28},{12,20},{4,12},{1,5},{9... | collective-permute-start | bytes 884744 | tf_op jit(solution)/shard_map/ppermute | solution.py:152
  78.2 13.4 %collective-permute-start.14 = (bf16[192,1152]{1,0:T(8,128)(2,1)S(1)}, bf16[192,1152]{1,0:T(8,128)(2,1)}, u32[]{:S(2)}, u32[]{:S(2)}) collective-permute-start(bf16[192,1152]{1,0:T(8,128)(2,1)S(1)} %pad_maximum_fusion.1), channel_id=1, source_target_pairs={{0,8},{8,16},{16,24},{24,28},{28,20},{20,12},{12,4},{4,0},{1,9},{9... | collective-permute-start | bytes 1327112 | tf_op jit(solution)/shard_map/ppermute | solution.py:162
  79.9 13.4 %collective-permute-start.15 = (bf16[192,1152]{1,0:T(8,128)(2,1)S(1)}, bf16[192,1152]{1,0:T(8,128)(2,1)}, u32[]{:S(2)}, u32[]{:S(2)}) collective-permute-start(bf16[192,1152]{1,0:T(8,128)(2,1)S(1)} %pad_maximum_fusion.1), channel_id=1, source_target_pairs={{0,4},{8,0},{16,8},{24,16},{28,24},{20,28},{12,20},{4,12},{1,5},{9... | collective-permute-start | bytes 1327112 | tf_op jit(solution)/shard_map/ppermute | solution.py:165
  83.7 3.6 %copy-start.56 = (bf16[512,384]{0,1:T(8,128)(2,1)S(1)}, bf16[512,384]{0,1:T(8,128)(2,1)}, u32[]{:S(2)}) copy-start(bf16[512,384]{0,1:T(8,128)(2,1)} %convolution_convert_fusion.4) | copy-start | bytes 1179652
  91.1 4.9 %collective-permute-start.10 = (bf16[2,128,1536]{2,1,0:T(8,128)(2,1)S(1)}, bf16[2,128,1536]{2,1,0:T(8,128)(2,1)S(1)}, u32[]{:S(2)}, u32[]{:S(2)}) collective-permute-start(bf16[2,128,1536]{2,1,0:T(8,128)(2,1)S(1)} %dynamic-slice_bitcast_fusion.1), channel_id=1, source_target_pairs={{0,1},{1,0},{2,3},{3,2},{4,5},{5,4},{6,7},{7,6},{8,9},{9,8},{10,11... | collective-permute-start | bytes 2359304 | tf_op jit(solution)/shard_map/ppermute | solution.py:78
  91.7 12.8 %collective-permute-start.16 = (bf16[192,1152]{1,0:T(8,128)(2,1)}, bf16[192,1152]{1,0:T(8,128)(2,1)S(1)}, u32[]{:S(2)}, u32[]{:S(2)}) collective-permute-start(bf16[192,1152]{1,0:T(8,128)(2,1)} %collective-permute-done.14), channel_id=1, source_target_pairs={{0,8},{8,16},{16,24},{24,28},{28,20},{20,12},{12,4},{4,0},{1,9},{9... | collective-permute-start | bytes 1327112 | tf_op jit(solution)/shard_map/ppermute | solution.py:162
  93.3 12.8 %collective-permute-start.17 = (bf16[192,1152]{1,0:T(8,128)(2,1)}, bf16[192,1152]{1,0:T(8,128)(2,1)S(1)}, u32[]{:S(2)}, u32[]{:S(2)}) collective-permute-start(bf16[192,1152]{1,0:T(8,128)(2,1)} %collective-permute-done.15), channel_id=1, source_target_pairs={{0,4},{8,0},{16,8},{24,16},{28,24},{20,28},{12,20},{4,12},{1,5},{9... | collective-permute-start | bytes 1327112 | tf_op jit(solution)/shard_map/ppermute | solution.py:165
  96.3 11.0 %collective-permute-start.11 = (bf16[128,1536]{1,0:T(8,128)(2,1)S(1)}, bf16[128,1536]{1,0:T(8,128)(2,1)S(1)}, u32[]{:S(2)}, u32[]{:S(2)}) collective-permute-start(bf16[128,1536]{1,0:T(8,128)(2,1)S(1)} %fusion.30), channel_id=1, source_target_pairs={{0,2},{1,3},{2,0},{3,1},{4,6},{5,7},{6,4},{7,5},{8,10},{9,11},{10,... | collective-permute-start | bytes 1179656 | tf_op jit(solution)/shard_map/ppermute | solution.py:84
  104.5 11.8 %collective-permute-start.18 = (bf16[192,1152]{1,0:T(8,128)(2,1)S(1)}, bf16[192,1152]{1,0:T(8,128)(2,1)S(1)}, u32[]{:S(2)}, u32[]{:S(2)}) collective-permute-start(bf16[192,1152]{1,0:T(8,128)(2,1)S(1)} %collective-permute-done.16), channel_id=1, source_target_pairs={{0,8},{8,16},{16,24},{24,28},{28,20},{20,12},{12,4},{4,0},{1,9},{9... | collective-permute-start | bytes 1327112 | tf_op jit(solution)/shard_map/ppermute | solution.py:162
  106.1 11.9 %collective-permute-start.19 = (bf16[192,1152]{1,0:T(8,128)(2,1)S(1)}, bf16[192,1152]{1,0:T(8,128)(2,1)S(1)}, u32[]{:S(2)}, u32[]{:S(2)}) collective-permute-start(bf16[192,1152]{1,0:T(8,128)(2,1)S(1)} %collective-permute-done.17), channel_id=1, source_target_pairs={{0,4},{8,0},{16,8},{24,16},{28,24},{20,28},{12,20},{4,12},{1,5},{9... | collective-permute-start | bytes 1327112 | tf_op jit(solution)/shard_map/ppermute | solution.py:165
  108.2 10.2 %collective-permute-start.12 = (bf16[128,1536]{1,0:T(8,128)(2,1)S(1)}, bf16[128,1536]{1,0:T(8,128)(2,1)S(1)}, u32[]{:S(2)}, u32[]{:S(2)}) collective-permute-start(bf16[128,1536]{1,0:T(8,128)(2,1)S(1)} %get-tuple-element.60), channel_id=1, source_target_pairs={{0,2},{1,3},{2,0},{3,1},{4,6},{5,7},{6,4},{7,5},{8,10},{9,11},{10,... | collective-permute-start | bytes 1179656 | tf_op jit(solution)/shard_map/ppermute | solution.py:36
  116.3 6.2 %collective-permute-start.20 = (bf16[96,1152]{1,0:T(8,128)(2,1)S(1)}, bf16[96,1152]{1,0:T(8,128)(2,1)S(1)}, u32[]{:S(2)}, u32[]{:S(2)}) collective-permute-start(bf16[96,1152]{1,0:T(8,128)(2,1)S(1)} %slice.696), channel_id=1, source_target_pairs={{0,8},{8,16},{16,24},{24,28},{28,20},{20,12},{12,4},{4,0},{1,9},{9... | collective-permute-start | bytes 663560 | tf_op jit(solution)/shard_map/ppermute | solution.py:151
  118.0 6.0 %collective-permute-start.21 = (bf16[96,1152]{1,0:T(8,128)(2,1)S(1)}, bf16[96,1152]{1,0:T(8,128)(2,1)S(1)}, u32[]{:S(2)}, u32[]{:S(2)}) collective-permute-start(bf16[96,1152]{1,0:T(8,128)(2,1)S(1)} %slice.698), channel_id=1, source_target_pairs={{0,4},{8,0},{16,8},{24,16},{28,24},{20,28},{12,20},{4,12},{1,5},{9... | collective-permute-start | bytes 663560 | tf_op jit(solution)/shard_map/ppermute | solution.py:152
  118.5 5.5 %collective-permute-start.13 = (bf16[2,128,1536]{2,1,0:T(8,128)(2,1)S(1)}, bf16[2,128,1536]{2,1,0:T(8,128)(2,1)S(1)}, u32[]{:S(2)}, u32[]{:S(2)}) collective-permute-start(bf16[2,128,1536]{2,1,0:T(8,128)(2,1)S(1)} %get-tuple-element.107), channel_id=1, source_target_pairs={{0,1},{1,0},{2,3},{3,2},{4,5},{5,4},{6,7},{7,6},{8,9},{9,8},{10,11... | collective-permute-start | bytes 2359304 | tf_op jit(solution)/shard_map/ppermute | solution.py:42
  125.2 1.4 copy-start.11
  125.2 1.4 copy-start.12
  125.2 1.4 copy-start.13
  125.2 1.4 copy-start.14
  125.2 1.4 copy-start.15
  125.2 1.4 copy-start.16
  125.2 1.4 copy-start.17
  125.2 1.4 copy-start.18
  125.2 1.4 copy-start.19
  125.2 1.4 copy-start.20
  125.3 1.4 copy-start.21
  125.3 1.4 copy-start.22
  125.3 1.4 copy-start.23
  134.7 2.4 %collective-permute-start.22 = (bf16[2,128,1536]{2,1,0:T(8,128)(2,1)S(1)}, bf16[2,128,1536]{2,1,0:T(8,128)(2,1)S(1)}, u32[]{:S(2)}, u32[]{:S(2)}) collective-permute-start(bf16[2,128,1536]{2,1,0:T(8,128)(2,1)S(1)} %dynamic-slice_bitcast_fusion), channel_id=1, source_target_pairs={{0,1},{1,0},{2,3},{3,2},{4,5},{5,4},{6,7},{7,6},{8,9},{9,8},{10,11... | collective-permute-start | bytes 2359304 | tf_op jit(solution)/shard_map/ppermute | solution.py:78
  137.4 11.2 %collective-permute-start.23 = (bf16[128,1536]{1,0:T(8,128)(2,1)S(1)}, bf16[128,1536]{1,0:T(8,128)(2,1)S(1)}, u32[]{:S(2)}, u32[]{:S(2)}) collective-permute-start(bf16[128,1536]{1,0:T(8,128)(2,1)S(1)} %fusion.31), channel_id=1, source_target_pairs={{0,2},{1,3},{2,0},{3,1},{4,6},{5,7},{6,4},{7,5},{8,10},{9,11},{10,... | collective-permute-start | bytes 1179656 | tf_op jit(solution)/shard_map/ppermute | solution.py:84
  (34 other events, 44.7 us)

commit v17 on v16

--- a/solution.py
+++ b/solution.py
@@ -210,7 +210,9 @@
     for tap_index in range(kernel.shape[0]):
         window = padded[tap_index : tap_index + count].astype(jnp.float32)
         same = (seg_near[tap_index : tap_index + count] == seg_here)[:, None]
-        total_acc = total_acc + jnp.where(same, window * kernel[tap_index].astype(jnp.float32), 0.0)
+        total_acc = total_acc + window * kernel[tap_index].astype(jnp.float32) * same.astype(
+            jnp.float32
+        )
     return jax.nn.silu(total_acc).astype(jnp.bfloat16)
 
 

time: 150 us -> 149 us (level)
  transfers between devices with their start and end apart: 24 -> 24, of which waited for: 11 -> 11; matrix products, arithmetic and copies ran while one was open for 19% -> 20% of each run, Pallas kernels for 0% -> 0%
where the time goes in v17:
time: 149 us
  waiting for transfers between devices  63.6 us (43%)
  starting transfers between devices  21.5 us (14%)
  between operations  19.8 us (13%)
  other arithmetic  16.4 us (11%)
  local copies, waits for them, and re-layouts  13.6 us (9%)
  matrix products  13.6 us (9%)
    ppermute x6, waiting for transfers between devices, ring_gather(): ahead = lax.ppermute(ahead, 'dp', forward)  38.2 us
    ppermute x2, waiting for transfers between devices, seq_scatter_sum(): lax.ppermute(piece.astype(jnp.bfloat16), 'seq', [(i, (i + 2 * shift) % co...  11.3 us
    ppermute x6, starting transfers between devices, ring_gather(): ahead = lax.ppermute(ahead, 'dp', forward)  11 us
    ppermute x2, waiting for transfers between devices, ring_gather(): front = lax.ppermute(ahead[:rows], 'dp', forward)  9.13 us
    convert_element_type x1, other arithmetic, depthwise(): return jax.nn.silu(total_acc).astype(jnp.bfloat16)  5.81 us
    dynamic_update_slice x19, local copies, waits for them, and re-layouts, place(): lax.dynamic_update_index_in_dim(out, piece[..., lo:hi], where, 0)  5.69 us
    sub x1, matrix products, one_block(): weights = jnp.exp(scores - top_score)  3.64 us
    ppermute x2, starting transfers between devices, ring_gather(): front = lax.ppermute(ahead[:rows], 'dp', forward)  3.26 us
  transfers between devices with their start and end apart: 24, of which 11 were waited for; matrix products, arithmetic and copies ran while one was open for 20% of the time, Pallas kernels for 0%

profile of v17, /device:TPU:0, one launch (start us, length us, event | category | flops | bytes accessed | tf_op | source)
XLA Modules:
  0.0 148.6 jit_solution(14431493735950812367)
XLA Ops:
  0.0 1.1 copy.28
  1.1 1.8 %pad_maximum_fusion = bf16[192,1536]{1,0:T(8,128)(2,1)} fusion(bf16[192,384]{1,0:T(8,128)(2,1)} %bitcast.383, bf16[192,1152]{1,0:T(8,128)(2,1)S(1)} %bitcast.368), kind=kLoop, calls=%fused_computation.53 | loop fusion | flops 1179648 | bytes 1179648 | tf_op jit(solution)/shard_map/concatenate | solution.py:228
  2.9 3.0 %collective-permute-start.2 = (bf16[192,1536]{1,0:T(8,128)(2,1)}, bf16[192,1536]{1,0:T(8,128)(2,1)}, u32[]{:S(2)}, u32[]{:S(2)}) collective-permute-start(bf16[192,1536]{1,0:T(8,128)(2,1)} %pad_maximum_fusion), channel_id=1, source_target_pairs={{0,8},{8,16},{16,24},{24,28},{28,20},{20,12},{12,4},{4,0},{1,9},{9... | collective-permute-start | bytes 1769480 | tf_op jit(solution)/shard_map/ppermute | solution.py:162
  6.4 1.0 fusion.22
  7.4 1.9 %collective-permute-start = (bf16[128,1536]{1,0:T(8,128)(2,1)}, bf16[128,1536]{1,0:T(8,128)(2,1)}, u32[]{:S(2)}, u32[]{:S(2)}) collective-permute-start(bf16[128,1536]{1,0:T(8,128)(2,1)} %fusion.22), channel_id=1, source_target_pairs={{0,2},{1,3},{2,0},{3,1},{4,6},{5,7},{6,4},{7,5},{8,10},{9,11},{10,... | collective-permute-start | bytes 1179656 | tf_op jit(solution)/shard_map/ppermute | solution.py:36
  9.3 0.7 dynamic_slice.80
  15.0 0.7 fusion.127
  25.3 0.7 copy-done.1
  26.7 0.9 broadcast_compare_fusion
  27.6 1.0 copy.29
  28.7 0.7 fusion.92
  29.5 0.7 convert_reduce_fusion.34
  34.7 0.9 pad_maximum_fusion.1
  36.1 1.2 bitcast_dynamic-update-slice_fusion.4
  37.4 0.7 fusion.93
  38.1 1.6 %collective-permute-start.4 = (bf16[192,1536]{1,0:T(8,128)(2,1)}, bf16[192,1536]{1,0:T(8,128)(2,1)S(1)}, u32[]{:S(2)}, u32[]{:S(2)}) collective-permute-start(bf16[192,1536]{1,0:T(8,128)(2,1)} %collective-permute-done.2), channel_id=1, source_target_pairs={{0,8},{8,16},{16,24},{24,28},{28,20},{20,12},{12,4},{4,0},{1,9},{9... | collective-permute-start | bytes 1769480 | tf_op jit(solution)/shard_map/ppermute | solution.py:162
  40.2 0.7 convert_reduce_fusion.33
  40.8 1.2 fusion.56
  42.1 1.2 fusion.55
  43.3 10.8 %collective-permute-done.4 = bf16[192,1536]{1,0:T(8,128)(2,1)S(1)} collective-permute-done((bf16[192,1536]{1,0:T(8,128)(2,1)}, bf16[192,1536]{1,0:T(8,128)(2,1)S(1)}, u32[]{:S(2)}, u32[]{:S(2)}) %collective-permute-start.4) | collective-permute-done | bytes 589856 | tf_op jit(solution)/shard_map/ppermute | solution.py:162
  54.1 1.6 %collective-permute-start.6 = (bf16[192,1536]{1,0:T(8,128)(2,1)S(1)}, bf16[192,1536]{1,0:T(8,128)(2,1)S(1)}, u32[]{:S(2)}, u32[]{:S(2)}) collective-permute-start(bf16[192,1536]{1,0:T(8,128)(2,1)S(1)} %collective-permute-done.4), channel_id=1, source_target_pairs={{0,8},{8,16},{16,24},{24,28},{28,20},{20,12},{12,4},{4,0},{1,9},{9... | collective-permute-start | bytes 1769480 | tf_op jit(solution)/shard_map/ppermute | solution.py:162
  56.4 12.6 %collective-permute-done.6 = bf16[192,1536]{1,0:T(8,128)(2,1)S(1)} collective-permute-done((bf16[192,1536]{1,0:T(8,128)(2,1)S(1)}, bf16[192,1536]{1,0:T(8,128)(2,1)S(1)}, u32[]{:S(2)}, u32[]{:S(2)}) %collective-permute-start.6) | collective-permute-done | bytes 589856 | tf_op jit(solution)/shard_map/ppermute | solution.py:162
  69.0 1.6 %collective-permute-start.8 = (bf16[96,1536]{1,0:T(8,128)(2,1)S(1)}, bf16[96,1536]{1,0:T(8,128)(2,1)S(1)}, u32[]{:S(2)}, u32[]{:S(2)}) collective-permute-start(bf16[96,1536]{1,0:T(8,128)(2,1)S(1)} %slice.658), channel_id=1, source_target_pairs={{0,8},{8,16},{16,24},{24,28},{28,20},{20,12},{12,4},{4,0},{1,9},{9... | collective-permute-start | bytes 884744 | tf_op jit(solution)/shard_map/ppermute | solution.py:151
  71.4 5.4 %collective-permute-done.8 = bf16[96,1536]{1,0:T(8,128)(2,1)S(1)} collective-permute-done((bf16[96,1536]{1,0:T(8,128)(2,1)S(1)}, bf16[96,1536]{1,0:T(8,128)(2,1)S(1)}, u32[]{:S(2)}, u32[]{:S(2)}) %collective-permute-start.8) | collective-permute-done | bytes 294944 | tf_op jit(solution)/shard_map/ppermute | solution.py:151
  76.9 1.3 collective-permute-done.9
  78.3 1.6 %collective-permute-start.14 = (bf16[192,1152]{1,0:T(8,128)(2,1)S(1)}, bf16[192,1152]{1,0:T(8,128)(2,1)}, u32[]{:S(2)}, u32[]{:S(2)}) collective-permute-start(bf16[192,1152]{1,0:T(8,128)(2,1)S(1)} %pad_maximum_fusion.1), channel_id=1, source_target_pairs={{0,8},{8,16},{16,24},{24,28},{28,20},{20,12},{12,4},{4,0},{1,9},{9... | collective-permute-start | bytes 1327112 | tf_op jit(solution)/shard_map/ppermute | solution.py:162
  80.3 1.6 %convolution_convert_fusion.4 = bf16[512,384]{0,1:T(8,128)(2,1)} fusion(bf16[512,1536]{1,0:T(8,128)(2,1)S(1)} %bitcast.372, bf16[1536,384]{1,0:T(8,128)(2,1)S(1)} %bitcast.378), kind=kOutput, calls=%fused_computation.22 | convolution fusion | flops 604176384 | bytes 3145728 | tf_op jit(solution)/shard_map/dot_general | solution.py:251
  81.9 0.8 convolution_convert_fusion.3
  82.8 0.8 convolution_convert_fusion.2
  83.7 3.6 %fusion.128 = (f32[4,512]{1,0:T(4,128)S(1)}, f32[4,512,512]{1,2,0:T(8,128)}) fusion(pred[512,512]{0,1:T(8,128)(4,1)S(1)} %copy-done.6, bf16[512,4,96]{0,2,1:T(8,128)(2,1)S(1)} %bitcast.392, bf16[512,4,96]{0,2,1:T(8,128)(2,1)S(1)} %bitcast.393), kind=kOutput, calls=%fused_computation.303 | convolution fusion | flops 205521408 | bytes 5251072 | tf_op jit(solution)/shard_map/while/body/eval_jaxpr/sub | solution.py:193
  87.3 2.7 %fusion.10 = bf16[4,96,512]{2,1,0:T(8,128)(2,1)S(1)} fusion(bf16[512,4,96]{0,2,1:T(8,128)(2,1)S(1)} %bitcast.391, f32[4,512,512]{1,2,0:T(8,128)} %get-tuple-element.164, f32[4,512]{1,0:T(4,128)S(1)} %get-tuple-element.163), kind=kOutput, calls=%fused_computation.19 | convolution fusion | flops 203620352 | bytes 4988928 | tf_op jit(solution)/shard_map/while/body/eval_jaxpr/hqk,khe->qhe/dot_general | solution.py:195
  90.0 1.0 convolution_convert_fusion.1
  91.7 1.6 %collective-permute-start.16 = (bf16[192,1152]{1,0:T(8,128)(2,1)}, bf16[192,1152]{1,0:T(8,128)(2,1)S(1)}, u32[]{:S(2)}, u32[]{:S(2)}) collective-permute-start(bf16[192,1152]{1,0:T(8,128)(2,1)} %collective-permute-done.14), channel_id=1, source_target_pairs={{0,8},{8,16},{16,24},{24,28},{28,20},{20,12},{12,4},{4,0},{1,9},{9... | collective-permute-start | bytes 1327112 | tf_op jit(solution)/shard_map/ppermute | solution.py:162
  93.8 1.1 fusion.38
  94.9 1.1 fusion.37
  96.9 7.6 %collective-permute-done.16 = bf16[192,1152]{1,0:T(8,128)(2,1)S(1)} collective-permute-done((bf16[192,1152]{1,0:T(8,128)(2,1)}, bf16[192,1152]{1,0:T(8,128)(2,1)S(1)}, u32[]{:S(2)}, u32[]{:S(2)}) %collective-permute-start.16) | collective-permute-done | bytes 442400 | tf_op jit(solution)/shard_map/ppermute | solution.py:162
  104.5 1.6 %collective-permute-start.18 = (bf16[192,1152]{1,0:T(8,128)(2,1)S(1)}, bf16[192,1152]{1,0:T(8,128)(2,1)S(1)}, u32[]{:S(2)}, u32[]{:S(2)}) collective-permute-start(bf16[192,1152]{1,0:T(8,128)(2,1)S(1)} %collective-permute-done.16), channel_id=1, source_target_pairs={{0,8},{8,16},{16,24},{24,28},{28,20},{20,12},{12,4},{4,0},{1,9},{9... | collective-permute-start | bytes 1327112 | tf_op jit(solution)/shard_map/ppermute | solution.py:162
  109.0 7.3 %collective-permute-done.18 = bf16[192,1152]{1,0:T(8,128)(2,1)S(1)} collective-permute-done((bf16[192,1152]{1,0:T(8,128)(2,1)S(1)}, bf16[192,1152]{1,0:T(8,128)(2,1)S(1)}, u32[]{:S(2)}, u32[]{:S(2)}) %collective-permute-start.18) | collective-permute-done | bytes 442400 | tf_op jit(solution)/shard_map/ppermute | solution.py:162
  116.3 1.6 %collective-permute-start.20 = (bf16[96,1152]{1,0:T(8,128)(2,1)S(1)}, bf16[96,1152]{1,0:T(8,128)(2,1)S(1)}, u32[]{:S(2)}, u32[]{:S(2)}) collective-permute-start(bf16[96,1152]{1,0:T(8,128)(2,1)S(1)} %slice.696), channel_id=1, source_target_pairs={{0,8},{8,16},{16,24},{24,28},{28,20},{20,12},{12,4},{4,0},{1,9},{9... | collective-permute-start | bytes 663560 | tf_op jit(solution)/shard_map/ppermute | solution.py:151
  118.8 3.7 %collective-permute-done.20 = bf16[96,1152]{1,0:T(8,128)(2,1)S(1)} collective-permute-done((bf16[96,1152]{1,0:T(8,128)(2,1)S(1)}, bf16[96,1152]{1,0:T(8,128)(2,1)S(1)}, u32[]{:S(2)}, u32[]{:S(2)}) %collective-permute-start.20) | collective-permute-done | bytes 221216 | tf_op jit(solution)/shard_map/ppermute | solution.py:151
  122.6 1.4 collective-permute-done.21
  124.1 1.1 fusion.8
  125.5 1.0 fusion.9
  126.9 5.8 %multiply_convert_fusion = bf16[512,384]{1,0:T(8,128)(2,1)S(1)} fusion(bf16[512,384]{1,0:T(8,128)(2,1)S(1)} %fusion.9, f32[512]{0:T(512)S(1)} %copy-done.15, f32[384]{0:T(512)} %get-tuple-element.57, f32[512]{0:T(512)S(1)} %copy-done.17, f32[384]{0:T(512)} %get-tuple-element.58, f32[512]{0:T(512)S(1)} %copy-done.18, f32[384]{0:T(512)S(1)} %copy-done.35, ...), kind=kLoop, calls=%fused_computation.50 | loop fusion | flops 25165824 | bytes 897536 | tf_op jit(solution)/shard_map/convert_element_type | solution.py:216
  132.7 1.0 convolution_convert_fusion
  133.9 2.3 %collective-permute-done.22 = bf16[2,128,1536]{2,1,0:T(8,128)(2,1)S(1)} collective-permute-done((bf16[2,128,1536]{2,1,0:T(8,128)(2,1)S(1)}, bf16[2,128,1536]{2,1,0:T(8,128)(2,1)S(1)}, u32[]{:S(2)}, u32[]{:S(2)}) %collective-permute-start.22) | collective-permute-done | bytes 786464 | tf_op jit(solution)/shard_map/ppermute | solution.py:78
  137.1 10.6 %collective-permute-done.23 = bf16[128,1536]{1,0:T(8,128)(2,1)S(1)} collective-permute-done((bf16[128,1536]{1,0:T(8,128)(2,1)S(1)}, bf16[128,1536]{1,0:T(8,128)(2,1)S(1)}, u32[]{:S(2)}, u32[]{:S(2)}) %collective-permute-start.23) | collective-permute-done | bytes 393248 | tf_op jit(solution)/shard_map/ppermute | solution.py:84
  147.7 0.9 fusion.32
  (196 shorter events, 11.7 us)
Async XLA Ops:
  0.0 5.9 %copy-start = (bf16[1,128,1536]{2,1,0:T(8,128)(2,1)S(1)}, bf16[1,128,1536]{2,1,0:T(8,128)(2,1)}, u32[]{:S(2)}) copy-start(bf16[1,128,1536]{2,1,0:T(8,128)(2,1)} %param.13) | copy-start | bytes 1179652
  1.1 5.2 %copy-start.8 = (f32[1536]{0:T(1024)S(1)}, f32[1536]{0:T(1024)}, u32[]{:S(2)}) copy-start(f32[1536]{0:T(1024)} %param.15) | copy-start | bytes 18436
  1.1 8.2 %copy-start.53 = (s32[8]{0:T(128)S(1)}, s32[8]{0:T(128)}, u32[]{:S(2)}) copy-start(s32[8]{0:T(128)} %constant.377.clone) | copy-start | bytes 100
  2.9 12.1 %copy-start.9 = (s32[8]{0:T(128)S(1)}, s32[8]{0:T(128)}, u32[]{:S(2)}) copy-start(s32[8]{0:T(128)} %constant.378.clone) | copy-start | bytes 100
  2.9 35.2 %collective-permute-start.2 = (bf16[192,1536]{1,0:T(8,128)(2,1)}, bf16[192,1536]{1,0:T(8,128)(2,1)}, u32[]{:S(2)}, u32[]{:S(2)}) collective-permute-start(bf16[192,1536]{1,0:T(8,128)(2,1)} %pad_maximum_fusion), channel_id=1, source_target_pairs={{0,8},{8,16},{16,24},{24,28},{28,20},{20,12},{12,4},{4,0},{1,9},{9... | collective-permute-start | bytes 1769480 | tf_op jit(solution)/shard_map/ppermute | solution.py:162
  5.9 33.8 %collective-permute-start.3 = (bf16[192,1536]{1,0:T(8,128)(2,1)}, bf16[192,1536]{1,0:T(8,128)(2,1)}, u32[]{:S(2)}, u32[]{:S(2)}) collective-permute-start(bf16[192,1536]{1,0:T(8,128)(2,1)} %pad_maximum_fusion), channel_id=1, source_target_pairs={{0,4},{8,0},{16,8},{24,16},{28,24},{20,28},{12,20},{4,12},{1,5},{9... | collective-permute-start | bytes 1769480 | tf_op jit(solution)/shard_map/ppermute | solution.py:165
  6.4 18.5 %copy-start.5 = (bf16[384,192]{0,1:T(8,128)(2,1)S(1)}, bf16[384,192]{0,1:T(8,128)(2,1)}, u32[]{:S(2)}) copy-start(bf16[384,192]{0,1:T(8,128)(2,1)} %param.18) | copy-start | bytes 442372
  7.4 28.7 %collective-permute-start = (bf16[128,1536]{1,0:T(8,128)(2,1)}, bf16[128,1536]{1,0:T(8,128)(2,1)}, u32[]{:S(2)}, u32[]{:S(2)}) collective-permute-start(bf16[128,1536]{1,0:T(8,128)(2,1)} %fusion.22), channel_id=1, source_target_pairs={{0,2},{1,3},{2,0},{3,1},{4,6},{5,7},{6,4},{7,5},{8,10},{9,11},{10,... | collective-permute-start | bytes 1179656 | tf_op jit(solution)/shard_map/ppermute | solution.py:36
  25.2 4.3 %copy-start.7 = (bf16[31,384]{1,0:T(8,128)(2,1)S(1)}, bf16[31,384]{1,0:T(8,128)(2,1)}, u32[]{:S(2)}) copy-start(bf16[31,384]{1,0:T(8,128)(2,1)} %param.20) | copy-start | bytes 71428
  35.8 5.0 %copy-start.2 = (bf16[8,192,384]{2,1,0:T(8,128)(2,1)S(1)}, bf16[8,192,384]{2,1,0:T(8,128)(2,1)}, u32[]{:S(2)}) copy-start(bf16[8,192,384]{2,1,0:T(8,128)(2,1)} %copy-done.1) | copy-start | bytes 3538948
  35.8 5.0 %copy-start.4 = (bf16[8,192,384]{2,1,0:T(8,128)(2,1)S(1)}, bf16[8,192,384]{2,1,0:T(8,128)(2,1)}, u32[]{:S(2)}) copy-start(bf16[8,192,384]{2,1,0:T(8,128)(2,1)} %copy-done.3) | copy-start | bytes 3538948
  37.4 18.7 %collective-permute-start.1 = (bf16[2,128,1536]{2,1,0:T(8,128)(2,1)S(1)}, bf16[2,128,1536]{2,1,0:T(8,128)(2,1)S(1)}, u32[]{:S(2)}, u32[]{:S(2)}) collective-permute-start(bf16[2,128,1536]{2,1,0:T(8,128)(2,1)S(1)} %get-tuple-element.109), channel_id=1, source_target_pairs={{0,1},{1,0},{2,3},{3,2},{4,5},{5,4},{6,7},{7,6},{8,9},{9,8},{10,11... | collective-permute-start | bytes 2359304 | tf_op jit(solution)/shard_map/ppermute | solution.py:42
  38.1 15.9 %collective-permute-start.4 = (bf16[192,1536]{1,0:T(8,128)(2,1)}, bf16[192,1536]{1,0:T(8,128)(2,1)S(1)}, u32[]{:S(2)}, u32[]{:S(2)}) collective-permute-start(bf16[192,1536]{1,0:T(8,128)(2,1)} %collective-permute-done.2), channel_id=1, source_target_pairs={{0,8},{8,16},{16,24},{24,28},{28,20},{20,12},{12,4},{4,0},{1,9},{9... | collective-permute-start | bytes 1769480 | tf_op jit(solution)/shard_map/ppermute | solution.py:162
  39.7 15.9 %collective-permute-start.5 = (bf16[192,1536]{1,0:T(8,128)(2,1)}, bf16[192,1536]{1,0:T(8,128)(2,1)S(1)}, u32[]{:S(2)}, u32[]{:S(2)}) collective-permute-start(bf16[192,1536]{1,0:T(8,128)(2,1)} %collective-permute-done.3), channel_id=1, source_target_pairs={{0,4},{8,0},{16,8},{24,16},{28,24},{20,28},{12,20},{4,12},{1,5},{9... | collective-permute-start | bytes 1769480 | tf_op jit(solution)/shard_map/ppermute | solution.py:165
  54.1 14.9 %collective-permute-start.6 = (bf16[192,1536]{1,0:T(8,128)(2,1)S(1)}, bf16[192,1536]{1,0:T(8,128)(2,1)S(1)}, u32[]{:S(2)}, u32[]{:S(2)}) collective-permute-start(bf16[192,1536]{1,0:T(8,128)(2,1)S(1)} %collective-permute-done.4), channel_id=1, source_target_pairs={{0,8},{8,16},{16,24},{24,28},{28,20},{20,12},{12,4},{4,0},{1,9},{9... | collective-permute-start | bytes 1769480 | tf_op jit(solution)/shard_map/ppermute | solution.py:162
  55.7 15.0 %collective-permute-start.7 = (bf16[192,1536]{1,0:T(8,128)(2,1)S(1)}, bf16[192,1536]{1,0:T(8,128)(2,1)S(1)}, u32[]{:S(2)}, u32[]{:S(2)}) collective-permute-start(bf16[192,1536]{1,0:T(8,128)(2,1)S(1)} %collective-permute-done.5), channel_id=1, source_target_pairs={{0,4},{8,0},{16,8},{24,16},{28,24},{20,28},{12,20},{4,12},{1,5},{9... | collective-permute-start | bytes 1769480 | tf_op jit(solution)/shard_map/ppermute | solution.py:165
  69.0 7.8 %collective-permute-start.8 = (bf16[96,1536]{1,0:T(8,128)(2,1)S(1)}, bf16[96,1536]{1,0:T(8,128)(2,1)S(1)}, u32[]{:S(2)}, u32[]{:S(2)}) collective-permute-start(bf16[96,1536]{1,0:T(8,128)(2,1)S(1)} %slice.658), channel_id=1, source_target_pairs={{0,8},{8,16},{16,24},{24,28},{28,20},{20,12},{12,4},{4,0},{1,9},{9... | collective-permute-start | bytes 884744 | tf_op jit(solution)/shard_map/ppermute | solution.py:151
  70.7 7.5 %collective-permute-start.9 = (bf16[96,1536]{1,0:T(8,128)(2,1)S(1)}, bf16[96,1536]{1,0:T(8,128)(2,1)S(1)}, u32[]{:S(2)}, u32[]{:S(2)}) collective-permute-start(bf16[96,1536]{1,0:T(8,128)(2,1)S(1)} %slice.660), channel_id=1, source_target_pairs={{0,4},{8,0},{16,8},{24,16},{28,24},{20,28},{12,20},{4,12},{1,5},{9... | collective-permute-start | bytes 884744 | tf_op jit(solution)/shard_map/ppermute | solution.py:152
  78.3 13.4 %collective-permute-start.14 = (bf16[192,1152]{1,0:T(8,128)(2,1)S(1)}, bf16[192,1152]{1,0:T(8,128)(2,1)}, u32[]{:S(2)}, u32[]{:S(2)}) collective-permute-start(bf16[192,1152]{1,0:T(8,128)(2,1)S(1)} %pad_maximum_fusion.1), channel_id=1, source_target_pairs={{0,8},{8,16},{16,24},{24,28},{28,20},{20,12},{12,4},{4,0},{1,9},{9... | collective-permute-start | bytes 1327112 | tf_op jit(solution)/shard_map/ppermute | solution.py:162
  79.9 13.4 %collective-permute-start.15 = (bf16[192,1152]{1,0:T(8,128)(2,1)S(1)}, bf16[192,1152]{1,0:T(8,128)(2,1)}, u32[]{:S(2)}, u32[]{:S(2)}) collective-permute-start(bf16[192,1152]{1,0:T(8,128)(2,1)S(1)} %pad_maximum_fusion.1), channel_id=1, source_target_pairs={{0,4},{8,0},{16,8},{24,16},{28,24},{20,28},{12,20},{4,12},{1,5},{9... | collective-permute-start | bytes 1327112 | tf_op jit(solution)/shard_map/ppermute | solution.py:165
  83.7 3.6 %copy-start.52 = (bf16[512,384]{0,1:T(8,128)(2,1)S(1)}, bf16[512,384]{0,1:T(8,128)(2,1)}, u32[]{:S(2)}) copy-start(bf16[512,384]{0,1:T(8,128)(2,1)} %convolution_convert_fusion.4) | copy-start | bytes 1179652
  91.1 4.9 %collective-permute-start.10 = (bf16[2,128,1536]{2,1,0:T(8,128)(2,1)S(1)}, bf16[2,128,1536]{2,1,0:T(8,128)(2,1)S(1)}, u32[]{:S(2)}, u32[]{:S(2)}) collective-permute-start(bf16[2,128,1536]{2,1,0:T(8,128)(2,1)S(1)} %dynamic-slice_bitcast_fusion.1), channel_id=1, source_target_pairs={{0,1},{1,0},{2,3},{3,2},{4,5},{5,4},{6,7},{7,6},{8,9},{9,8},{10,11... | collective-permute-start | bytes 2359304 | tf_op jit(solution)/shard_map/ppermute | solution.py:78
  91.7 12.8 %collective-permute-start.16 = (bf16[192,1152]{1,0:T(8,128)(2,1)}, bf16[192,1152]{1,0:T(8,128)(2,1)S(1)}, u32[]{:S(2)}, u32[]{:S(2)}) collective-permute-start(bf16[192,1152]{1,0:T(8,128)(2,1)} %collective-permute-done.14), channel_id=1, source_target_pairs={{0,8},{8,16},{16,24},{24,28},{28,20},{20,12},{12,4},{4,0},{1,9},{9... | collective-permute-start | bytes 1327112 | tf_op jit(solution)/shard_map/ppermute | solution.py:162
  93.3 12.8 %collective-permute-start.17 = (bf16[192,1152]{1,0:T(8,128)(2,1)}, bf16[192,1152]{1,0:T(8,128)(2,1)S(1)}, u32[]{:S(2)}, u32[]{:S(2)}) collective-permute-start(bf16[192,1152]{1,0:T(8,128)(2,1)} %collective-permute-done.15), channel_id=1, source_target_pairs={{0,4},{8,0},{16,8},{24,16},{28,24},{20,28},{12,20},{4,12},{1,5},{9... | collective-permute-start | bytes 1327112 | tf_op jit(solution)/shard_map/ppermute | solution.py:165
  96.3 11.0 %collective-permute-start.11 = (bf16[128,1536]{1,0:T(8,128)(2,1)S(1)}, bf16[128,1536]{1,0:T(8,128)(2,1)S(1)}, u32[]{:S(2)}, u32[]{:S(2)}) collective-permute-start(bf16[128,1536]{1,0:T(8,128)(2,1)S(1)} %fusion.30), channel_id=1, source_target_pairs={{0,2},{1,3},{2,0},{3,1},{4,6},{5,7},{6,4},{7,5},{8,10},{9,11},{10,... | collective-permute-start | bytes 1179656 | tf_op jit(solution)/shard_map/ppermute | solution.py:84
  104.5 11.8 %collective-permute-start.18 = (bf16[192,1152]{1,0:T(8,128)(2,1)S(1)}, bf16[192,1152]{1,0:T(8,128)(2,1)S(1)}, u32[]{:S(2)}, u32[]{:S(2)}) collective-permute-start(bf16[192,1152]{1,0:T(8,128)(2,1)S(1)} %collective-permute-done.16), channel_id=1, source_target_pairs={{0,8},{8,16},{16,24},{24,28},{28,20},{20,12},{12,4},{4,0},{1,9},{9... | collective-permute-start | bytes 1327112 | tf_op jit(solution)/shard_map/ppermute | solution.py:162
  106.1 11.9 %collective-permute-start.19 = (bf16[192,1152]{1,0:T(8,128)(2,1)S(1)}, bf16[192,1152]{1,0:T(8,128)(2,1)S(1)}, u32[]{:S(2)}, u32[]{:S(2)}) collective-permute-start(bf16[192,1152]{1,0:T(8,128)(2,1)S(1)} %collective-permute-done.17), channel_id=1, source_target_pairs={{0,4},{8,0},{16,8},{24,16},{28,24},{20,28},{12,20},{4,12},{1,5},{9... | collective-permute-start | bytes 1327112 | tf_op jit(solution)/shard_map/ppermute | solution.py:165
  108.2 10.3 %collective-permute-start.12 = (bf16[128,1536]{1,0:T(8,128)(2,1)S(1)}, bf16[128,1536]{1,0:T(8,128)(2,1)S(1)}, u32[]{:S(2)}, u32[]{:S(2)}) collective-permute-start(bf16[128,1536]{1,0:T(8,128)(2,1)S(1)} %get-tuple-element.60), channel_id=1, source_target_pairs={{0,2},{1,3},{2,0},{3,1},{4,6},{5,7},{6,4},{7,5},{8,10},{9,11},{10,... | collective-permute-start | bytes 1179656 | tf_op jit(solution)/shard_map/ppermute | solution.py:36
  116.3 6.2 %collective-permute-start.20 = (bf16[96,1152]{1,0:T(8,128)(2,1)S(1)}, bf16[96,1152]{1,0:T(8,128)(2,1)S(1)}, u32[]{:S(2)}, u32[]{:S(2)}) collective-permute-start(bf16[96,1152]{1,0:T(8,128)(2,1)S(1)} %slice.696), channel_id=1, source_target_pairs={{0,8},{8,16},{16,24},{24,28},{28,20},{20,12},{12,4},{4,0},{1,9},{9... | collective-permute-start | bytes 663560 | tf_op jit(solution)/shard_map/ppermute | solution.py:151
  118.0 6.0 %collective-permute-start.21 = (bf16[96,1152]{1,0:T(8,128)(2,1)S(1)}, bf16[96,1152]{1,0:T(8,128)(2,1)S(1)}, u32[]{:S(2)}, u32[]{:S(2)}) collective-permute-start(bf16[96,1152]{1,0:T(8,128)(2,1)S(1)} %slice.698), channel_id=1, source_target_pairs={{0,4},{8,0},{16,8},{24,16},{28,24},{20,28},{12,20},{4,12},{1,5},{9... | collective-permute-start | bytes 663560 | tf_op jit(solution)/shard_map/ppermute | solution.py:152
  118.5 5.5 %collective-permute-start.13 = (bf16[2,128,1536]{2,1,0:T(8,128)(2,1)S(1)}, bf16[2,128,1536]{2,1,0:T(8,128)(2,1)S(1)}, u32[]{:S(2)}, u32[]{:S(2)}) collective-permute-start(bf16[2,128,1536]{2,1,0:T(8,128)(2,1)S(1)} %get-tuple-element.107), channel_id=1, source_target_pairs={{0,1},{1,0},{2,3},{3,2},{4,5},{5,4},{6,7},{7,6},{8,9},{9,8},{10,11... | collective-permute-start | bytes 2359304 | tf_op jit(solution)/shard_map/ppermute | solution.py:42
  125.1 1.4 copy-start.11
  125.2 1.4 copy-start.12
  125.2 1.4 copy-start.13
  125.2 1.4 copy-start.14
  125.2 1.4 copy-start.15
  125.2 1.4 copy-start.16
  125.2 1.4 copy-start.17
  125.2 1.4 copy-start.18
  125.2 1.4 copy-start.19
  125.2 1.4 copy-start.20
  125.2 1.4 copy-start.21
  125.3 1.4 copy-start.22
  125.3 1.4 copy-start.23
  125.3 1.4 copy-start.24
  125.3 1.4 copy-start.25
  133.8 2.4 %collective-permute-start.22 = (bf16[2,128,1536]{2,1,0:T(8,128)(2,1)S(1)}, bf16[2,128,1536]{2,1,0:T(8,128)(2,1)S(1)}, u32[]{:S(2)}, u32[]{:S(2)}) collective-permute-start(bf16[2,128,1536]{2,1,0:T(8,128)(2,1)S(1)} %dynamic-slice_bitcast_fusion), channel_id=1, source_target_pairs={{0,1},{1,0},{2,3},{3,2},{4,5},{5,4},{6,7},{7,6},{8,9},{9,8},{10,11... | collective-permute-start | bytes 2359304 | tf_op jit(solution)/shard_map/ppermute | solution.py:78
  136.5 11.2 %collective-permute-start.23 = (bf16[128,1536]{1,0:T(8,128)(2,1)S(1)}, bf16[128,1536]{1,0:T(8,128)(2,1)S(1)}, u32[]{:S(2)}, u32[]{:S(2)}) collective-permute-start(bf16[128,1536]{1,0:T(8,128)(2,1)S(1)} %fusion.31), channel_id=1, source_target_pairs={{0,2},{1,3},{2,0},{3,1},{4,6},{5,7},{6,4},{7,5},{8,10},{9,11},{10,... | collective-permute-start | bytes 1179656 | tf_op jit(solution)/shard_map/ppermute | solution.py:84
  (30 other events, 40.4 us)

commit v18 on v17

--- a/solution.py
+++ b/solution.py
@@ -143,9 +143,11 @@
 
     outs = place(outs, block, me)
     ahead = behind = block
+    early = block
     far = count // 2
     for step in range(1, far + 1):
         if step == far and count % 2 == 0:
+            early = ahead
             rows = block.shape[0] // 2
             where = order[(my_pos - step) % count]
             front = lax.ppermute(ahead[:rows], "dp", forward)
@@ -164,7 +166,8 @@
         if step < far or count % 2 == 1:
             behind = lax.ppermute(behind, "dp", backward)
             outs = place(outs, behind, order[(my_pos + step) % count])
-    return outs
+        early = ahead
+    return outs, early
 
 
 def after(token, value):
@@ -224,7 +227,7 @@
     group_width = model_width // seq_count
     kernel_reach = dw_kernel.shape[0] // 2
     qkv_local = w_qkv.reshape(w_qkv.shape[0], 3 * group_width)
-    query_parts, key_parts, value_parts_a, out_parts = ring_gather(
+    (query_parts, key_parts, value_parts_a, out_parts), first_early = ring_gather(
         jnp.concatenate([qkv_local, w_out.T], axis=1),
         ring,
         [group_width, 2 * group_width, 3 * group_width],
@@ -234,8 +237,8 @@
     out_cols = out_parts.reshape(model_width, w_out.shape[0])
     glu_rows = w_glu.shape[0]
     glu_local = w_glu.reshape(glu_rows, 2 * group_width)
-    value_parts, gate_parts, proj_parts = ring_gather(
-        after(out_parts, jnp.concatenate([glu_local, w_proj.T], axis=1)),
+    (value_parts, gate_parts, proj_parts), _ = ring_gather(
+        after(first_early, jnp.concatenate([glu_local, w_proj.T], axis=1)),
         ring,
         [group_width, 2 * group_width],
     )

time: 149 us -> 172 us (1.15)
  local copies, waits for them, and re-layouts: 13.6 us -> 25.2 us
  waiting for transfers between devices: 63.6 us -> 75.1 us
  starting transfers between devices: 21.5 us -> 24.5 us
  other arithmetic: 16.4 us -> 14.2 us
    ppermute x6, waiting for transfers between devices: 38.2 us -> 23.1 us  [ring_gather(): ahead = lax.ppermute(ahead, 'dp', forward)]
    ppermute x2, waiting for transfers between devices: 0.01 us -> 11.1 us  [seq_gather(): lax.ppermute(block, 'seq', [(i, (i + 2 * shift) % count) for i in range(c...]
    ppermute x2, waiting for transfers between devices: 11.3 us -> 19.4 us  [seq_scatter_sum(): lax.ppermute(piece.astype(jnp.bfloat16), 'seq', [(i, (i + 2 * shift) % co...]
    dynamic_update_slice x19, local copies, waits for them, and re-layouts: 5.69 us -> 12 us  [place(): lax.dynamic_update_index_in_dim(out, piece[..., lo:hi], where, 0)]
    ppermute x2, waiting for transfers between devices: 9.13 us -> 13.2 us  [ring_gather(): front = lax.ppermute(ahead[:rows], 'dp', forward)]
    ppermute x2, waiting for transfers between devices: 2.27 us -> 4.52 us  [seq_scatter_sum(): got = lax.ppermute(theirs, 'seq', [(i, i ^ 1) for i in range(count)])]
    dynamic_update_slice x4, local copies, waits for them, and re-layouts: 0.13 us -> 2.12 us  [seq_gather(): out = lax.dynamic_update_index_in_dim(out, other[k], 2 * k + partner % 2, 0)]
    unnamed x109 -> x57, local copies, waits for them, and re-layouts: 2.42 us -> 4.33 us
  transfers between devices with their start and end apart: 24 -> 24, of which waited for: 11 -> 14; matrix products, arithmetic and copies ran while one was open for 20% -> 14% of each run, Pallas kernels for 0% -> 0%
where the time goes in v18:
time: 172 us; the launch traced here: 171 us
  waiting for transfers between devices  75.1 us (44%)
  local copies, waits for them, and re-layouts  25.2 us (15%)
  starting transfers between devices  24.5 us (14%)
  between operations  18.9 us (11%)
  other arithmetic  14.2 us (8%)
  matrix products  12.9 us (8%)
    ppermute x6, waiting for transfers between devices, ring_gather(): ahead = lax.ppermute(ahead, 'dp', forward)  23.1 us
    ppermute x2, waiting for transfers between devices, seq_scatter_sum(): lax.ppermute(piece.astype(jnp.bfloat16), 'seq', [(i, (i + 2 * shift) % co...  19.4 us
    ppermute x2, waiting for transfers between devices, ring_gather(): front = lax.ppermute(ahead[:rows], 'dp', forward)  13.2 us
    dynamic_update_slice x19, local copies, waits for them, and re-layouts, place(): lax.dynamic_update_index_in_dim(out, piece[..., lo:hi], where, 0)  12 us
    ppermute x6, starting transfers between devices, ring_gather(): ahead = lax.ppermute(ahead, 'dp', forward)  11.7 us
    ppermute x2, waiting for transfers between devices, seq_gather(): lax.ppermute(block, 'seq', [(i, (i + 2 * shift) % count) for i in range(c...  11.1 us
    convert_element_type x1, other arithmetic, depthwise(): return jax.nn.silu(total_acc).astype(jnp.bfloat16)  5.24 us
    ppermute x2, waiting for transfers between devices, seq_scatter_sum(): got = lax.ppermute(theirs, 'seq', [(i, i ^ 1) for i in range(count)])  4.52 us
  transfers between devices with their start and end apart: 24, of which 14 were waited for; matrix products, arithmetic and copies ran while one was open for 14% of the time, Pallas kernels for 0%

profile of v18, /device:TPU:0, one launch (start us, length us, event | category | flops | bytes accessed | tf_op | source)
XLA Modules:
  0.0 170.9 jit_solution(3142379246606665179)
XLA Ops:
  0.0 1.1 copy.28
  1.1 1.8 %pad_maximum_fusion = bf16[192,1536]{1,0:T(8,128)(2,1)} fusion(bf16[192,384]{1,0:T(8,128)(2,1)} %bitcast.383, bf16[192,1152]{1,0:T(8,128)(2,1)S(1)} %bitcast.368), kind=kLoop, calls=%fused_computation.53 | loop fusion | flops 1179648 | bytes 1179648 | tf_op jit(solution)/shard_map/concatenate | solution.py:231
  2.9 3.0 %collective-permute-start.2 = (bf16[192,1536]{1,0:T(8,128)(2,1)}, bf16[192,1536]{1,0:T(8,128)(2,1)}, u32[]{:S(2)}, u32[]{:S(2)}) collective-permute-start(bf16[192,1536]{1,0:T(8,128)(2,1)} %pad_maximum_fusion), channel_id=1, source_target_pairs={{0,8},{8,16},{16,24},{24,28},{28,20},{20,12},{12,4},{4,0},{1,9},{9... | collective-permute-start | bytes 1769480 | tf_op jit(solution)/shard_map/ppermute | solution.py:164
  6.7 2.0 %collective-permute-start = (bf16[128,1536]{1,0:T(8,128)(2,1)S(1)}, bf16[128,1536]{1,0:T(8,128)(2,1)}, u32[]{:S(2)}, u32[]{:S(2)}) collective-permute-start(bf16[128,1536]{1,0:T(8,128)(2,1)S(1)} %fusion.22), channel_id=1, source_target_pairs={{0,2},{1,3},{2,0},{3,1},{4,6},{5,7},{6,4},{7,5},{8,10},{9,11},{10,... | collective-permute-start | bytes 1179656 | tf_op jit(solution)/shard_map/ppermute | solution.py:36
  13.0 1.0 broadcast.151.clone
  14.0 1.0 constant_dynamic-update-slice_fusion
  15.0 2.4 %collective-permute-done = bf16[128,1536]{1,0:T(8,128)(2,1)} collective-permute-done((bf16[128,1536]{1,0:T(8,128)(2,1)S(1)}, bf16[128,1536]{1,0:T(8,128)(2,1)}, u32[]{:S(2)}, u32[]{:S(2)}) %collective-permute-start) | collective-permute-done | bytes 393248 | tf_op jit(solution)/shard_map/ppermute | solution.py:36
  17.4 1.8 %bitcast_dynamic-update-slice_fusion.4 = (bf16[2,128,1536]{2,1,0:T(8,128)(2,1)}, bf16[4,128,1536]{2,1,0:T(8,128)(2,1)S(1)}) fusion(bf16[2,128,1536]{2,1,0:T(8,128)(2,1)} %get-tuple-element.105, s32[]{:T(128)S(6)} %select_n.289, bf16[128,1536]{1,0:T(8,128)(2,1)} %collective-permute-done, bf16[4,128,1536]{2,1,0:T(8,128)(2,1)S(1)} %get-tuple-element.106, ...), kind=kLoop, calls=%fused_computation.68 | loop fusion | bytes 1179656 | tf_op jit(solution)/shard_map/jit(dynamic_update_index_in_dim)/dynamic_update_slice | solution.py:40
  19.5 1.8 %collective-permute-start.4 = (bf16[192,1536]{1,0:T(8,128)(2,1)}, bf16[192,1536]{1,0:T(8,128)(2,1)}, u32[]{:S(2)}, u32[]{:S(2)}) collective-permute-start(bf16[192,1536]{1,0:T(8,128)(2,1)} %collective-permute-done.2), channel_id=1, source_target_pairs={{0,8},{8,16},{16,24},{24,28},{28,20},{20,12},{12,4},{4,0},{1,9},{9... | collective-permute-start | bytes 1769480 | tf_op jit(solution)/shard_map/ppermute | solution.py:164
  41.3 1.9 %fusion.56 = (bf16[8,192,384]{2,1,0:T(8,128)(2,1)S(1)}, bf16[8,192,384]{2,1,0:T(8,128)(2,1)}, bf16[8,192,384]{2,1,0:T(8,128)(2,1)}, bf16[8,192,384]{2,1,0:T(8,128)(2,1)}) fusion(bf16[8,192,384]{2,1,0:T(8,128)(2,1)S(1)} %bitcast_dynamic-update-slice_fusion.6, s32[]{:T(128)S(6)} %select_n.296, bf16[192,1536]{1,0:T(8,128)(2,1)} %collective-permute-done.2, ...), kind=kLoop, calls=%fused_computation.122 | loop fusion | bytes 1179652 | tf_op jit(solution)/shard_map/jit(dynamic_update_index_in_dim)/dynamic_update_slice | solution.py:140
  43.2 1.9 %fusion.55 = (bf16[8,192,384]{2,1,0:T(8,128)(2,1)S(1)}, bf16[8,192,384]{2,1,0:T(8,128)(2,1)}, bf16[8,192,384]{2,1,0:T(8,128)(2,1)}, bf16[8,192,384]{2,1,0:T(8,128)(2,1)}) fusion(bf16[8,192,384]{2,1,0:T(8,128)(2,1)S(1)} %get-tuple-element.83, s32[]{:T(128)S(6)} %select_n.299, bf16[192,1536]{1,0:T(8,128)(2,1)} %collective-permute-done.3, ...), kind=kLoop, calls=%fused_computation.120 | loop fusion | bytes 1179652 | tf_op jit(solution)/shard_map/jit(dynamic_update_index_in_dim)/dynamic_update_slice | solution.py:140
  45.2 1.8 %collective-permute-start.6 = (bf16[192,1536]{1,0:T(8,128)(2,1)}, bf16[192,1536]{1,0:T(8,128)(2,1)S(1)}, u32[]{:S(2)}, u32[]{:S(2)}) collective-permute-start(bf16[192,1536]{1,0:T(8,128)(2,1)} %collective-permute-done.4), channel_id=1, source_target_pairs={{0,8},{8,16},{16,24},{24,28},{28,20},{20,12},{12,4},{4,0},{1,9},{9... | collective-permute-start | bytes 1769480 | tf_op jit(solution)/shard_map/ppermute | solution.py:164
  47.2 1.0 slice_dynamic-update-slice_fusion.3
  48.3 1.0 slice_dynamic-update-slice_fusion.2
  49.3 2.5 %fusion.54 = (bf16[8,192,384]{2,1,0:T(8,128)(2,1)S(1)}, bf16[8,192,384]{2,1,0:T(8,128)(2,1)}, bf16[8,192,384]{2,1,0:T(8,128)(2,1)}, bf16[8,192,384]{2,1,0:T(8,128)(2,1)S(1)}) fusion(bf16[8,192,384]{2,1,0:T(8,128)(2,1)S(1)} %get-tuple-element.79, s32[]{:T(128)S(6)} %select_n.302, bf16[192,1536]{1,0:T(8,128)(2,1)} %collective-permute-done.4, ...), kind=kLoop, calls=%fused_computation.118 | loop fusion | bytes 1179652 | tf_op jit(solution)/shard_map/jit(dynamic_update_index_in_dim)/dynamic_update_slice | solution.py:140
  51.8 1.9 %fusion.53 = (bf16[8,192,384]{2,1,0:T(8,128)(2,1)S(1)}, bf16[8,192,384]{2,1,0:T(8,128)(2,1)}, bf16[8,192,384]{2,1,0:T(8,128)(2,1)}, bf16[8,192,384]{2,1,0:T(8,128)(2,1)S(1)}) fusion(bf16[8,192,384]{2,1,0:T(8,128)(2,1)S(1)} %get-tuple-element.75, s32[]{:T(128)S(6)} %select_n.305, bf16[192,1536]{1,0:T(8,128)(2,1)} %collective-permute-done.5, ...), kind=kLoop, calls=%fused_computation.116 | loop fusion | bytes 1179652 | tf_op jit(solution)/shard_map/jit(dynamic_update_index_in_dim)/dynamic_update_slice | solution.py:140
  53.7 6.7 %collective-permute-done.6 = bf16[192,1536]{1,0:T(8,128)(2,1)S(1)} collective-permute-done((bf16[192,1536]{1,0:T(8,128)(2,1)}, bf16[192,1536]{1,0:T(8,128)(2,1)S(1)}, u32[]{:S(2)}, u32[]{:S(2)}) %collective-permute-start.6) | collective-permute-done | bytes 589856 | tf_op jit(solution)/shard_map/ppermute | solution.py:164
  60.4 1.7 %collective-permute-start.14 = (bf16[192,1152]{1,0:T(8,128)(2,1)}, bf16[192,1152]{1,0:T(8,128)(2,1)S(1)}, u32[]{:S(2)}, u32[]{:S(2)}) collective-permute-start(bf16[192,1152]{1,0:T(8,128)(2,1)} %pad_maximum_fusion.1), channel_id=1, source_target_pairs={{0,8},{8,16},{16,24},{24,28},{28,20},{20,12},{12,4},{4,0},{1,9},{9... | collective-permute-start | bytes 1327112 | tf_op jit(solution)/shard_map/ppermute | solution.py:164
  62.5 1.8 %collective-permute-start.8 = (bf16[96,1536]{1,0:T(8,128)(2,1)S(1)}, bf16[96,1536]{1,0:T(8,128)(2,1)S(1)}, u32[]{:S(2)}, u32[]{:S(2)}) collective-permute-start(bf16[96,1536]{1,0:T(8,128)(2,1)S(1)} %slice.658), channel_id=1, source_target_pairs={{0,8},{8,16},{16,24},{24,28},{28,20},{20,12},{12,4},{4,0},{1,9},{9... | collective-permute-start | bytes 884744 | tf_op jit(solution)/shard_map/ppermute | solution.py:153
  64.4 1.1 bitcast_dynamic-update-slice_fusion.7
  65.6 0.9 bitcast_dynamic-update-slice_fusion.8
  68.2 9.7 %collective-permute-done.8 = bf16[96,1536]{1,0:T(8,128)(2,1)S(1)} collective-permute-done((bf16[96,1536]{1,0:T(8,128)(2,1)S(1)}, bf16[96,1536]{1,0:T(8,128)(2,1)S(1)}, u32[]{:S(2)}, u32[]{:S(2)}) %collective-permute-start.8) | collective-permute-done | bytes 294944 | tf_op jit(solution)/shard_map/ppermute | solution.py:153
  78.0 1.7 collective-permute-start.16
  80.3 8.1 %collective-permute-done.16 = bf16[192,1152]{1,0:T(8,128)(2,1)S(1)} collective-permute-done((bf16[192,1152]{1,0:T(8,128)(2,1)S(1)}, bf16[192,1152]{1,0:T(8,128)(2,1)S(1)}, u32[]{:S(2)}, u32[]{:S(2)}) %collective-permute-start.16) | collective-permute-done | bytes 442400 | tf_op jit(solution)/shard_map/ppermute | solution.py:164
  88.4 1.6 collective-permute-start.18
  90.6 8.1 %collective-permute-done.18 = bf16[192,1152]{1,0:T(8,128)(2,1)S(1)} collective-permute-done((bf16[192,1152]{1,0:T(8,128)(2,1)S(1)}, bf16[192,1152]{1,0:T(8,128)(2,1)S(1)}, u32[]{:S(2)}, u32[]{:S(2)}) %collective-permute-start.18) | collective-permute-done | bytes 442400 | tf_op jit(solution)/shard_map/ppermute | solution.py:164
  98.7 1.7 collective-permute-start.20
  101.2 3.5 %collective-permute-done.20 = bf16[96,1152]{1,0:T(8,128)(2,1)S(1)} collective-permute-done((bf16[96,1152]{1,0:T(8,128)(2,1)S(1)}, bf16[96,1152]{1,0:T(8,128)(2,1)S(1)}, u32[]{:S(2)}, u32[]{:S(2)}) %collective-permute-start.20) | collective-permute-done | bytes 221216 | tf_op jit(solution)/shard_map/ppermute | solution.py:153
  104.7 1.8 %collective-permute-done.21 = bf16[96,1152]{1,0:T(8,128)(2,1)S(1)} collective-permute-done((bf16[96,1152]{1,0:T(8,128)(2,1)S(1)}, bf16[96,1152]{1,0:T(8,128)(2,1)S(1)}, u32[]{:S(2)}, u32[]{:S(2)}) %collective-permute-start.21) | collective-permute-done | bytes 221216 | tf_op jit(solution)/shard_map/ppermute | solution.py:154
  106.7 1.0 copy-done.7
  107.7 1.0 copy-done.13
  111.2 3.6 %fusion.128 = (f32[4,512]{1,0:T(4,128)S(1)}, f32[4,512,512]{1,2,0:T(8,128)}) fusion(pred[512,512]{0,1:T(8,128)(4,1)S(1)} %broadcast_compare_fusion, bf16[512,4,96]{0,2,1:T(8,128)(2,1)S(1)} %bitcast.393, bf16[512,4,96]{0,2,1:T(8,128)(2,1)S(1)} %bitcast.391), kind=kOutput, calls=%fused_computation.303 | convolution fusion | flops 205521408 | bytes 5251072 | tf_op jit(solution)/shard_map/while/body/eval_jaxpr/sub | solution.py:196
  114.8 2.7 %fusion.10 = bf16[4,96,512]{2,1,0:T(8,128)(2,1)S(1)} fusion(bf16[512,4,96]{0,2,1:T(8,128)(2,1)S(1)} %bitcast.392, f32[4,512,512]{1,2,0:T(8,128)} %get-tuple-element.164, f32[4,512]{1,0:T(4,128)S(1)} %get-tuple-element.163), kind=kOutput, calls=%fused_computation.19 | convolution fusion | flops 203620352 | bytes 4988928 | tf_op jit(solution)/shard_map/while/body/eval_jaxpr/hqk,khe->qhe/dot_general | solution.py:198
  117.5 1.0 convolution_convert_fusion.1
  118.7 2.4 %collective-permute-done.10 = bf16[2,128,1536]{2,1,0:T(8,128)(2,1)} collective-permute-done((bf16[2,128,1536]{2,1,0:T(8,128)(2,1)S(1)}, bf16[2,128,1536]{2,1,0:T(8,128)(2,1)}, u32[]{:S(2)}, u32[]{:S(2)}) %collective-permute-start.10) | collective-permute-done | bytes 786464 | tf_op jit(solution)/shard_map/ppermute | solution.py:78
  121.1 1.3 convert_add_fusion.1
  122.5 1.5 collective-permute-start.11
  124.0 9.7 %collective-permute-done.11 = bf16[128,1536]{1,0:T(8,128)(2,1)S(1)} collective-permute-done((bf16[128,1536]{1,0:T(8,128)(2,1)S(1)}, bf16[128,1536]{1,0:T(8,128)(2,1)S(1)}, u32[]{:S(2)}, u32[]{:S(2)}) %collective-permute-start.11) | collective-permute-done | bytes 393248 | tf_op jit(solution)/shard_map/ppermute | solution.py:84
  134.6 1.5 collective-permute-start.12
  136.3 8.7 %collective-permute-done.12 = bf16[128,1536]{1,0:T(8,128)(2,1)S(1)} collective-permute-done((bf16[128,1536]{1,0:T(8,128)(2,1)S(1)}, bf16[128,1536]{1,0:T(8,128)(2,1)S(1)}, u32[]{:S(2)}, u32[]{:S(2)}) %collective-permute-start.12) | collective-permute-done | bytes 393248 | tf_op jit(solution)/shard_map/ppermute | solution.py:36
  145.6 1.8 %collective-permute-done.13 = bf16[2,128,1536]{2,1,0:T(8,128)(2,1)S(1)} collective-permute-done((bf16[2,128,1536]{2,1,0:T(8,128)(2,1)S(1)}, bf16[2,128,1536]{2,1,0:T(8,128)(2,1)S(1)}, u32[]{:S(2)}, u32[]{:S(2)}) %collective-permute-start.13) | collective-permute-done | bytes 786464 | tf_op jit(solution)/shard_map/ppermute | solution.py:42
  147.5 1.1 fusion.8
  148.8 1.0 fusion.9
  149.8 5.2 %multiply_convert_fusion = bf16[512,384]{1,0:T(8,128)(2,1)S(1)} fusion(bf16[512,384]{1,0:T(8,128)(2,1)S(1)} %fusion.9, f32[512]{0:T(512)S(1)} %get-tuple-element.155, f32[384]{0:T(512)S(1)} %get-tuple-element.57, f32[512]{0:T(512)S(1)} %get-tuple-element.126, f32[384]{0:T(512)S(1)} %get-tuple-element.58, f32[512]{0:T(512)S(1)} %get-tuple-element.127, ...), kind=kLoop, calls=%fused_computation.50 | loop fusion | flops 25165824 | bytes 897536 | tf_op jit(solution)/shard_map/convert_element_type | solution.py:219
  155.0 1.0 convolution_convert_fusion
  156.3 2.1 %collective-permute-done.22 = bf16[2,128,1536]{2,1,0:T(8,128)(2,1)S(1)} collective-permute-done((bf16[2,128,1536]{2,1,0:T(8,128)(2,1)S(1)}, bf16[2,128,1536]{2,1,0:T(8,128)(2,1)S(1)}, u32[]{:S(2)}, u32[]{:S(2)}) %collective-permute-start.22) | collective-permute-done | bytes 786464 | tf_op jit(solution)/shard_map/ppermute | solution.py:78
  158.8 1.5 collective-permute-start.23
  160.3 9.7 %collective-permute-done.23 = bf16[128,1536]{1,0:T(8,128)(2,1)S(1)} collective-permute-done((bf16[128,1536]{1,0:T(8,128)(2,1)S(1)}, bf16[128,1536]{1,0:T(8,128)(2,1)S(1)}, u32[]{:S(2)}, u32[]{:S(2)}) %collective-permute-start.23) | collective-permute-done | bytes 393248 | tf_op jit(solution)/shard_map/ppermute | solution.py:84
  (143 shorter events, 17.4 us)
Async XLA Ops:
  0.0 5.9 %copy-start = (bf16[1,128,1536]{2,1,0:T(8,128)(2,1)S(1)}, bf16[1,128,1536]{2,1,0:T(8,128)(2,1)}, u32[]{:S(2)}) copy-start(bf16[1,128,1536]{2,1,0:T(8,128)(2,1)} %param.13) | copy-start | bytes 1179652
  1.1 5.2 %copy-start.19 = (f32[1536]{0:T(1024)S(1)}, f32[1536]{0:T(1024)}, u32[]{:S(2)}) copy-start(f32[1536]{0:T(1024)} %param.15) | copy-start | bytes 18436
  2.9 16.6 %collective-permute-start.2 = (bf16[192,1536]{1,0:T(8,128)(2,1)}, bf16[192,1536]{1,0:T(8,128)(2,1)}, u32[]{:S(2)}, u32[]{:S(2)}) collective-permute-start(bf16[192,1536]{1,0:T(8,128)(2,1)} %pad_maximum_fusion), channel_id=1, source_target_pairs={{0,8},{8,16},{16,24},{24,28},{28,20},{20,12},{12,4},{4,0},{1,9},{9... | collective-permute-start | bytes 1769480 | tf_op jit(solution)/shard_map/ppermute | solution.py:164
  5.9 15.4 %collective-permute-start.3 = (bf16[192,1536]{1,0:T(8,128)(2,1)}, bf16[192,1536]{1,0:T(8,128)(2,1)}, u32[]{:S(2)}, u32[]{:S(2)}) collective-permute-start(bf16[192,1536]{1,0:T(8,128)(2,1)} %pad_maximum_fusion), channel_id=1, source_target_pairs={{0,4},{8,0},{16,8},{24,16},{28,24},{20,28},{12,20},{4,12},{1,5},{9... | collective-permute-start | bytes 1769480 | tf_op jit(solution)/shard_map/ppermute | solution.py:167
  6.4 2.4 %copy-start.22 = (f32[128]{0:T(128)}, f32[128]{0:T(128)S(1)}, u32[]{:S(2)}) copy-start(f32[128]{0:T(128)S(1)} %add_rsqrt_fusion.1) | copy-start | bytes 1540
  6.7 10.7 %collective-permute-start = (bf16[128,1536]{1,0:T(8,128)(2,1)S(1)}, bf16[128,1536]{1,0:T(8,128)(2,1)}, u32[]{:S(2)}, u32[]{:S(2)}) collective-permute-start(bf16[128,1536]{1,0:T(8,128)(2,1)S(1)} %fusion.22), channel_id=1, source_target_pairs={{0,2},{1,3},{2,0},{3,1},{4,6},{5,7},{6,4},{7,5},{8,10},{9,11},{10,... | collective-permute-start | bytes 1179656 | tf_op jit(solution)/shard_map/ppermute | solution.py:36
  9.9 1.1 copy-start.15
  10.0 1.3 copy-start.16
  10.0 1.3 copy-start.26
  10.0 2.1 %copy-start.17 = (bf16[384,192]{0,1:T(8,128)(2,1)S(1)}, bf16[384,192]{0,1:T(8,128)(2,1)}, u32[]{:S(2)}) copy-start(bf16[384,192]{0,1:T(8,128)(2,1)} %param.21) | copy-start | bytes 442372
  10.1 1.2 copy-start.5
  12.9 1.1 copy-start.23
  14.0 5.2 %copy-start.24 = (s32[4,1]{0,1:T(1,128)S(1)}, s32[4,1]{0,1:T(1,128)}, u32[]{:S(2)}) copy-start(s32[4,1]{0,1:T(1,128)} %reduce-window.8) | copy-start | bytes 52
  14.0 7.8 %copy-start.27 = (s32[8]{0:T(128)S(1)}, s32[8]{0:T(128)}, u32[]{:S(2)}) copy-start(s32[8]{0:T(128)} %constant.377.clone) | copy-start | bytes 100
  14.0 13.0 %copy-start.20 = (s32[8]{0:T(128)S(1)}, s32[8]{0:T(128)}, u32[]{:S(2)}) copy-start(s32[8]{0:T(128)} %constant.378.clone) | copy-start | bytes 100
  19.2 28.0 %collective-permute-start.1 = (bf16[2,128,1536]{2,1,0:T(8,128)(2,1)}, bf16[2,128,1536]{2,1,0:T(8,128)(2,1)}, u32[]{:S(2)}, u32[]{:S(2)}) collective-permute-start(bf16[2,128,1536]{2,1,0:T(8,128)(2,1)} %get-tuple-element.109), channel_id=1, source_target_pairs={{0,1},{1,0},{2,3},{3,2},{4,5},{5,4},{6,7},{7,6},{8,9},{9,8},{10,11... | collective-permute-start | bytes 2359304 | tf_op jit(solution)/shard_map/ppermute | solution.py:42
  19.5 25.6 %collective-permute-start.4 = (bf16[192,1536]{1,0:T(8,128)(2,1)}, bf16[192,1536]{1,0:T(8,128)(2,1)}, u32[]{:S(2)}, u32[]{:S(2)}) collective-permute-start(bf16[192,1536]{1,0:T(8,128)(2,1)} %collective-permute-done.2), channel_id=1, source_target_pairs={{0,8},{8,16},{16,24},{24,28},{28,20},{20,12},{12,4},{4,0},{1,9},{9... | collective-permute-start | bytes 1769480 | tf_op jit(solution)/shard_map/ppermute | solution.py:164
  21.3 25.7 %collective-permute-start.5 = (bf16[192,1536]{1,0:T(8,128)(2,1)}, bf16[192,1536]{1,0:T(8,128)(2,1)}, u32[]{:S(2)}, u32[]{:S(2)}) collective-permute-start(bf16[192,1536]{1,0:T(8,128)(2,1)} %collective-permute-done.3), channel_id=1, source_target_pairs={{0,4},{8,0},{16,8},{24,16},{28,24},{20,28},{12,20},{4,12},{1,5},{9... | collective-permute-start | bytes 1769480 | tf_op jit(solution)/shard_map/ppermute | solution.py:167
  45.2 4.1 %copy-start.6 = (bf16[8,192,384]{2,1,0:T(8,128)(2,1)S(1)}, bf16[8,192,384]{2,1,0:T(8,128)(2,1)}, u32[]{:S(2)}) copy-start(bf16[8,192,384]{2,1,0:T(8,128)(2,1)} %get-tuple-element.82) | copy-start | bytes 3538948
  45.2 15.3 %collective-permute-start.6 = (bf16[192,1536]{1,0:T(8,128)(2,1)}, bf16[192,1536]{1,0:T(8,128)(2,1)S(1)}, u32[]{:S(2)}, u32[]{:S(2)}) collective-permute-start(bf16[192,1536]{1,0:T(8,128)(2,1)} %collective-permute-done.4), channel_id=1, source_target_pairs={{0,8},{8,16},{16,24},{24,28},{28,20},{20,12},{12,4},{4,0},{1,9},{9... | collective-permute-start | bytes 1769480 | tf_op jit(solution)/shard_map/ppermute | solution.py:164
  47.0 19.6 %collective-permute-start.7 = (bf16[192,1536]{1,0:T(8,128)(2,1)}, bf16[192,1536]{1,0:T(8,128)(2,1)S(1)}, u32[]{:S(2)}, u32[]{:S(2)}) collective-permute-start(bf16[192,1536]{1,0:T(8,128)(2,1)} %collective-permute-done.5), channel_id=1, source_target_pairs={{0,4},{8,0},{16,8},{24,16},{28,24},{20,28},{12,20},{4,12},{1,5},{9... | collective-permute-start | bytes 1769480 | tf_op jit(solution)/shard_map/ppermute | solution.py:167
  49.3 4.4 %copy-start.3 = (bf16[4,128,1536]{2,1,0:T(8,128)(2,1)}, bf16[4,128,1536]{2,1,0:T(8,128)(2,1)S(1)}, u32[]{:S(2)}) copy-start(bf16[4,128,1536]{2,1,0:T(8,128)(2,1)S(1)} %slice_dynamic-update-slice_fusion.2) | copy-start | bytes 4718596
  60.4 17.6 %collective-permute-start.14 = (bf16[192,1152]{1,0:T(8,128)(2,1)}, bf16[192,1152]{1,0:T(8,128)(2,1)S(1)}, u32[]{:S(2)}, u32[]{:S(2)}) collective-permute-start(bf16[192,1152]{1,0:T(8,128)(2,1)} %pad_maximum_fusion.1), channel_id=1, source_target_pairs={{0,8},{8,16},{16,24},{24,28},{28,20},{20,12},{12,4},{4,0},{1,9},{9... | collective-permute-start | bytes 1327112 | tf_op jit(solution)/shard_map/ppermute | solution.py:164
  62.2 17.6 %collective-permute-start.15 = (bf16[192,1152]{1,0:T(8,128)(2,1)}, bf16[192,1152]{1,0:T(8,128)(2,1)S(1)}, u32[]{:S(2)}, u32[]{:S(2)}) collective-permute-start(bf16[192,1152]{1,0:T(8,128)(2,1)} %pad_maximum_fusion.1), channel_id=1, source_target_pairs={{0,4},{8,0},{16,8},{24,16},{28,24},{20,28},{12,20},{4,12},{1,5},{9... | collective-permute-start | bytes 1327112 | tf_op jit(solution)/shard_map/ppermute | solution.py:167
  62.5 15.5 %collective-permute-start.8 = (bf16[96,1536]{1,0:T(8,128)(2,1)S(1)}, bf16[96,1536]{1,0:T(8,128)(2,1)S(1)}, u32[]{:S(2)}, u32[]{:S(2)}) collective-permute-start(bf16[96,1536]{1,0:T(8,128)(2,1)S(1)} %slice.658), channel_id=1, source_target_pairs={{0,8},{8,16},{16,24},{24,28},{28,20},{20,12},{12,4},{4,0},{1,9},{9... | collective-permute-start | bytes 884744 | tf_op jit(solution)/shard_map/ppermute | solution.py:153
  64.4 2.6 %copy-start.10 = (bf16[8,192,384]{2,1,0:T(8,128)(2,1)S(1)}, bf16[8,192,384]{2,1,0:T(8,128)(2,1)}, u32[]{:S(2)}) copy-start(bf16[8,192,384]{2,1,0:T(8,128)(2,1)} %get-tuple-element.72) | copy-start | bytes 3538948
  64.4 2.6 %copy-start.12 = (bf16[8,192,384]{2,1,0:T(8,128)(2,1)S(1)}, bf16[8,192,384]{2,1,0:T(8,128)(2,1)}, u32[]{:S(2)}) copy-start(bf16[8,192,384]{2,1,0:T(8,128)(2,1)} %get-tuple-element.73) | copy-start | bytes 3538948
  66.6 38.2 %collective-permute-start.9 = (bf16[96,1536]{1,0:T(8,128)(2,1)S(1)}, bf16[96,1536]{1,0:T(8,128)(2,1)S(1)}, u32[]{:S(2)}, u32[]{:S(2)}) collective-permute-start(bf16[96,1536]{1,0:T(8,128)(2,1)S(1)} %slice.660), channel_id=1, source_target_pairs={{0,4},{8,0},{16,8},{24,16},{28,24},{20,28},{12,20},{4,12},{1,5},{9... | collective-permute-start | bytes 884744 | tf_op jit(solution)/shard_map/ppermute | solution.py:154
  78.0 10.4 %collective-permute-start.16 = (bf16[192,1152]{1,0:T(8,128)(2,1)S(1)}, bf16[192,1152]{1,0:T(8,128)(2,1)S(1)}, u32[]{:S(2)}, u32[]{:S(2)}) collective-permute-start(bf16[192,1152]{1,0:T(8,128)(2,1)S(1)} %collective-permute-done.14), channel_id=1, source_target_pairs={{0,8},{8,16},{16,24},{24,28},{28,20},{20,12},{12,4},{4,0},{1,9},{9... | collective-permute-start | bytes 1327112 | tf_op jit(solution)/shard_map/ppermute | solution.py:164
  79.7 10.3 %collective-permute-start.17 = (bf16[192,1152]{1,0:T(8,128)(2,1)S(1)}, bf16[192,1152]{1,0:T(8,128)(2,1)S(1)}, u32[]{:S(2)}, u32[]{:S(2)}) collective-permute-start(bf16[192,1152]{1,0:T(8,128)(2,1)S(1)} %collective-permute-done.15), channel_id=1, source_target_pairs={{0,4},{8,0},{16,8},{24,16},{28,24},{20,28},{12,20},{4,12},{1,5},{9... | collective-permute-start | bytes 1327112 | tf_op jit(solution)/shard_map/ppermute | solution.py:167
  88.4 10.3 %collective-permute-start.18 = (bf16[192,1152]{1,0:T(8,128)(2,1)S(1)}, bf16[192,1152]{1,0:T(8,128)(2,1)S(1)}, u32[]{:S(2)}, u32[]{:S(2)}) collective-permute-start(bf16[192,1152]{1,0:T(8,128)(2,1)S(1)} %collective-permute-done.16), channel_id=1, source_target_pairs={{0,8},{8,16},{16,24},{24,28},{28,20},{20,12},{12,4},{4,0},{1,9},{9... | collective-permute-start | bytes 1327112 | tf_op jit(solution)/shard_map/ppermute | solution.py:164
  90.1 10.3 %collective-permute-start.19 = (bf16[192,1152]{1,0:T(8,128)(2,1)S(1)}, bf16[192,1152]{1,0:T(8,128)(2,1)S(1)}, u32[]{:S(2)}, u32[]{:S(2)}) collective-permute-start(bf16[192,1152]{1,0:T(8,128)(2,1)S(1)} %collective-permute-done.17), channel_id=1, source_target_pairs={{0,4},{8,0},{16,8},{24,16},{28,24},{20,28},{12,20},{4,12},{1,5},{9... | collective-permute-start | bytes 1327112 | tf_op jit(solution)/shard_map/ppermute | solution.py:167
  98.7 6.0 %collective-permute-start.20 = (bf16[96,1152]{1,0:T(8,128)(2,1)S(1)}, bf16[96,1152]{1,0:T(8,128)(2,1)S(1)}, u32[]{:S(2)}, u32[]{:S(2)}) collective-permute-start(bf16[96,1152]{1,0:T(8,128)(2,1)S(1)} %slice.696), channel_id=1, source_target_pairs={{0,8},{8,16},{16,24},{24,28},{28,20},{20,12},{12,4},{4,0},{1,9},{9... | collective-permute-start | bytes 663560 | tf_op jit(solution)/shard_map/ppermute | solution.py:153
  100.4 6.2 %collective-permute-start.21 = (bf16[96,1152]{1,0:T(8,128)(2,1)S(1)}, bf16[96,1152]{1,0:T(8,128)(2,1)S(1)}, u32[]{:S(2)}, u32[]{:S(2)}) collective-permute-start(bf16[96,1152]{1,0:T(8,128)(2,1)S(1)} %slice.698), channel_id=1, source_target_pairs={{0,4},{8,0},{16,8},{24,16},{28,24},{20,28},{12,20},{4,12},{1,5},{9... | collective-permute-start | bytes 663560 | tf_op jit(solution)/shard_map/ppermute | solution.py:154
  101.1 7.6 %copy-start.4 = (bf16[4,128,1536]{2,1,0:T(8,128)(2,1)S(1)}, bf16[4,128,1536]{2,1,0:T(8,128)(2,1)}, u32[]{:S(2)}) copy-start(bf16[4,128,1536]{2,1,0:T(8,128)(2,1)} %copy-done.3) | copy-start | bytes 4718596
  107.7 1.8 %copy-start.1 = (bf16[8,192,384]{2,1,0:T(8,128)(2,1)}, bf16[8,192,384]{2,1,0:T(8,128)(2,1)S(1)}, u32[]{:S(2)}) copy-start(bf16[8,192,384]{2,1,0:T(8,128)(2,1)S(1)} %get-tuple-element.119) | copy-start | bytes 3538948
  118.6 2.5 %collective-permute-start.10 = (bf16[2,128,1536]{2,1,0:T(8,128)(2,1)S(1)}, bf16[2,128,1536]{2,1,0:T(8,128)(2,1)}, u32[]{:S(2)}, u32[]{:S(2)}) collective-permute-start(bf16[2,128,1536]{2,1,0:T(8,128)(2,1)S(1)} %dynamic-slice_bitcast_fusion.1), channel_id=1, source_target_pairs={{0,1},{1,0},{2,3},{3,2},{4,5},{5,4},{6,7},{7,6},{8,9},{9,8},{10,11... | collective-permute-start | bytes 2359304 | tf_op jit(solution)/shard_map/ppermute | solution.py:78
  122.5 11.2 %collective-permute-start.11 = (bf16[128,1536]{1,0:T(8,128)(2,1)S(1)}, bf16[128,1536]{1,0:T(8,128)(2,1)S(1)}, u32[]{:S(2)}, u32[]{:S(2)}) collective-permute-start(bf16[128,1536]{1,0:T(8,128)(2,1)S(1)} %fusion.30), channel_id=1, source_target_pairs={{0,2},{1,3},{2,0},{3,1},{4,6},{5,7},{6,4},{7,5},{8,10},{9,11},{10,... | collective-permute-start | bytes 1179656 | tf_op jit(solution)/shard_map/ppermute | solution.py:84
  124.0 10.3 %copy-start.21 = (f32[1536]{0:T(1024)S(1)}, f32[1536]{0:T(1024)}, u32[]{:S(2)}) copy-start(f32[1536]{0:T(1024)} %param.16) | copy-start | bytes 18436
  134.6 10.4 %collective-permute-start.12 = (bf16[128,1536]{1,0:T(8,128)(2,1)S(1)}, bf16[128,1536]{1,0:T(8,128)(2,1)S(1)}, u32[]{:S(2)}, u32[]{:S(2)}) collective-permute-start(bf16[128,1536]{1,0:T(8,128)(2,1)S(1)} %get-tuple-element.60), channel_id=1, source_target_pairs={{0,2},{1,3},{2,0},{3,1},{4,6},{5,7},{6,4},{7,5},{8,10},{9,11},{10,... | collective-permute-start | bytes 1179656 | tf_op jit(solution)/shard_map/ppermute | solution.py:36
  136.2 8.9 %copy-start.25 = (s32[4,1]{0,1:T(1,128)S(1)}, s32[4,1]{0,1:T(1,128)}, u32[]{:S(2)}) copy-start(s32[4,1]{0,1:T(1,128)} %reduce-window.8) | copy-start | bytes 52
  136.3 9.0 %copy-start.18 = (bf16[31,384]{1,0:T(8,128)(2,1)S(1)}, bf16[31,384]{1,0:T(8,128)(2,1)}, u32[]{:S(2)}) copy-start(bf16[31,384]{1,0:T(8,128)(2,1)} %param.20) | copy-start | bytes 71428
  145.1 2.4 %copy-start.14 = (bf16[8,192,384]{2,1,0:T(8,128)(2,1)S(1)}, bf16[8,192,384]{2,1,0:T(8,128)(2,1)}, u32[]{:S(2)}) copy-start(bf16[8,192,384]{2,1,0:T(8,128)(2,1)} %copy-done.13) | copy-start | bytes 3538948
  145.1 2.4 %collective-permute-start.13 = (bf16[2,128,1536]{2,1,0:T(8,128)(2,1)S(1)}, bf16[2,128,1536]{2,1,0:T(8,128)(2,1)S(1)}, u32[]{:S(2)}, u32[]{:S(2)}) collective-permute-start(bf16[2,128,1536]{2,1,0:T(8,128)(2,1)S(1)} %get-tuple-element.107), channel_id=1, source_target_pairs={{0,1},{1,0},{2,3},{3,2},{4,5},{5,4},{6,7},{7,6},{8,9},{9,8},{10,11... | collective-permute-start | bytes 2359304 | tf_op jit(solution)/shard_map/ppermute | solution.py:42
  147.5 1.3 copy-start.8
  148.8 6.2 %copy-start.2 = (bf16[8,192,384]{2,1,0:T(8,128)(2,1)S(1)}, bf16[8,192,384]{2,1,0:T(8,128)(2,1)}, u32[]{:S(2)}) copy-start(bf16[8,192,384]{2,1,0:T(8,128)(2,1)} %copy-done.1) | copy-start | bytes 3538948
  156.1 2.4 %collective-permute-start.22 = (bf16[2,128,1536]{2,1,0:T(8,128)(2,1)S(1)}, bf16[2,128,1536]{2,1,0:T(8,128)(2,1)S(1)}, u32[]{:S(2)}, u32[]{:S(2)}) collective-permute-start(bf16[2,128,1536]{2,1,0:T(8,128)(2,1)S(1)} %dynamic-slice_bitcast_fusion), channel_id=1, source_target_pairs={{0,1},{1,0},{2,3},{3,2},{4,5},{5,4},{6,7},{7,6},{8,9},{9,8},{10,11... | collective-permute-start | bytes 2359304 | tf_op jit(solution)/shard_map/ppermute | solution.py:78
  158.8 11.2 %collective-permute-start.23 = (bf16[128,1536]{1,0:T(8,128)(2,1)S(1)}, bf16[128,1536]{1,0:T(8,128)(2,1)S(1)}, u32[]{:S(2)}, u32[]{:S(2)}) collective-permute-start(bf16[128,1536]{1,0:T(8,128)(2,1)S(1)} %fusion.31), channel_id=1, source_target_pairs={{0,2},{1,3},{2,0},{3,1},{4,6},{5,7},{6,4},{7,5},{8,10},{9,11},{10,... | collective-permute-start | bytes 1179656 | tf_op jit(solution)/shard_map/ppermute | solution.py:84
  (4 other events, 4.1 us)
